TPU v7x, 32 devices: a whole 2x2x4 slice. The times are simulated.
32 devices in a mesh: row: 4 (over y, x), col: 8 (over z, core).
Axes of the slice: x: 2, y: 2, z: 4, core: 2. Of those that a mesh axis runs over, the one named last changes fastest.
Arguments:
- matrix_in: bfloat16 [2048, 2048], P('row', 'col'), as said below
- pattern: int32 [16, 16], replicated, may hold values from 0 to 1, as said below
Outputs:
- sign_step: float32 [2048, 2048], P('row', 'col')
Inputs may be any that keep to these rules, and one draw needn't show every extreme that they name: `pattern`: symmetric, every diagonal block is 1, and every block (i, (i + 8) mod 16) is 1. `matrix_in`: exactly symmetric.
All inputs are finite; a program needn't handle non-finite values.
Results may differ from a plain program's by a relative error of at most 0.0029.
Values may be sent and summed in bfloat16 or wider, within the bound.
No kernel may reach another device: no remote copies, remote signals or barrier semaphores. Data moves between devices by JAX's collectives and lax.ppermute only.
A program may use at most 64 MiB of HBM per device.

v0:
```python
import jax
import jax.numpy as jnp
from jax import lax
from jax.sharding import PartitionSpec as P

B = 128


def body(matrix_in, pattern):
    block_rows = matrix_in.shape[0] // B
    block_cols = matrix_in.shape[1] // B
    row_index = lax.axis_index("row")
    col_index = lax.axis_index("col")
    local_blocks = lax.dynamic_slice(
        pattern, (row_index * block_rows, col_index * block_cols), (block_rows, block_cols)
    )
    local_mask = jnp.repeat(jnp.repeat(local_blocks, B, axis=0), B, axis=1)
    masked = matrix_in * local_mask.astype(jnp.bfloat16)
    rows_all = lax.all_gather(masked, "col", axis=1, tiled=True)
    left_part = rows_all
    square = jnp.dot(
        left_part,
        lax.all_gather(masked, "row", axis=0, tiled=True),
        preferred_element_type=jnp.float32,
    )
    mask_float = local_mask.astype(jnp.float32)
    filtered = (mask_float * square).astype(jnp.bfloat16)
    left_part = rows_all
    cubic = jnp.dot(
        left_part,
        lax.all_gather(filtered, "row", axis=0, tiled=True),
        preferred_element_type=jnp.float32,
    )
    return mask_float * (1.5 * masked.astype(jnp.float32) - 0.5 * cubic)


def solution(mesh):
    return jax.shard_map(
        body,
        mesh=mesh,
        in_specs=(P("row", "col"), P()),
        out_specs=P("row", "col"),
        check_vma=False,
    )
```

profile of v0, /device:TPU:16, one launch (start us, length us, event | category | flops | bytes accessed | tf_op | source)
XLA Modules:
  0.0 109.2 jit_solution(12114034085471506654)
XLA Ops:
  6.5 0.0 all-gather.6.cloned.1.call-start
  6.5 0.8 dynamic-slice_convert_fusion.1
  7.3 0.6 broadcast_in_dim.13
  7.9 1.7 %bitcast_multiply_fusion = bf16[512,256]{1,0:T(8,128)(2,1)} fusion(bf16[512,256]{1,0:T(8,128)(2,1)} %param.2, bf16[64,8,2,128]{3,2,1,0:T(2,128)(2,1)S(1)} %bitcast.13), kind=kLoop, calls=%fused_computation.5 | loop fusion | flops 131072 | bytes 786432 | tf_op jit(solution)/shard_map/mul | solution.py:18
  9.6 0.0 all-gather.6.cloned.1.call-update
  9.6 0.0 all-gather.4.cloned.1.call-start
  9.7 0.7 all-gather.4.cloned.1.call-update
  10.4 0.0 all-gather.8.cloned.1.call-start
  10.4 27.1 %all-gather.6.cloned.1.call-done = bf16[2048,256]{1,0:T(8,128)(2,1)} async-done(((bf16[512,256]{1,0:T(8,128)(2,1)}), bf16[2048,256]{1,0:T(8,128)(2,1)}) %all-gather.6.cloned.1.call-update) | async-done | bytes 1048592 | tf_op jit(solution)/shard_map/all_gather | solution.py:23
  37.5 30.5 %all-gather.4.cloned.1.call-done = bf16[512,2048]{1,0:T(8,128)(2,1)} async-done(((bf16[512,256]{1,0:T(8,128)(2,1)}), bf16[512,2048]{1,0:T(8,128)(2,1)}) %all-gather.4.cloned.1.call-update) | async-done | bytes 2097168 | tf_op jit(solution)/shard_map/all_gather | solution.py:19
  68.0 0.6 broadcast_in_dim.11
  68.6 0.0 copy-start
  68.7 0.0 copy-start.1
  68.7 3.4 %fusion.2 = bf16[512,256]{1,0:T(8,128)(2,1)} fusion(bf16[512,2048]{1,0:T(8,128)(2,1)} %all-gather.4.cloned.1.call-done, bf16[2048,256]{1,0:T(8,128)(2,1)} %all-gather.6.cloned.1.call-done, f32[64,8,2,128]{3,2,1,0:T(2,128)S(1)} %bitcast.16), kind=kOutput, calls=%fused_computation.4 | convolution fusion | flops 537133056 | bytes 3932160 | tf_op jit(solution)/shard_map/dot_general | solution.py:21
  72.1 0.0 all-gather.8.cloned.1.call-update
  72.1 27.8 %all-gather.8.cloned.1.call-done = bf16[2048,256]{1,0:T(8,128)(2,1)} async-done(((bf16[512,256]{1,0:T(8,128)(2,1)}), bf16[2048,256]{1,0:T(8,128)(2,1)}) %all-gather.8.cloned.1.call-update) | async-done | bytes 1048592 | tf_op jit(solution)/shard_map/all_gather | solution.py:31
  99.9 0.0 copy-done
  99.9 0.0 copy-done.1
  99.9 2.7 %fusion.1 = f32[512,256]{1,0:T(8,128)} fusion(bf16[512,2048]{1,0:T(8,128)(2,1)S(1)} %copy-done.1, bf16[2048,256]{1,0:T(8,128)(2,1)} %all-gather.8.cloned.1.call-done, bf16[512,256]{1,0:T(8,128)(2,1)S(1)} %copy-done, f32[64,8,2,128]{3,2,1,0:T(2,128)S(1)} %bitcast.17), kind=kOutput, calls=%fused_computation.3 | convolution fusion | flops 537526272 | bytes 4456448 | tf_op jit(solution)/shard_map/dot_general | solution.py:29
  (2 shorter events, 0.0 us)
Async XLA Ops:
  6.5 31.0 %all-gather.6.cloned.1.call-start = ((), (), s32[]{:S(2)}) async-start(), calls=%async_computation.1 | async-start | bytes 1310720 | tf_op jit(solution)/shard_map/all_gather | solution.py:23
  9.6 58.4 %all-gather.4.cloned.1.call-start = ((), (), s32[]{:S(2)}) async-start(), calls=%async_computation | async-start | bytes 2359296 | tf_op jit(solution)/shard_map/all_gather | solution.py:19
  10.4 89.5 %all-gather.8.cloned.1.call-start = ((), (), s32[]{:S(2)}) async-start(), calls=%async_computation.2 | async-start | bytes 1310720 | tf_op jit(solution)/shard_map/all_gather | solution.py:31
  68.6 31.3 %copy-start = (bf16[512,256]{1,0:T(8,128)(2,1)S(1)}, bf16[512,256]{1,0:T(8,128)(2,1)}, u32[]{:S(2)}) copy-start(bf16[512,256]{1,0:T(8,128)(2,1)} %bitcast_multiply_fusion) | copy-start | bytes 786436
  68.7 31.2 %copy-start.1 = (bf16[512,2048]{1,0:T(8,128)(2,1)S(1)}, bf16[512,2048]{1,0:T(8,128)(2,1)}, u32[]{:S(2)}) copy-start(bf16[512,2048]{1,0:T(8,128)(2,1)} %all-gather.4.cloned.1.call-done) | copy-start | bytes 6291460
Sparse Core Ops, SparseCore 0:
  9.8 27.6 all-gather.5
  39.1 28.8 all-gather.3
  72.2 27.6 all-gather.7
where the time goes:
time: 111 us; the launch traced here: 109 us
  waiting for transfers between devices  86.1 us (78%)
  between operations  13.1 us (12%)
  matrix products  6.16 us (6%)
  other arithmetic  2.45 us (2%)
  local copies, waits for them, and re-layouts  1.25 us (1%)
    all_gather x1, waiting for transfers between devices, body(): rows_all = lax.all_gather(masked, 'col', axis=1, tiled=True)  30.5 us
    all_gather x1, waiting for transfers between devices, body(): lax.all_gather(filtered, 'row', axis=0, tiled=True)  27.8 us
    all_gather x1, waiting for transfers between devices, body(): lax.all_gather(masked, 'row', axis=0, tiled=True)  27.1 us
    dot_general x1, matrix products, body(): jnp.dot(left_part, lax.all_gather(masked, 'row', axis=0, tiled=True), pre...  3.43 us
    dot_general x1, matrix products, body(): jnp.dot(left_part, lax.all_gather(filtered, 'row', axis=0, tiled=True), p...  2.73 us
  transfers between devices with their start and end apart: 3, of which 3 were waited for; matrix products, arithmetic and copies ran while one was open for 0% of the time, Pallas kernels for 0%

commit v1 on v0

v1 whole, which is shorter than its diff:
```python
import jax
import jax.numpy as jnp
from jax import lax
from jax.sharding import PartitionSpec as P

B = 128


def _xor_gather(x, axis, n, index, stride=1):
    pieces = [x]
    for k in range(1, n):
        d = k * stride
        perm = [(i, i ^ d) for i in range(n * stride)]
        pieces.append(lax.ppermute(x, axis, perm))
    stacked = jnp.stack(pieces)
    order = jnp.arange(n, dtype=jnp.int32) ^ index
    return jnp.take(stacked, order, axis=0)


def make_body(n_row, n_col):
    n_z = n_col // 2

    def body(matrix_in, pattern):
        rows, cols = matrix_in.shape
        block_rows = rows // B
        block_cols = cols // B
        row_index = lax.axis_index("row")
        col_index = lax.axis_index("col")
        z_index = col_index // 2
        core = col_index % 2
        local_blocks = lax.dynamic_slice(
            pattern, (row_index * block_rows, col_index * block_cols), (block_rows, block_cols)
        )
        local_mask = jnp.repeat(jnp.repeat(local_blocks, B, axis=0), B, axis=1)
        masked = matrix_in * local_mask.astype(jnp.bfloat16)

        col_panel = _xor_gather(masked, "row", n_row, row_index).reshape(n_row * rows, cols)

        own = _xor_gather(masked, "col", n_z, z_index, stride=2)
        other = lax.ppermute(own, "col", [(i, i ^ 1) for i in range(n_col)])
        first = jnp.where(core == 0, own, other)
        second = jnp.where(core == 0, other, own)
        row_panel = jnp.stack([first, second], axis=1)
        row_panel = jnp.transpose(row_panel, (2, 0, 1, 3)).reshape(rows, n_col * cols)

        square = jnp.dot(row_panel, col_panel, preferred_element_type=jnp.float32)
        mask_float = local_mask.astype(jnp.float32)
        filtered = (mask_float * square).astype(jnp.bfloat16)
        f_panel = _xor_gather(filtered, "row", n_row, row_index).reshape(n_row * rows, cols)
        cubic = jnp.dot(row_panel, f_panel, preferred_element_type=jnp.float32)
        return mask_float * (1.5 * masked.astype(jnp.float32) - 0.5 * cubic)

    return body


def solution(mesh):
    return jax.shard_map(
        make_body(mesh.shape["row"], mesh.shape["col"]),
        mesh=mesh,
        in_specs=(P("row", "col"), P()),
        out_specs=P("row", "col"),
        check_vma=False,
    )
```

time: 111 us -> 64 us (0.58); the launches traced: 109 us -> 63.6 us
  waiting for transfers between devices: 86.1 us -> 35.8 us
  between operations: 13.1 us -> 0.15 us
  starting transfers between devices: 0.08 us -> 9.47 us
  local copies, waits for them, and re-layouts: 1.25 us -> 6.96 us
  other arithmetic: 2.45 us -> 7.16 us
  matrix products: 6.16 us -> 4.08 us
    all_gather x3 -> x0, waiting for transfers between devices: 85.4 us -> none  [the longest x1 30.5 us: body(): rows_all = lax.all_gather(masked, 'col', axis=1, tiled=True)]
    ppermute x0 -> x10, waiting for transfers between devices: none -> 35.8 us  [the longest x9 34.6 us: _xor_gather(): pieces.append(lax.ppermute(x, axis, perm))]
    ppermute x0 -> x10, starting transfers between devices: none -> 9.47 us  [the longest x9 9.47 us: _xor_gather(): pieces.append(lax.ppermute(x, axis, perm))]
    another operation x0 -> x3, other arithmetic: none -> 2.74 us  [the longest x1 1.43 us: body(): row_panel = jnp.stack([first, second], axis=1)]
    select_n x0 -> x5, other arithmetic: none -> 2.45 us  [_xor_gather(): return jnp.take(stacked, order, axis=0)]
    transpose x0 -> x1, local copies, waits for them, and re-layouts: none -> 2.4 us  [body(): jnp.transpose(row_panel, (2, 0, 1, 3)).reshape(rows, n_col * cols)]
    dot_general x2, matrix products: 6.16 us -> 4.08 us  [the longest x1 2.54 us: body(): square = jnp.dot(row_panel, col_panel, preferred_element_type=jnp.float32)]
    gather x0 -> x3, local copies, waits for them, and re-layouts: none -> 1.84 us  [_xor_gather(): return jnp.take(stacked, order, axis=0)]
  transfers between devices with their start and end apart: 3 -> 10, of which waited for: 3 -> 7; matrix products, arithmetic and copies ran while one was open for 0% -> 3% of each run, Pallas kernels for 0% -> 0%
where the time goes in v1:
time: 64 us; the launch traced here: 63.6 us
  waiting for transfers between devices  35.8 us (56%)
  starting transfers between devices  9.47 us (15%)
  other arithmetic  7.16 us (11%)
  local copies, waits for them, and re-layouts  6.96 us (11%)
  matrix products  4.08 us (6%)
    ppermute x9, waiting for transfers between devices, _xor_gather(): pieces.append(lax.ppermute(x, axis, perm))  34.6 us
    ppermute x9, starting transfers between devices, _xor_gather(): pieces.append(lax.ppermute(x, axis, perm))  9.47 us
    dot_general x1, matrix products, body(): square = jnp.dot(row_panel, col_panel, preferred_element_type=jnp.float32)  2.54 us
    select_n x5, other arithmetic, _xor_gather(): return jnp.take(stacked, order, axis=0)  2.45 us
    transpose x1, local copies, waits for them, and re-layouts, body(): jnp.transpose(row_panel, (2, 0, 1, 3)).reshape(rows, n_col * cols)  2.4 us
    gather x3, local copies, waits for them, and re-layouts, _xor_gather(): return jnp.take(stacked, order, axis=0)  1.84 us
    dot_general x1, matrix products, body(): cubic = jnp.dot(row_panel, f_panel, preferred_element_type=jnp.float32)  1.54 us
    unnamed x10, local copies, waits for them, and re-layouts  1.47 us
  transfers between devices with their start and end apart: 10, of which 7 were waited for; matrix products, arithmetic and copies ran while one was open for 3% of the time, Pallas kernels for 0%

profile of v1, /device:TPU:16, one launch (start us, length us, event | category | flops | bytes accessed | tf_op | source)
XLA Modules:
  0.0 63.6 jit_solution(12112589351045057661)
XLA Ops:
  0.0 0.8 %dynamic-slice_convert_fusion.1 = (f32[4,2]{1,0:T(4,128)S(1)}, bf16[4,2]{1,0:T(4,128)(2,1)S(1)}) fusion(s32[16,16]{1,0:T(8,128)} %param.5, s32[]{:T(128)S(6)} %select_n.36, s32[]{:T(128)S(6)} %select_n.37), kind=kLoop, calls=%fused_computation.29 | loop fusion | flops 16 | bytes 88 | tf_op jit(solution)/shard_map/convert_element_type | solution.py:47
  0.8 0.6 broadcast_in_dim.22
  1.4 1.0 %bitcast_multiply_fusion = bf16[512,256]{1,0:T(8,128)(2,1)S(1)} fusion(bf16[512,256]{1,0:T(8,128)(2,1)} %param.4, bf16[64,8,2,128]{3,2,1,0:T(2,128)(2,1)S(1)} %bitcast.37), kind=kLoop, calls=%fused_computation.21 | loop fusion | flops 131072 | bytes 786432 | tf_op jit(solution)/shard_map/mul | solution.py:35
  2.4 1.6 %collective-permute-start.4 = (bf16[512,256]{1,0:T(8,128)(2,1)S(1)}, bf16[512,256]{1,0:T(8,128)(2,1)S(1)}, u32[]{:S(2)}, u32[]{:S(2)}) collective-permute-start(bf16[512,256]{1,0:T(8,128)(2,1)S(1)} %bitcast_multiply_fusion), channel_id=1, source_target_pairs={{0,8},{8,0},{16,24},{24,16},{1,9},{9,1},{17,25},{25,17},{2,10},{10... | collective-permute-start | bytes 786440 | tf_op jit(solution)/shard_map/ppermute | solution.py:14
  3.9 1.5 %collective-permute-start.5 = (bf16[512,256]{1,0:T(8,128)(2,1)S(1)}, bf16[512,256]{1,0:T(8,128)(2,1)S(1)}, u32[]{:S(2)}, u32[]{:S(2)}) collective-permute-start(bf16[512,256]{1,0:T(8,128)(2,1)S(1)} %bitcast_multiply_fusion), channel_id=1, source_target_pairs={{0,16},{8,24},{16,0},{24,8},{1,17},{9,25},{17,1},{25,9},{2,18},{10... | collective-permute-start | bytes 786440 | tf_op jit(solution)/shard_map/ppermute | solution.py:14
  5.5 0.5 collective-permute-start.6
  5.9 1.6 %collective-permute-start = (bf16[512,256]{1,0:T(8,128)(2,1)S(1)}, bf16[512,256]{1,0:T(8,128)(2,1)S(1)}, u32[]{:S(2)}, u32[]{:S(2)}) collective-permute-start(bf16[512,256]{1,0:T(8,128)(2,1)S(1)} %bitcast_multiply_fusion), channel_id=1, source_target_pairs={{0,2},{1,3},{2,0},{3,1},{4,6},{5,7},{6,4},{7,5},{8,10},{9,11},{10,... | collective-permute-start | bytes 786440 | tf_op jit(solution)/shard_map/ppermute | solution.py:14
  7.5 0.3 collective-permute-start.1
  7.9 3.8 %collective-permute-done.4 = bf16[512,256]{1,0:T(8,128)(2,1)S(1)} collective-permute-done((bf16[512,256]{1,0:T(8,128)(2,1)S(1)}, bf16[512,256]{1,0:T(8,128)(2,1)S(1)}, u32[]{:S(2)}, u32[]{:S(2)}) %collective-permute-start.4) | collective-permute-done | bytes 262176 | tf_op jit(solution)/shard_map/ppermute | solution.py:14
  11.6 0.4 collective-permute-start.2
  12.1 5.2 %collective-permute-done.5 = bf16[512,256]{1,0:T(8,128)(2,1)S(1)} collective-permute-done((bf16[512,256]{1,0:T(8,128)(2,1)S(1)}, bf16[512,256]{1,0:T(8,128)(2,1)S(1)}, u32[]{:S(2)}, u32[]{:S(2)}) %collective-permute-start.5) | collective-permute-done | bytes 262176 | tf_op jit(solution)/shard_map/ppermute | solution.py:14
  17.3 0.0 collective-permute-done.6
  17.3 0.0 collective-permute-done
  17.3 8.5 %collective-permute-done.1 = bf16[512,256]{1,0:T(8,128)(2,1)S(1)} collective-permute-done((bf16[512,256]{1,0:T(8,128)(2,1)S(1)}, bf16[512,256]{1,0:T(8,128)(2,1)S(1)}, u32[]{:S(2)}, u32[]{:S(2)}) %collective-permute-start.1) | collective-permute-done | bytes 262176 | tf_op jit(solution)/shard_map/ppermute | solution.py:14
  25.9 0.0 copy-start.4
  25.9 5.4 %collective-permute-done.2 = bf16[512,256]{1,0:T(8,128)(2,1)S(1)} collective-permute-done((bf16[512,256]{1,0:T(8,128)(2,1)S(1)}, bf16[512,256]{1,0:T(8,128)(2,1)S(1)}, u32[]{:S(2)}, u32[]{:S(2)}) %collective-permute-start.2) | collective-permute-done | bytes 262176 | tf_op jit(solution)/shard_map/ppermute | solution.py:14
  31.2 0.0 copy-done.4
  31.2 1.2 %fusion.6 = (bf16[4,512,256]{2,1,0:T(8,128)(2,1)S(1)}, bf16[4,512,256]{2,1,0:T(8,128)(2,1)S(1)}) fusion(bf16[1,512,256]{2,1,0:T(8,128)(2,1)S(1)} %bitcast.39, bf16[1,512,256]{2,1,0:T(8,128)(2,1)S(1)} %bitcast.49, bf16[1,512,256]{2,1,0:T(8,128)(2,1)S(1)} %bitcast.48, bf16[1,512,256]{2,1,0:T(8,128)(2,1)S(1)} %bitcast.47, bf16[1,512,256]{2,1,0:T(8,128)(2,1)S(1)} %bitcast.52, ...), kind=kLoop, calls=%fused_computation.14 | loop fusion | flops 3145728 | bytes 3932160 | tf_op jit(solution)/shard_map/stack | solution.py:15
  32.4 0.6 gather_fusion
  33.0 1.2 %broadcast_select_fusion.2 = bf16[4,512,256]{2,1,0:T(8,128)(2,1)} fusion(bf16[4,512,256]{2,1,0:T(8,128)(2,1)S(1)} %gather_fusion, pred[4]{0:T(512)(128)(4,1)S(1)} %compare_and_fusion.1), kind=kLoop, calls=%fused_computation.20 | loop fusion | flops 524288 | bytes 2097156 | tf_op jit(solution)/shard_map/jit(_take)/select_n | solution.py:17
  34.2 0.0 collective-permute-start.3
  34.2 0.6 gather_fusion.1
  34.8 1.1 %broadcast_select_fusion = bf16[4,512,256]{2,1,0:T(8,128)(2,1)} fusion(bf16[4,512,256]{2,1,0:T(8,128)(2,1)S(1)} %gather_fusion.1, pred[4]{0:T(512)(128)(4,1)S(1)} %compare_and_fusion), kind=kLoop, calls=%fused_computation.18 | loop fusion | flops 524288 | bytes 2097156 | tf_op jit(solution)/shard_map/jit(_take)/select_n | solution.py:17
  36.0 1.2 %collective-permute-done.3 = bf16[4,512,256]{2,1,0:T(8,128)(2,1)} collective-permute-done((bf16[4,512,256]{2,1,0:T(8,128)(2,1)}, bf16[4,512,256]{2,1,0:T(8,128)(2,1)}, u32[]{:S(2)}, u32[]{:S(2)}) %collective-permute-start.3) | collective-permute-done | bytes 1048608 | tf_op jit(solution)/shard_map/ppermute | solution.py:40
  37.2 1.4 %select_bitcast_fusion.1 = (bf16[4,1,512,256]{3,2,0,1:T(8,128)(2,1)S(1)}, bf16[4,1,512,256]{3,2,0,1:T(8,128)(2,1)S(1)}) fusion(bf16[4,512,256]{2,1,0:T(8,128)(2,1)} %collective-permute-done.3, pred[]{:T(512)S(6)} %eq.6, bf16[4,512,256]{2,1,0:T(8,128)(2,1)S(1)} %gather_fusion, pred[4]{0:T(512)(128)(4,1)S(1)} %compare_and_fusion.1), kind=kLoop, calls=%fused_computation.17 | loop fusion | flops 1572864 | bytes 4194309 | tf_op jit(solution)/shard_map/stack | solution.py:43
  38.6 0.2 maximum_bitcast_fusion
  38.8 0.0 copy-start.1
  38.8 2.4 %copy.3 = bf16[512,4,2,256]{0,3,2,1:T(8,128)(2,1)} copy(bf16[512,4,2,256]{3,0,1,2:T(8,128)(2,1)S(1)} %maximum_bitcast_fusion) | data formatting | bytes 4194304 | tf_op jit(solution)/shard_map/transpose | solution.py:44
  41.3 0.6 broadcast_in_dim.20
  41.9 0.0 copy-start.2
  41.9 0.0 copy-done.1
  41.9 2.5 %fusion.2 = bf16[512,256]{1,0:T(8,128)(2,1)S(1)} fusion(bf16[512,2048]{0,1:T(8,128)(2,1)} %bitcast.33, bf16[2048,256]{1,0:T(8,128)(2,1)S(1)} %bitcast.35, f32[64,8,2,128]{3,2,1,0:T(2,128)S(1)} %bitcast.41), kind=kOutput, calls=%fused_computation.10 | convolution fusion | flops 537133056 | bytes 3932160 | tf_op jit(solution)/shard_map/dot_general | solution.py:46
  44.4 0.0 copy-done.2
  44.4 1.6 %collective-permute-start.7 = (bf16[512,256]{1,0:T(8,128)(2,1)S(1)}, bf16[512,256]{1,0:T(8,128)(2,1)S(1)}, u32[]{:S(2)}, u32[]{:S(2)}) collective-permute-start(bf16[512,256]{1,0:T(8,128)(2,1)S(1)} %fusion.2), channel_id=1, source_target_pairs={{0,8},{8,0},{16,24},{24,16},{1,9},{9,1},{17,25},{25,17},{2,10},{10... | collective-permute-start | bytes 786440 | tf_op jit(solution)/shard_map/ppermute | solution.py:14
  46.0 1.5 %collective-permute-start.8 = (bf16[512,256]{1,0:T(8,128)(2,1)S(1)}, bf16[512,256]{1,0:T(8,128)(2,1)S(1)}, u32[]{:S(2)}, u32[]{:S(2)}) collective-permute-start(bf16[512,256]{1,0:T(8,128)(2,1)S(1)} %fusion.2), channel_id=1, source_target_pairs={{0,16},{8,24},{16,0},{24,8},{1,17},{9,25},{17,1},{25,9},{2,18},{10... | collective-permute-start | bytes 786440 | tf_op jit(solution)/shard_map/ppermute | solution.py:14
  47.5 0.5 collective-permute-start.9
  48.0 5.7 %collective-permute-done.7 = bf16[512,256]{1,0:T(8,128)(2,1)S(1)} collective-permute-done((bf16[512,256]{1,0:T(8,128)(2,1)S(1)}, bf16[512,256]{1,0:T(8,128)(2,1)S(1)}, u32[]{:S(2)}, u32[]{:S(2)}) %collective-permute-start.7) | collective-permute-done | bytes 262176 | tf_op jit(solution)/shard_map/ppermute | solution.py:14
  53.6 6.0 %collective-permute-done.8 = bf16[512,256]{1,0:T(8,128)(2,1)S(1)} collective-permute-done((bf16[512,256]{1,0:T(8,128)(2,1)S(1)}, bf16[512,256]{1,0:T(8,128)(2,1)S(1)}, u32[]{:S(2)}, u32[]{:S(2)}) %collective-permute-start.8) | collective-permute-done | bytes 262176 | tf_op jit(solution)/shard_map/ppermute | solution.py:14
  59.7 0.0 collective-permute-done.9
  59.7 0.1 pad_maximum_fusion.2
  59.8 0.0 copy-start.3
  59.8 0.6 gather_fusion.2
  60.4 0.0 copy-start
  60.5 0.2 broadcast_select_fusion.1
  60.6 0.2 copy-done.3
  60.9 1.2 %copy-done = bf16[512,4,2,256]{0,3,2,1:T(8,128)(2,1)S(1)} copy-done((bf16[512,4,2,256]{0,3,2,1:T(8,128)(2,1)S(1)}, bf16[512,4,2,256]{0,3,2,1:T(8,128)(2,1)}, u32[]{:S(2)}) %copy-start) | copy-done | bytes 2097176
  62.1 1.5 %fusion.1 = f32[512,256]{1,0:T(8,128)} fusion(bf16[512,2048]{0,1:T(8,128)(2,1)S(1)} %bitcast.34, bf16[2048,256]{1,0:T(8,128)(2,1)S(1)} %bitcast.36, bf16[512,256]{1,0:T(8,128)(2,1)S(1)} %bitcast_multiply_fusion, f32[64,8,2,128]{3,2,1,0:T(2,128)S(1)} %bitcast.42), kind=kOutput, calls=%fused_computation.9 | convolution fusion | flops 537526272 | bytes 4456448 | tf_op jit(solution)/shard_map/dot_general | solution.py:50
  (8 shorter events, 0.1 us)
Async XLA Ops:
  2.4 9.3 %collective-permute-start.4 = (bf16[512,256]{1,0:T(8,128)(2,1)S(1)}, bf16[512,256]{1,0:T(8,128)(2,1)S(1)}, u32[]{:S(2)}, u32[]{:S(2)}) collective-permute-start(bf16[512,256]{1,0:T(8,128)(2,1)S(1)} %bitcast_multiply_fusion), channel_id=1, source_target_pairs={{0,8},{8,0},{16,24},{24,16},{1,9},{9,1},{17,25},{25,17},{2,10},{10... | collective-permute-start | bytes 786440 | tf_op jit(solution)/shard_map/ppermute | solution.py:14
  3.9 13.4 %collective-permute-start.5 = (bf16[512,256]{1,0:T(8,128)(2,1)S(1)}, bf16[512,256]{1,0:T(8,128)(2,1)S(1)}, u32[]{:S(2)}, u32[]{:S(2)}) collective-permute-start(bf16[512,256]{1,0:T(8,128)(2,1)S(1)} %bitcast_multiply_fusion), channel_id=1, source_target_pairs={{0,16},{8,24},{16,0},{24,8},{1,17},{9,25},{17,1},{25,9},{2,18},{10... | collective-permute-start | bytes 786440 | tf_op jit(solution)/shard_map/ppermute | solution.py:14
  5.5 11.9 %collective-permute-start.6 = (bf16[512,256]{1,0:T(8,128)(2,1)S(1)}, bf16[512,256]{1,0:T(8,128)(2,1)S(1)}, u32[]{:S(2)}, u32[]{:S(2)}) collective-permute-start(bf16[512,256]{1,0:T(8,128)(2,1)S(1)} %bitcast_multiply_fusion), channel_id=1, source_target_pairs={{0,24},{8,16},{16,8},{24,0},{1,25},{9,17},{17,9},{25,1},{2,26},{10... | collective-permute-start | bytes 786440 | tf_op jit(solution)/shard_map/ppermute | solution.py:14
  5.9 11.4 %collective-permute-start = (bf16[512,256]{1,0:T(8,128)(2,1)S(1)}, bf16[512,256]{1,0:T(8,128)(2,1)S(1)}, u32[]{:S(2)}, u32[]{:S(2)}) collective-permute-start(bf16[512,256]{1,0:T(8,128)(2,1)S(1)} %bitcast_multiply_fusion), channel_id=1, source_target_pairs={{0,2},{1,3},{2,0},{3,1},{4,6},{5,7},{6,4},{7,5},{8,10},{9,11},{10,... | collective-permute-start | bytes 786440 | tf_op jit(solution)/shard_map/ppermute | solution.py:14
  7.5 18.3 %collective-permute-start.1 = (bf16[512,256]{1,0:T(8,128)(2,1)S(1)}, bf16[512,256]{1,0:T(8,128)(2,1)S(1)}, u32[]{:S(2)}, u32[]{:S(2)}) collective-permute-start(bf16[512,256]{1,0:T(8,128)(2,1)S(1)} %bitcast_multiply_fusion), channel_id=1, source_target_pairs={{0,4},{1,5},{2,6},{3,7},{4,0},{5,1},{6,2},{7,3},{8,12},{9,13},{10,... | collective-permute-start | bytes 786440 | tf_op jit(solution)/shard_map/ppermute | solution.py:14
  11.6 19.6 %collective-permute-start.2 = (bf16[512,256]{1,0:T(8,128)(2,1)S(1)}, bf16[512,256]{1,0:T(8,128)(2,1)S(1)}, u32[]{:S(2)}, u32[]{:S(2)}) collective-permute-start(bf16[512,256]{1,0:T(8,128)(2,1)S(1)} %bitcast_multiply_fusion), channel_id=1, source_target_pairs={{0,6},{1,7},{2,4},{3,5},{4,2},{5,3},{6,0},{7,1},{8,14},{9,15},{10,... | collective-permute-start | bytes 786440 | tf_op jit(solution)/shard_map/ppermute | solution.py:14
  25.9 5.4 %copy-start.4 = (bf16[512,256]{1,0:T(8,128)(2,1)}, bf16[512,256]{1,0:T(8,128)(2,1)S(1)}, u32[]{:S(2)}) copy-start(bf16[512,256]{1,0:T(8,128)(2,1)S(1)} %collective-permute-done.1) | copy-start | bytes 786436
  34.2 3.0 %collective-permute-start.3 = (bf16[4,512,256]{2,1,0:T(8,128)(2,1)}, bf16[4,512,256]{2,1,0:T(8,128)(2,1)}, u32[]{:S(2)}, u32[]{:S(2)}) collective-permute-start(bf16[4,512,256]{2,1,0:T(8,128)(2,1)} %broadcast_select_fusion.2), channel_id=1, source_target_pairs={{0,1},{1,0},{2,3},{3,2},{4,5},{5,4},{6,7},{7,6},{8,9},{9,8},{10,11... | collective-permute-start | bytes 3145736 | tf_op jit(solution)/shard_map/ppermute | solution.py:40
  38.8 3.0 %copy-start.1 = (bf16[4,512,256]{2,1,0:T(8,128)(2,1)S(1)}, bf16[4,512,256]{2,1,0:T(8,128)(2,1)}, u32[]{:S(2)}) copy-start(bf16[4,512,256]{2,1,0:T(8,128)(2,1)} %broadcast_select_fusion) | copy-start | bytes 3145732
  41.9 2.6 %copy-start.2 = (f32[512,2,128]{2,1,0:T(2,128)}, f32[512,2,128]{2,1,0:T(2,128)S(1)}, u32[]{:S(2)}) copy-start(f32[512,2,128]{2,1,0:T(2,128)S(1)} %broadcast_in_dim.20) | copy-start | bytes 1572868
  44.4 9.2 %collective-permute-start.7 = (bf16[512,256]{1,0:T(8,128)(2,1)S(1)}, bf16[512,256]{1,0:T(8,128)(2,1)S(1)}, u32[]{:S(2)}, u32[]{:S(2)}) collective-permute-start(bf16[512,256]{1,0:T(8,128)(2,1)S(1)} %fusion.2), channel_id=1, source_target_pairs={{0,8},{8,0},{16,24},{24,16},{1,9},{9,1},{17,25},{25,17},{2,10},{10... | collective-permute-start | bytes 786440 | tf_op jit(solution)/shard_map/ppermute | solution.py:14
  46.0 13.7 %collective-permute-start.8 = (bf16[512,256]{1,0:T(8,128)(2,1)S(1)}, bf16[512,256]{1,0:T(8,128)(2,1)S(1)}, u32[]{:S(2)}, u32[]{:S(2)}) collective-permute-start(bf16[512,256]{1,0:T(8,128)(2,1)S(1)} %fusion.2), channel_id=1, source_target_pairs={{0,16},{8,24},{16,0},{24,8},{1,17},{9,25},{17,1},{25,9},{2,18},{10... | collective-permute-start | bytes 786440 | tf_op jit(solution)/shard_map/ppermute | solution.py:14
  47.5 12.2 %collective-permute-start.9 = (bf16[512,256]{1,0:T(8,128)(2,1)S(1)}, bf16[512,256]{1,0:T(8,128)(2,1)S(1)}, u32[]{:S(2)}, u32[]{:S(2)}) collective-permute-start(bf16[512,256]{1,0:T(8,128)(2,1)S(1)} %fusion.2), channel_id=1, source_target_pairs={{0,24},{8,16},{16,8},{24,0},{1,25},{9,17},{17,9},{25,1},{2,26},{10... | collective-permute-start | bytes 786440 | tf_op jit(solution)/shard_map/ppermute | solution.py:14
  59.8 1.0 %copy-start.3 = (f32[512,2,128]{2,1,0:T(2,128)S(1)}, f32[512,2,128]{2,1,0:T(2,128)}, u32[]{:S(2)}) copy-start(f32[512,2,128]{2,1,0:T(2,128)} %copy-done.2) | copy-start | bytes 1572868
  60.4 1.6 %copy-start = (bf16[512,4,2,256]{0,3,2,1:T(8,128)(2,1)S(1)}, bf16[512,4,2,256]{0,3,2,1:T(8,128)(2,1)}, u32[]{:S(2)}) copy-start(bf16[512,4,2,256]{0,3,2,1:T(8,128)(2,1)} %copy.3) | copy-start | bytes 6291460

commit v2 on v1

v2 whole, which is shorter than its diff:
```python
import jax
import jax.numpy as jnp
from jax import lax
from jax.sharding import PartitionSpec as P

B = 128


def _swap(x, axis, size, d):
    return lax.ppermute(x, axis, [(i, i ^ d) for i in range(size)])


def make_body(n_row, n_col):
    n_z = n_col // 2

    def body(matrix_in, pattern):
        rows, cols = matrix_in.shape
        ratio = rows // cols
        block_rows = rows // B
        block_cols = cols // B
        row_index = lax.axis_index("row")
        col_index = lax.axis_index("col")
        local_blocks = lax.dynamic_slice(
            pattern, (row_index * block_rows, col_index * block_cols), (block_rows, block_cols)
        )
        local_mask = jnp.repeat(jnp.repeat(local_blocks, B, axis=0), B, axis=1)
        masked = matrix_in * local_mask.astype(jnp.bfloat16)

        row_pieces = [None] * n_col
        row_pieces[0] = masked
        row_pieces[1] = _swap(masked, "col", n_col, 1)
        for k in range(1, n_z):
            piece = _swap(masked, "col", n_col, 2 * k)
            row_pieces[2 * k] = piece
            row_pieces[2 * k + 1] = _swap(piece, "col", n_col, 1)

        col_pieces = [masked] + [_swap(masked, "row", n_row, k) for k in range(1, n_row)]

        slots = jnp.arange(n_col, dtype=jnp.int32) ^ col_index
        sub_index = ((slots // ratio) ^ row_index) * ratio + slots % ratio

        def in_slot_order(pieces):
            stacked = jnp.stack(pieces).reshape(n_row * ratio, cols, cols)
            return jnp.take(stacked, sub_index, axis=0)

        row_stack = jnp.stack(row_pieces)
        col_slot = in_slot_order(col_pieces)
        square = jnp.einsum(
            "tmj,tjn->mn", row_stack, col_slot, preferred_element_type=jnp.float32
        )
        mask_float = local_mask.astype(jnp.float32)
        filtered = (mask_float * square).astype(jnp.bfloat16)
        f_pieces = [filtered] + [_swap(filtered, "row", n_row, k) for k in range(1, n_row)]
        f_slot = in_slot_order(f_pieces)
        cubic = jnp.einsum("tmj,tjn->mn", row_stack, f_slot, preferred_element_type=jnp.float32)
        return mask_float * (1.5 * masked.astype(jnp.float32) - 0.5 * cubic)

    return body


def solution(mesh):
    return jax.shard_map(
        make_body(mesh.shape["row"], mesh.shape["col"]),
        mesh=mesh,
        in_specs=(P("row", "col"), P()),
        out_specs=P("row", "col"),
        check_vma=False,
    )
```

time: 64 us -> 64.2 us (level)
  other arithmetic: 7.16 us -> 2.77 us
  waiting for transfers between devices: 35.8 us -> 38.8 us
  matrix products: 4.08 us -> 5.54 us
    ppermute x10 -> x13, waiting for transfers between devices: 35.8 us -> 38.8 us  [_swap(): return lax.ppermute(x, axis, [(i, i ^ d) for i in range(size)])]
    unnamed x10 -> x6, local copies, waits for them, and re-layouts: 1.47 us -> 4.37 us
    another operation x3 -> x2, other arithmetic: 2.74 us -> 0.27 us  [in_slot_order(): stacked = jnp.stack(pieces).reshape(n_row * ratio, cols, cols)]
    select_n x5 -> x0, other arithmetic: 2.45 us -> none  [_xor_gather(): return jnp.take(stacked, order, axis=0)]
    transpose x1 -> x0, local copies, waits for them, and re-layouts: 2.4 us -> none  [body(): jnp.transpose(row_panel, (2, 0, 1, 3)).reshape(rows, n_col * cols)]
    unnamed x0 -> x1, other arithmetic: none -> 1.72 us
    dot_general x2, matrix products: 4.08 us -> 5.54 us  [the longest x1 3.17 us: body(): jnp.einsum('tmj,tjn->mn', row_stack, f_slot, preferred_element_type=jnp.f...]
    mul x1 -> x0, other arithmetic: 0.99 us -> none  [body(): masked = matrix_in * local_mask.astype(jnp.bfloat16)]
  transfers between devices with their start and end apart: 10 -> 13, of which waited for: 7 -> 6; matrix products, arithmetic and copies ran while one was open for 3% -> 8% of each run, Pallas kernels for 0% -> 0%
where the time goes in v2:
time: 64.2 us; the launch traced here: 63.9 us
  waiting for transfers between devices  38.8 us (60%)
  starting transfers between devices  9.15 us (14%)
  local copies, waits for them, and re-layouts  7.58 us (12%)
  matrix products  5.54 us (9%)
  other arithmetic  2.77 us (4%)
    ppermute x13, waiting for transfers between devices, _swap(): return lax.ppermute(x, axis, [(i, i ^ d) for i in range(size)])  38.8 us
    ppermute x13, starting transfers between devices, _swap(): return lax.ppermute(x, axis, [(i, i ^ d) for i in range(size)])  9.15 us
    unnamed x6, local copies, waits for them, and re-layouts  4.37 us
    dot_general x1, matrix products, body(): jnp.einsum('tmj,tjn->mn', row_stack, f_slot, preferred_element_type=jnp.f...  3.17 us
    dot_general x1, matrix products, body(): jnp.einsum('tmj,tjn->mn', row_stack, col_slot, preferred_element_type=jnp...  2.38 us
    unnamed x1, other arithmetic  1.72 us
  transfers between devices with their start and end apart: 13, of which 6 were waited for; matrix products, arithmetic and copies ran while one was open for 8% of the time, Pallas kernels for 0%

profile of v2, /device:TPU:16, one launch (start us, length us, event | category | flops | bytes accessed | tf_op | source)
XLA Modules:
  0.0 63.9 jit_solution(11864928877042611916)
XLA Ops:
  0.0 0.8 %dynamic-slice_convert_fusion.1 = (f32[4,2]{1,0:T(4,128)S(1)}, bf16[4,2]{1,0:T(4,128)(2,1)S(1)}) fusion(s32[16,16]{1,0:T(8,128)} %param.5, s32[]{:T(128)S(6)} %select_n.24, s32[]{:T(128)S(6)} %select_n.25), kind=kLoop, calls=%fused_computation.32 | loop fusion | flops 16 | bytes 88 | tf_op jit(solution)/shard_map/convert_element_type | solution.py:51
  0.8 0.6 broadcast_in_dim.22
  1.4 1.7 %constant_dynamic-update-slice_fusion = (bf16[8,512,256]{2,1,0:T(8,128)(2,1)}, bf16[512,256]{1,0:T(8,128)(2,1)S(1)}) fusion(bf16[512,256]{1,0:T(8,128)(2,1)} %param.4, bf16[64,8,2,128]{3,2,1,0:T(2,128)(2,1)S(1)} %bitcast.54), kind=kLoop, calls=%fused_computation.25 | loop fusion | flops 524287 | bytes 1048576
  3.1 1.5 %collective-permute-start.7 = (bf16[512,256]{1,0:T(8,128)(2,1)S(1)}, bf16[512,256]{1,0:T(8,128)(2,1)S(1)}, u32[]{:S(2)}, u32[]{:S(2)}) collective-permute-start(bf16[512,256]{1,0:T(8,128)(2,1)S(1)} %get-tuple-element.9), channel_id=1, source_target_pairs={{0,8},{8,0},{16,24},{24,16},{1,9},{9,1},{17,25},{25,17},{2,10},{10... | collective-permute-start | bytes 786440 | tf_op jit(solution)/shard_map/ppermute | solution.py:10
  4.6 1.5 %collective-permute-start.8 = (bf16[512,256]{1,0:T(8,128)(2,1)S(1)}, bf16[512,256]{1,0:T(8,128)(2,1)S(1)}, u32[]{:S(2)}, u32[]{:S(2)}) collective-permute-start(bf16[512,256]{1,0:T(8,128)(2,1)S(1)} %get-tuple-element.9), channel_id=1, source_target_pairs={{0,16},{8,24},{16,0},{24,8},{1,17},{9,25},{17,1},{25,9},{2,18},{10... | collective-permute-start | bytes 786440 | tf_op jit(solution)/shard_map/ppermute | solution.py:10
  6.1 0.5 collective-permute-start.9
  6.6 0.0 collective-permute-start
  6.6 1.6 %collective-permute-start.1 = (bf16[512,256]{1,0:T(8,128)(2,1)S(1)}, bf16[512,256]{1,0:T(8,128)(2,1)S(1)}, u32[]{:S(2)}, u32[]{:S(2)}) collective-permute-start(bf16[512,256]{1,0:T(8,128)(2,1)S(1)} %get-tuple-element.9), channel_id=1, source_target_pairs={{0,2},{1,3},{2,0},{3,1},{4,6},{5,7},{6,4},{7,5},{8,10},{9,11},{10,... | collective-permute-start | bytes 786440 | tf_op jit(solution)/shard_map/ppermute | solution.py:10
  8.2 4.1 %collective-permute-done.7 = bf16[512,256]{1,0:T(8,128)(2,1)S(1)} collective-permute-done((bf16[512,256]{1,0:T(8,128)(2,1)S(1)}, bf16[512,256]{1,0:T(8,128)(2,1)S(1)}, u32[]{:S(2)}, u32[]{:S(2)}) %collective-permute-start.7) | collective-permute-done | bytes 262176 | tf_op jit(solution)/shard_map/ppermute | solution.py:10
  12.3 0.0 collective-permute-start.3
  12.3 5.7 %collective-permute-done.8 = bf16[512,256]{1,0:T(8,128)(2,1)S(1)} collective-permute-done((bf16[512,256]{1,0:T(8,128)(2,1)S(1)}, bf16[512,256]{1,0:T(8,128)(2,1)S(1)}, u32[]{:S(2)}, u32[]{:S(2)}) %collective-permute-start.8) | collective-permute-done | bytes 262176 | tf_op jit(solution)/shard_map/ppermute | solution.py:10
  18.0 0.4 collective-permute-start.5
  18.5 0.0 collective-permute-done.9
  18.5 0.1 pad_maximum_fusion
  18.6 0.6 gather_fusion
  19.2 0.0 collective-permute-done.1
  19.3 0.1 collective-permute-start.2
  19.3 11.0 %collective-permute-done.3 = bf16[512,256]{1,0:T(8,128)(2,1)S(1)} collective-permute-done((bf16[512,256]{1,0:T(8,128)(2,1)S(1)}, bf16[512,256]{1,0:T(8,128)(2,1)S(1)}, u32[]{:S(2)}, u32[]{:S(2)}) %collective-permute-start.3) | collective-permute-done | bytes 262176 | tf_op jit(solution)/shard_map/ppermute | solution.py:10
  30.3 0.0 collective-permute-start.4
  30.3 5.9 %collective-permute-done.5 = bf16[512,256]{1,0:T(8,128)(2,1)S(1)} collective-permute-done((bf16[512,256]{1,0:T(8,128)(2,1)S(1)}, bf16[512,256]{1,0:T(8,128)(2,1)S(1)}, u32[]{:S(2)}, u32[]{:S(2)}) %collective-permute-start.5) | collective-permute-done | bytes 262176 | tf_op jit(solution)/shard_map/ppermute | solution.py:10
  36.2 0.0 collective-permute-start.6
  36.2 0.0 collective-permute-done
  36.3 0.7 %bitcast_dynamic-update-slice_fusion.6 = bf16[8,512,256]{2,1,0:T(8,128)(2,1)} fusion(bf16[8,512,256]{2,1,0:T(8,128)(2,1)} %get-tuple-element.8, bf16[512,256]{1,0:T(8,128)(2,1)S(1)} %collective-permute-done), kind=kLoop, calls=%fused_computation.24 | loop fusion | bytes 524288
  37.0 0.7 %bitcast_dynamic-update-slice_fusion.5 = bf16[8,512,256]{2,1,0:T(8,128)(2,1)} fusion(bf16[8,512,256]{2,1,0:T(8,128)(2,1)} %bitcast_dynamic-update-slice_fusion.6, bf16[512,256]{1,0:T(8,128)(2,1)S(1)} %collective-permute-done.1), kind=kLoop, calls=%fused_computation.23 | loop fusion | bytes 524288
  37.7 0.0 collective-permute-done.2
  37.7 0.7 %bitcast_dynamic-update-slice_fusion.4 = bf16[8,512,256]{2,1,0:T(8,128)(2,1)} fusion(bf16[8,512,256]{2,1,0:T(8,128)(2,1)} %bitcast_dynamic-update-slice_fusion.5, bf16[512,256]{1,0:T(8,128)(2,1)S(1)} %collective-permute-done.2), kind=kLoop, calls=%fused_computation.22 | loop fusion | bytes 524288
  38.4 0.7 %bitcast_dynamic-update-slice_fusion.3 = bf16[8,512,256]{2,1,0:T(8,128)(2,1)} fusion(bf16[8,512,256]{2,1,0:T(8,128)(2,1)} %bitcast_dynamic-update-slice_fusion.4, bf16[512,256]{1,0:T(8,128)(2,1)S(1)} %collective-permute-done.3), kind=kLoop, calls=%fused_computation.21 | loop fusion | bytes 524288
  39.2 0.0 collective-permute-done.4
  39.2 0.7 %bitcast_dynamic-update-slice_fusion.2 = bf16[8,512,256]{2,1,0:T(8,128)(2,1)} fusion(bf16[8,512,256]{2,1,0:T(8,128)(2,1)} %bitcast_dynamic-update-slice_fusion.3, bf16[512,256]{1,0:T(8,128)(2,1)S(1)} %collective-permute-done.4), kind=kLoop, calls=%fused_computation.20 | loop fusion | bytes 524288
  39.9 0.7 %bitcast_dynamic-update-slice_fusion.1 = bf16[8,512,256]{2,1,0:T(8,128)(2,1)} fusion(bf16[8,512,256]{2,1,0:T(8,128)(2,1)} %bitcast_dynamic-update-slice_fusion.2, bf16[512,256]{1,0:T(8,128)(2,1)S(1)} %collective-permute-done.5), kind=kLoop, calls=%fused_computation.19 | loop fusion | bytes 524288
  40.6 0.0 collective-permute-done.6
  40.6 0.7 %bitcast_dynamic-update-slice_fusion = bf16[8,512,256]{2,1,0:T(8,128)(2,1)} fusion(bf16[8,512,256]{2,1,0:T(8,128)(2,1)} %bitcast_dynamic-update-slice_fusion.1, bf16[512,256]{1,0:T(8,128)(2,1)S(1)} %collective-permute-done.6), kind=kLoop, calls=%fused_computation.18 | loop fusion | bytes 524288 | tf_op jit(solution)/shard_map/stack | solution.py:46
  41.4 0.6 broadcast_in_dim.20
  42.0 2.4 %fusion.4 = bf16[512,256]{1,0:T(8,128)(2,1)S(1)} fusion(bf16[8,512,256]{2,1,0:T(8,128)(2,1)} %bitcast_dynamic-update-slice_fusion, bf16[8,256,256]{2,1,0:T(8,128)(2,1)S(1)} %gather_fusion, pred[8]{0:T(512)(128)(4,1)S(1)} %get-tuple-element.6, f32[64,8,2,128]{3,2,1,0:T(2,128)S(1)} %bitcast.57), kind=kOutput, calls=%fused_computation.8 | convolution fusion | flops 537657344 | bytes 3932168 | tf_op jit(solution)/shard_map/tmj,tjn->mn/dot_general | solution.py:48
  44.4 1.6 %collective-permute-start.10 = (bf16[512,256]{1,0:T(8,128)(2,1)S(1)}, bf16[512,256]{1,0:T(8,128)(2,1)S(1)}, u32[]{:S(2)}, u32[]{:S(2)}) collective-permute-start(bf16[512,256]{1,0:T(8,128)(2,1)S(1)} %fusion.4), channel_id=1, source_target_pairs={{0,8},{8,0},{16,24},{24,16},{1,9},{9,1},{17,25},{25,17},{2,10},{10... | collective-permute-start | bytes 786440 | tf_op jit(solution)/shard_map/ppermute | solution.py:10
  45.9 1.5 %collective-permute-start.11 = (bf16[512,256]{1,0:T(8,128)(2,1)S(1)}, bf16[512,256]{1,0:T(8,128)(2,1)S(1)}, u32[]{:S(2)}, u32[]{:S(2)}) collective-permute-start(bf16[512,256]{1,0:T(8,128)(2,1)S(1)} %fusion.4), channel_id=1, source_target_pairs={{0,16},{8,24},{16,0},{24,8},{1,17},{9,25},{17,1},{25,9},{2,18},{10... | collective-permute-start | bytes 786440 | tf_op jit(solution)/shard_map/ppermute | solution.py:10
  47.5 0.5 collective-permute-start.12
  47.9 5.6 %collective-permute-done.10 = bf16[512,256]{1,0:T(8,128)(2,1)S(1)} collective-permute-done((bf16[512,256]{1,0:T(8,128)(2,1)S(1)}, bf16[512,256]{1,0:T(8,128)(2,1)S(1)}, u32[]{:S(2)}, u32[]{:S(2)}) %collective-permute-start.10) | collective-permute-done | bytes 262176 | tf_op jit(solution)/shard_map/ppermute | solution.py:10
  53.5 6.4 %collective-permute-done.11 = bf16[512,256]{1,0:T(8,128)(2,1)S(1)} collective-permute-done((bf16[512,256]{1,0:T(8,128)(2,1)S(1)}, bf16[512,256]{1,0:T(8,128)(2,1)S(1)}, u32[]{:S(2)}, u32[]{:S(2)}) %collective-permute-start.11) | collective-permute-done | bytes 262176 | tf_op jit(solution)/shard_map/ppermute | solution.py:10
  60.0 0.0 collective-permute-done.12
  60.0 0.1 pad_maximum_fusion.1
  60.1 0.6 gather_fusion.1
  60.8 3.2 %fusion.3 = f32[512,256]{1,0:T(8,128)} fusion(bf16[8,512,256]{2,1,0:T(8,128)(2,1)} %bitcast_dynamic-update-slice_fusion, bf16[8,256,256]{2,1,0:T(8,128)(2,1)S(1)} %gather_fusion.1, pred[8]{0:T(512)(128)(4,1)S(1)} %get-tuple-element.6, bf16[512,256]{1,0:T(8,128)(2,1)S(1)} %get-tuple-element.9, f32[64,8,2,128]{3,2,1,0:T(2,128)S(1)} %bitcast.58), kind=kOutput, calls=%fused_computation.7 | convolution fusion | flops 538050560 | bytes 4456456 | tf_op jit(solution)/shard_map/tmj,tjn->mn/dot_general | solution.py:55
  (4 shorter events, 0.1 us)
Async XLA Ops:
  3.1 9.2 %collective-permute-start.7 = (bf16[512,256]{1,0:T(8,128)(2,1)S(1)}, bf16[512,256]{1,0:T(8,128)(2,1)S(1)}, u32[]{:S(2)}, u32[]{:S(2)}) collective-permute-start(bf16[512,256]{1,0:T(8,128)(2,1)S(1)} %get-tuple-element.9), channel_id=1, source_target_pairs={{0,8},{8,0},{16,24},{24,16},{1,9},{9,1},{17,25},{25,17},{2,10},{10... | collective-permute-start | bytes 786440 | tf_op jit(solution)/shard_map/ppermute | solution.py:10
  4.6 13.4 %collective-permute-start.8 = (bf16[512,256]{1,0:T(8,128)(2,1)S(1)}, bf16[512,256]{1,0:T(8,128)(2,1)S(1)}, u32[]{:S(2)}, u32[]{:S(2)}) collective-permute-start(bf16[512,256]{1,0:T(8,128)(2,1)S(1)} %get-tuple-element.9), channel_id=1, source_target_pairs={{0,16},{8,24},{16,0},{24,8},{1,17},{9,25},{17,1},{25,9},{2,18},{10... | collective-permute-start | bytes 786440 | tf_op jit(solution)/shard_map/ppermute | solution.py:10
  6.1 12.3 %collective-permute-start.9 = (bf16[512,256]{1,0:T(8,128)(2,1)S(1)}, bf16[512,256]{1,0:T(8,128)(2,1)S(1)}, u32[]{:S(2)}, u32[]{:S(2)}) collective-permute-start(bf16[512,256]{1,0:T(8,128)(2,1)S(1)} %get-tuple-element.9), channel_id=1, source_target_pairs={{0,24},{8,16},{16,8},{24,0},{1,25},{9,17},{17,9},{25,1},{2,26},{10... | collective-permute-start | bytes 786440 | tf_op jit(solution)/shard_map/ppermute | solution.py:10
  6.6 29.6 %collective-permute-start = (bf16[512,256]{1,0:T(8,128)(2,1)S(1)}, bf16[512,256]{1,0:T(8,128)(2,1)S(1)}, u32[]{:S(2)}, u32[]{:S(2)}) collective-permute-start(bf16[512,256]{1,0:T(8,128)(2,1)S(1)} %get-tuple-element.9), channel_id=1, source_target_pairs={{0,1},{1,0},{2,3},{3,2},{4,5},{5,4},{6,7},{7,6},{8,9},{9,8},{10,11... | collective-permute-start | bytes 786440 | tf_op jit(solution)/shard_map/ppermute | solution.py:10
  6.6 12.6 %collective-permute-start.1 = (bf16[512,256]{1,0:T(8,128)(2,1)S(1)}, bf16[512,256]{1,0:T(8,128)(2,1)S(1)}, u32[]{:S(2)}, u32[]{:S(2)}) collective-permute-start(bf16[512,256]{1,0:T(8,128)(2,1)S(1)} %get-tuple-element.9), channel_id=1, source_target_pairs={{0,2},{1,3},{2,0},{3,1},{4,6},{5,7},{6,4},{7,5},{8,10},{9,11},{10,... | collective-permute-start | bytes 786440 | tf_op jit(solution)/shard_map/ppermute | solution.py:10
  12.3 18.0 %collective-permute-start.3 = (bf16[512,256]{1,0:T(8,128)(2,1)S(1)}, bf16[512,256]{1,0:T(8,128)(2,1)S(1)}, u32[]{:S(2)}, u32[]{:S(2)}) collective-permute-start(bf16[512,256]{1,0:T(8,128)(2,1)S(1)} %get-tuple-element.9), channel_id=1, source_target_pairs={{0,4},{1,5},{2,6},{3,7},{4,0},{5,1},{6,2},{7,3},{8,12},{9,13},{10,... | collective-permute-start | bytes 786440 | tf_op jit(solution)/shard_map/ppermute | solution.py:10
  18.0 18.3 %collective-permute-start.5 = (bf16[512,256]{1,0:T(8,128)(2,1)S(1)}, bf16[512,256]{1,0:T(8,128)(2,1)S(1)}, u32[]{:S(2)}, u32[]{:S(2)}) collective-permute-start(bf16[512,256]{1,0:T(8,128)(2,1)S(1)} %get-tuple-element.9), channel_id=1, source_target_pairs={{0,6},{1,7},{2,4},{3,5},{4,2},{5,3},{6,0},{7,1},{8,14},{9,15},{10,... | collective-permute-start | bytes 786440 | tf_op jit(solution)/shard_map/ppermute | solution.py:10
  19.3 18.4 %collective-permute-start.2 = (bf16[512,256]{1,0:T(8,128)(2,1)S(1)}, bf16[512,256]{1,0:T(8,128)(2,1)S(1)}, u32[]{:S(2)}, u32[]{:S(2)}) collective-permute-start(bf16[512,256]{1,0:T(8,128)(2,1)S(1)} %collective-permute-done.1), channel_id=1, source_target_pairs={{0,1},{1,0},{2,3},{3,2},{4,5},{5,4},{6,7},{7,6},{8,9},{9,8},{10,11... | collective-permute-start | bytes 786440 | tf_op jit(solution)/shard_map/ppermute | solution.py:10
  30.3 8.9 %collective-permute-start.4 = (bf16[512,256]{1,0:T(8,128)(2,1)S(1)}, bf16[512,256]{1,0:T(8,128)(2,1)S(1)}, u32[]{:S(2)}, u32[]{:S(2)}) collective-permute-start(bf16[512,256]{1,0:T(8,128)(2,1)S(1)} %collective-permute-done.3), channel_id=1, source_target_pairs={{0,1},{1,0},{2,3},{3,2},{4,5},{5,4},{6,7},{7,6},{8,9},{9,8},{10,11... | collective-permute-start | bytes 786440 | tf_op jit(solution)/shard_map/ppermute | solution.py:10
  36.2 4.4 %collective-permute-start.6 = (bf16[512,256]{1,0:T(8,128)(2,1)S(1)}, bf16[512,256]{1,0:T(8,128)(2,1)S(1)}, u32[]{:S(2)}, u32[]{:S(2)}) collective-permute-start(bf16[512,256]{1,0:T(8,128)(2,1)S(1)} %collective-permute-done.5), channel_id=1, source_target_pairs={{0,1},{1,0},{2,3},{3,2},{4,5},{5,4},{6,7},{7,6},{8,9},{9,8},{10,11... | collective-permute-start | bytes 786440 | tf_op jit(solution)/shard_map/ppermute | solution.py:10
  44.4 9.2 %collective-permute-start.10 = (bf16[512,256]{1,0:T(8,128)(2,1)S(1)}, bf16[512,256]{1,0:T(8,128)(2,1)S(1)}, u32[]{:S(2)}, u32[]{:S(2)}) collective-permute-start(bf16[512,256]{1,0:T(8,128)(2,1)S(1)} %fusion.4), channel_id=1, source_target_pairs={{0,8},{8,0},{16,24},{24,16},{1,9},{9,1},{17,25},{25,17},{2,10},{10... | collective-permute-start | bytes 786440 | tf_op jit(solution)/shard_map/ppermute | solution.py:10
  45.9 14.1 %collective-permute-start.11 = (bf16[512,256]{1,0:T(8,128)(2,1)S(1)}, bf16[512,256]{1,0:T(8,128)(2,1)S(1)}, u32[]{:S(2)}, u32[]{:S(2)}) collective-permute-start(bf16[512,256]{1,0:T(8,128)(2,1)S(1)} %fusion.4), channel_id=1, source_target_pairs={{0,16},{8,24},{16,0},{24,8},{1,17},{9,25},{17,1},{25,9},{2,18},{10... | collective-permute-start | bytes 786440 | tf_op jit(solution)/shard_map/ppermute | solution.py:10
  47.5 12.5 %collective-permute-start.12 = (bf16[512,256]{1,0:T(8,128)(2,1)S(1)}, bf16[512,256]{1,0:T(8,128)(2,1)S(1)}, u32[]{:S(2)}, u32[]{:S(2)}) collective-permute-start(bf16[512,256]{1,0:T(8,128)(2,1)S(1)} %fusion.4), channel_id=1, source_target_pairs={{0,24},{8,16},{16,8},{24,0},{1,25},{9,17},{17,9},{25,1},{2,26},{10... | collective-permute-start | bytes 786440 | tf_op jit(solution)/shard_map/ppermute | solution.py:10

commit v3 on v2

v3 whole, which is shorter than its diff:
```python
import jax
import jax.numpy as jnp
from jax import lax
from jax.sharding import PartitionSpec as P

B = 128


def _swap(x, axis, size, d):
    return lax.ppermute(x, axis, [(i, i ^ d) for i in range(size)])


def make_body(n_row, n_col):
    n_z = n_col // 2

    def body(matrix_in, pattern):
        rows, cols = matrix_in.shape
        ratio = rows // cols
        block_rows = rows // B
        block_cols = cols // B
        row_index = lax.axis_index("row")
        col_index = lax.axis_index("col")
        z_index = col_index // 2
        core = col_index % 2
        local_blocks = lax.dynamic_slice(
            pattern, (row_index * block_rows, col_index * block_cols), (block_rows, block_cols)
        )
        local_mask = jnp.repeat(jnp.repeat(local_blocks, B, axis=0), B, axis=1)
        masked = matrix_in * local_mask.astype(jnp.bfloat16)

        col_pieces = [masked] + [_swap(masked, "row", n_row, k) for k in range(1, n_row)]

        own = [(masked, z_index)]
        to_right, to_left = masked, masked
        for s in range(1, n_z):
            right_pairs = [(2 * (z - 1) + c, 2 * z + c) for z in range(s, n_z) for c in range(2)]
            left_pairs = [(2 * (z + 1) + c, 2 * z + c) for z in range(0, n_z - s) for c in range(2)]
            to_right = lax.ppermute(to_right, "col", right_pairs)
            to_left = lax.ppermute(to_left, "col", left_pairs)
            own.append((to_right, z_index - s))
            own.append((to_left, z_index + s))
        slots = [(p, 2 * zz + core) for p, zz in own]
        slots += [(_swap(p, "col", n_col, 1), 2 * zz + 1 - core) for p, zz in own]

        block = jnp.stack([jnp.clip(c, 0, n_col - 1) for _, c in slots])
        sub_index = ((block // ratio) ^ row_index) * ratio + block % ratio
        row_cat = jnp.concatenate([p for p, _ in slots], axis=1)

        def in_slot_order(pieces):
            stacked = jnp.stack(pieces).reshape(n_row * ratio, cols, cols)
            return jnp.take(stacked, sub_index, axis=0).reshape(len(slots) * cols, cols)

        square = jnp.dot(row_cat, in_slot_order(col_pieces), preferred_element_type=jnp.float32)
        mask_float = local_mask.astype(jnp.float32)
        filtered = (mask_float * square).astype(jnp.bfloat16)
        f_pieces = [filtered] + [_swap(filtered, "row", n_row, k) for k in range(1, n_row)]
        cubic = jnp.dot(row_cat, in_slot_order(f_pieces), preferred_element_type=jnp.float32)
        return mask_float * (1.5 * masked.astype(jnp.float32) - 0.5 * cubic)

    return body


def solution(mesh):
    return jax.shard_map(
        make_body(mesh.shape["row"], mesh.shape["col"]),
        mesh=mesh,
        in_specs=(P("row", "col"), P()),
        out_specs=P("row", "col"),
        check_vma=False,
    )
```

time: 64.2 us -> 71.9 us (1.12)
  the two profiles are of different devices: /device:TPU:16 before, /device:TPU:0 now
where the time goes in v3:
time: 71.9 us; the launch traced here: 71.5 us
  waiting for transfers between devices  37.7 us (52%)
  starting transfers between devices  19.5 us (27%)
  local copies, waits for them, and re-layouts  5.61 us (8%)
  matrix products  5.06 us (7%)
  other arithmetic  3.27 us (5%)
    ppermute x13, waiting for transfers between devices, _swap(): return lax.ppermute(x, axis, [(i, i ^ d) for i in range(size)])  24 us
    ppermute x3, waiting for transfers between devices, body(): to_left = lax.ppermute(to_left, 'col', left_pairs)  13.7 us
    ppermute x13, starting transfers between devices, _swap(): return lax.ppermute(x, axis, [(i, i ^ d) for i in range(size)])  8.4 us
    ppermute x3, starting transfers between devices, body(): to_right = lax.ppermute(to_right, 'col', right_pairs)  7.1 us
    ppermute x3, starting transfers between devices, body(): to_left = lax.ppermute(to_left, 'col', left_pairs)  3.98 us
    dot_general x1, matrix products, body(): jnp.dot(row_cat, in_slot_order(f_pieces), preferred_element_type=jnp.floa...  3.95 us
    unnamed x20, local copies, waits for them, and re-layouts  2.93 us
    unnamed x1, other arithmetic  1.74 us
  transfers between devices with their start and end apart: 19, of which 8 were waited for; matrix products, arithmetic and copies ran while one was open for 5% of the time, Pallas kernels for 0%

profile of v3, /device:TPU:0, one launch (start us, length us, event | category | flops | bytes accessed | tf_op | source)
XLA Modules:
  0.0 71.5 jit_solution(17875798088900565568)
XLA Ops:
  0.0 0.8 %dynamic-slice_convert_fusion.1 = (f32[4,2]{1,0:T(4,128)S(1)}, bf16[4,2]{1,0:T(4,128)(2,1)S(1)}) fusion(s32[16,16]{1,0:T(8,128)} %param.5, s32[]{:T(128)S(6)} %select_n.34, s32[]{:T(128)S(6)} %select_n.35), kind=kLoop, calls=%fused_computation.32 | loop fusion | flops 16 | bytes 88 | tf_op jit(solution)/shard_map/convert_element_type | solution.py:54
  0.8 0.6 broadcast_in_dim.22
  1.4 1.7 %constant_dynamic-update-slice_fusion.13 = (bf16[512,3584]{1,0:T(8,128)(2,1)}, bf16[512,256]{1,0:T(8,128)(2,1)S(1)}) fusion(bf16[512,256]{1,0:T(8,128)(2,1)} %param.4, bf16[64,8,2,128]{3,2,1,0:T(2,128)(2,1)S(1)} %bitcast.45), kind=kLoop, calls=%fused_computation.25 | loop fusion | flops 524287 | bytes 1048576
  3.1 5.6 %collective-permute-start = (bf16[512,256]{1,0:T(8,128)(2,1)S(1)}, bf16[512,256]{1,0:T(8,128)(2,1)}, u32[]{:S(2)}, u32[]{:S(2)}) collective-permute-start(bf16[512,256]{1,0:T(8,128)(2,1)S(1)} %get-tuple-element.9), channel_id=1, source_target_pairs={{0,2},{1,3},{2,4},{3,5},{4,6},{5,7},{8,10},{9,11},{10,12},{11,13},... | collective-permute-start | bytes 786440 | tf_op jit(solution)/shard_map/ppermute | solution.py:38
  8.8 1.3 %collective-permute-start.1 = (bf16[512,256]{1,0:T(8,128)(2,1)S(1)}, bf16[512,256]{1,0:T(8,128)(2,1)S(1)}, u32[]{:S(2)}, u32[]{:S(2)}) collective-permute-start(bf16[512,256]{1,0:T(8,128)(2,1)S(1)} %get-tuple-element.9), channel_id=1, source_target_pairs={{2,0},{3,1},{4,2},{5,3},{6,4},{7,5},{10,8},{11,9},{12,10},{13,11},... | collective-permute-start | bytes 786440 | tf_op jit(solution)/shard_map/ppermute | solution.py:39
  10.0 1.6 %collective-permute-start.13 = (bf16[512,256]{1,0:T(8,128)(2,1)S(1)}, bf16[512,256]{1,0:T(8,128)(2,1)S(1)}, u32[]{:S(2)}, u32[]{:S(2)}) collective-permute-start(bf16[512,256]{1,0:T(8,128)(2,1)S(1)} %get-tuple-element.9), channel_id=1, source_target_pairs={{0,8},{8,0},{16,24},{24,16},{1,9},{9,1},{17,25},{25,17},{2,10},{10... | collective-permute-start | bytes 786440 | tf_op jit(solution)/shard_map/ppermute | solution.py:10
  11.6 1.5 %collective-permute-start.14 = (bf16[512,256]{1,0:T(8,128)(2,1)S(1)}, bf16[512,256]{1,0:T(8,128)(2,1)S(1)}, u32[]{:S(2)}, u32[]{:S(2)}) collective-permute-start(bf16[512,256]{1,0:T(8,128)(2,1)S(1)} %get-tuple-element.9), channel_id=1, source_target_pairs={{0,16},{8,24},{16,0},{24,8},{1,17},{9,25},{17,1},{25,9},{2,18},{10... | collective-permute-start | bytes 786440 | tf_op jit(solution)/shard_map/ppermute | solution.py:10
  13.1 0.5 collective-permute-start.15
  13.6 0.1 stack.94
  13.7 5.6 %collective-permute-done.13 = bf16[512,256]{1,0:T(8,128)(2,1)S(1)} collective-permute-done((bf16[512,256]{1,0:T(8,128)(2,1)S(1)}, bf16[512,256]{1,0:T(8,128)(2,1)S(1)}, u32[]{:S(2)}, u32[]{:S(2)}) %collective-permute-start.13) | collective-permute-done | bytes 262176 | tf_op jit(solution)/shard_map/ppermute | solution.py:10
  19.3 0.0 collective-permute-start.6
  19.3 5.4 %collective-permute-done.14 = bf16[512,256]{1,0:T(8,128)(2,1)S(1)} collective-permute-done((bf16[512,256]{1,0:T(8,128)(2,1)S(1)}, bf16[512,256]{1,0:T(8,128)(2,1)S(1)}, u32[]{:S(2)}, u32[]{:S(2)}) %collective-permute-start.14) | collective-permute-done | bytes 262176 | tf_op jit(solution)/shard_map/ppermute | solution.py:10
  24.7 0.0 collective-permute-done.15
  24.7 0.1 pad_maximum_fusion
  24.8 0.7 gather_fusion
  25.5 0.0 copy-start.2
  25.5 0.0 collective-permute-done
  25.5 0.8 %collective-permute-start.2 = (bf16[512,256]{1,0:T(8,128)(2,1)}, bf16[512,256]{1,0:T(8,128)(2,1)S(1)}, u32[]{:S(2)}, u32[]{:S(2)}) collective-permute-start(bf16[512,256]{1,0:T(8,128)(2,1)} %collective-permute-done), channel_id=1, source_target_pairs={{2,4},{3,5},{4,6},{5,7},{10,12},{11,13},{12,14},{13,15},{18,20},{1... | collective-permute-start | bytes 786440 | tf_op jit(solution)/shard_map/ppermute | solution.py:38
  26.3 0.0 collective-permute-done.1
  26.4 1.4 %collective-permute-start.3 = (bf16[512,256]{1,0:T(8,128)(2,1)S(1)}, bf16[512,256]{1,0:T(8,128)(2,1)S(1)}, u32[]{:S(2)}, u32[]{:S(2)}) collective-permute-start(bf16[512,256]{1,0:T(8,128)(2,1)S(1)} %collective-permute-done.1), channel_id=1, source_target_pairs={{2,0},{3,1},{4,2},{5,3},{10,8},{11,9},{12,10},{13,11},{18,16},{19,... | collective-permute-start | bytes 786440 | tf_op jit(solution)/shard_map/ppermute | solution.py:39
  27.8 0.2 broadcast_select_fusion
  28.0 0.1 collective-permute-start.7
  28.1 0.5 collective-permute-start.8
  28.6 0.0 copy-done.2
  28.6 1.0 %constant_dynamic-update-slice_fusion.12 = bf16[512,3584]{1,0:T(8,128)(2,1)S(1)} fusion(bf16[512,3584]{1,0:T(8,128)(2,1)S(1)} %copy-done.2, bf16[512,256]{1,0:T(8,128)(2,1)} %collective-permute-done), kind=kLoop, calls=%fused_computation.24 | loop fusion | bytes 524288
  29.6 0.0 collective-permute-done.2
  29.6 0.7 collective-permute-start.4
  30.3 6.9 %collective-permute-done.3 = bf16[512,256]{1,0:T(8,128)(2,1)S(1)} collective-permute-done((bf16[512,256]{1,0:T(8,128)(2,1)S(1)}, bf16[512,256]{1,0:T(8,128)(2,1)S(1)}, u32[]{:S(2)}, u32[]{:S(2)}) %collective-permute-start.3) | collective-permute-done | bytes 262176 | tf_op jit(solution)/shard_map/ppermute | solution.py:39
  37.3 1.3 %collective-permute-start.5 = (bf16[512,256]{1,0:T(8,128)(2,1)S(1)}, bf16[512,256]{1,0:T(8,128)(2,1)S(1)}, u32[]{:S(2)}, u32[]{:S(2)}) collective-permute-start(bf16[512,256]{1,0:T(8,128)(2,1)S(1)} %collective-permute-done.3), channel_id=1, source_target_pairs={{2,0},{3,1},{10,8},{11,9},{18,16},{19,17},{26,24},{27,25}} | collective-permute-start | bytes 786440 | tf_op jit(solution)/shard_map/ppermute | solution.py:39
  38.6 0.0 collective-permute-done.4
  38.6 0.1 collective-permute-start.9
  38.7 6.8 %collective-permute-done.5 = bf16[512,256]{1,0:T(8,128)(2,1)S(1)} collective-permute-done((bf16[512,256]{1,0:T(8,128)(2,1)S(1)}, bf16[512,256]{1,0:T(8,128)(2,1)S(1)}, u32[]{:S(2)}, u32[]{:S(2)}) %collective-permute-start.5) | collective-permute-done | bytes 262176 | tf_op jit(solution)/shard_map/ppermute | solution.py:39
  45.5 0.0 collective-permute-start.10
  45.5 0.0 collective-permute-done.6
  45.5 0.6 collective-permute-start.11
  46.1 1.0 %constant_dynamic-update-slice_fusion.6 = bf16[512,3584]{1,0:T(8,128)(2,1)S(1)} fusion(bf16[512,3584]{1,0:T(8,128)(2,1)S(1)} %constant_dynamic-update-slice_fusion.7, bf16[512,256]{1,0:T(8,128)(2,1)} %collective-permute-done.6), kind=kLoop, calls=%fused_computation.18 | loop fusion | bytes 524288
  47.1 0.0 collective-permute-done.7
  47.1 0.1 collective-permute-start.12
  47.2 0.0 collective-permute-done.8
  47.2 0.0 collective-permute-done.9
  47.3 0.0 collective-permute-done.10
  47.3 0.1 collective-permute-done.11
  47.4 1.3 %collective-permute-done.12 = bf16[512,256]{1,0:T(8,128)(2,1)S(1)} collective-permute-done((bf16[512,256]{1,0:T(8,128)(2,1)S(1)}, bf16[512,256]{1,0:T(8,128)(2,1)S(1)}, u32[]{:S(2)}, u32[]{:S(2)}) %collective-permute-start.12) | collective-permute-done | bytes 262176 | tf_op jit(solution)/shard_map/ppermute | solution.py:10
  48.7 0.0 copy-start.3
  48.8 0.6 broadcast_in_dim.20
  49.4 0.0 copy-start
  49.4 1.1 %fusion.2 = bf16[512,256]{1,0:T(8,128)(2,1)S(1)} fusion(bf16[512,3584]{1,0:T(8,128)(2,1)S(1)} %constant_dynamic-update-slice_fusion, bf16[3584,256]{1,0:T(8,128)(2,1)S(1)} %bitcast.42, f32[64,8,2,128]{3,2,1,0:T(2,128)S(1)} %bitcast.48), kind=kOutput, calls=%fused_computation.8 | convolution fusion | flops 939786240 | bytes 6291456 | tf_op jit(solution)/shard_map/dot_general | solution.py:53
  50.5 1.5 %collective-permute-start.16 = (bf16[512,256]{1,0:T(8,128)(2,1)S(1)}, bf16[512,256]{1,0:T(8,128)(2,1)S(1)}, u32[]{:S(2)}, u32[]{:S(2)}) collective-permute-start(bf16[512,256]{1,0:T(8,128)(2,1)S(1)} %fusion.2), channel_id=1, source_target_pairs={{0,8},{8,0},{16,24},{24,16},{1,9},{9,1},{17,25},{25,17},{2,10},{10... | collective-permute-start | bytes 786440 | tf_op jit(solution)/shard_map/ppermute | solution.py:10
  52.0 0.6 collective-permute-start.17
  52.6 1.4 %collective-permute-start.18 = (bf16[512,256]{1,0:T(8,128)(2,1)S(1)}, bf16[512,256]{1,0:T(8,128)(2,1)S(1)}, u32[]{:S(2)}, u32[]{:S(2)}) collective-permute-start(bf16[512,256]{1,0:T(8,128)(2,1)S(1)} %fusion.2), channel_id=1, source_target_pairs={{0,24},{8,16},{16,8},{24,0},{1,25},{9,17},{17,9},{25,1},{2,26},{10... | collective-permute-start | bytes 786440 | tf_op jit(solution)/shard_map/ppermute | solution.py:10
  54.0 5.7 %collective-permute-done.16 = bf16[512,256]{1,0:T(8,128)(2,1)S(1)} collective-permute-done((bf16[512,256]{1,0:T(8,128)(2,1)S(1)}, bf16[512,256]{1,0:T(8,128)(2,1)S(1)}, u32[]{:S(2)}, u32[]{:S(2)}) %collective-permute-start.16) | collective-permute-done | bytes 262176 | tf_op jit(solution)/shard_map/ppermute | solution.py:10
  59.7 6.0 %collective-permute-done.17 = bf16[512,256]{1,0:T(8,128)(2,1)S(1)} collective-permute-done((bf16[512,256]{1,0:T(8,128)(2,1)S(1)}, bf16[512,256]{1,0:T(8,128)(2,1)S(1)}, u32[]{:S(2)}, u32[]{:S(2)}) %collective-permute-start.17) | collective-permute-done | bytes 262176 | tf_op jit(solution)/shard_map/ppermute | solution.py:10
  65.7 0.0 collective-permute-done.18
  65.7 0.1 pad_maximum_fusion.1
  65.8 0.0 copy-done.3
  65.8 0.0 copy-done
  65.8 0.7 gather_fusion.1
  66.5 0.0 copy-start.1
  66.5 0.2 broadcast_select_fusion.1
  66.7 0.8 %copy-done.1 = f32[512,2,128]{2,1,0:T(2,128)S(1)} copy-done((f32[512,2,128]{2,1,0:T(2,128)S(1)}, f32[512,2,128]{2,1,0:T(2,128)}, u32[]{:S(2)}) %copy-start.1) | copy-done | bytes 524312
  67.5 4.0 %fusion.1 = f32[512,256]{1,0:T(8,128)} fusion(bf16[512,3584]{1,0:T(8,128)(2,1)} %copy-done.3, bf16[3584,256]{1,0:T(8,128)(2,1)S(1)} %bitcast.43, bf16[512,256]{1,0:T(8,128)(2,1)S(1)} %get-tuple-element.9, f32[64,8,2,128]{3,2,1,0:T(2,128)S(1)} %bitcast.49), kind=kOutput, calls=%fused_computation.7 | convolution fusion | flops 940179456 | bytes 6815744 | tf_op jit(solution)/shard_map/dot_general | solution.py:57
  (15 shorter events, 0.3 us)
Async XLA Ops:
  3.1 22.4 %collective-permute-start = (bf16[512,256]{1,0:T(8,128)(2,1)S(1)}, bf16[512,256]{1,0:T(8,128)(2,1)}, u32[]{:S(2)}, u32[]{:S(2)}) collective-permute-start(bf16[512,256]{1,0:T(8,128)(2,1)S(1)} %get-tuple-element.9), channel_id=1, source_target_pairs={{0,2},{1,3},{2,4},{3,5},{4,6},{5,7},{8,10},{9,11},{10,12},{11,13},... | collective-permute-start | bytes 786440 | tf_op jit(solution)/shard_map/ppermute | solution.py:38
  8.8 17.6 %collective-permute-start.1 = (bf16[512,256]{1,0:T(8,128)(2,1)S(1)}, bf16[512,256]{1,0:T(8,128)(2,1)S(1)}, u32[]{:S(2)}, u32[]{:S(2)}) collective-permute-start(bf16[512,256]{1,0:T(8,128)(2,1)S(1)} %get-tuple-element.9), channel_id=1, source_target_pairs={{2,0},{3,1},{4,2},{5,3},{6,4},{7,5},{10,8},{11,9},{12,10},{13,11},... | collective-permute-start | bytes 786440 | tf_op jit(solution)/shard_map/ppermute | solution.py:39
  10.0 9.3 %collective-permute-start.13 = (bf16[512,256]{1,0:T(8,128)(2,1)S(1)}, bf16[512,256]{1,0:T(8,128)(2,1)S(1)}, u32[]{:S(2)}, u32[]{:S(2)}) collective-permute-start(bf16[512,256]{1,0:T(8,128)(2,1)S(1)} %get-tuple-element.9), channel_id=1, source_target_pairs={{0,8},{8,0},{16,24},{24,16},{1,9},{9,1},{17,25},{25,17},{2,10},{10... | collective-permute-start | bytes 786440 | tf_op jit(solution)/shard_map/ppermute | solution.py:10
  11.6 13.1 %collective-permute-start.14 = (bf16[512,256]{1,0:T(8,128)(2,1)S(1)}, bf16[512,256]{1,0:T(8,128)(2,1)S(1)}, u32[]{:S(2)}, u32[]{:S(2)}) collective-permute-start(bf16[512,256]{1,0:T(8,128)(2,1)S(1)} %get-tuple-element.9), channel_id=1, source_target_pairs={{0,16},{8,24},{16,0},{24,8},{1,17},{9,25},{17,1},{25,9},{2,18},{10... | collective-permute-start | bytes 786440 | tf_op jit(solution)/shard_map/ppermute | solution.py:10
  13.1 11.6 %collective-permute-start.15 = (bf16[512,256]{1,0:T(8,128)(2,1)S(1)}, bf16[512,256]{1,0:T(8,128)(2,1)S(1)}, u32[]{:S(2)}, u32[]{:S(2)}) collective-permute-start(bf16[512,256]{1,0:T(8,128)(2,1)S(1)} %get-tuple-element.9), channel_id=1, source_target_pairs={{0,24},{8,16},{16,8},{24,0},{1,25},{9,17},{17,9},{25,1},{2,26},{10... | collective-permute-start | bytes 786440 | tf_op jit(solution)/shard_map/ppermute | solution.py:10
  19.3 26.2 %collective-permute-start.6 = (bf16[512,256]{1,0:T(8,128)(2,1)S(1)}, bf16[512,256]{1,0:T(8,128)(2,1)}, u32[]{:S(2)}, u32[]{:S(2)}) collective-permute-start(bf16[512,256]{1,0:T(8,128)(2,1)S(1)} %get-tuple-element.9), channel_id=1, source_target_pairs={{0,1},{1,0},{2,3},{3,2},{4,5},{5,4},{6,7},{7,6},{8,9},{9,8},{10,11... | collective-permute-start | bytes 786440 | tf_op jit(solution)/shard_map/ppermute | solution.py:10
  25.5 3.1 %copy-start.2 = (bf16[512,3584]{1,0:T(8,128)(2,1)S(1)}, bf16[512,3584]{1,0:T(8,128)(2,1)}, u32[]{:S(2)}) copy-start(bf16[512,3584]{1,0:T(8,128)(2,1)} %get-tuple-element.8) | copy-start | bytes 11010052
  25.5 4.1 %collective-permute-start.2 = (bf16[512,256]{1,0:T(8,128)(2,1)}, bf16[512,256]{1,0:T(8,128)(2,1)S(1)}, u32[]{:S(2)}, u32[]{:S(2)}) collective-permute-start(bf16[512,256]{1,0:T(8,128)(2,1)} %collective-permute-done), channel_id=1, source_target_pairs={{2,4},{3,5},{4,6},{5,7},{10,12},{11,13},{12,14},{13,15},{18,20},{1... | collective-permute-start | bytes 786440 | tf_op jit(solution)/shard_map/ppermute | solution.py:38
  26.4 10.9 %collective-permute-start.3 = (bf16[512,256]{1,0:T(8,128)(2,1)S(1)}, bf16[512,256]{1,0:T(8,128)(2,1)S(1)}, u32[]{:S(2)}, u32[]{:S(2)}) collective-permute-start(bf16[512,256]{1,0:T(8,128)(2,1)S(1)} %collective-permute-done.1), channel_id=1, source_target_pairs={{2,0},{3,1},{4,2},{5,3},{10,8},{11,9},{12,10},{13,11},{18,16},{19,... | collective-permute-start | bytes 786440 | tf_op jit(solution)/shard_map/ppermute | solution.py:39
  28.0 19.1 %collective-permute-start.7 = (bf16[512,256]{1,0:T(8,128)(2,1)}, bf16[512,256]{1,0:T(8,128)(2,1)S(1)}, u32[]{:S(2)}, u32[]{:S(2)}) collective-permute-start(bf16[512,256]{1,0:T(8,128)(2,1)} %collective-permute-done), channel_id=1, source_target_pairs={{0,1},{1,0},{2,3},{3,2},{4,5},{5,4},{6,7},{7,6},{8,9},{9,8},{10,11... | collective-permute-start | bytes 786440 | tf_op jit(solution)/shard_map/ppermute | solution.py:10
  28.1 19.1 %collective-permute-start.8 = (bf16[512,256]{1,0:T(8,128)(2,1)S(1)}, bf16[512,256]{1,0:T(8,128)(2,1)S(1)}, u32[]{:S(2)}, u32[]{:S(2)}) collective-permute-start(bf16[512,256]{1,0:T(8,128)(2,1)S(1)} %collective-permute-done.1), channel_id=1, source_target_pairs={{0,1},{1,0},{2,3},{3,2},{4,5},{5,4},{6,7},{7,6},{8,9},{9,8},{10,11... | collective-permute-start | bytes 786440 | tf_op jit(solution)/shard_map/ppermute | solution.py:10
  29.6 9.0 %collective-permute-start.4 = (bf16[512,256]{1,0:T(8,128)(2,1)S(1)}, bf16[512,256]{1,0:T(8,128)(2,1)S(1)}, u32[]{:S(2)}, u32[]{:S(2)}) collective-permute-start(bf16[512,256]{1,0:T(8,128)(2,1)S(1)} %collective-permute-done.2), channel_id=1, source_target_pairs={{4,6},{5,7},{12,14},{13,15},{20,22},{21,23},{28,30},{29,31}} | collective-permute-start | bytes 786440 | tf_op jit(solution)/shard_map/ppermute | solution.py:38
  37.3 8.3 %collective-permute-start.5 = (bf16[512,256]{1,0:T(8,128)(2,1)S(1)}, bf16[512,256]{1,0:T(8,128)(2,1)S(1)}, u32[]{:S(2)}, u32[]{:S(2)}) collective-permute-start(bf16[512,256]{1,0:T(8,128)(2,1)S(1)} %collective-permute-done.3), channel_id=1, source_target_pairs={{2,0},{3,1},{10,8},{11,9},{18,16},{19,17},{26,24},{27,25}} | collective-permute-start | bytes 786440 | tf_op jit(solution)/shard_map/ppermute | solution.py:39
  38.6 8.6 %collective-permute-start.9 = (bf16[512,256]{1,0:T(8,128)(2,1)S(1)}, bf16[512,256]{1,0:T(8,128)(2,1)S(1)}, u32[]{:S(2)}, u32[]{:S(2)}) collective-permute-start(bf16[512,256]{1,0:T(8,128)(2,1)S(1)} %collective-permute-done.2), channel_id=1, source_target_pairs={{0,1},{1,0},{2,3},{3,2},{4,5},{5,4},{6,7},{7,6},{8,9},{9,8},{10,11... | collective-permute-start | bytes 786440 | tf_op jit(solution)/shard_map/ppermute | solution.py:10
  45.5 1.8 %collective-permute-start.10 = (bf16[512,256]{1,0:T(8,128)(2,1)S(1)}, bf16[512,256]{1,0:T(8,128)(2,1)S(1)}, u32[]{:S(2)}, u32[]{:S(2)}) collective-permute-start(bf16[512,256]{1,0:T(8,128)(2,1)S(1)} %collective-permute-done.3), channel_id=1, source_target_pairs={{0,1},{1,0},{2,3},{3,2},{4,5},{5,4},{6,7},{7,6},{8,9},{9,8},{10,11... | collective-permute-start | bytes 786440 | tf_op jit(solution)/shard_map/ppermute | solution.py:10
  45.5 1.9 %collective-permute-start.11 = (bf16[512,256]{1,0:T(8,128)(2,1)S(1)}, bf16[512,256]{1,0:T(8,128)(2,1)S(1)}, u32[]{:S(2)}, u32[]{:S(2)}) collective-permute-start(bf16[512,256]{1,0:T(8,128)(2,1)S(1)} %collective-permute-done.4), channel_id=1, source_target_pairs={{0,1},{1,0},{2,3},{3,2},{4,5},{5,4},{6,7},{7,6},{8,9},{9,8},{10,11... | collective-permute-start | bytes 786440 | tf_op jit(solution)/shard_map/ppermute | solution.py:10
  47.1 1.6 %collective-permute-start.12 = (bf16[512,256]{1,0:T(8,128)(2,1)S(1)}, bf16[512,256]{1,0:T(8,128)(2,1)S(1)}, u32[]{:S(2)}, u32[]{:S(2)}) collective-permute-start(bf16[512,256]{1,0:T(8,128)(2,1)S(1)} %collective-permute-done.5), channel_id=1, source_target_pairs={{0,1},{1,0},{2,3},{3,2},{4,5},{5,4},{6,7},{7,6},{8,9},{9,8},{10,11... | collective-permute-start | bytes 786440 | tf_op jit(solution)/shard_map/ppermute | solution.py:10
  48.7 17.1 %copy-start.3 = (bf16[512,3584]{1,0:T(8,128)(2,1)}, bf16[512,3584]{1,0:T(8,128)(2,1)S(1)}, u32[]{:S(2)}) copy-start(bf16[512,3584]{1,0:T(8,128)(2,1)S(1)} %constant_dynamic-update-slice_fusion) | copy-start | bytes 11010052
  49.4 16.5 %copy-start = (f32[512,2,128]{2,1,0:T(2,128)}, f32[512,2,128]{2,1,0:T(2,128)S(1)}, u32[]{:S(2)}) copy-start(f32[512,2,128]{2,1,0:T(2,128)S(1)} %broadcast_in_dim.20) | copy-start | bytes 1572868
  50.5 9.2 %collective-permute-start.16 = (bf16[512,256]{1,0:T(8,128)(2,1)S(1)}, bf16[512,256]{1,0:T(8,128)(2,1)S(1)}, u32[]{:S(2)}, u32[]{:S(2)}) collective-permute-start(bf16[512,256]{1,0:T(8,128)(2,1)S(1)} %fusion.2), channel_id=1, source_target_pairs={{0,8},{8,0},{16,24},{24,16},{1,9},{9,1},{17,25},{25,17},{2,10},{10... | collective-permute-start | bytes 786440 | tf_op jit(solution)/shard_map/ppermute | solution.py:10
  52.0 13.7 %collective-permute-start.17 = (bf16[512,256]{1,0:T(8,128)(2,1)S(1)}, bf16[512,256]{1,0:T(8,128)(2,1)S(1)}, u32[]{:S(2)}, u32[]{:S(2)}) collective-permute-start(bf16[512,256]{1,0:T(8,128)(2,1)S(1)} %fusion.2), channel_id=1, source_target_pairs={{0,16},{8,24},{16,0},{24,8},{1,17},{9,25},{17,1},{25,9},{2,18},{10... | collective-permute-start | bytes 786440 | tf_op jit(solution)/shard_map/ppermute | solution.py:10
  52.6 13.1 %collective-permute-start.18 = (bf16[512,256]{1,0:T(8,128)(2,1)S(1)}, bf16[512,256]{1,0:T(8,128)(2,1)S(1)}, u32[]{:S(2)}, u32[]{:S(2)}) collective-permute-start(bf16[512,256]{1,0:T(8,128)(2,1)S(1)} %fusion.2), channel_id=1, source_target_pairs={{0,24},{8,16},{16,8},{24,0},{1,25},{9,17},{17,9},{25,1},{2,26},{10... | collective-permute-start | bytes 786440 | tf_op jit(solution)/shard_map/ppermute | solution.py:10
  66.5 1.0 %copy-start.1 = (f32[512,2,128]{2,1,0:T(2,128)S(1)}, f32[512,2,128]{2,1,0:T(2,128)}, u32[]{:S(2)}) copy-start(f32[512,2,128]{2,1,0:T(2,128)} %copy-done) | copy-start | bytes 1572868

commit v4 on v2

--- a/solution.py
+++ b/solution.py
@@ -41,18 +41,15 @@
 
         def in_slot_order(pieces):
             stacked = jnp.stack(pieces).reshape(n_row * ratio, cols, cols)
-            return jnp.take(stacked, sub_index, axis=0)
+            return jnp.take(stacked, sub_index, axis=0).reshape(n_col * cols, cols)
 
-        row_stack = jnp.stack(row_pieces)
-        col_slot = in_slot_order(col_pieces)
-        square = jnp.einsum(
-            "tmj,tjn->mn", row_stack, col_slot, preferred_element_type=jnp.float32
-        )
+        row_cat = jnp.concatenate(row_pieces, axis=1)
+        square = jnp.dot(row_cat, in_slot_order(col_pieces), preferred_element_type=jnp.float32)
         mask_float = local_mask.astype(jnp.float32)
         filtered = (mask_float * square).astype(jnp.bfloat16)
         f_pieces = [filtered] + [_swap(filtered, "row", n_row, k) for k in range(1, n_row)]
         f_slot = in_slot_order(f_pieces)
-        cubic = jnp.einsum("tmj,tjn->mn", row_stack, f_slot, preferred_element_type=jnp.float32)
+        cubic = jnp.dot(row_cat, f_slot, preferred_element_type=jnp.float32)
         return mask_float * (1.5 * masked.astype(jnp.float32) - 0.5 * cubic)
 
     return body

time: 64.2 us -> 58.6 us (0.913)
  local copies, waits for them, and re-layouts: 7.58 us -> 4.07 us
  matrix products: 5.54 us -> 2.22 us
  waiting for transfers between devices: 38.8 us -> 39.6 us
    dot_general x2, matrix products: 5.54 us -> 2.22 us  [the longest x1 1.51 us: body(): cubic = jnp.dot(row_cat, f_slot, preferred_element_type=jnp.float32)]
    unnamed x6 -> x12, local copies, waits for them, and re-layouts: 4.37 us -> 1.58 us
    ppermute x13, waiting for transfers between devices: 38.8 us -> 39.6 us  [_swap(): return lax.ppermute(x, axis, [(i, i ^ d) for i in range(size)])]
    another operation x1 -> x0, local copies, waits for them, and re-layouts: 0.74 us -> none  [body(): row_stack = jnp.stack(row_pieces)]
  transfers between devices with their start and end apart: 13 -> 13, of which waited for: 6 -> 7; matrix products, arithmetic and copies ran while one was open for 8% -> 2% of each run, Pallas kernels for 0% -> 0%
where the time goes in v4:
time: 58.6 us; the launch traced here: 58.4 us
  waiting for transfers between devices  39.6 us (68%)
  starting transfers between devices  9.15 us (16%)
  local copies, waits for them, and re-layouts  4.07 us (7%)
  other arithmetic  3.17 us (5%)
  matrix products  2.22 us (4%)
    ppermute x13, waiting for transfers between devices, _swap(): return lax.ppermute(x, axis, [(i, i ^ d) for i in range(size)])  39.6 us
    ppermute x13, starting transfers between devices, _swap(): return lax.ppermute(x, axis, [(i, i ^ d) for i in range(size)])  9.15 us
    unnamed x1, other arithmetic  1.79 us
    unnamed x12, local copies, waits for them, and re-layouts  1.58 us
    dot_general x1, matrix products, body(): cubic = jnp.dot(row_cat, f_slot, preferred_element_type=jnp.float32)  1.51 us
    broadcast_in_dim x4, local copies, waits for them, and re-layouts, body(): local_mask = jnp.repeat(jnp.repeat(local_blocks, B, axis=0), B, axis=1)  1.24 us
    gather x2, local copies, waits for them, and re-layouts, in_slot_order(): return jnp.take(stacked, sub_index, axis=0).reshape(n_col * cols, cols)  1.23 us
  transfers between devices with their start and end apart: 13, of which 7 were waited for; matrix products, arithmetic and copies ran while one was open for 2% of the time, Pallas kernels for 0%

profile of v4, /device:TPU:16, one launch (start us, length us, event | category | flops | bytes accessed | tf_op | source)
XLA Modules:
  0.0 58.4 jit_solution(7862055883823726192)
XLA Ops:
  0.0 0.8 %dynamic-slice_convert_fusion.1 = (f32[4,2]{1,0:T(4,128)S(1)}, bf16[4,2]{1,0:T(4,128)(2,1)S(1)}) fusion(s32[16,16]{1,0:T(8,128)} %param.5, s32[]{:T(128)S(6)} %select_n.24, s32[]{:T(128)S(6)} %select_n.25), kind=kLoop, calls=%fused_computation.26 | loop fusion | flops 16 | bytes 88 | tf_op jit(solution)/shard_map/convert_element_type | solution.py:48
  0.8 0.6 %broadcast_in_dim.22 = bf16[512,2,128]{2,1,0:T(2,128)(2,1)S(1)} broadcast(bf16[512,2]{1,0:T(8,128)(2,1)S(1)} %bitcast.33), dimensions={0,1} | broadcast | bytes 264192 | tf_op jit(solution)/shard_map/broadcast_in_dim | solution.py:26
  1.4 1.8 %constant_dynamic-update-slice_fusion.7 = (bf16[512,2048]{1,0:T(8,128)(2,1)}, bf16[512,256]{1,0:T(8,128)(2,1)S(1)}) fusion(bf16[512,256]{1,0:T(8,128)(2,1)} %param.4, bf16[64,8,2,128]{3,2,1,0:T(2,128)(2,1)S(1)} %bitcast.31), kind=kLoop, calls=%fused_computation.19 | loop fusion | flops 524287 | bytes 1048576
  3.2 1.5 %collective-permute-start.7 = (bf16[512,256]{1,0:T(8,128)(2,1)S(1)}, bf16[512,256]{1,0:T(8,128)(2,1)S(1)}, u32[]{:S(2)}, u32[]{:S(2)}) collective-permute-start(bf16[512,256]{1,0:T(8,128)(2,1)S(1)} %get-tuple-element.9), channel_id=1, source_target_pairs={{0,8},{8,0},{16,24},{24,16},{1,9},{9,1},{17,25},{25,17},{2,10},{10... | collective-permute-start | bytes 786440 | tf_op jit(solution)/shard_map/ppermute | solution.py:10
  4.7 1.5 %collective-permute-start.8 = (bf16[512,256]{1,0:T(8,128)(2,1)S(1)}, bf16[512,256]{1,0:T(8,128)(2,1)S(1)}, u32[]{:S(2)}, u32[]{:S(2)}) collective-permute-start(bf16[512,256]{1,0:T(8,128)(2,1)S(1)} %get-tuple-element.9), channel_id=1, source_target_pairs={{0,16},{8,24},{16,0},{24,8},{1,17},{9,25},{17,1},{25,9},{2,18},{10... | collective-permute-start | bytes 786440 | tf_op jit(solution)/shard_map/ppermute | solution.py:10
  6.2 0.5 collective-permute-start.9
  6.7 0.0 collective-permute-start
  6.7 1.6 %collective-permute-start.1 = (bf16[512,256]{1,0:T(8,128)(2,1)S(1)}, bf16[512,256]{1,0:T(8,128)(2,1)S(1)}, u32[]{:S(2)}, u32[]{:S(2)}) collective-permute-start(bf16[512,256]{1,0:T(8,128)(2,1)S(1)} %get-tuple-element.9), channel_id=1, source_target_pairs={{0,2},{1,3},{2,0},{3,1},{4,6},{5,7},{6,4},{7,5},{8,10},{9,11},{10,... | collective-permute-start | bytes 786440 | tf_op jit(solution)/shard_map/ppermute | solution.py:10
  8.3 4.1 %collective-permute-done.7 = bf16[512,256]{1,0:T(8,128)(2,1)S(1)} collective-permute-done((bf16[512,256]{1,0:T(8,128)(2,1)S(1)}, bf16[512,256]{1,0:T(8,128)(2,1)S(1)}, u32[]{:S(2)}, u32[]{:S(2)}) %collective-permute-start.7) | collective-permute-done | bytes 262176 | tf_op jit(solution)/shard_map/ppermute | solution.py:10
  12.4 0.0 collective-permute-start.3
  12.4 5.7 %collective-permute-done.8 = bf16[512,256]{1,0:T(8,128)(2,1)S(1)} collective-permute-done((bf16[512,256]{1,0:T(8,128)(2,1)S(1)}, bf16[512,256]{1,0:T(8,128)(2,1)S(1)}, u32[]{:S(2)}, u32[]{:S(2)}) %collective-permute-start.8) | collective-permute-done | bytes 262176 | tf_op jit(solution)/shard_map/ppermute | solution.py:10
  18.1 0.4 collective-permute-start.5
  18.5 0.0 collective-permute-done.9
  18.5 0.1 pad_maximum_fusion
  18.7 0.6 %gather_fusion = bf16[8,256,256]{2,1,0:T(8,128)(2,1)S(1)} fusion(bf16[8,256,256]{2,1,0:T(8,128)(2,1)S(1)} %bitcast.27, s32[1024]{0:T(1024)S(1)} %pad_clamp_fusion), kind=kCustom, calls=%fused_computation.clone | custom fusion | bytes 2097184 | tf_op jit(solution)/shard_map/jit(_take)/gather | solution.py:44
  19.3 0.0 copy-start
  19.3 0.0 collective-permute-done.1
  19.3 0.1 collective-permute-start.2
  19.4 0.2 broadcast_select_fusion
  19.5 10.8 %collective-permute-done.3 = bf16[512,256]{1,0:T(8,128)(2,1)S(1)} collective-permute-done((bf16[512,256]{1,0:T(8,128)(2,1)S(1)}, bf16[512,256]{1,0:T(8,128)(2,1)S(1)}, u32[]{:S(2)}, u32[]{:S(2)}) %collective-permute-start.3) | collective-permute-done | bytes 262176 | tf_op jit(solution)/shard_map/ppermute | solution.py:10
  30.4 0.0 collective-permute-start.4
  30.4 0.0 collective-permute-done
  30.4 0.0 copy-done
  30.5 5.9 %collective-permute-done.5 = bf16[512,256]{1,0:T(8,128)(2,1)S(1)} collective-permute-done((bf16[512,256]{1,0:T(8,128)(2,1)S(1)}, bf16[512,256]{1,0:T(8,128)(2,1)S(1)}, u32[]{:S(2)}, u32[]{:S(2)}) %collective-permute-start.5) | collective-permute-done | bytes 262176 | tf_op jit(solution)/shard_map/ppermute | solution.py:10
  36.3 0.0 collective-permute-start.6
  36.3 0.0 collective-permute-done.2
  36.4 0.0 collective-permute-done.4
  36.5 1.4 %collective-permute-done.6 = bf16[512,256]{1,0:T(8,128)(2,1)S(1)} collective-permute-done((bf16[512,256]{1,0:T(8,128)(2,1)S(1)}, bf16[512,256]{1,0:T(8,128)(2,1)S(1)}, u32[]{:S(2)}, u32[]{:S(2)}) %collective-permute-start.6) | collective-permute-done | bytes 262176 | tf_op jit(solution)/shard_map/ppermute | solution.py:10
  37.9 0.0 copy-start.1
  37.9 0.6 %broadcast_in_dim.20 = f32[512,2,128]{2,1,0:T(2,128)S(1)} broadcast(f32[512,2]{1,0:T(8,128)S(1)} %bitcast.30), dimensions={0,1} | broadcast | bytes 528384 | tf_op jit(solution)/shard_map/broadcast_in_dim | solution.py:26
  38.5 0.7 %fusion.2 = bf16[512,256]{1,0:T(8,128)(2,1)S(1)} fusion(bf16[512,2048]{1,0:T(8,128)(2,1)S(1)} %constant_dynamic-update-slice_fusion, bf16[2048,256]{1,0:T(8,128)(2,1)S(1)} %bitcast.28, f32[64,8,2,128]{3,2,1,0:T(2,128)S(1)} %bitcast.34), kind=kOutput, calls=%fused_computation.6 | convolution fusion | flops 537133056 | bytes 3932160 | tf_op jit(solution)/shard_map/dot_general | solution.py:47
  39.2 0.0 copy-done.1
  39.3 1.6 %collective-permute-start.11 = (bf16[512,256]{1,0:T(8,128)(2,1)S(1)}, bf16[512,256]{1,0:T(8,128)(2,1)S(1)}, u32[]{:S(2)}, u32[]{:S(2)}) collective-permute-start(bf16[512,256]{1,0:T(8,128)(2,1)S(1)} %fusion.2), channel_id=1, source_target_pairs={{0,16},{8,24},{16,0},{24,8},{1,17},{9,25},{17,1},{25,9},{2,18},{10... | collective-permute-start | bytes 786440 | tf_op jit(solution)/shard_map/ppermute | solution.py:10
  40.8 1.4 %collective-permute-start.12 = (bf16[512,256]{1,0:T(8,128)(2,1)S(1)}, bf16[512,256]{1,0:T(8,128)(2,1)S(1)}, u32[]{:S(2)}, u32[]{:S(2)}) collective-permute-start(bf16[512,256]{1,0:T(8,128)(2,1)S(1)} %fusion.2), channel_id=1, source_target_pairs={{0,24},{8,16},{16,8},{24,0},{1,25},{9,17},{17,9},{25,1},{2,26},{10... | collective-permute-start | bytes 786440 | tf_op jit(solution)/shard_map/ppermute | solution.py:10
  42.3 0.5 collective-permute-start.10
  42.8 10.5 %collective-permute-done.11 = bf16[512,256]{1,0:T(8,128)(2,1)S(1)} collective-permute-done((bf16[512,256]{1,0:T(8,128)(2,1)S(1)}, bf16[512,256]{1,0:T(8,128)(2,1)S(1)}, u32[]{:S(2)}, u32[]{:S(2)}) %collective-permute-start.11) | collective-permute-done | bytes 262176 | tf_op jit(solution)/shard_map/ppermute | solution.py:10
  53.3 0.0 collective-permute-done.12
  53.3 1.2 %collective-permute-done.10 = bf16[512,256]{1,0:T(8,128)(2,1)S(1)} collective-permute-done((bf16[512,256]{1,0:T(8,128)(2,1)S(1)}, bf16[512,256]{1,0:T(8,128)(2,1)S(1)}, u32[]{:S(2)}, u32[]{:S(2)}) %collective-permute-start.10) | collective-permute-done | bytes 262176 | tf_op jit(solution)/shard_map/ppermute | solution.py:10
  54.5 0.1 pad_maximum_fusion.1
  54.6 0.6 %gather_fusion.1 = bf16[8,256,256]{2,1,0:T(8,128)(2,1)S(1)} fusion(bf16[8,256,256]{2,1,0:T(8,128)(2,1)S(1)} %bitcast.26, s32[1024]{0:T(1024)S(1)} %pad_clamp_fusion), kind=kCustom, calls=%fused_computation.1.clone | custom fusion | bytes 2097184 | tf_op jit(solution)/shard_map/jit(_take)/gather | solution.py:44
  55.3 0.0 copy-start.2
  55.3 0.2 broadcast_select_fusion.1
  55.5 1.4 %copy-done.2 = bf16[512,2048]{1,0:T(8,128)(2,1)S(1)} copy-done((bf16[512,2048]{1,0:T(8,128)(2,1)S(1)}, bf16[512,2048]{1,0:T(8,128)(2,1)}, u32[]{:S(2)}) %copy-start.2) | copy-done | bytes 2097176
  56.9 1.5 %fusion.1 = f32[512,256]{1,0:T(8,128)} fusion(bf16[512,2048]{1,0:T(8,128)(2,1)S(1)} %copy-done.2, bf16[2048,256]{1,0:T(8,128)(2,1)S(1)} %bitcast.29, bf16[512,256]{1,0:T(8,128)(2,1)S(1)} %get-tuple-element.9, f32[64,8,2,128]{3,2,1,0:T(2,128)S(1)} %bitcast.35), kind=kOutput, calls=%fused_computation.5 | convolution fusion | flops 537526272 | bytes 4456448 | tf_op jit(solution)/shard_map/dot_general | solution.py:52
  (11 shorter events, 0.2 us)
Async XLA Ops:
  3.2 9.2 %collective-permute-start.7 = (bf16[512,256]{1,0:T(8,128)(2,1)S(1)}, bf16[512,256]{1,0:T(8,128)(2,1)S(1)}, u32[]{:S(2)}, u32[]{:S(2)}) collective-permute-start(bf16[512,256]{1,0:T(8,128)(2,1)S(1)} %get-tuple-element.9), channel_id=1, source_target_pairs={{0,8},{8,0},{16,24},{24,16},{1,9},{9,1},{17,25},{25,17},{2,10},{10... | collective-permute-start | bytes 786440 | tf_op jit(solution)/shard_map/ppermute | solution.py:10
  4.7 13.4 %collective-permute-start.8 = (bf16[512,256]{1,0:T(8,128)(2,1)S(1)}, bf16[512,256]{1,0:T(8,128)(2,1)S(1)}, u32[]{:S(2)}, u32[]{:S(2)}) collective-permute-start(bf16[512,256]{1,0:T(8,128)(2,1)S(1)} %get-tuple-element.9), channel_id=1, source_target_pairs={{0,16},{8,24},{16,0},{24,8},{1,17},{9,25},{17,1},{25,9},{2,18},{10... | collective-permute-start | bytes 786440 | tf_op jit(solution)/shard_map/ppermute | solution.py:10
  6.2 12.3 %collective-permute-start.9 = (bf16[512,256]{1,0:T(8,128)(2,1)S(1)}, bf16[512,256]{1,0:T(8,128)(2,1)S(1)}, u32[]{:S(2)}, u32[]{:S(2)}) collective-permute-start(bf16[512,256]{1,0:T(8,128)(2,1)S(1)} %get-tuple-element.9), channel_id=1, source_target_pairs={{0,24},{8,16},{16,8},{24,0},{1,25},{9,17},{17,9},{25,1},{2,26},{10... | collective-permute-start | bytes 786440 | tf_op jit(solution)/shard_map/ppermute | solution.py:10
  6.7 23.7 %collective-permute-start = (bf16[512,256]{1,0:T(8,128)(2,1)S(1)}, bf16[512,256]{1,0:T(8,128)(2,1)S(1)}, u32[]{:S(2)}, u32[]{:S(2)}) collective-permute-start(bf16[512,256]{1,0:T(8,128)(2,1)S(1)} %get-tuple-element.9), channel_id=1, source_target_pairs={{0,1},{1,0},{2,3},{3,2},{4,5},{5,4},{6,7},{7,6},{8,9},{9,8},{10,11... | collective-permute-start | bytes 786440 | tf_op jit(solution)/shard_map/ppermute | solution.py:10
  6.7 12.6 %collective-permute-start.1 = (bf16[512,256]{1,0:T(8,128)(2,1)S(1)}, bf16[512,256]{1,0:T(8,128)(2,1)S(1)}, u32[]{:S(2)}, u32[]{:S(2)}) collective-permute-start(bf16[512,256]{1,0:T(8,128)(2,1)S(1)} %get-tuple-element.9), channel_id=1, source_target_pairs={{0,2},{1,3},{2,0},{3,1},{4,6},{5,7},{6,4},{7,5},{8,10},{9,11},{10,... | collective-permute-start | bytes 786440 | tf_op jit(solution)/shard_map/ppermute | solution.py:10
  12.4 18.0 %collective-permute-start.3 = (bf16[512,256]{1,0:T(8,128)(2,1)S(1)}, bf16[512,256]{1,0:T(8,128)(2,1)S(1)}, u32[]{:S(2)}, u32[]{:S(2)}) collective-permute-start(bf16[512,256]{1,0:T(8,128)(2,1)S(1)} %get-tuple-element.9), channel_id=1, source_target_pairs={{0,4},{1,5},{2,6},{3,7},{4,0},{5,1},{6,2},{7,3},{8,12},{9,13},{10,... | collective-permute-start | bytes 786440 | tf_op jit(solution)/shard_map/ppermute | solution.py:10
  18.1 18.3 %collective-permute-start.5 = (bf16[512,256]{1,0:T(8,128)(2,1)S(1)}, bf16[512,256]{1,0:T(8,128)(2,1)S(1)}, u32[]{:S(2)}, u32[]{:S(2)}) collective-permute-start(bf16[512,256]{1,0:T(8,128)(2,1)S(1)} %get-tuple-element.9), channel_id=1, source_target_pairs={{0,6},{1,7},{2,4},{3,5},{4,2},{5,3},{6,0},{7,1},{8,14},{9,15},{10,... | collective-permute-start | bytes 786440 | tf_op jit(solution)/shard_map/ppermute | solution.py:10
  19.3 11.1 %copy-start = (bf16[512,2048]{1,0:T(8,128)(2,1)S(1)}, bf16[512,2048]{1,0:T(8,128)(2,1)}, u32[]{:S(2)}) copy-start(bf16[512,2048]{1,0:T(8,128)(2,1)} %get-tuple-element.8) | copy-start | bytes 6291460
  19.3 17.0 %collective-permute-start.2 = (bf16[512,256]{1,0:T(8,128)(2,1)S(1)}, bf16[512,256]{1,0:T(8,128)(2,1)S(1)}, u32[]{:S(2)}, u32[]{:S(2)}) collective-permute-start(bf16[512,256]{1,0:T(8,128)(2,1)S(1)} %collective-permute-done.1), channel_id=1, source_target_pairs={{0,1},{1,0},{2,3},{3,2},{4,5},{5,4},{6,7},{7,6},{8,9},{9,8},{10,11... | collective-permute-start | bytes 786440 | tf_op jit(solution)/shard_map/ppermute | solution.py:10
  30.4 6.0 %collective-permute-start.4 = (bf16[512,256]{1,0:T(8,128)(2,1)S(1)}, bf16[512,256]{1,0:T(8,128)(2,1)S(1)}, u32[]{:S(2)}, u32[]{:S(2)}) collective-permute-start(bf16[512,256]{1,0:T(8,128)(2,1)S(1)} %collective-permute-done.3), channel_id=1, source_target_pairs={{0,1},{1,0},{2,3},{3,2},{4,5},{5,4},{6,7},{7,6},{8,9},{9,8},{10,11... | collective-permute-start | bytes 786440 | tf_op jit(solution)/shard_map/ppermute | solution.py:10
  36.3 1.5 %collective-permute-start.6 = (bf16[512,256]{1,0:T(8,128)(2,1)S(1)}, bf16[512,256]{1,0:T(8,128)(2,1)S(1)}, u32[]{:S(2)}, u32[]{:S(2)}) collective-permute-start(bf16[512,256]{1,0:T(8,128)(2,1)S(1)} %collective-permute-done.5), channel_id=1, source_target_pairs={{0,1},{1,0},{2,3},{3,2},{4,5},{5,4},{6,7},{7,6},{8,9},{9,8},{10,11... | collective-permute-start | bytes 786440 | tf_op jit(solution)/shard_map/ppermute | solution.py:10
  37.9 1.4 %copy-start.1 = (bf16[512,2048]{1,0:T(8,128)(2,1)}, bf16[512,2048]{1,0:T(8,128)(2,1)S(1)}, u32[]{:S(2)}) copy-start(bf16[512,2048]{1,0:T(8,128)(2,1)S(1)} %constant_dynamic-update-slice_fusion) | copy-start | bytes 6291460
  39.3 14.0 %collective-permute-start.11 = (bf16[512,256]{1,0:T(8,128)(2,1)S(1)}, bf16[512,256]{1,0:T(8,128)(2,1)S(1)}, u32[]{:S(2)}, u32[]{:S(2)}) collective-permute-start(bf16[512,256]{1,0:T(8,128)(2,1)S(1)} %fusion.2), channel_id=1, source_target_pairs={{0,16},{8,24},{16,0},{24,8},{1,17},{9,25},{17,1},{25,9},{2,18},{10... | collective-permute-start | bytes 786440 | tf_op jit(solution)/shard_map/ppermute | solution.py:10
  40.8 12.4 %collective-permute-start.12 = (bf16[512,256]{1,0:T(8,128)(2,1)S(1)}, bf16[512,256]{1,0:T(8,128)(2,1)S(1)}, u32[]{:S(2)}, u32[]{:S(2)}) collective-permute-start(bf16[512,256]{1,0:T(8,128)(2,1)S(1)} %fusion.2), channel_id=1, source_target_pairs={{0,24},{8,16},{16,8},{24,0},{1,25},{9,17},{17,9},{25,1},{2,26},{10... | collective-permute-start | bytes 786440 | tf_op jit(solution)/shard_map/ppermute | solution.py:10
  42.3 12.2 %collective-permute-start.10 = (bf16[512,256]{1,0:T(8,128)(2,1)S(1)}, bf16[512,256]{1,0:T(8,128)(2,1)S(1)}, u32[]{:S(2)}, u32[]{:S(2)}) collective-permute-start(bf16[512,256]{1,0:T(8,128)(2,1)S(1)} %fusion.2), channel_id=1, source_target_pairs={{0,8},{8,0},{16,24},{24,16},{1,9},{9,1},{17,25},{25,17},{2,10},{10... | collective-permute-start | bytes 786440 | tf_op jit(solution)/shard_map/ppermute | solution.py:10
  55.3 1.6 %copy-start.2 = (bf16[512,2048]{1,0:T(8,128)(2,1)S(1)}, bf16[512,2048]{1,0:T(8,128)(2,1)}, u32[]{:S(2)}) copy-start(bf16[512,2048]{1,0:T(8,128)(2,1)} %copy-done.1) | copy-start | bytes 6291460

commit v5 on v4

--- a/solution.py
+++ b/solution.py
@@ -23,8 +23,13 @@
         local_blocks = lax.dynamic_slice(
             pattern, (row_index * block_rows, col_index * block_cols), (block_rows, block_cols)
         )
-        local_mask = jnp.repeat(jnp.repeat(local_blocks, B, axis=0), B, axis=1)
-        masked = matrix_in * local_mask.astype(jnp.bfloat16)
+        keep = local_blocks.reshape(block_rows, 1, block_cols, 1) != 0
+
+        def apply_mask(x):
+            x4 = x.reshape(block_rows, B, block_cols, B)
+            return jnp.where(keep, x4, jnp.zeros_like(x4)).reshape(rows, cols)
+
+        masked = apply_mask(matrix_in)
 
         row_pieces = [None] * n_col
         row_pieces[0] = masked
@@ -45,12 +50,11 @@
 
         row_cat = jnp.concatenate(row_pieces, axis=1)
         square = jnp.dot(row_cat, in_slot_order(col_pieces), preferred_element_type=jnp.float32)
-        mask_float = local_mask.astype(jnp.float32)
-        filtered = (mask_float * square).astype(jnp.bfloat16)
+        filtered = apply_mask(square).astype(jnp.bfloat16)
         f_pieces = [filtered] + [_swap(filtered, "row", n_row, k) for k in range(1, n_row)]
         f_slot = in_slot_order(f_pieces)
         cubic = jnp.dot(row_cat, f_slot, preferred_element_type=jnp.float32)
-        return mask_float * (1.5 * masked.astype(jnp.float32) - 0.5 * cubic)
+        return apply_mask(1.5 * masked.astype(jnp.float32) - 0.5 * cubic)
 
     return body
 

time: 58.6 us -> 65.8 us (1.12)
  local copies, waits for them, and re-layouts: 4.07 us -> 17.8 us
  waiting for transfers between devices: 39.6 us -> 29.7 us
  matrix products: 2.22 us -> 5.43 us
    unnamed x12 -> x18, local copies, waits for them, and re-layouts: 1.58 us -> 13.7 us
    ppermute x13, waiting for transfers between devices: 39.6 us -> 29.7 us  [_swap(): return lax.ppermute(x, axis, [(i, i ^ d) for i in range(size)])]
    dot_general x1, matrix products: 0.71 us -> 2.33 us  [body(): jnp.dot(row_cat, in_slot_order(col_pieces), preferred_element_type=jnp.fl...]
    dot_general x1, matrix products: 1.51 us -> 3.1 us  [body(): cubic = jnp.dot(row_cat, f_slot, preferred_element_type=jnp.float32)]
    concatenate x1 -> x2, local copies, waits for them, and re-layouts: 0.02 us -> 1.51 us  [body(): row_cat = jnp.concatenate(row_pieces, axis=1)]
    broadcast_in_dim x4 -> x1, local copies, waits for them, and re-layouts: 1.24 us -> 0.21 us  [apply_mask(): return jnp.where(keep, x4, jnp.zeros_like(x4)).reshape(rows, cols)]
    ne x0 -> x1, other arithmetic: none -> 0.76 us  [body(): keep = local_blocks.reshape(block_rows, 1, block_cols, 1) != 0]
    convert_element_type x1 -> x0, other arithmetic: 0.76 us -> none  [body(): mask_float = local_mask.astype(jnp.float32)]
  transfers between devices with their start and end apart: 13 -> 13, of which waited for: 7 -> 5; matrix products, arithmetic and copies ran while one was open for 2% -> 25% of each run, Pallas kernels for 0% -> 0%
where the time goes in v5:
time: 65.8 us; the launch traced here: 65.4 us
  waiting for transfers between devices  29.7 us (45%)
  local copies, waits for them, and re-layouts  17.8 us (27%)
  starting transfers between devices  9.04 us (14%)
  matrix products  5.43 us (8%)
  other arithmetic  3.28 us (5%)
    ppermute x13, waiting for transfers between devices, _swap(): return lax.ppermute(x, axis, [(i, i ^ d) for i in range(size)])  29.7 us
    unnamed x18, local copies, waits for them, and re-layouts  13.7 us
    ppermute x13, starting transfers between devices, _swap(): return lax.ppermute(x, axis, [(i, i ^ d) for i in range(size)])  9.04 us
    dot_general x1, matrix products, body(): cubic = jnp.dot(row_cat, f_slot, preferred_element_type=jnp.float32)  3.1 us
    dot_general x1, matrix products, body(): jnp.dot(row_cat, in_slot_order(col_pieces), preferred_element_type=jnp.fl...  2.33 us
    unnamed x1, other arithmetic  1.89 us
    concatenate x2, local copies, waits for them, and re-layouts, body(): row_cat = jnp.concatenate(row_pieces, axis=1)  1.51 us
  transfers between devices with their start and end apart: 13, of which 5 were waited for; matrix products, arithmetic and copies ran while one was open for 25% of the time, Pallas kernels for 0%

profile of v5, /device:TPU:16, one launch (start us, length us, event | category | flops | bytes accessed | tf_op | source)
XLA Modules:
  0.0 65.4 jit_solution(11810459054310726246)
XLA Ops:
  0.0 0.8 %dynamic-slice_compare_fusion = pred[4,2]{1,0:T(4,128)(4,1)S(1)} fusion(s32[16,16]{1,0:T(8,128)} %param.5, s32[]{:T(128)S(6)} %select_n.41, s32[]{:T(128)S(6)} %select_n.42), kind=kLoop, calls=%fused_computation.33 | loop fusion | flops 8 | bytes 48 | tf_op jit(solution)/shard_map/ne | solution.py:26
  0.8 0.2 broadcast_in_dim.31.clone
  1.0 0.0 copy-start
  1.0 1.9 %constant_dynamic-update-slice_fusion.7 = (bf16[512,2048]{1,0:T(8,128)(2,1)}, bf16[512,256]{1,0:T(8,128)(2,1)S(1)}) fusion(bf16[512,256]{1,0:T(8,128)(2,1)} %param.4, pred[64,8,2,128]{3,2,1,0:T(4,128)(4,1)S(1)} %bitcast.60), kind=kLoop, calls=%fused_computation.22 | loop fusion | flops 131071 | bytes 917504
  2.9 0.0 collective-permute-start
  2.9 1.6 %collective-permute-start.1 = (bf16[512,256]{1,0:T(8,128)(2,1)S(1)}, bf16[512,256]{1,0:T(8,128)(2,1)S(1)}, u32[]{:S(2)}, u32[]{:S(2)}) collective-permute-start(bf16[512,256]{1,0:T(8,128)(2,1)S(1)} %get-tuple-element.9), channel_id=1, source_target_pairs={{0,2},{1,3},{2,0},{3,1},{4,6},{5,7},{6,4},{7,5},{8,10},{9,11},{10,... | collective-permute-start | bytes 786440 | tf_op jit(solution)/shard_map/ppermute | solution.py:10
  4.5 1.5 %collective-permute-start.7 = (bf16[512,256]{1,0:T(8,128)(2,1)S(1)}, bf16[512,256]{1,0:T(8,128)(2,1)S(1)}, u32[]{:S(2)}, u32[]{:S(2)}) collective-permute-start(bf16[512,256]{1,0:T(8,128)(2,1)S(1)} %get-tuple-element.9), channel_id=1, source_target_pairs={{0,8},{8,0},{16,24},{24,16},{1,9},{9,1},{17,25},{25,17},{2,10},{10... | collective-permute-start | bytes 786440 | tf_op jit(solution)/shard_map/ppermute | solution.py:10
  6.0 1.5 %collective-permute-start.8 = (bf16[512,256]{1,0:T(8,128)(2,1)S(1)}, bf16[512,256]{1,0:T(8,128)(2,1)S(1)}, u32[]{:S(2)}, u32[]{:S(2)}) collective-permute-start(bf16[512,256]{1,0:T(8,128)(2,1)S(1)} %get-tuple-element.9), channel_id=1, source_target_pairs={{0,16},{8,24},{16,0},{24,8},{1,17},{9,25},{17,1},{25,9},{2,18},{10... | collective-permute-start | bytes 786440 | tf_op jit(solution)/shard_map/ppermute | solution.py:10
  7.5 0.5 collective-permute-start.9
  8.0 0.7 %constant_dynamic-update-slice_fusion.15 = bf16[4,128,2048]{2,1,0:T(8,128)(2,1)} fusion(bf16[4,128,256]{2,1,0:T(8,128)(2,1)S(1)} %bitcast.51), kind=kLoop, calls=%fused_computation.30 | loop fusion | bytes 524288
  8.7 4.9 %collective-permute-done.7 = bf16[512,256]{1,0:T(8,128)(2,1)S(1)} collective-permute-done((bf16[512,256]{1,0:T(8,128)(2,1)S(1)}, bf16[512,256]{1,0:T(8,128)(2,1)S(1)}, u32[]{:S(2)}, u32[]{:S(2)}) %collective-permute-start.7) | collective-permute-done | bytes 262176 | tf_op jit(solution)/shard_map/ppermute | solution.py:10
  13.6 0.3 collective-permute-start.3
  13.9 5.8 %collective-permute-done.8 = bf16[512,256]{1,0:T(8,128)(2,1)S(1)} collective-permute-done((bf16[512,256]{1,0:T(8,128)(2,1)S(1)}, bf16[512,256]{1,0:T(8,128)(2,1)S(1)}, u32[]{:S(2)}, u32[]{:S(2)}) %collective-permute-start.8) | collective-permute-done | bytes 262176 | tf_op jit(solution)/shard_map/ppermute | solution.py:10
  19.7 0.0 collective-permute-start.5
  19.7 0.0 collective-permute-done.9
  19.7 0.0 copy-done
  19.7 0.1 pad_maximum_fusion
  19.9 0.6 gather_fusion
  20.5 0.2 broadcast_select_fusion
  20.7 0.0 collective-permute-done.1
  20.7 0.1 collective-permute-start.2
  20.8 0.0 collective-permute-done
  20.8 0.7 %constant_dynamic-update-slice_fusion.14 = bf16[4,128,2048]{2,1,0:T(8,128)(2,1)} fusion(bf16[4,128,2048]{2,1,0:T(8,128)(2,1)} %constant_dynamic-update-slice_fusion.15, bf16[4,128,256]{2,1,0:T(8,128)(2,1)S(1)} %bitcast.58), kind=kLoop, calls=%fused_computation.29 | loop fusion | bytes 524288
  21.5 0.7 %constant_dynamic-update-slice_fusion.13 = bf16[4,128,2048]{2,1,0:T(8,128)(2,1)} fusion(bf16[4,128,2048]{2,1,0:T(8,128)(2,1)} %constant_dynamic-update-slice_fusion.14, bf16[4,128,256]{2,1,0:T(8,128)(2,1)S(1)} %bitcast.57), kind=kLoop, calls=%fused_computation.28 | loop fusion | bytes 524288
  22.3 7.5 %collective-permute-done.3 = bf16[512,256]{1,0:T(8,128)(2,1)S(1)} collective-permute-done((bf16[512,256]{1,0:T(8,128)(2,1)S(1)}, bf16[512,256]{1,0:T(8,128)(2,1)S(1)}, u32[]{:S(2)}, u32[]{:S(2)}) %collective-permute-start.3) | collective-permute-done | bytes 262176 | tf_op jit(solution)/shard_map/ppermute | solution.py:10
  29.7 0.0 collective-permute-start.4
  29.7 0.7 %constant_dynamic-update-slice_fusion.6 = bf16[512,2048]{1,0:T(8,128)(2,1)} fusion(bf16[512,2048]{1,0:T(8,128)(2,1)} %get-tuple-element.8, bf16[512,256]{1,0:T(8,128)(2,1)S(1)} %collective-permute-done), kind=kLoop, calls=%fused_computation.21 | loop fusion | bytes 524288
  30.5 0.7 %constant_dynamic-update-slice_fusion.5 = bf16[512,2048]{1,0:T(8,128)(2,1)} fusion(bf16[512,2048]{1,0:T(8,128)(2,1)} %constant_dynamic-update-slice_fusion.6, bf16[512,256]{1,0:T(8,128)(2,1)S(1)} %collective-permute-done.1), kind=kLoop, calls=%fused_computation.20 | loop fusion | bytes 524288
  31.2 0.6 copy.6
  31.9 5.4 %collective-permute-done.5 = bf16[512,256]{1,0:T(8,128)(2,1)S(1)} collective-permute-done((bf16[512,256]{1,0:T(8,128)(2,1)S(1)}, bf16[512,256]{1,0:T(8,128)(2,1)S(1)}, u32[]{:S(2)}, u32[]{:S(2)}) %collective-permute-start.5) | collective-permute-done | bytes 262176 | tf_op jit(solution)/shard_map/ppermute | solution.py:10
  37.3 0.0 collective-permute-start.6
  37.3 0.0 collective-permute-done.2
  37.3 1.7 %constant_dynamic-update-slice_fusion.12 = bf16[4,128,2048]{2,1,0:T(8,128)(2,1)} fusion(bf16[4,128,2048]{2,1,0:T(8,128)(2,1)} %constant_dynamic-update-slice_fusion.13, bf16[4,128,256]{2,1,0:T(8,128)(2,1)} %bitcast.3), kind=kLoop, calls=%fused_computation.27 | loop fusion | bytes 524288
  39.0 0.7 %constant_dynamic-update-slice_fusion.11 = bf16[4,128,2048]{2,1,0:T(8,128)(2,1)} fusion(bf16[4,128,2048]{2,1,0:T(8,128)(2,1)} %constant_dynamic-update-slice_fusion.12, bf16[4,128,256]{2,1,0:T(8,128)(2,1)S(1)} %bitcast.56), kind=kLoop, calls=%fused_computation.26 | loop fusion | bytes 524288
  39.7 0.0 collective-permute-done.4
  39.7 1.7 %constant_dynamic-update-slice_fusion.10 = bf16[4,128,2048]{2,1,0:T(8,128)(2,1)} fusion(bf16[4,128,2048]{2,1,0:T(8,128)(2,1)} %constant_dynamic-update-slice_fusion.11, bf16[4,128,256]{2,1,0:T(8,128)(2,1)} %bitcast.5), kind=kLoop, calls=%fused_computation.25 | loop fusion | bytes 524288
  41.4 0.7 %constant_dynamic-update-slice_fusion.9 = bf16[4,128,2048]{2,1,0:T(8,128)(2,1)} fusion(bf16[4,128,2048]{2,1,0:T(8,128)(2,1)} %constant_dynamic-update-slice_fusion.10, bf16[4,128,256]{2,1,0:T(8,128)(2,1)S(1)} %bitcast.55), kind=kLoop, calls=%fused_computation.24 | loop fusion | bytes 524288
  42.2 0.0 collective-permute-done.6
  42.2 0.8 %constant_dynamic-update-slice_fusion.8 = bf16[4,128,2048]{2,1,0:T(8,128)(2,1)} fusion(bf16[4,128,2048]{2,1,0:T(8,128)(2,1)} %constant_dynamic-update-slice_fusion.9, bf16[4,128,256]{2,1,0:T(8,128)(2,1)S(1)} %bitcast.59), kind=kLoop, calls=%fused_computation.23 | loop fusion | bytes 524288 | tf_op jit(solution)/shard_map/concatenate | solution.py:51
  42.9 2.3 %fusion.7 = bf16[4,128,2,128]{3,1,2,0:T(8,128)(2,1)S(1)} fusion(bf16[2,128,2048,1]{2,1,0,3:T(8,128)(2,1)S(1)} %bitcast.54, bf16[4,128,2048]{2,1,0:T(8,128)(2,1)} %constant_dynamic-update-slice_fusion.8, pred[4,2]{1,0:T(4,128)(4,1)S(1)} %dynamic-slice_compare_fusion), kind=kOutput, calls=%fused_computation.8 | convolution fusion | flops 537133056 | bytes 3407880 | tf_op jit(solution)/shard_map/dot_general | solution.py:52
  45.3 0.3 copy.7
  45.6 1.6 %collective-permute-start.10 = (bf16[512,256]{1,0:T(8,128)(2,1)S(1)}, bf16[512,256]{1,0:T(8,128)(2,1)S(1)}, u32[]{:S(2)}, u32[]{:S(2)}) collective-permute-start(bf16[512,256]{1,0:T(8,128)(2,1)S(1)} %bitcast.62), channel_id=1, source_target_pairs={{0,8},{8,0},{16,24},{24,16},{1,9},{9,1},{17,25},{25,17},{2,10},{10... | collective-permute-start | bytes 786440 | tf_op jit(solution)/shard_map/ppermute | solution.py:10
  47.1 1.5 %collective-permute-start.11 = (bf16[512,256]{1,0:T(8,128)(2,1)S(1)}, bf16[512,256]{1,0:T(8,128)(2,1)S(1)}, u32[]{:S(2)}, u32[]{:S(2)}) collective-permute-start(bf16[512,256]{1,0:T(8,128)(2,1)S(1)} %bitcast.63), channel_id=1, source_target_pairs={{0,16},{8,24},{16,0},{24,8},{1,17},{9,25},{17,1},{25,9},{2,18},{10... | collective-permute-start | bytes 786440 | tf_op jit(solution)/shard_map/ppermute | solution.py:10
  48.7 0.5 collective-permute-start.12
  49.1 1.7 %constant_dynamic-update-slice_fusion.4 = bf16[512,2048]{1,0:T(8,128)(2,1)} fusion(bf16[512,2048]{1,0:T(8,128)(2,1)} %constant_dynamic-update-slice_fusion.5, bf16[512,256]{1,0:T(8,128)(2,1)} %collective-permute-done.2), kind=kLoop, calls=%fused_computation.19 | loop fusion | bytes 524288
  50.9 0.8 %constant_dynamic-update-slice_fusion.3 = bf16[512,2048]{1,0:T(8,128)(2,1)} fusion(bf16[512,2048]{1,0:T(8,128)(2,1)} %constant_dynamic-update-slice_fusion.4, bf16[512,256]{1,0:T(8,128)(2,1)S(1)} %collective-permute-done.3), kind=kLoop, calls=%fused_computation.18 | loop fusion | bytes 524288
  51.6 1.7 %constant_dynamic-update-slice_fusion.2 = bf16[512,2048]{1,0:T(8,128)(2,1)} fusion(bf16[512,2048]{1,0:T(8,128)(2,1)} %constant_dynamic-update-slice_fusion.3, bf16[512,256]{1,0:T(8,128)(2,1)} %collective-permute-done.4), kind=kLoop, calls=%fused_computation.17 | loop fusion | bytes 524288
  53.4 0.2 convert_element_type.21
  53.5 0.7 %constant_dynamic-update-slice_fusion.1 = bf16[512,2048]{1,0:T(8,128)(2,1)} fusion(bf16[512,2048]{1,0:T(8,128)(2,1)} %constant_dynamic-update-slice_fusion.2, bf16[512,256]{1,0:T(8,128)(2,1)S(1)} %collective-permute-done.5), kind=kLoop, calls=%fused_computation.16 | loop fusion | bytes 524288
  54.3 0.8 %constant_dynamic-update-slice_fusion = bf16[512,2048]{1,0:T(8,128)(2,1)} fusion(bf16[512,2048]{1,0:T(8,128)(2,1)} %constant_dynamic-update-slice_fusion.1, bf16[512,256]{1,0:T(8,128)(2,1)S(1)} %collective-permute-done.6), kind=kLoop, calls=%fused_computation.15 | loop fusion | bytes 524288 | tf_op jit(solution)/shard_map/concatenate | solution.py:51
  55.0 0.0 collective-permute-done.10
  55.0 6.2 %collective-permute-done.11 = bf16[512,256]{1,0:T(8,128)(2,1)S(1)} collective-permute-done((bf16[512,256]{1,0:T(8,128)(2,1)S(1)}, bf16[512,256]{1,0:T(8,128)(2,1)S(1)}, u32[]{:S(2)}, u32[]{:S(2)}) %collective-permute-start.11) | collective-permute-done | bytes 262176 | tf_op jit(solution)/shard_map/ppermute | solution.py:10
  61.2 0.0 collective-permute-done.12
  61.2 0.1 pad_maximum_fusion.1
  61.3 0.0 copy-start.1
  61.4 0.6 gather_fusion.1
  62.0 0.2 broadcast_select_fusion.1
  62.1 0.1 copy-done.1
  62.3 3.1 %fusion.6 = f32[512,256]{1,0:T(8,128)} fusion(bf16[512,2048]{1,0:T(8,128)(2,1)} %constant_dynamic-update-slice_fusion, bf16[2048,256]{1,0:T(8,128)(2,1)S(1)} %bitcast.53, bf16[512,256]{1,0:T(8,128)(2,1)S(1)} %get-tuple-element.9, pred[64,8,2,128]{3,2,1,0:T(4,128)(4,1)S(1)} %bitcast.61), kind=kOutput, calls=%fused_computation.7 | convolution fusion | flops 537526272 | bytes 4063232 | tf_op jit(solution)/shard_map/dot_general | solution.py:56
  (3 shorter events, 0.1 us)
Async XLA Ops:
  1.0 18.8 %copy-start = (pred[4,128,2,128]{3,2,1,0:T(4,128)(4,1)}, pred[4,128,2,128]{3,2,1,0:T(4,128)(4,1)S(1)}, u32[]{:S(2)}) copy-start(pred[4,128,2,128]{3,2,1,0:T(4,128)(4,1)S(1)} %broadcast_in_dim.31.clone) | copy-start | bytes 393220
  2.9 17.9 %collective-permute-start = (bf16[512,256]{1,0:T(8,128)(2,1)S(1)}, bf16[512,256]{1,0:T(8,128)(2,1)S(1)}, u32[]{:S(2)}, u32[]{:S(2)}) collective-permute-start(bf16[512,256]{1,0:T(8,128)(2,1)S(1)} %get-tuple-element.9), channel_id=1, source_target_pairs={{0,1},{1,0},{2,3},{3,2},{4,5},{5,4},{6,7},{7,6},{8,9},{9,8},{10,11... | collective-permute-start | bytes 786440 | tf_op jit(solution)/shard_map/ppermute | solution.py:10
  2.9 17.8 %collective-permute-start.1 = (bf16[512,256]{1,0:T(8,128)(2,1)S(1)}, bf16[512,256]{1,0:T(8,128)(2,1)S(1)}, u32[]{:S(2)}, u32[]{:S(2)}) collective-permute-start(bf16[512,256]{1,0:T(8,128)(2,1)S(1)} %get-tuple-element.9), channel_id=1, source_target_pairs={{0,2},{1,3},{2,0},{3,1},{4,6},{5,7},{6,4},{7,5},{8,10},{9,11},{10,... | collective-permute-start | bytes 786440 | tf_op jit(solution)/shard_map/ppermute | solution.py:10
  4.5 9.1 %collective-permute-start.7 = (bf16[512,256]{1,0:T(8,128)(2,1)S(1)}, bf16[512,256]{1,0:T(8,128)(2,1)S(1)}, u32[]{:S(2)}, u32[]{:S(2)}) collective-permute-start(bf16[512,256]{1,0:T(8,128)(2,1)S(1)} %get-tuple-element.9), channel_id=1, source_target_pairs={{0,8},{8,0},{16,24},{24,16},{1,9},{9,1},{17,25},{25,17},{2,10},{10... | collective-permute-start | bytes 786440 | tf_op jit(solution)/shard_map/ppermute | solution.py:10
  6.0 13.8 %collective-permute-start.8 = (bf16[512,256]{1,0:T(8,128)(2,1)S(1)}, bf16[512,256]{1,0:T(8,128)(2,1)S(1)}, u32[]{:S(2)}, u32[]{:S(2)}) collective-permute-start(bf16[512,256]{1,0:T(8,128)(2,1)S(1)} %get-tuple-element.9), channel_id=1, source_target_pairs={{0,16},{8,24},{16,0},{24,8},{1,17},{9,25},{17,1},{25,9},{2,18},{10... | collective-permute-start | bytes 786440 | tf_op jit(solution)/shard_map/ppermute | solution.py:10
  7.5 12.3 %collective-permute-start.9 = (bf16[512,256]{1,0:T(8,128)(2,1)S(1)}, bf16[512,256]{1,0:T(8,128)(2,1)S(1)}, u32[]{:S(2)}, u32[]{:S(2)}) collective-permute-start(bf16[512,256]{1,0:T(8,128)(2,1)S(1)} %get-tuple-element.9), channel_id=1, source_target_pairs={{0,24},{8,16},{16,8},{24,0},{1,25},{9,17},{17,9},{25,1},{2,26},{10... | collective-permute-start | bytes 786440 | tf_op jit(solution)/shard_map/ppermute | solution.py:10
  13.6 16.1 %collective-permute-start.3 = (bf16[512,256]{1,0:T(8,128)(2,1)S(1)}, bf16[512,256]{1,0:T(8,128)(2,1)S(1)}, u32[]{:S(2)}, u32[]{:S(2)}) collective-permute-start(bf16[512,256]{1,0:T(8,128)(2,1)S(1)} %get-tuple-element.9), channel_id=1, source_target_pairs={{0,4},{1,5},{2,6},{3,7},{4,0},{5,1},{6,2},{7,3},{8,12},{9,13},{10,... | collective-permute-start | bytes 786440 | tf_op jit(solution)/shard_map/ppermute | solution.py:10
  19.7 17.5 %collective-permute-start.5 = (bf16[512,256]{1,0:T(8,128)(2,1)S(1)}, bf16[512,256]{1,0:T(8,128)(2,1)S(1)}, u32[]{:S(2)}, u32[]{:S(2)}) collective-permute-start(bf16[512,256]{1,0:T(8,128)(2,1)S(1)} %get-tuple-element.9), channel_id=1, source_target_pairs={{0,6},{1,7},{2,4},{3,5},{4,2},{5,3},{6,0},{7,1},{8,14},{9,15},{10,... | collective-permute-start | bytes 786440 | tf_op jit(solution)/shard_map/ppermute | solution.py:10
  20.7 16.6 %collective-permute-start.2 = (bf16[512,256]{1,0:T(8,128)(2,1)S(1)}, bf16[512,256]{1,0:T(8,128)(2,1)}, u32[]{:S(2)}, u32[]{:S(2)}) collective-permute-start(bf16[512,256]{1,0:T(8,128)(2,1)S(1)} %collective-permute-done.1), channel_id=1, source_target_pairs={{0,1},{1,0},{2,3},{3,2},{4,5},{5,4},{6,7},{7,6},{8,9},{9,8},{10,11... | collective-permute-start | bytes 786440 | tf_op jit(solution)/shard_map/ppermute | solution.py:10
  29.7 10.0 %collective-permute-start.4 = (bf16[512,256]{1,0:T(8,128)(2,1)S(1)}, bf16[512,256]{1,0:T(8,128)(2,1)}, u32[]{:S(2)}, u32[]{:S(2)}) collective-permute-start(bf16[512,256]{1,0:T(8,128)(2,1)S(1)} %collective-permute-done.3), channel_id=1, source_target_pairs={{0,1},{1,0},{2,3},{3,2},{4,5},{5,4},{6,7},{7,6},{8,9},{9,8},{10,11... | collective-permute-start | bytes 786440 | tf_op jit(solution)/shard_map/ppermute | solution.py:10
  37.3 4.9 %collective-permute-start.6 = (bf16[512,256]{1,0:T(8,128)(2,1)S(1)}, bf16[512,256]{1,0:T(8,128)(2,1)S(1)}, u32[]{:S(2)}, u32[]{:S(2)}) collective-permute-start(bf16[512,256]{1,0:T(8,128)(2,1)S(1)} %collective-permute-done.5), channel_id=1, source_target_pairs={{0,1},{1,0},{2,3},{3,2},{4,5},{5,4},{6,7},{7,6},{8,9},{9,8},{10,11... | collective-permute-start | bytes 786440 | tf_op jit(solution)/shard_map/ppermute | solution.py:10
  45.6 9.4 %collective-permute-start.10 = (bf16[512,256]{1,0:T(8,128)(2,1)S(1)}, bf16[512,256]{1,0:T(8,128)(2,1)S(1)}, u32[]{:S(2)}, u32[]{:S(2)}) collective-permute-start(bf16[512,256]{1,0:T(8,128)(2,1)S(1)} %bitcast.62), channel_id=1, source_target_pairs={{0,8},{8,0},{16,24},{24,16},{1,9},{9,1},{17,25},{25,17},{2,10},{10... | collective-permute-start | bytes 786440 | tf_op jit(solution)/shard_map/ppermute | solution.py:10
  47.1 14.1 %collective-permute-start.11 = (bf16[512,256]{1,0:T(8,128)(2,1)S(1)}, bf16[512,256]{1,0:T(8,128)(2,1)S(1)}, u32[]{:S(2)}, u32[]{:S(2)}) collective-permute-start(bf16[512,256]{1,0:T(8,128)(2,1)S(1)} %bitcast.63), channel_id=1, source_target_pairs={{0,16},{8,24},{16,0},{24,8},{1,17},{9,25},{17,1},{25,9},{2,18},{10... | collective-permute-start | bytes 786440 | tf_op jit(solution)/shard_map/ppermute | solution.py:10
  48.7 12.5 %collective-permute-start.12 = (bf16[512,256]{1,0:T(8,128)(2,1)S(1)}, bf16[512,256]{1,0:T(8,128)(2,1)S(1)}, u32[]{:S(2)}, u32[]{:S(2)}) collective-permute-start(bf16[512,256]{1,0:T(8,128)(2,1)S(1)} %bitcast.64), channel_id=1, source_target_pairs={{0,24},{8,16},{16,8},{24,0},{1,25},{9,17},{17,9},{25,1},{2,26},{10... | collective-permute-start | bytes 786440 | tf_op jit(solution)/shard_map/ppermute | solution.py:10
  61.3 1.0 %copy-start.1 = (pred[4,128,2,128]{3,2,1,0:T(4,128)(4,1)S(1)}, pred[4,128,2,128]{3,2,1,0:T(4,128)(4,1)}, u32[]{:S(2)}) copy-start(pred[4,128,2,128]{3,2,1,0:T(4,128)(4,1)} %copy-done) | copy-start | bytes 393220

commit v6 on v4

--- a/solution.py
+++ b/solution.py
@@ -26,24 +26,24 @@
         local_mask = jnp.repeat(jnp.repeat(local_blocks, B, axis=0), B, axis=1)
         masked = matrix_in * local_mask.astype(jnp.bfloat16)
 
-        row_pieces = [None] * n_col
-        row_pieces[0] = masked
-        row_pieces[1] = _swap(masked, "col", n_col, 1)
-        for k in range(1, n_z):
-            piece = _swap(masked, "col", n_col, 2 * k)
-            row_pieces[2 * k] = piece
-            row_pieces[2 * k + 1] = _swap(piece, "col", n_col, 1)
+        col_pieces = [masked] + [_swap(masked, "row", n_row, j) for j in range(1, n_row)]
 
-        col_pieces = [masked] + [_swap(masked, "row", n_row, k) for k in range(1, n_row)]
+        late, _ = lax.optimization_barrier((masked, col_pieces[1]))
+        own = jnp.concatenate(
+            [masked]
+            + [_swap(late if k == 1 else masked, "col", n_col, 2 * k) for k in range(1, n_z)],
+            axis=1,
+        )
+        row_cat = jnp.concatenate([own, _swap(own, "col", n_col, 1)], axis=1)
 
-        slots = jnp.arange(n_col, dtype=jnp.int32) ^ col_index
+        members = jnp.arange(n_z, dtype=jnp.int32) * 2
+        slots = jnp.concatenate([members, members + 1]) ^ col_index
         sub_index = ((slots // ratio) ^ row_index) * ratio + slots % ratio
 
         def in_slot_order(pieces):
             stacked = jnp.stack(pieces).reshape(n_row * ratio, cols, cols)
             return jnp.take(stacked, sub_index, axis=0).reshape(n_col * cols, cols)
 
-        row_cat = jnp.concatenate(row_pieces, axis=1)
         square = jnp.dot(row_cat, in_slot_order(col_pieces), preferred_element_type=jnp.float32)
         mask_float = local_mask.astype(jnp.float32)
         filtered = (mask_float * square).astype(jnp.bfloat16)

time: 58.6 us -> 59.2 us (1.010)
  waiting for transfers between devices: 39.6 us -> 29.8 us
  local copies, waits for them, and re-layouts: 4.07 us -> 7.98 us
  starting transfers between devices: 9.15 us -> 12.6 us
  matrix products: 2.22 us -> 3.81 us
  other arithmetic: 3.17 us -> 4.4 us
    ppermute x13 -> x10, waiting for transfers between devices: 39.6 us -> 29.8 us  [_swap(): return lax.ppermute(x, axis, [(i, i ^ d) for i in range(size)])]
    ppermute x13 -> x10, starting transfers between devices: 9.15 us -> 12.6 us  [_swap(): return lax.ppermute(x, axis, [(i, i ^ d) for i in range(size)])]
    unnamed x12 -> x17, local copies, waits for them, and re-layouts: 1.58 us -> 4.46 us
    dot_general x1, matrix products: 0.71 us -> 2.3 us  [body(): jnp.dot(row_cat, in_slot_order(col_pieces), preferred_element_type=jnp.fl...]
    concatenate x0 -> x1, other arithmetic: none -> 1.15 us  [body(): jnp.concatenate([masked] + [_swap(late if k == 1 else masked, 'col', n_co...]
    concatenate x1, local copies, waits for them, and re-layouts: 0.02 us -> 1.05 us  [body(): row_cat = jnp.concatenate([own, _swap(own, 'col', n_col, 1)], axis=1)]
  transfers between devices with their start and end apart: 13 -> 10, of which waited for: 7 -> 6; matrix products, arithmetic and copies ran while one was open for 2% -> 8% of each run, Pallas kernels for 0% -> 0%
where the time goes in v6:
time: 59.2 us; the launch traced here: 58.8 us
  waiting for transfers between devices  29.8 us (50%)
  starting transfers between devices  12.6 us (21%)
  local copies, waits for them, and re-layouts  7.98 us (13%)
  other arithmetic  4.4 us (7%)
  matrix products  3.81 us (6%)
    ppermute x10, waiting for transfers between devices, _swap(): return lax.ppermute(x, axis, [(i, i ^ d) for i in range(size)])  29.8 us
    ppermute x10, starting transfers between devices, _swap(): return lax.ppermute(x, axis, [(i, i ^ d) for i in range(size)])  12.6 us
    unnamed x17, local copies, waits for them, and re-layouts  4.46 us
    dot_general x1, matrix products, body(): jnp.dot(row_cat, in_slot_order(col_pieces), preferred_element_type=jnp.fl...  2.3 us
    unnamed x1, other arithmetic  1.79 us
    dot_general x1, matrix products, body(): cubic = jnp.dot(row_cat, f_slot, preferred_element_type=jnp.float32)  1.51 us
    broadcast_in_dim x4, local copies, waits for them, and re-layouts, body(): local_mask = jnp.repeat(jnp.repeat(local_blocks, B, axis=0), B, axis=1)  1.24 us
    gather x2, local copies, waits for them, and re-layouts, in_slot_order(): return jnp.take(stacked, sub_index, axis=0).reshape(n_col * cols, cols)  1.23 us
  transfers between devices with their start and end apart: 10, of which 6 were waited for; matrix products, arithmetic and copies ran while one was open for 8% of the time, Pallas kernels for 0%

profile of v6, /device:TPU:16, one launch (start us, length us, event | category | flops | bytes accessed | tf_op | source)
XLA Modules:
  0.0 58.8 jit_solution(8715729822953370953)
XLA Ops:
  0.0 0.8 %dynamic-slice_convert_fusion.1 = (f32[4,2]{1,0:T(4,128)S(1)}, bf16[4,2]{1,0:T(4,128)(2,1)S(1)}) fusion(s32[16,16]{1,0:T(8,128)} %param.5, s32[]{:T(128)S(6)} %select_n.24, s32[]{:T(128)S(6)} %select_n.25), kind=kLoop, calls=%fused_computation.24 | loop fusion | flops 16 | bytes 88 | tf_op jit(solution)/shard_map/convert_element_type | solution.py:48
  0.8 0.6 %broadcast_in_dim.22 = bf16[512,2,128]{2,1,0:T(2,128)(2,1)S(1)} broadcast(bf16[512,2]{1,0:T(8,128)(2,1)S(1)} %bitcast.33), dimensions={0,1} | broadcast | bytes 264192 | tf_op jit(solution)/shard_map/broadcast_in_dim | solution.py:26
  1.4 1.8 %constant_dynamic-update-slice_fusion.4 = (bf16[512,2048]{1,0:T(8,128)(2,1)}, bf16[512,256]{1,0:T(8,128)(2,1)S(1)}) fusion(bf16[512,256]{1,0:T(8,128)(2,1)} %param.4, bf16[64,8,2,128]{3,2,1,0:T(2,128)(2,1)S(1)} %bitcast.32), kind=kLoop, calls=%fused_computation.17 | loop fusion | flops 524287 | bytes 1048576
  3.2 1.5 %collective-permute-start = (bf16[512,256]{1,0:T(8,128)(2,1)S(1)}, bf16[512,256]{1,0:T(8,128)(2,1)S(1)}, u32[]{:S(2)}, u32[]{:S(2)}) collective-permute-start(bf16[512,256]{1,0:T(8,128)(2,1)S(1)} %get-tuple-element.7), channel_id=1, source_target_pairs={{0,8},{8,0},{16,24},{24,16},{1,9},{9,1},{17,25},{25,17},{2,10},{10... | collective-permute-start | bytes 786440 | tf_op jit(solution)/shard_map/ppermute | solution.py:10
  4.7 0.3 collective-permute-start.2
  5.0 2.7 %collective-permute-start.3 = (bf16[512,256]{1,0:T(8,128)(2,1)S(1)}, bf16[512,256]{1,0:T(8,128)(2,1)S(1)}, u32[]{:S(2)}, u32[]{:S(2)}) collective-permute-start(bf16[512,256]{1,0:T(8,128)(2,1)S(1)} %get-tuple-element.7), channel_id=1, source_target_pairs={{0,6},{1,7},{2,4},{3,5},{4,2},{5,3},{6,0},{7,1},{8,14},{9,15},{10,... | collective-permute-start | bytes 786440 | tf_op jit(solution)/shard_map/ppermute | solution.py:10
  7.7 3.5 %collective-permute-done = bf16[512,256]{1,0:T(8,128)(2,1)S(1)} collective-permute-done((bf16[512,256]{1,0:T(8,128)(2,1)S(1)}, bf16[512,256]{1,0:T(8,128)(2,1)S(1)}, u32[]{:S(2)}, u32[]{:S(2)}) %collective-permute-start) | collective-permute-done | bytes 262176 | tf_op jit(solution)/shard_map/ppermute | solution.py:10
  11.2 1.6 %collective-permute-start.1 = (bf16[512,256]{1,0:T(8,128)(2,1)S(1)}, bf16[512,256]{1,0:T(8,128)(2,1)S(1)}, u32[]{:S(2)}, u32[]{:S(2)}) collective-permute-start(bf16[512,256]{1,0:T(8,128)(2,1)S(1)} %get-tuple-element.7), channel_id=1, source_target_pairs={{0,2},{1,3},{2,0},{3,1},{4,6},{5,7},{6,4},{7,5},{8,10},{9,11},{10,... | collective-permute-start | bytes 786440 | tf_op jit(solution)/shard_map/ppermute | solution.py:10
  12.8 2.4 %collective-permute-start.6 = (bf16[512,256]{1,0:T(8,128)(2,1)S(1)}, bf16[512,256]{1,0:T(8,128)(2,1)S(1)}, u32[]{:S(2)}, u32[]{:S(2)}) collective-permute-start(bf16[512,256]{1,0:T(8,128)(2,1)S(1)} %get-tuple-element.7), channel_id=1, source_target_pairs={{0,24},{8,16},{16,8},{24,0},{1,25},{9,17},{17,9},{25,1},{2,26},{10... | collective-permute-start | bytes 786440 | tf_op jit(solution)/shard_map/ppermute | solution.py:10
  15.3 0.5 collective-permute-start.5
  15.8 7.0 %collective-permute-done.2 = bf16[512,256]{1,0:T(8,128)(2,1)S(1)} collective-permute-done((bf16[512,256]{1,0:T(8,128)(2,1)S(1)}, bf16[512,256]{1,0:T(8,128)(2,1)S(1)}, u32[]{:S(2)}, u32[]{:S(2)}) %collective-permute-start.2) | collective-permute-done | bytes 262176 | tf_op jit(solution)/shard_map/ppermute | solution.py:10
  22.7 0.0 copy-start
  22.7 7.5 %collective-permute-done.3 = bf16[512,256]{1,0:T(8,128)(2,1)S(1)} collective-permute-done((bf16[512,256]{1,0:T(8,128)(2,1)S(1)}, bf16[512,256]{1,0:T(8,128)(2,1)S(1)}, u32[]{:S(2)}, u32[]{:S(2)}) %collective-permute-start.3) | collective-permute-done | bytes 262176 | tf_op jit(solution)/shard_map/ppermute | solution.py:10
  30.2 0.0 copy-start.2
  30.2 0.0 collective-permute-done.1
  30.2 0.0 copy-start.4
  30.2 1.1 %pad_maximum_fusion = bf16[512,1024]{1,0:T(8,128)(2,1)} fusion(bf16[512,256]{1,0:T(8,128)(2,1)S(1)} %collective-permute-done.3, bf16[512,256]{1,0:T(8,128)(2,1)S(1)} %collective-permute-done.2, bf16[512,256]{1,0:T(8,128)(2,1)S(1)} %collective-permute-done.1, bf16[512,256]{1,0:T(8,128)(2,1)S(1)} %get-tuple-element.7), kind=kLoop, calls=%fused_computation.7 | loop fusion | flops 4194304 | bytes 2097152 | tf_op jit(solution)/shard_map/concatenate | solution.py:32
  31.4 0.0 collective-permute-start.4
  31.4 0.1 compare_and_fusion
  31.5 0.0 collective-permute-done.6
  31.5 0.0 collective-permute-done.5
  31.5 0.1 pad_maximum_fusion.1
  31.7 0.0 copy-done
  31.7 0.0 copy-done.2
  31.7 0.0 copy-done.4
  31.7 0.6 %gather_fusion = bf16[8,256,256]{2,1,0:T(8,128)(2,1)S(1)} fusion(bf16[8,256,256]{2,1,0:T(8,128)(2,1)S(1)} %bitcast.27, s32[1024]{0:T(1024)S(1)} %pad_clamp_fusion), kind=kCustom, calls=%fused_computation.clone | custom fusion | bytes 2097184 | tf_op jit(solution)/shard_map/jit(_take)/gather | solution.py:45
  32.3 0.0 copy-start.5
  32.3 0.0 copy-start.1
  32.4 0.0 copy-start.3
  32.4 0.2 broadcast_select_fusion
  32.5 0.8 %copy-done.5 = bf16[512,256]{1,0:T(8,128)(2,1)S(1)} copy-done((bf16[512,256]{1,0:T(8,128)(2,1)S(1)}, bf16[512,256]{1,0:T(8,128)(2,1)}, u32[]{:S(2)}) %copy-start.5) | copy-done | bytes 262168
  33.3 0.7 %constant_dynamic-update-slice_fusion.3 = bf16[512,2048]{1,0:T(8,128)(2,1)} fusion(bf16[512,2048]{1,0:T(8,128)(2,1)} %get-tuple-element.10, bf16[512,256]{1,0:T(8,128)(2,1)S(1)} %copy-done.5), kind=kLoop, calls=%fused_computation.16 | loop fusion | bytes 524288
  34.0 0.0 copy-done.1
  34.0 0.7 %constant_dynamic-update-slice_fusion.2 = bf16[512,2048]{1,0:T(8,128)(2,1)} fusion(bf16[512,2048]{1,0:T(8,128)(2,1)} %constant_dynamic-update-slice_fusion.3, bf16[512,256]{1,0:T(8,128)(2,1)S(1)} %copy-done.1), kind=kLoop, calls=%fused_computation.15 | loop fusion | bytes 524288
  34.8 0.0 copy-done.3
  34.8 0.8 %constant_dynamic-update-slice_fusion.1 = bf16[512,2048]{1,0:T(8,128)(2,1)} fusion(bf16[512,2048]{1,0:T(8,128)(2,1)} %constant_dynamic-update-slice_fusion.2, bf16[512,256]{1,0:T(8,128)(2,1)S(1)} %copy-done.3), kind=kLoop, calls=%fused_computation.14 | loop fusion | bytes 524288
  35.6 0.0 collective-permute-done.4
  35.6 1.0 %constant_dynamic-update-slice_fusion = bf16[512,2048]{1,0:T(8,128)(2,1)} fusion(bf16[512,2048]{1,0:T(8,128)(2,1)} %constant_dynamic-update-slice_fusion.1, bf16[512,1024]{1,0:T(8,128)(2,1)S(1)} %collective-permute-done.4), kind=kLoop, calls=%fused_computation.13 | loop fusion | bytes 2097152 | tf_op jit(solution)/shard_map/concatenate | solution.py:37
  36.6 0.6 %broadcast_in_dim.20 = f32[512,2,128]{2,1,0:T(2,128)S(1)} broadcast(f32[512,2]{1,0:T(8,128)S(1)} %bitcast.31), dimensions={0,1} | broadcast | bytes 528384 | tf_op jit(solution)/shard_map/broadcast_in_dim | solution.py:26
  37.2 2.3 %fusion.2 = bf16[512,256]{1,0:T(8,128)(2,1)S(1)} fusion(bf16[512,2048]{1,0:T(8,128)(2,1)} %constant_dynamic-update-slice_fusion, bf16[2048,256]{1,0:T(8,128)(2,1)S(1)} %bitcast.29, f32[64,8,2,128]{3,2,1,0:T(2,128)S(1)} %bitcast.34), kind=kOutput, calls=%fused_computation.6 | convolution fusion | flops 537133056 | bytes 3932160 | tf_op jit(solution)/shard_map/dot_general | solution.py:47
  39.6 1.6 %collective-permute-start.9 = (bf16[512,256]{1,0:T(8,128)(2,1)S(1)}, bf16[512,256]{1,0:T(8,128)(2,1)S(1)}, u32[]{:S(2)}, u32[]{:S(2)}) collective-permute-start(bf16[512,256]{1,0:T(8,128)(2,1)S(1)} %fusion.2), channel_id=1, source_target_pairs={{0,24},{8,16},{16,8},{24,0},{1,25},{9,17},{17,9},{25,1},{2,26},{10... | collective-permute-start | bytes 786440 | tf_op jit(solution)/shard_map/ppermute | solution.py:10
  41.1 0.5 collective-permute-start.8
  41.6 1.5 %collective-permute-start.7 = (bf16[512,256]{1,0:T(8,128)(2,1)S(1)}, bf16[512,256]{1,0:T(8,128)(2,1)S(1)}, u32[]{:S(2)}, u32[]{:S(2)}) collective-permute-start(bf16[512,256]{1,0:T(8,128)(2,1)S(1)} %fusion.2), channel_id=1, source_target_pairs={{0,8},{8,0},{16,24},{24,16},{1,9},{9,1},{17,25},{25,17},{2,10},{10... | collective-permute-start | bytes 786440 | tf_op jit(solution)/shard_map/ppermute | solution.py:10
  43.1 6.6 %collective-permute-done.9 = bf16[512,256]{1,0:T(8,128)(2,1)S(1)} collective-permute-done((bf16[512,256]{1,0:T(8,128)(2,1)S(1)}, bf16[512,256]{1,0:T(8,128)(2,1)S(1)}, u32[]{:S(2)}, u32[]{:S(2)}) %collective-permute-start.9) | collective-permute-done | bytes 262176 | tf_op jit(solution)/shard_map/ppermute | solution.py:10
  49.7 5.2 %collective-permute-done.8 = bf16[512,256]{1,0:T(8,128)(2,1)S(1)} collective-permute-done((bf16[512,256]{1,0:T(8,128)(2,1)S(1)}, bf16[512,256]{1,0:T(8,128)(2,1)S(1)}, u32[]{:S(2)}, u32[]{:S(2)}) %collective-permute-start.8) | collective-permute-done | bytes 262176 | tf_op jit(solution)/shard_map/ppermute | solution.py:10
  54.8 0.1 collective-permute-done.7
  54.9 0.1 pad_maximum_fusion.2
  55.1 0.6 %gather_fusion.1 = bf16[8,256,256]{2,1,0:T(8,128)(2,1)S(1)} fusion(bf16[8,256,256]{2,1,0:T(8,128)(2,1)S(1)} %bitcast.26, s32[1024]{0:T(1024)S(1)} %pad_clamp_fusion), kind=kCustom, calls=%fused_computation.1.clone | custom fusion | bytes 2097184 | tf_op jit(solution)/shard_map/jit(_take)/gather | solution.py:45
  55.7 0.0 copy-start.6
  55.7 0.2 broadcast_select_fusion.1
  55.9 1.4 %copy-done.6 = bf16[512,2048]{1,0:T(8,128)(2,1)S(1)} copy-done((bf16[512,2048]{1,0:T(8,128)(2,1)S(1)}, bf16[512,2048]{1,0:T(8,128)(2,1)}, u32[]{:S(2)}) %copy-start.6) | copy-done | bytes 2097176
  57.3 1.5 %fusion.1 = f32[512,256]{1,0:T(8,128)} fusion(bf16[512,2048]{1,0:T(8,128)(2,1)S(1)} %copy-done.6, bf16[2048,256]{1,0:T(8,128)(2,1)S(1)} %bitcast.30, bf16[512,256]{1,0:T(8,128)(2,1)S(1)} %get-tuple-element.7, f32[64,8,2,128]{3,2,1,0:T(2,128)S(1)} %bitcast.35), kind=kOutput, calls=%fused_computation.5 | convolution fusion | flops 537526272 | bytes 4456448 | tf_op jit(solution)/shard_map/dot_general | solution.py:52
  (4 shorter events, 0.0 us)
Async XLA Ops:
  3.2 8.0 %collective-permute-start = (bf16[512,256]{1,0:T(8,128)(2,1)S(1)}, bf16[512,256]{1,0:T(8,128)(2,1)S(1)}, u32[]{:S(2)}, u32[]{:S(2)}) collective-permute-start(bf16[512,256]{1,0:T(8,128)(2,1)S(1)} %get-tuple-element.7), channel_id=1, source_target_pairs={{0,8},{8,0},{16,24},{24,16},{1,9},{9,1},{17,25},{25,17},{2,10},{10... | collective-permute-start | bytes 786440 | tf_op jit(solution)/shard_map/ppermute | solution.py:10
  4.7 18.1 %collective-permute-start.2 = (bf16[512,256]{1,0:T(8,128)(2,1)S(1)}, bf16[512,256]{1,0:T(8,128)(2,1)S(1)}, u32[]{:S(2)}, u32[]{:S(2)}) collective-permute-start(bf16[512,256]{1,0:T(8,128)(2,1)S(1)} %get-tuple-element.7), channel_id=1, source_target_pairs={{0,4},{1,5},{2,6},{3,7},{4,0},{5,1},{6,2},{7,3},{8,12},{9,13},{10,... | collective-permute-start | bytes 786440 | tf_op jit(solution)/shard_map/ppermute | solution.py:10
  5.0 25.2 %collective-permute-start.3 = (bf16[512,256]{1,0:T(8,128)(2,1)S(1)}, bf16[512,256]{1,0:T(8,128)(2,1)S(1)}, u32[]{:S(2)}, u32[]{:S(2)}) collective-permute-start(bf16[512,256]{1,0:T(8,128)(2,1)S(1)} %get-tuple-element.7), channel_id=1, source_target_pairs={{0,6},{1,7},{2,4},{3,5},{4,2},{5,3},{6,0},{7,1},{8,14},{9,15},{10,... | collective-permute-start | bytes 786440 | tf_op jit(solution)/shard_map/ppermute | solution.py:10
  11.2 19.0 %collective-permute-start.1 = (bf16[512,256]{1,0:T(8,128)(2,1)S(1)}, bf16[512,256]{1,0:T(8,128)(2,1)S(1)}, u32[]{:S(2)}, u32[]{:S(2)}) collective-permute-start(bf16[512,256]{1,0:T(8,128)(2,1)S(1)} %get-tuple-element.7), channel_id=1, source_target_pairs={{0,2},{1,3},{2,0},{3,1},{4,6},{5,7},{6,4},{7,5},{8,10},{9,11},{10,... | collective-permute-start | bytes 786440 | tf_op jit(solution)/shard_map/ppermute | solution.py:10
  12.8 18.7 %collective-permute-start.6 = (bf16[512,256]{1,0:T(8,128)(2,1)S(1)}, bf16[512,256]{1,0:T(8,128)(2,1)S(1)}, u32[]{:S(2)}, u32[]{:S(2)}) collective-permute-start(bf16[512,256]{1,0:T(8,128)(2,1)S(1)} %get-tuple-element.7), channel_id=1, source_target_pairs={{0,24},{8,16},{16,8},{24,0},{1,25},{9,17},{17,9},{25,1},{2,26},{10... | collective-permute-start | bytes 786440 | tf_op jit(solution)/shard_map/ppermute | solution.py:10
  15.3 16.3 %collective-permute-start.5 = (bf16[512,256]{1,0:T(8,128)(2,1)S(1)}, bf16[512,256]{1,0:T(8,128)(2,1)S(1)}, u32[]{:S(2)}, u32[]{:S(2)}) collective-permute-start(bf16[512,256]{1,0:T(8,128)(2,1)S(1)} %get-tuple-element.7), channel_id=1, source_target_pairs={{0,16},{8,24},{16,0},{24,8},{1,17},{9,25},{17,1},{25,9},{2,18},{10... | collective-permute-start | bytes 786440 | tf_op jit(solution)/shard_map/ppermute | solution.py:10
  22.7 8.9 %copy-start = (bf16[512,256]{1,0:T(8,128)(2,1)}, bf16[512,256]{1,0:T(8,128)(2,1)S(1)}, u32[]{:S(2)}) copy-start(bf16[512,256]{1,0:T(8,128)(2,1)S(1)} %collective-permute-done.2) | copy-start | bytes 786436
  30.2 1.5 %copy-start.2 = (bf16[512,256]{1,0:T(8,128)(2,1)}, bf16[512,256]{1,0:T(8,128)(2,1)S(1)}, u32[]{:S(2)}) copy-start(bf16[512,256]{1,0:T(8,128)(2,1)S(1)} %collective-permute-done.3) | copy-start | bytes 786436
  30.2 1.5 %copy-start.4 = (bf16[512,256]{1,0:T(8,128)(2,1)}, bf16[512,256]{1,0:T(8,128)(2,1)S(1)}, u32[]{:S(2)}) copy-start(bf16[512,256]{1,0:T(8,128)(2,1)S(1)} %collective-permute-done.1) | copy-start | bytes 786436
  31.4 4.2 %collective-permute-start.4 = (bf16[512,1024]{1,0:T(8,128)(2,1)}, bf16[512,1024]{1,0:T(8,128)(2,1)S(1)}, u32[]{:S(2)}, u32[]{:S(2)}) collective-permute-start(bf16[512,1024]{1,0:T(8,128)(2,1)} %pad_maximum_fusion), channel_id=1, source_target_pairs={{0,1},{1,0},{2,3},{3,2},{4,5},{5,4},{6,7},{7,6},{8,9},{9,8},{10,11... | collective-permute-start | bytes 3145736 | tf_op jit(solution)/shard_map/ppermute | solution.py:10
  32.3 1.0 %copy-start.5 = (bf16[512,256]{1,0:T(8,128)(2,1)S(1)}, bf16[512,256]{1,0:T(8,128)(2,1)}, u32[]{:S(2)}) copy-start(bf16[512,256]{1,0:T(8,128)(2,1)} %copy-done.4) | copy-start | bytes 786436
  32.3 1.7 %copy-start.1 = (bf16[512,256]{1,0:T(8,128)(2,1)S(1)}, bf16[512,256]{1,0:T(8,128)(2,1)}, u32[]{:S(2)}) copy-start(bf16[512,256]{1,0:T(8,128)(2,1)} %copy-done) | copy-start | bytes 786436
  32.4 2.4 %copy-start.3 = (bf16[512,256]{1,0:T(8,128)(2,1)S(1)}, bf16[512,256]{1,0:T(8,128)(2,1)}, u32[]{:S(2)}) copy-start(bf16[512,256]{1,0:T(8,128)(2,1)} %copy-done.2) | copy-start | bytes 786436
  39.6 10.1 %collective-permute-start.9 = (bf16[512,256]{1,0:T(8,128)(2,1)S(1)}, bf16[512,256]{1,0:T(8,128)(2,1)S(1)}, u32[]{:S(2)}, u32[]{:S(2)}) collective-permute-start(bf16[512,256]{1,0:T(8,128)(2,1)S(1)} %fusion.2), channel_id=1, source_target_pairs={{0,24},{8,16},{16,8},{24,0},{1,25},{9,17},{17,9},{25,1},{2,26},{10... | collective-permute-start | bytes 786440 | tf_op jit(solution)/shard_map/ppermute | solution.py:10
  41.1 13.7 %collective-permute-start.8 = (bf16[512,256]{1,0:T(8,128)(2,1)S(1)}, bf16[512,256]{1,0:T(8,128)(2,1)S(1)}, u32[]{:S(2)}, u32[]{:S(2)}) collective-permute-start(bf16[512,256]{1,0:T(8,128)(2,1)S(1)} %fusion.2), channel_id=1, source_target_pairs={{0,16},{8,24},{16,0},{24,8},{1,17},{9,25},{17,1},{25,9},{2,18},{10... | collective-permute-start | bytes 786440 | tf_op jit(solution)/shard_map/ppermute | solution.py:10
  41.6 13.3 %collective-permute-start.7 = (bf16[512,256]{1,0:T(8,128)(2,1)S(1)}, bf16[512,256]{1,0:T(8,128)(2,1)S(1)}, u32[]{:S(2)}, u32[]{:S(2)}) collective-permute-start(bf16[512,256]{1,0:T(8,128)(2,1)S(1)} %fusion.2), channel_id=1, source_target_pairs={{0,8},{8,0},{16,24},{24,16},{1,9},{9,1},{17,25},{25,17},{2,10},{10... | collective-permute-start | bytes 786440 | tf_op jit(solution)/shard_map/ppermute | solution.py:10
  55.7 1.6 %copy-start.6 = (bf16[512,2048]{1,0:T(8,128)(2,1)S(1)}, bf16[512,2048]{1,0:T(8,128)(2,1)}, u32[]{:S(2)}) copy-start(bf16[512,2048]{1,0:T(8,128)(2,1)} %constant_dynamic-update-slice_fusion) | copy-start | bytes 6291460

commit v7 on v4

--- a/solution.py
+++ b/solution.py
@@ -26,15 +26,16 @@
         local_mask = jnp.repeat(jnp.repeat(local_blocks, B, axis=0), B, axis=1)
         masked = matrix_in * local_mask.astype(jnp.bfloat16)
 
+        col_pieces = [masked] + [_swap(masked, "row", n_row, j) for j in range(1, n_row)]
+
+        late, _ = lax.optimization_barrier((masked, col_pieces[1]))
         row_pieces = [None] * n_col
         row_pieces[0] = masked
-        row_pieces[1] = _swap(masked, "col", n_col, 1)
+        row_pieces[1] = _swap(late, "col", n_col, 1)
         for k in range(1, n_z):
-            piece = _swap(masked, "col", n_col, 2 * k)
+            piece = _swap(late if k == 1 else masked, "col", n_col, 2 * k)
             row_pieces[2 * k] = piece
             row_pieces[2 * k + 1] = _swap(piece, "col", n_col, 1)
-
-        col_pieces = [masked] + [_swap(masked, "row", n_row, k) for k in range(1, n_row)]
 
         slots = jnp.arange(n_col, dtype=jnp.int32) ^ col_index
         sub_index = ((slots // ratio) ^ row_index) * ratio + slots % ratio

time: 58.6 us -> 53.9 us (0.920)
  waiting for transfers between devices: 39.6 us -> 31.8 us
  starting transfers between devices: 9.15 us -> 12.2 us
    ppermute x13, waiting for transfers between devices: 39.6 us -> 31.8 us  [_swap(): return lax.ppermute(x, axis, [(i, i ^ d) for i in range(size)])]
    ppermute x13, starting transfers between devices: 9.15 us -> 12.2 us  [_swap(): return lax.ppermute(x, axis, [(i, i ^ d) for i in range(size)])]
where the time goes in v7:
time: 53.9 us; the launch traced here: 53.7 us
  waiting for transfers between devices  31.8 us (59%)
  starting transfers between devices  12.2 us (23%)
  local copies, waits for them, and re-layouts  4.07 us (8%)
  other arithmetic  3.17 us (6%)
  matrix products  2.22 us (4%)
    ppermute x13, waiting for transfers between devices, _swap(): return lax.ppermute(x, axis, [(i, i ^ d) for i in range(size)])  31.8 us
    ppermute x13, starting transfers between devices, _swap(): return lax.ppermute(x, axis, [(i, i ^ d) for i in range(size)])  12.2 us
    unnamed x1, other arithmetic  1.79 us
    unnamed x12, local copies, waits for them, and re-layouts  1.58 us
    dot_general x1, matrix products, body(): cubic = jnp.dot(row_cat, f_slot, preferred_element_type=jnp.float32)  1.51 us
    broadcast_in_dim x4, local copies, waits for them, and re-layouts, body(): local_mask = jnp.repeat(jnp.repeat(local_blocks, B, axis=0), B, axis=1)  1.24 us
    gather x2, local copies, waits for them, and re-layouts, in_slot_order(): return jnp.take(stacked, sub_index, axis=0).reshape(n_col * cols, cols)  1.23 us
  transfers between devices with their start and end apart: 13, of which 7 were waited for; matrix products, arithmetic and copies ran while one was open for 2% of the time, Pallas kernels for 0%

profile of v7, /device:TPU:16, one launch (start us, length us, event | category | flops | bytes accessed | tf_op | source)
XLA Modules:
  0.0 53.7 jit_solution(2686882377411855817)
XLA Ops:
  0.0 0.8 %dynamic-slice_convert_fusion.1 = (f32[4,2]{1,0:T(4,128)S(1)}, bf16[4,2]{1,0:T(4,128)(2,1)S(1)}) fusion(s32[16,16]{1,0:T(8,128)} %param.5, s32[]{:T(128)S(6)} %select_n.24, s32[]{:T(128)S(6)} %select_n.25), kind=kLoop, calls=%fused_computation.26 | loop fusion | flops 16 | bytes 88 | tf_op jit(solution)/shard_map/convert_element_type | solution.py:49
  0.8 0.6 %broadcast_in_dim.22 = bf16[512,2,128]{2,1,0:T(2,128)(2,1)S(1)} broadcast(bf16[512,2]{1,0:T(8,128)(2,1)S(1)} %bitcast.33), dimensions={0,1} | broadcast | bytes 264192 | tf_op jit(solution)/shard_map/broadcast_in_dim | solution.py:26
  1.4 1.8 %constant_dynamic-update-slice_fusion.7 = (bf16[512,2048]{1,0:T(8,128)(2,1)}, bf16[512,256]{1,0:T(8,128)(2,1)S(1)}) fusion(bf16[512,256]{1,0:T(8,128)(2,1)} %param.4, bf16[64,8,2,128]{3,2,1,0:T(2,128)(2,1)S(1)} %bitcast.31), kind=kLoop, calls=%fused_computation.19 | loop fusion | flops 524287 | bytes 1048576
  3.2 1.5 %collective-permute-start = (bf16[512,256]{1,0:T(8,128)(2,1)S(1)}, bf16[512,256]{1,0:T(8,128)(2,1)S(1)}, u32[]{:S(2)}, u32[]{:S(2)}) collective-permute-start(bf16[512,256]{1,0:T(8,128)(2,1)S(1)} %get-tuple-element.7), channel_id=1, source_target_pairs={{0,8},{8,0},{16,24},{24,16},{1,9},{9,1},{17,25},{25,17},{2,10},{10... | collective-permute-start | bytes 786440 | tf_op jit(solution)/shard_map/ppermute | solution.py:10
  4.7 1.5 %collective-permute-start.8 = (bf16[512,256]{1,0:T(8,128)(2,1)S(1)}, bf16[512,256]{1,0:T(8,128)(2,1)S(1)}, u32[]{:S(2)}, u32[]{:S(2)}) collective-permute-start(bf16[512,256]{1,0:T(8,128)(2,1)S(1)} %get-tuple-element.7), channel_id=1, source_target_pairs={{0,16},{8,24},{16,0},{24,8},{1,17},{9,25},{17,1},{25,9},{2,18},{10... | collective-permute-start | bytes 786440 | tf_op jit(solution)/shard_map/ppermute | solution.py:10
  6.2 0.5 collective-permute-start.9
  6.7 0.0 collective-permute-start.4
  6.7 3.0 %collective-permute-start.6 = (bf16[512,256]{1,0:T(8,128)(2,1)S(1)}, bf16[512,256]{1,0:T(8,128)(2,1)S(1)}, u32[]{:S(2)}, u32[]{:S(2)}) collective-permute-start(bf16[512,256]{1,0:T(8,128)(2,1)S(1)} %get-tuple-element.7), channel_id=1, source_target_pairs={{0,6},{1,7},{2,4},{3,5},{4,2},{5,3},{6,0},{7,1},{8,14},{9,15},{10,... | collective-permute-start | bytes 786440 | tf_op jit(solution)/shard_map/ppermute | solution.py:10
  9.7 2.7 %collective-permute-done = bf16[512,256]{1,0:T(8,128)(2,1)S(1)} collective-permute-done((bf16[512,256]{1,0:T(8,128)(2,1)S(1)}, bf16[512,256]{1,0:T(8,128)(2,1)S(1)}, u32[]{:S(2)}, u32[]{:S(2)}) %collective-permute-start) | collective-permute-done | bytes 262176 | tf_op jit(solution)/shard_map/ppermute | solution.py:10
  12.4 1.6 %collective-permute-start.2 = (bf16[512,256]{1,0:T(8,128)(2,1)S(1)}, bf16[512,256]{1,0:T(8,128)(2,1)S(1)}, u32[]{:S(2)}, u32[]{:S(2)}) collective-permute-start(bf16[512,256]{1,0:T(8,128)(2,1)S(1)} %get-tuple-element.7), channel_id=1, source_target_pairs={{0,2},{1,3},{2,0},{3,1},{4,6},{5,7},{6,4},{7,5},{8,10},{9,11},{10,... | collective-permute-start | bytes 786440 | tf_op jit(solution)/shard_map/ppermute | solution.py:10
  14.0 4.1 %collective-permute-done.8 = bf16[512,256]{1,0:T(8,128)(2,1)S(1)} collective-permute-done((bf16[512,256]{1,0:T(8,128)(2,1)S(1)}, bf16[512,256]{1,0:T(8,128)(2,1)S(1)}, u32[]{:S(2)}, u32[]{:S(2)}) %collective-permute-start.8) | collective-permute-done | bytes 262176 | tf_op jit(solution)/shard_map/ppermute | solution.py:10
  18.1 0.0 collective-permute-start.1
  18.1 0.0 collective-permute-done.9
  18.1 0.1 pad_maximum_fusion
  18.2 0.6 %gather_fusion = bf16[8,256,256]{2,1,0:T(8,128)(2,1)S(1)} fusion(bf16[8,256,256]{2,1,0:T(8,128)(2,1)S(1)} %bitcast.27, s32[1024]{0:T(1024)S(1)} %pad_clamp_fusion), kind=kCustom, calls=%fused_computation.clone | custom fusion | bytes 2097184 | tf_op jit(solution)/shard_map/jit(_take)/gather | solution.py:45
  18.8 0.0 copy-start
  18.8 9.8 %collective-permute-done.2 = bf16[512,256]{1,0:T(8,128)(2,1)S(1)} collective-permute-done((bf16[512,256]{1,0:T(8,128)(2,1)S(1)}, bf16[512,256]{1,0:T(8,128)(2,1)S(1)}, u32[]{:S(2)}, u32[]{:S(2)}) %collective-permute-start.2) | collective-permute-done | bytes 262176 | tf_op jit(solution)/shard_map/ppermute | solution.py:10
  28.6 0.0 collective-permute-start.3
  28.6 0.2 broadcast_select_fusion
  28.8 0.0 collective-permute-done.4
  28.8 0.6 %collective-permute-start.5 = (bf16[512,256]{1,0:T(8,128)(2,1)S(1)}, bf16[512,256]{1,0:T(8,128)(2,1)S(1)}, u32[]{:S(2)}, u32[]{:S(2)}) collective-permute-start(bf16[512,256]{1,0:T(8,128)(2,1)S(1)} %collective-permute-done.4), channel_id=1, source_target_pairs={{0,1},{1,0},{2,3},{3,2},{4,5},{5,4},{6,7},{7,6},{8,9},{9,8},{10,11... | collective-permute-start | bytes 786440 | tf_op jit(solution)/shard_map/ppermute | solution.py:10
  29.4 2.3 %collective-permute-done.6 = bf16[512,256]{1,0:T(8,128)(2,1)S(1)} collective-permute-done((bf16[512,256]{1,0:T(8,128)(2,1)S(1)}, bf16[512,256]{1,0:T(8,128)(2,1)S(1)}, u32[]{:S(2)}, u32[]{:S(2)}) %collective-permute-start.6) | collective-permute-done | bytes 262176 | tf_op jit(solution)/shard_map/ppermute | solution.py:10
  31.7 0.0 collective-permute-start.7
  31.7 0.0 collective-permute-done.1
  31.7 0.0 copy-done
  31.8 0.0 collective-permute-done.3
  31.8 0.0 collective-permute-done.5
  31.9 1.3 %collective-permute-done.7 = bf16[512,256]{1,0:T(8,128)(2,1)S(1)} collective-permute-done((bf16[512,256]{1,0:T(8,128)(2,1)S(1)}, bf16[512,256]{1,0:T(8,128)(2,1)S(1)}, u32[]{:S(2)}, u32[]{:S(2)}) %collective-permute-start.7) | collective-permute-done | bytes 262176 | tf_op jit(solution)/shard_map/ppermute | solution.py:10
  33.2 0.0 copy-start.1
  33.3 0.6 %broadcast_in_dim.20 = f32[512,2,128]{2,1,0:T(2,128)S(1)} broadcast(f32[512,2]{1,0:T(8,128)S(1)} %bitcast.30), dimensions={0,1} | broadcast | bytes 528384 | tf_op jit(solution)/shard_map/broadcast_in_dim | solution.py:26
  33.9 0.7 %fusion.2 = bf16[512,256]{1,0:T(8,128)(2,1)S(1)} fusion(bf16[512,2048]{1,0:T(8,128)(2,1)S(1)} %constant_dynamic-update-slice_fusion, bf16[2048,256]{1,0:T(8,128)(2,1)S(1)} %bitcast.28, f32[64,8,2,128]{3,2,1,0:T(2,128)S(1)} %bitcast.34), kind=kOutput, calls=%fused_computation.6 | convolution fusion | flops 537133056 | bytes 3932160 | tf_op jit(solution)/shard_map/dot_general | solution.py:48
  34.6 0.0 copy-done.1
  34.6 1.6 %collective-permute-start.11 = (bf16[512,256]{1,0:T(8,128)(2,1)S(1)}, bf16[512,256]{1,0:T(8,128)(2,1)S(1)}, u32[]{:S(2)}, u32[]{:S(2)}) collective-permute-start(bf16[512,256]{1,0:T(8,128)(2,1)S(1)} %fusion.2), channel_id=1, source_target_pairs={{0,16},{8,24},{16,0},{24,8},{1,17},{9,25},{17,1},{25,9},{2,18},{10... | collective-permute-start | bytes 786440 | tf_op jit(solution)/shard_map/ppermute | solution.py:10
  36.2 1.4 %collective-permute-start.12 = (bf16[512,256]{1,0:T(8,128)(2,1)S(1)}, bf16[512,256]{1,0:T(8,128)(2,1)S(1)}, u32[]{:S(2)}, u32[]{:S(2)}) collective-permute-start(bf16[512,256]{1,0:T(8,128)(2,1)S(1)} %fusion.2), channel_id=1, source_target_pairs={{0,24},{8,16},{16,8},{24,0},{1,25},{9,17},{17,9},{25,1},{2,26},{10... | collective-permute-start | bytes 786440 | tf_op jit(solution)/shard_map/ppermute | solution.py:10
  37.6 0.5 collective-permute-start.10
  38.2 10.5 %collective-permute-done.11 = bf16[512,256]{1,0:T(8,128)(2,1)S(1)} collective-permute-done((bf16[512,256]{1,0:T(8,128)(2,1)S(1)}, bf16[512,256]{1,0:T(8,128)(2,1)S(1)}, u32[]{:S(2)}, u32[]{:S(2)}) %collective-permute-start.11) | collective-permute-done | bytes 262176 | tf_op jit(solution)/shard_map/ppermute | solution.py:10
  48.6 0.0 collective-permute-done.12
  48.6 1.2 %collective-permute-done.10 = bf16[512,256]{1,0:T(8,128)(2,1)S(1)} collective-permute-done((bf16[512,256]{1,0:T(8,128)(2,1)S(1)}, bf16[512,256]{1,0:T(8,128)(2,1)S(1)}, u32[]{:S(2)}, u32[]{:S(2)}) %collective-permute-start.10) | collective-permute-done | bytes 262176 | tf_op jit(solution)/shard_map/ppermute | solution.py:10
  49.9 0.1 pad_maximum_fusion.1
  50.0 0.6 %gather_fusion.1 = bf16[8,256,256]{2,1,0:T(8,128)(2,1)S(1)} fusion(bf16[8,256,256]{2,1,0:T(8,128)(2,1)S(1)} %bitcast.26, s32[1024]{0:T(1024)S(1)} %pad_clamp_fusion), kind=kCustom, calls=%fused_computation.1.clone | custom fusion | bytes 2097184 | tf_op jit(solution)/shard_map/jit(_take)/gather | solution.py:45
  50.6 0.0 copy-start.2
  50.6 0.2 broadcast_select_fusion.1
  50.8 1.4 %copy-done.2 = bf16[512,2048]{1,0:T(8,128)(2,1)S(1)} copy-done((bf16[512,2048]{1,0:T(8,128)(2,1)S(1)}, bf16[512,2048]{1,0:T(8,128)(2,1)}, u32[]{:S(2)}) %copy-start.2) | copy-done | bytes 2097176
  52.2 1.5 %fusion.1 = f32[512,256]{1,0:T(8,128)} fusion(bf16[512,2048]{1,0:T(8,128)(2,1)S(1)} %copy-done.2, bf16[2048,256]{1,0:T(8,128)(2,1)S(1)} %bitcast.29, bf16[512,256]{1,0:T(8,128)(2,1)S(1)} %get-tuple-element.7, f32[64,8,2,128]{3,2,1,0:T(2,128)S(1)} %bitcast.35), kind=kOutput, calls=%fused_computation.5 | convolution fusion | flops 537526272 | bytes 4456448 | tf_op jit(solution)/shard_map/dot_general | solution.py:53
  (11 shorter events, 0.2 us)
Async XLA Ops:
  3.2 9.2 %collective-permute-start = (bf16[512,256]{1,0:T(8,128)(2,1)S(1)}, bf16[512,256]{1,0:T(8,128)(2,1)S(1)}, u32[]{:S(2)}, u32[]{:S(2)}) collective-permute-start(bf16[512,256]{1,0:T(8,128)(2,1)S(1)} %get-tuple-element.7), channel_id=1, source_target_pairs={{0,8},{8,0},{16,24},{24,16},{1,9},{9,1},{17,25},{25,17},{2,10},{10... | collective-permute-start | bytes 786440 | tf_op jit(solution)/shard_map/ppermute | solution.py:10
  4.7 13.4 %collective-permute-start.8 = (bf16[512,256]{1,0:T(8,128)(2,1)S(1)}, bf16[512,256]{1,0:T(8,128)(2,1)S(1)}, u32[]{:S(2)}, u32[]{:S(2)}) collective-permute-start(bf16[512,256]{1,0:T(8,128)(2,1)S(1)} %get-tuple-element.7), channel_id=1, source_target_pairs={{0,16},{8,24},{16,0},{24,8},{1,17},{9,25},{17,1},{25,9},{2,18},{10... | collective-permute-start | bytes 786440 | tf_op jit(solution)/shard_map/ppermute | solution.py:10
  6.2 11.9 %collective-permute-start.9 = (bf16[512,256]{1,0:T(8,128)(2,1)S(1)}, bf16[512,256]{1,0:T(8,128)(2,1)S(1)}, u32[]{:S(2)}, u32[]{:S(2)}) collective-permute-start(bf16[512,256]{1,0:T(8,128)(2,1)S(1)} %get-tuple-element.7), channel_id=1, source_target_pairs={{0,24},{8,16},{16,8},{24,0},{1,25},{9,17},{17,9},{25,1},{2,26},{10... | collective-permute-start | bytes 786440 | tf_op jit(solution)/shard_map/ppermute | solution.py:10
  6.7 22.1 %collective-permute-start.4 = (bf16[512,256]{1,0:T(8,128)(2,1)S(1)}, bf16[512,256]{1,0:T(8,128)(2,1)S(1)}, u32[]{:S(2)}, u32[]{:S(2)}) collective-permute-start(bf16[512,256]{1,0:T(8,128)(2,1)S(1)} %get-tuple-element.7), channel_id=1, source_target_pairs={{0,4},{1,5},{2,6},{3,7},{4,0},{5,1},{6,2},{7,3},{8,12},{9,13},{10,... | collective-permute-start | bytes 786440 | tf_op jit(solution)/shard_map/ppermute | solution.py:10
  6.7 25.0 %collective-permute-start.6 = (bf16[512,256]{1,0:T(8,128)(2,1)S(1)}, bf16[512,256]{1,0:T(8,128)(2,1)S(1)}, u32[]{:S(2)}, u32[]{:S(2)}) collective-permute-start(bf16[512,256]{1,0:T(8,128)(2,1)S(1)} %get-tuple-element.7), channel_id=1, source_target_pairs={{0,6},{1,7},{2,4},{3,5},{4,2},{5,3},{6,0},{7,1},{8,14},{9,15},{10,... | collective-permute-start | bytes 786440 | tf_op jit(solution)/shard_map/ppermute | solution.py:10
  12.4 16.2 %collective-permute-start.2 = (bf16[512,256]{1,0:T(8,128)(2,1)S(1)}, bf16[512,256]{1,0:T(8,128)(2,1)S(1)}, u32[]{:S(2)}, u32[]{:S(2)}) collective-permute-start(bf16[512,256]{1,0:T(8,128)(2,1)S(1)} %get-tuple-element.7), channel_id=1, source_target_pairs={{0,2},{1,3},{2,0},{3,1},{4,6},{5,7},{6,4},{7,5},{8,10},{9,11},{10,... | collective-permute-start | bytes 786440 | tf_op jit(solution)/shard_map/ppermute | solution.py:10
  18.1 13.6 %collective-permute-start.1 = (bf16[512,256]{1,0:T(8,128)(2,1)S(1)}, bf16[512,256]{1,0:T(8,128)(2,1)S(1)}, u32[]{:S(2)}, u32[]{:S(2)}) collective-permute-start(bf16[512,256]{1,0:T(8,128)(2,1)S(1)} %get-tuple-element.7), channel_id=1, source_target_pairs={{0,1},{1,0},{2,3},{3,2},{4,5},{5,4},{6,7},{7,6},{8,9},{9,8},{10,11... | collective-permute-start | bytes 786440 | tf_op jit(solution)/shard_map/ppermute | solution.py:10
  18.8 12.9 %copy-start = (bf16[512,2048]{1,0:T(8,128)(2,1)S(1)}, bf16[512,2048]{1,0:T(8,128)(2,1)}, u32[]{:S(2)}) copy-start(bf16[512,2048]{1,0:T(8,128)(2,1)} %get-tuple-element.10) | copy-start | bytes 6291460
  28.6 3.1 %collective-permute-start.3 = (bf16[512,256]{1,0:T(8,128)(2,1)S(1)}, bf16[512,256]{1,0:T(8,128)(2,1)S(1)}, u32[]{:S(2)}, u32[]{:S(2)}) collective-permute-start(bf16[512,256]{1,0:T(8,128)(2,1)S(1)} %collective-permute-done.2), channel_id=1, source_target_pairs={{0,1},{1,0},{2,3},{3,2},{4,5},{5,4},{6,7},{7,6},{8,9},{9,8},{10,11... | collective-permute-start | bytes 786440 | tf_op jit(solution)/shard_map/ppermute | solution.py:10
  28.8 3.0 %collective-permute-start.5 = (bf16[512,256]{1,0:T(8,128)(2,1)S(1)}, bf16[512,256]{1,0:T(8,128)(2,1)S(1)}, u32[]{:S(2)}, u32[]{:S(2)}) collective-permute-start(bf16[512,256]{1,0:T(8,128)(2,1)S(1)} %collective-permute-done.4), channel_id=1, source_target_pairs={{0,1},{1,0},{2,3},{3,2},{4,5},{5,4},{6,7},{7,6},{8,9},{9,8},{10,11... | collective-permute-start | bytes 786440 | tf_op jit(solution)/shard_map/ppermute | solution.py:10
  31.7 1.5 %collective-permute-start.7 = (bf16[512,256]{1,0:T(8,128)(2,1)S(1)}, bf16[512,256]{1,0:T(8,128)(2,1)S(1)}, u32[]{:S(2)}, u32[]{:S(2)}) collective-permute-start(bf16[512,256]{1,0:T(8,128)(2,1)S(1)} %collective-permute-done.6), channel_id=1, source_target_pairs={{0,1},{1,0},{2,3},{3,2},{4,5},{5,4},{6,7},{7,6},{8,9},{9,8},{10,11... | collective-permute-start | bytes 786440 | tf_op jit(solution)/shard_map/ppermute | solution.py:10
  33.2 1.4 %copy-start.1 = (bf16[512,2048]{1,0:T(8,128)(2,1)}, bf16[512,2048]{1,0:T(8,128)(2,1)S(1)}, u32[]{:S(2)}) copy-start(bf16[512,2048]{1,0:T(8,128)(2,1)S(1)} %constant_dynamic-update-slice_fusion) | copy-start | bytes 6291460
  34.6 14.0 %collective-permute-start.11 = (bf16[512,256]{1,0:T(8,128)(2,1)S(1)}, bf16[512,256]{1,0:T(8,128)(2,1)S(1)}, u32[]{:S(2)}, u32[]{:S(2)}) collective-permute-start(bf16[512,256]{1,0:T(8,128)(2,1)S(1)} %fusion.2), channel_id=1, source_target_pairs={{0,16},{8,24},{16,0},{24,8},{1,17},{9,25},{17,1},{25,9},{2,18},{10... | collective-permute-start | bytes 786440 | tf_op jit(solution)/shard_map/ppermute | solution.py:10
  36.2 12.4 %collective-permute-start.12 = (bf16[512,256]{1,0:T(8,128)(2,1)S(1)}, bf16[512,256]{1,0:T(8,128)(2,1)S(1)}, u32[]{:S(2)}, u32[]{:S(2)}) collective-permute-start(bf16[512,256]{1,0:T(8,128)(2,1)S(1)} %fusion.2), channel_id=1, source_target_pairs={{0,24},{8,16},{16,8},{24,0},{1,25},{9,17},{17,9},{25,1},{2,26},{10... | collective-permute-start | bytes 786440 | tf_op jit(solution)/shard_map/ppermute | solution.py:10
  37.6 12.2 %collective-permute-start.10 = (bf16[512,256]{1,0:T(8,128)(2,1)S(1)}, bf16[512,256]{1,0:T(8,128)(2,1)S(1)}, u32[]{:S(2)}, u32[]{:S(2)}) collective-permute-start(bf16[512,256]{1,0:T(8,128)(2,1)S(1)} %fusion.2), channel_id=1, source_target_pairs={{0,8},{8,0},{16,24},{24,16},{1,9},{9,1},{17,25},{25,17},{2,10},{10... | collective-permute-start | bytes 786440 | tf_op jit(solution)/shard_map/ppermute | solution.py:10
  50.6 1.6 %copy-start.2 = (bf16[512,2048]{1,0:T(8,128)(2,1)S(1)}, bf16[512,2048]{1,0:T(8,128)(2,1)}, u32[]{:S(2)}) copy-start(bf16[512,2048]{1,0:T(8,128)(2,1)} %copy-done.1) | copy-start | bytes 6291460

commit v8 on v7

--- a/solution.py
+++ b/solution.py
@@ -29,13 +29,6 @@
         col_pieces = [masked] + [_swap(masked, "row", n_row, j) for j in range(1, n_row)]
 
         late, _ = lax.optimization_barrier((masked, col_pieces[1]))
-        row_pieces = [None] * n_col
-        row_pieces[0] = masked
-        row_pieces[1] = _swap(late, "col", n_col, 1)
-        for k in range(1, n_z):
-            piece = _swap(late if k == 1 else masked, "col", n_col, 2 * k)
-            row_pieces[2 * k] = piece
-            row_pieces[2 * k + 1] = _swap(piece, "col", n_col, 1)
 
         slots = jnp.arange(n_col, dtype=jnp.int32) ^ col_index
         sub_index = ((slots // ratio) ^ row_index) * ratio + slots % ratio
@@ -44,13 +37,50 @@
             stacked = jnp.stack(pieces).reshape(n_row * ratio, cols, cols)
             return jnp.take(stacked, sub_index, axis=0).reshape(n_col * cols, cols)
 
-        row_cat = jnp.concatenate(row_pieces, axis=1)
-        square = jnp.dot(row_cat, in_slot_order(col_pieces), preferred_element_type=jnp.float32)
+        col_slot = None
         mask_float = local_mask.astype(jnp.float32)
-        filtered = (mask_float * square).astype(jnp.bfloat16)
-        f_pieces = [filtered] + [_swap(filtered, "row", n_row, k) for k in range(1, n_row)]
+        waves = 2 if rows % (2 * B) == 0 else 1
+        half = rows // waves
+        row_cats, f_waves = [], []
+        previous = None
+        for w in range(waves):
+            part = masked[w * half:(w + 1) * half]
+            early = late[w * half:(w + 1) * half]
+            if previous is not None:
+                part, _ = lax.optimization_barrier((part, previous))
+                early = part
+            pieces = [None] * n_col
+            pieces[0] = part
+            pieces[1] = _swap(early, "col", n_col, 1)
+            for k in range(1, n_z):
+                piece = _swap(early if k == 1 else part, "col", n_col, 2 * k)
+                pieces[2 * k] = piece
+                pieces[2 * k + 1] = _swap(piece, "col", n_col, 1)
+            row_cat = jnp.concatenate(pieces, axis=1)
+            row_cats.append(row_cat)
+            if col_slot is None:
+                col_slot = in_slot_order(col_pieces)
+            square = jnp.dot(row_cat, col_slot, preferred_element_type=jnp.float32)
+            filtered = (mask_float[w * half:(w + 1) * half] * square).astype(jnp.bfloat16)
+            previous = filtered
+            f_wave = [filtered] + [None] * (n_row - 1)
+            if w + 1 < waves:
+                step = 1
+                while step < n_row:
+                    got = _swap(jnp.stack(f_wave[:step]), "row", n_row, step)
+                    for j in range(step):
+                        f_wave[j ^ step] = got[j]
+                    step *= 2
+            else:
+                for j in range(1, n_row):
+                    f_wave[j] = _swap(filtered, "row", n_row, j)
+            f_waves.append(f_wave)
+
+        f_pieces = [jnp.concatenate([fw[j] for fw in f_waves], axis=0) for j in range(n_row)]
         f_slot = in_slot_order(f_pieces)
-        cubic = jnp.dot(row_cat, f_slot, preferred_element_type=jnp.float32)
+        cubic = jnp.concatenate(
+            [jnp.dot(rc, f_slot, preferred_element_type=jnp.float32) for rc in row_cats], axis=0
+        )
         return mask_float * (1.5 * masked.astype(jnp.float32) - 0.5 * cubic)
 
     return body

time: 53.9 us -> 66.3 us (1.23); the launches traced: 53.7 us -> 65.3 us
  local copies, waits for them, and re-layouts: 4.07 us -> 12.2 us
  starting transfers between devices: 12.2 us -> 18 us
  waiting for transfers between devices: 31.8 us -> 29.6 us
    ppermute x13 -> x22, starting transfers between devices: 12.2 us -> 18 us  [_swap(): return lax.ppermute(x, axis, [(i, i ^ d) for i in range(size)])]
    unnamed x12 -> x17, local copies, waits for them, and re-layouts: 1.58 us -> 5.65 us
    ppermute x13 -> x22, waiting for transfers between devices: 31.8 us -> 29.6 us  [_swap(): return lax.ppermute(x, axis, [(i, i ^ d) for i in range(size)])]
    unnamed x1 -> x0, other arithmetic: 1.79 us -> none
    slice x0 -> x3, local copies, waits for them, and re-layouts: none -> 1.28 us  [the longest x1 0.66 us: body(): early = late[w * half:(w + 1) * half]]
    gather x2, local copies, waits for them, and re-layouts: 1.23 us -> 2.45 us  [in_slot_order(): return jnp.take(stacked, sub_index, axis=0).reshape(n_col * cols, cols)]
    another operation x2 -> x6, other arithmetic: 0.26 us -> 1.35 us  [in_slot_order(): stacked = jnp.stack(pieces).reshape(n_row * ratio, cols, cols)]
    mul x0 -> x2, other arithmetic: none -> 0.93 us  [the longest x1 0.89 us: body(): return mask_float * (1.5 * masked.astype(jnp.float32) - 0.5 * cubic)]
  transfers between devices with their start and end apart: 13 -> 22, of which waited for: 7 -> 10; matrix products, arithmetic and copies ran while one was open for 2% -> 12% of each run, Pallas kernels for 0% -> 0%
where the time goes in v8:
time: 66.3 us; the launch traced here: 65.3 us
  waiting for transfers between devices  29.6 us (45%)
  starting transfers between devices  18 us (27%)
  local copies, waits for them, and re-layouts  12.2 us (18%)
  other arithmetic  3.42 us (5%)
  matrix products  1.76 us (3%)
    ppermute x22, waiting for transfers between devices, _swap(): return lax.ppermute(x, axis, [(i, i ^ d) for i in range(size)])  29.6 us
    ppermute x22, starting transfers between devices, _swap(): return lax.ppermute(x, axis, [(i, i ^ d) for i in range(size)])  18 us
    unnamed x17, local copies, waits for them, and re-layouts  5.65 us
    gather x2, local copies, waits for them, and re-layouts, in_slot_order(): return jnp.take(stacked, sub_index, axis=0).reshape(n_col * cols, cols)  2.45 us
    broadcast_in_dim x8, local copies, waits for them, and re-layouts, body(): local_mask = jnp.repeat(jnp.repeat(local_blocks, B, axis=0), B, axis=1)  1.92 us
    another operation x6, other arithmetic, in_slot_order(): stacked = jnp.stack(pieces).reshape(n_row * ratio, cols, cols)  1.35 us
  transfers between devices with their start and end apart: 22, of which 10 were waited for; matrix products, arithmetic and copies ran while one was open for 12% of the time, Pallas kernels for 0%

profile of v8, /device:TPU:16, one launch (start us, length us, event | category | flops | bytes accessed | tf_op | source)
XLA Modules:
  0.0 65.3 jit_solution(5535530380265392921)
XLA Ops:
  0.0 0.8 %dynamic-slice_convert_fusion = (bf16[4,2]{1,0:T(4,128)(2,1)S(1)}, f32[4,2]{1,0:T(4,128)S(1)}) fusion(s32[16,16]{1,0:T(8,128)} %param.5, s32[]{:T(128)S(6)} %select_n.24, s32[]{:T(128)S(6)} %select_n.25), kind=kLoop, calls=%fused_computation.42 | loop fusion | flops 16 | bytes 88 | tf_op jit(solution)/shard_map/convert_element_type | solution.py:27
  0.8 0.6 broadcast_in_dim.30
  1.4 0.3 copy-done
  1.8 1.6 %collective-permute-start = (bf16[512,256]{1,0:T(8,128)(2,1)S(1)}, bf16[512,256]{1,0:T(8,128)(2,1)S(1)}, u32[]{:S(2)}, u32[]{:S(2)}) collective-permute-start(bf16[512,256]{1,0:T(8,128)(2,1)S(1)} %bitcast_multiply_fusion.1), channel_id=1, source_target_pairs={{0,8},{8,0},{16,24},{24,16},{1,9},{9,1},{17,25},{25,17},{2,10},{10... | collective-permute-start | bytes 786440 | tf_op jit(solution)/shard_map/ppermute | solution.py:10
  3.3 0.4 collective-permute-start.4
  3.7 2.7 %collective-permute-start.6 = (bf16[256,256]{1,0:T(8,128)(2,1)S(1)}, bf16[256,256]{1,0:T(8,128)(2,1)}, u32[]{:S(2)}, u32[]{:S(2)}) collective-permute-start(bf16[256,256]{1,0:T(8,128)(2,1)S(1)} %get-tuple-element.14), channel_id=1, source_target_pairs={{0,6},{1,7},{2,4},{3,5},{4,2},{5,3},{6,0},{7,1},{8,14},{9,15},{10,... | collective-permute-start | bytes 393224 | tf_op jit(solution)/shard_map/ppermute | solution.py:10
  6.4 1.5 %collective-permute-start.8 = (bf16[512,256]{1,0:T(8,128)(2,1)S(1)}, bf16[512,256]{1,0:T(8,128)(2,1)S(1)}, u32[]{:S(2)}, u32[]{:S(2)}) collective-permute-start(bf16[512,256]{1,0:T(8,128)(2,1)S(1)} %bitcast_multiply_fusion.1), channel_id=1, source_target_pairs={{0,16},{8,24},{16,0},{24,8},{1,17},{9,25},{17,1},{25,9},{2,18},{10... | collective-permute-start | bytes 786440 | tf_op jit(solution)/shard_map/ppermute | solution.py:10
  8.0 0.5 collective-permute-start.9
  8.4 0.6 fusion.5
  9.1 3.9 %collective-permute-done.4 = bf16[256,256]{1,0:T(8,128)(2,1)} collective-permute-done((bf16[256,256]{1,0:T(8,128)(2,1)S(1)}, bf16[256,256]{1,0:T(8,128)(2,1)}, u32[]{:S(2)}, u32[]{:S(2)}) %collective-permute-start.4) | collective-permute-done | bytes 131104 | tf_op jit(solution)/shard_map/ppermute | solution.py:10
  13.0 0.0 collective-permute-start.5
  13.0 4.8 %collective-permute-done.6 = bf16[256,256]{1,0:T(8,128)(2,1)} collective-permute-done((bf16[256,256]{1,0:T(8,128)(2,1)S(1)}, bf16[256,256]{1,0:T(8,128)(2,1)}, u32[]{:S(2)}, u32[]{:S(2)}) %collective-permute-start.6) | collective-permute-done | bytes 131104 | tf_op jit(solution)/shard_map/ppermute | solution.py:10
  17.8 0.0 collective-permute-start.7
  17.8 0.0 collective-permute-done
  17.8 0.7 %slice.38 = bf16[256,256]{1,0:T(8,128)(2,1)} slice(bf16[512,256]{1,0:T(8,128)(2,1)S(1)} %bitcast_multiply_fusion.1), slice={[0:256], [0:256]} | slice | bytes 262144 | tf_op jit(solution)/shard_map/slice | solution.py:48
  18.5 0.5 collective-permute-start.1
  19.0 0.3 collective-permute-done.8
  19.3 1.3 %collective-permute-start.2 = (bf16[256,256]{1,0:T(8,128)(2,1)}, bf16[256,256]{1,0:T(8,128)(2,1)}, u32[]{:S(2)}, u32[]{:S(2)}) collective-permute-start(bf16[256,256]{1,0:T(8,128)(2,1)} %slice.38), channel_id=1, source_target_pairs={{0,2},{1,3},{2,0},{3,1},{4,6},{5,7},{6,4},{7,5},{8,10},{9,11},{10,... | collective-permute-start | bytes 393224 | tf_op jit(solution)/shard_map/ppermute | solution.py:10
  20.6 0.0 collective-permute-done.9
  20.6 0.1 pad_maximum_fusion
  20.8 0.6 gather_fusion
  21.4 0.2 broadcast_select_fusion
  21.6 3.2 %collective-permute-done.2 = bf16[256,256]{1,0:T(8,128)(2,1)} collective-permute-done((bf16[256,256]{1,0:T(8,128)(2,1)}, bf16[256,256]{1,0:T(8,128)(2,1)}, u32[]{:S(2)}, u32[]{:S(2)}) %collective-permute-start.2) | collective-permute-done | bytes 131104 | tf_op jit(solution)/shard_map/ppermute | solution.py:10
  24.7 0.0 collective-permute-start.3
  24.7 0.0 collective-permute-done.1
  24.7 0.9 %constant_dynamic-update-slice_fusion.6 = bf16[256,2048]{1,0:T(8,128)(2,1)S(1)} fusion(bf16[256,2048]{1,0:T(8,128)(2,1)S(1)} %get-tuple-element.15, bf16[256,256]{1,0:T(8,128)(2,1)} %collective-permute-done.1), kind=kLoop, calls=%fused_computation.27 | loop fusion | bytes 262144
  25.6 0.9 %constant_dynamic-update-slice_fusion.5 = bf16[256,2048]{1,0:T(8,128)(2,1)S(1)} fusion(bf16[256,2048]{1,0:T(8,128)(2,1)S(1)} %constant_dynamic-update-slice_fusion.6, bf16[256,256]{1,0:T(8,128)(2,1)} %collective-permute-done.2), kind=kLoop, calls=%fused_computation.26 | loop fusion | bytes 262144
  26.6 0.0 collective-permute-done.3
  26.6 0.9 %constant_dynamic-update-slice_fusion.3 = bf16[256,2048]{1,0:T(8,128)(2,1)S(1)} fusion(bf16[256,2048]{1,0:T(8,128)(2,1)S(1)} %constant_dynamic-update-slice_fusion.4, bf16[256,256]{1,0:T(8,128)(2,1)} %collective-permute-done.4), kind=kLoop, calls=%fused_computation.24 | loop fusion | bytes 262144
  27.5 0.0 collective-permute-done.5
  27.5 0.9 %constant_dynamic-update-slice_fusion.2 = bf16[256,2048]{1,0:T(8,128)(2,1)S(1)} fusion(bf16[256,2048]{1,0:T(8,128)(2,1)S(1)} %constant_dynamic-update-slice_fusion.3, bf16[256,256]{1,0:T(8,128)(2,1)} %collective-permute-done.5), kind=kLoop, calls=%fused_computation.23 | loop fusion | bytes 262144
  28.4 0.9 %constant_dynamic-update-slice_fusion.1 = bf16[256,2048]{1,0:T(8,128)(2,1)S(1)} fusion(bf16[256,2048]{1,0:T(8,128)(2,1)S(1)} %constant_dynamic-update-slice_fusion.2, bf16[256,256]{1,0:T(8,128)(2,1)} %collective-permute-done.6), kind=kLoop, calls=%fused_computation.22 | loop fusion | bytes 262144
  29.4 0.0 collective-permute-done.7
  29.4 0.9 %constant_dynamic-update-slice_fusion = bf16[256,2048]{1,0:T(8,128)(2,1)S(1)} fusion(bf16[256,2048]{1,0:T(8,128)(2,1)S(1)} %constant_dynamic-update-slice_fusion.1, bf16[256,256]{1,0:T(8,128)(2,1)} %collective-permute-done.7), kind=kLoop, calls=%fused_computation.21 | loop fusion | bytes 262144 | tf_op jit(solution)/shard_map/concatenate | solution.py:59
  30.3 0.7 %copy-done.1 = f32[2,2]{1,0:T(2,128)S(1)} copy-done((f32[2,2]{1,0:T(2,128)S(1)}, f32[2,2]{1,0:T(2,128)}, u32[]{:S(2)}) %copy-start.1) | copy-done | bytes 40
  31.0 0.3 broadcast_in_dim.32
  31.3 0.4 fusion
  31.8 0.6 collective-permute-start.17
  32.4 0.2 collective-permute-start.10
  32.6 1.2 %collective-permute-start.11 = (bf16[256,256]{1,0:T(8,128)(2,1)S(1)}, bf16[256,256]{1,0:T(8,128)(2,1)S(1)}, u32[]{:S(2)}, u32[]{:S(2)}) collective-permute-start(bf16[256,256]{1,0:T(8,128)(2,1)S(1)} %get-tuple-element.9), channel_id=1, source_target_pairs={{0,2},{1,3},{2,0},{3,1},{4,6},{5,7},{6,4},{7,5},{8,10},{9,11},{10,... | collective-permute-start | bytes 393224 | tf_op jit(solution)/shard_map/ppermute | solution.py:10
  33.8 0.4 collective-permute-start.13
  34.2 1.9 %collective-permute-start.15 = (bf16[256,256]{1,0:T(8,128)(2,1)S(1)}, bf16[256,256]{1,0:T(8,128)(2,1)S(1)}, u32[]{:S(2)}, u32[]{:S(2)}) collective-permute-start(bf16[256,256]{1,0:T(8,128)(2,1)S(1)} %get-tuple-element.9), channel_id=1, source_target_pairs={{0,6},{1,7},{2,4},{3,5},{4,2},{5,3},{6,0},{7,1},{8,14},{9,15},{10,... | collective-permute-start | bytes 393224 | tf_op jit(solution)/shard_map/ppermute | solution.py:10
  36.1 1.6 %collective-permute-done.17 = bf16[1,256,256]{2,1,0:T(8,128)(2,1)S(1)} collective-permute-done((bf16[1,256,256]{2,1,0:T(8,128)(2,1)S(1)}, bf16[1,256,256]{2,1,0:T(8,128)(2,1)S(1)}, u32[]{:S(2)}, u32[]{:S(2)}) %collective-permute-start.17) | collective-permute-done | bytes 131104 | tf_op jit(solution)/shard_map/ppermute | solution.py:10
  37.8 1.6 %collective-permute-start.19 = (bf16[2,256,256]{2,1,0:T(8,128)(2,1)S(1)}, bf16[2,256,256]{2,1,0:T(8,128)(2,1)S(1)}, u32[]{:S(2)}, u32[]{:S(2)}) collective-permute-start(bf16[2,256,256]{2,1,0:T(8,128)(2,1)S(1)} %pad_maximum_fusion.2), channel_id=1, source_target_pairs={{0,16},{8,24},{16,0},{24,8},{1,17},{9,25},{17,1},{25,9},{2,18},{10... | collective-permute-start | bytes 786440 | tf_op jit(solution)/shard_map/ppermute | solution.py:10
  39.3 0.0 collective-permute-done.11
  39.3 0.0 collective-permute-start.12
  39.4 4.2 %collective-permute-done.13 = bf16[256,256]{1,0:T(8,128)(2,1)S(1)} collective-permute-done((bf16[256,256]{1,0:T(8,128)(2,1)S(1)}, bf16[256,256]{1,0:T(8,128)(2,1)S(1)}, u32[]{:S(2)}, u32[]{:S(2)}) %collective-permute-start.13) | collective-permute-done | bytes 131104 | tf_op jit(solution)/shard_map/ppermute | solution.py:10
  43.6 0.0 collective-permute-start.14
  43.6 4.3 %collective-permute-done.15 = bf16[256,256]{1,0:T(8,128)(2,1)S(1)} collective-permute-done((bf16[256,256]{1,0:T(8,128)(2,1)S(1)}, bf16[256,256]{1,0:T(8,128)(2,1)S(1)}, u32[]{:S(2)}, u32[]{:S(2)}) %collective-permute-start.15) | collective-permute-done | bytes 131104 | tf_op jit(solution)/shard_map/ppermute | solution.py:10
  48.0 1.2 %collective-permute-done.16 = bf16[256,256]{1,0:T(8,128)(2,1)S(1)} collective-permute-done((bf16[256,256]{1,0:T(8,128)(2,1)S(1)}, bf16[256,256]{1,0:T(8,128)(2,1)S(1)}, u32[]{:S(2)}, u32[]{:S(2)}) %collective-permute-start.16) | collective-permute-done | bytes 131104 | tf_op jit(solution)/shard_map/ppermute | solution.py:10
  49.3 0.3 broadcast_in_dim.34
  49.6 0.4 fusion.1
  50.0 1.6 %collective-permute-start.18 = (bf16[256,256]{1,0:T(8,128)(2,1)S(1)}, bf16[256,256]{1,0:T(8,128)(2,1)S(1)}, u32[]{:S(2)}, u32[]{:S(2)}) collective-permute-start(bf16[256,256]{1,0:T(8,128)(2,1)S(1)} %fusion.1), channel_id=1, source_target_pairs={{0,8},{8,0},{16,24},{24,16},{1,9},{9,1},{17,25},{25,17},{2,10},{10... | collective-permute-start | bytes 393224 | tf_op jit(solution)/shard_map/ppermute | solution.py:10
  51.6 1.5 %collective-permute-start.20 = (bf16[256,256]{1,0:T(8,128)(2,1)S(1)}, bf16[256,256]{1,0:T(8,128)(2,1)S(1)}, u32[]{:S(2)}, u32[]{:S(2)}) collective-permute-start(bf16[256,256]{1,0:T(8,128)(2,1)S(1)} %fusion.1), channel_id=1, source_target_pairs={{0,16},{8,24},{16,0},{24,8},{1,17},{9,25},{17,1},{25,9},{2,18},{10... | collective-permute-start | bytes 393224 | tf_op jit(solution)/shard_map/ppermute | solution.py:10
  53.1 0.5 collective-permute-start.21
  53.7 2.3 %collective-permute-done.18 = bf16[256,256]{1,0:T(8,128)(2,1)S(1)} collective-permute-done((bf16[256,256]{1,0:T(8,128)(2,1)S(1)}, bf16[256,256]{1,0:T(8,128)(2,1)S(1)}, u32[]{:S(2)}, u32[]{:S(2)}) %collective-permute-start.18) | collective-permute-done | bytes 131104 | tf_op jit(solution)/shard_map/ppermute | solution.py:10
  56.0 3.7 %collective-permute-done.20 = bf16[256,256]{1,0:T(8,128)(2,1)S(1)} collective-permute-done((bf16[256,256]{1,0:T(8,128)(2,1)S(1)}, bf16[256,256]{1,0:T(8,128)(2,1)S(1)}, u32[]{:S(2)}, u32[]{:S(2)}) %collective-permute-start.20) | collective-permute-done | bytes 131104 | tf_op jit(solution)/shard_map/ppermute | solution.py:10
  59.7 1.1 %pad_maximum_fusion.1 = bf16[4,512,256]{2,1,0:T(8,128)(2,1)} fusion(bf16[1,512,256]{2,1,0:T(8,128)(2,1)S(1)} %maximum_bitcast_fusion.3, bf16[1,512,256]{2,1,0:T(8,128)(2,1)S(1)} %maximum_bitcast_fusion.2, bf16[1,512,256]{2,1,0:T(8,128)(2,1)S(1)} %maximum_bitcast_fusion.1, bf16[1,512,256]{2,1,0:T(8,128)(2,1)S(1)} %maximum_bitcast_fusion), kind=kLoop, calls=%fused_computation.7 | loop fusion | flops 1572864 | bytes 2097152 | tf_op jit(solution)/shard_map/stack | solution.py:37
  60.9 1.8 %gather_fusion.1 = bf16[8,256,256]{2,1,0:T(8,128)(2,1)S(1)} fusion(bf16[8,256,256]{2,1,0:T(8,128)(2,1)} %bitcast.51, s32[1024]{0:T(1024)S(1)} %pad_clamp_fusion), kind=kCustom, calls=%fused_computation.1.clone | custom fusion | bytes 2097184 | tf_op jit(solution)/shard_map/jit(_take)/gather | solution.py:38
  62.7 0.2 broadcast_select_fusion.1
  62.9 0.4 fusion.6
  63.3 0.4 fusion.7
  63.8 0.6 broadcast_in_dim.28
  64.4 0.9 %bitcast_multiply_fusion = f32[512,256]{1,0:T(8,128)} fusion(f32[64,8,2,128]{3,2,1,0:T(2,128)S(1)} %bitcast.53, f32[256,256]{1,0:T(8,128)S(1)} %fusion.7, f32[256,256]{1,0:T(8,128)S(1)} %fusion.6, bf16[512,256]{1,0:T(8,128)(2,1)S(1)} %bitcast_multiply_fusion.1), kind=kLoop, calls=%fused_computation.10 | loop fusion | flops 786432 | bytes 1835008 | tf_op jit(solution)/shard_map/mul | solution.py:84
  (31 shorter events, 0.4 us)
Async XLA Ops:
  0.8 0.9 %copy-start = (bf16[512,256]{1,0:T(8,128)(2,1)S(1)}, bf16[512,256]{1,0:T(8,128)(2,1)}, u32[]{:S(2)}) copy-start(bf16[512,256]{1,0:T(8,128)(2,1)} %param.4) | copy-start | bytes 786436
  1.8 16.1 %collective-permute-start = (bf16[512,256]{1,0:T(8,128)(2,1)S(1)}, bf16[512,256]{1,0:T(8,128)(2,1)S(1)}, u32[]{:S(2)}, u32[]{:S(2)}) collective-permute-start(bf16[512,256]{1,0:T(8,128)(2,1)S(1)} %bitcast_multiply_fusion.1), channel_id=1, source_target_pairs={{0,8},{8,0},{16,24},{24,16},{1,9},{9,1},{17,25},{25,17},{2,10},{10... | collective-permute-start | bytes 786440 | tf_op jit(solution)/shard_map/ppermute | solution.py:10
  3.3 9.7 %collective-permute-start.4 = (bf16[256,256]{1,0:T(8,128)(2,1)S(1)}, bf16[256,256]{1,0:T(8,128)(2,1)}, u32[]{:S(2)}, u32[]{:S(2)}) collective-permute-start(bf16[256,256]{1,0:T(8,128)(2,1)S(1)} %get-tuple-element.14), channel_id=1, source_target_pairs={{0,4},{1,5},{2,6},{3,7},{4,0},{5,1},{6,2},{7,3},{8,12},{9,13},{10,... | collective-permute-start | bytes 393224 | tf_op jit(solution)/shard_map/ppermute | solution.py:10
  3.7 14.1 %collective-permute-start.6 = (bf16[256,256]{1,0:T(8,128)(2,1)S(1)}, bf16[256,256]{1,0:T(8,128)(2,1)}, u32[]{:S(2)}, u32[]{:S(2)}) collective-permute-start(bf16[256,256]{1,0:T(8,128)(2,1)S(1)} %get-tuple-element.14), channel_id=1, source_target_pairs={{0,6},{1,7},{2,4},{3,5},{4,2},{5,3},{6,0},{7,1},{8,14},{9,15},{10,... | collective-permute-start | bytes 393224 | tf_op jit(solution)/shard_map/ppermute | solution.py:10
  6.4 12.8 %collective-permute-start.8 = (bf16[512,256]{1,0:T(8,128)(2,1)S(1)}, bf16[512,256]{1,0:T(8,128)(2,1)S(1)}, u32[]{:S(2)}, u32[]{:S(2)}) collective-permute-start(bf16[512,256]{1,0:T(8,128)(2,1)S(1)} %bitcast_multiply_fusion.1), channel_id=1, source_target_pairs={{0,16},{8,24},{16,0},{24,8},{1,17},{9,25},{17,1},{25,9},{2,18},{10... | collective-permute-start | bytes 786440 | tf_op jit(solution)/shard_map/ppermute | solution.py:10
  8.0 12.7 %collective-permute-start.9 = (bf16[512,256]{1,0:T(8,128)(2,1)S(1)}, bf16[512,256]{1,0:T(8,128)(2,1)S(1)}, u32[]{:S(2)}, u32[]{:S(2)}) collective-permute-start(bf16[512,256]{1,0:T(8,128)(2,1)S(1)} %bitcast_multiply_fusion.1), channel_id=1, source_target_pairs={{0,24},{8,16},{16,8},{24,0},{1,25},{9,17},{17,9},{25,1},{2,26},{10... | collective-permute-start | bytes 786440 | tf_op jit(solution)/shard_map/ppermute | solution.py:10
  13.0 14.5 %collective-permute-start.5 = (bf16[256,256]{1,0:T(8,128)(2,1)}, bf16[256,256]{1,0:T(8,128)(2,1)}, u32[]{:S(2)}, u32[]{:S(2)}) collective-permute-start(bf16[256,256]{1,0:T(8,128)(2,1)} %collective-permute-done.4), channel_id=1, source_target_pairs={{0,1},{1,0},{2,3},{3,2},{4,5},{5,4},{6,7},{7,6},{8,9},{9,8},{10,11... | collective-permute-start | bytes 393224 | tf_op jit(solution)/shard_map/ppermute | solution.py:10
  17.8 11.6 %collective-permute-start.7 = (bf16[256,256]{1,0:T(8,128)(2,1)}, bf16[256,256]{1,0:T(8,128)(2,1)}, u32[]{:S(2)}, u32[]{:S(2)}) collective-permute-start(bf16[256,256]{1,0:T(8,128)(2,1)} %collective-permute-done.6), channel_id=1, source_target_pairs={{0,1},{1,0},{2,3},{3,2},{4,5},{5,4},{6,7},{7,6},{8,9},{9,8},{10,11... | collective-permute-start | bytes 393224 | tf_op jit(solution)/shard_map/ppermute | solution.py:10
  18.5 6.2 %collective-permute-start.1 = (bf16[256,256]{1,0:T(8,128)(2,1)}, bf16[256,256]{1,0:T(8,128)(2,1)}, u32[]{:S(2)}, u32[]{:S(2)}) collective-permute-start(bf16[256,256]{1,0:T(8,128)(2,1)} %slice.38), channel_id=1, source_target_pairs={{0,1},{1,0},{2,3},{3,2},{4,5},{5,4},{6,7},{7,6},{8,9},{9,8},{10,11... | collective-permute-start | bytes 393224 | tf_op jit(solution)/shard_map/ppermute | solution.py:10
  19.3 5.4 %collective-permute-start.2 = (bf16[256,256]{1,0:T(8,128)(2,1)}, bf16[256,256]{1,0:T(8,128)(2,1)}, u32[]{:S(2)}, u32[]{:S(2)}) collective-permute-start(bf16[256,256]{1,0:T(8,128)(2,1)} %slice.38), channel_id=1, source_target_pairs={{0,2},{1,3},{2,0},{3,1},{4,6},{5,7},{6,4},{7,5},{8,10},{9,11},{10,... | collective-permute-start | bytes 393224 | tf_op jit(solution)/shard_map/ppermute | solution.py:10
  24.7 1.8 %collective-permute-start.3 = (bf16[256,256]{1,0:T(8,128)(2,1)}, bf16[256,256]{1,0:T(8,128)(2,1)S(1)}, u32[]{:S(2)}, u32[]{:S(2)}) collective-permute-start(bf16[256,256]{1,0:T(8,128)(2,1)} %collective-permute-done.2), channel_id=1, source_target_pairs={{0,1},{1,0},{2,3},{3,2},{4,5},{5,4},{6,7},{7,6},{8,9},{9,8},{10,11... | collective-permute-start | bytes 393224 | tf_op jit(solution)/shard_map/ppermute | solution.py:10
  30.3 0.7 %copy-start.1 = (f32[2,2]{1,0:T(2,128)S(1)}, f32[2,2]{1,0:T(2,128)}, u32[]{:S(2)}) copy-start(f32[2,2]{1,0:T(2,128)} %get-tuple-element.20) | copy-start | bytes 52
  31.8 6.0 %collective-permute-start.17 = (bf16[1,256,256]{2,1,0:T(8,128)(2,1)S(1)}, bf16[1,256,256]{2,1,0:T(8,128)(2,1)S(1)}, u32[]{:S(2)}, u32[]{:S(2)}) collective-permute-start(bf16[1,256,256]{2,1,0:T(8,128)(2,1)S(1)} %bitcast.54), channel_id=1, source_target_pairs={{0,8},{8,0},{16,24},{24,16},{1,9},{9,1},{17,25},{25,17},{2,10},{10... | collective-permute-start | bytes 393224 | tf_op jit(solution)/shard_map/ppermute | solution.py:10
  32.4 15.5 %collective-permute-start.10 = (bf16[256,256]{1,0:T(8,128)(2,1)S(1)}, bf16[256,256]{1,0:T(8,128)(2,1)S(1)}, u32[]{:S(2)}, u32[]{:S(2)}) collective-permute-start(bf16[256,256]{1,0:T(8,128)(2,1)S(1)} %get-tuple-element.9), channel_id=1, source_target_pairs={{0,1},{1,0},{2,3},{3,2},{4,5},{5,4},{6,7},{7,6},{8,9},{9,8},{10,11... | collective-permute-start | bytes 393224 | tf_op jit(solution)/shard_map/ppermute | solution.py:10
  32.6 6.8 %collective-permute-start.11 = (bf16[256,256]{1,0:T(8,128)(2,1)S(1)}, bf16[256,256]{1,0:T(8,128)(2,1)S(1)}, u32[]{:S(2)}, u32[]{:S(2)}) collective-permute-start(bf16[256,256]{1,0:T(8,128)(2,1)S(1)} %get-tuple-element.9), channel_id=1, source_target_pairs={{0,2},{1,3},{2,0},{3,1},{4,6},{5,7},{6,4},{7,5},{8,10},{9,11},{10,... | collective-permute-start | bytes 393224 | tf_op jit(solution)/shard_map/ppermute | solution.py:10
  33.8 9.8 %collective-permute-start.13 = (bf16[256,256]{1,0:T(8,128)(2,1)S(1)}, bf16[256,256]{1,0:T(8,128)(2,1)S(1)}, u32[]{:S(2)}, u32[]{:S(2)}) collective-permute-start(bf16[256,256]{1,0:T(8,128)(2,1)S(1)} %get-tuple-element.9), channel_id=1, source_target_pairs={{0,4},{1,5},{2,6},{3,7},{4,0},{5,1},{6,2},{7,3},{8,12},{9,13},{10,... | collective-permute-start | bytes 393224 | tf_op jit(solution)/shard_map/ppermute | solution.py:10
  34.2 13.7 %collective-permute-start.15 = (bf16[256,256]{1,0:T(8,128)(2,1)S(1)}, bf16[256,256]{1,0:T(8,128)(2,1)S(1)}, u32[]{:S(2)}, u32[]{:S(2)}) collective-permute-start(bf16[256,256]{1,0:T(8,128)(2,1)S(1)} %get-tuple-element.9), channel_id=1, source_target_pairs={{0,6},{1,7},{2,4},{3,5},{4,2},{5,3},{6,0},{7,1},{8,14},{9,15},{10,... | collective-permute-start | bytes 393224 | tf_op jit(solution)/shard_map/ppermute | solution.py:10
  37.8 15.9 %collective-permute-start.19 = (bf16[2,256,256]{2,1,0:T(8,128)(2,1)S(1)}, bf16[2,256,256]{2,1,0:T(8,128)(2,1)S(1)}, u32[]{:S(2)}, u32[]{:S(2)}) collective-permute-start(bf16[2,256,256]{2,1,0:T(8,128)(2,1)S(1)} %pad_maximum_fusion.2), channel_id=1, source_target_pairs={{0,16},{8,24},{16,0},{24,8},{1,17},{9,25},{17,1},{25,9},{2,18},{10... | collective-permute-start | bytes 786440 | tf_op jit(solution)/shard_map/ppermute | solution.py:10
  39.3 8.6 %collective-permute-start.12 = (bf16[256,256]{1,0:T(8,128)(2,1)S(1)}, bf16[256,256]{1,0:T(8,128)(2,1)S(1)}, u32[]{:S(2)}, u32[]{:S(2)}) collective-permute-start(bf16[256,256]{1,0:T(8,128)(2,1)S(1)} %collective-permute-done.11), channel_id=1, source_target_pairs={{0,1},{1,0},{2,3},{3,2},{4,5},{5,4},{6,7},{7,6},{8,9},{9,8},{10,11... | collective-permute-start | bytes 393224 | tf_op jit(solution)/shard_map/ppermute | solution.py:10
  43.6 4.4 %collective-permute-start.14 = (bf16[256,256]{1,0:T(8,128)(2,1)S(1)}, bf16[256,256]{1,0:T(8,128)(2,1)S(1)}, u32[]{:S(2)}, u32[]{:S(2)}) collective-permute-start(bf16[256,256]{1,0:T(8,128)(2,1)S(1)} %collective-permute-done.13), channel_id=1, source_target_pairs={{0,1},{1,0},{2,3},{3,2},{4,5},{5,4},{6,7},{7,6},{8,9},{9,8},{10,11... | collective-permute-start | bytes 393224 | tf_op jit(solution)/shard_map/ppermute | solution.py:10
  47.9 1.3 %collective-permute-start.16 = (bf16[256,256]{1,0:T(8,128)(2,1)S(1)}, bf16[256,256]{1,0:T(8,128)(2,1)S(1)}, u32[]{:S(2)}, u32[]{:S(2)}) collective-permute-start(bf16[256,256]{1,0:T(8,128)(2,1)S(1)} %collective-permute-done.15), channel_id=1, source_target_pairs={{0,1},{1,0},{2,3},{3,2},{4,5},{5,4},{6,7},{7,6},{8,9},{9,8},{10,11... | collective-permute-start | bytes 393224 | tf_op jit(solution)/shard_map/ppermute | solution.py:10
  50.0 6.0 %collective-permute-start.18 = (bf16[256,256]{1,0:T(8,128)(2,1)S(1)}, bf16[256,256]{1,0:T(8,128)(2,1)S(1)}, u32[]{:S(2)}, u32[]{:S(2)}) collective-permute-start(bf16[256,256]{1,0:T(8,128)(2,1)S(1)} %fusion.1), channel_id=1, source_target_pairs={{0,8},{8,0},{16,24},{24,16},{1,9},{9,1},{17,25},{25,17},{2,10},{10... | collective-permute-start | bytes 393224 | tf_op jit(solution)/shard_map/ppermute | solution.py:10
  51.6 8.1 %collective-permute-start.20 = (bf16[256,256]{1,0:T(8,128)(2,1)S(1)}, bf16[256,256]{1,0:T(8,128)(2,1)S(1)}, u32[]{:S(2)}, u32[]{:S(2)}) collective-permute-start(bf16[256,256]{1,0:T(8,128)(2,1)S(1)} %fusion.1), channel_id=1, source_target_pairs={{0,16},{8,24},{16,0},{24,8},{1,17},{9,25},{17,1},{25,9},{2,18},{10... | collective-permute-start | bytes 393224 | tf_op jit(solution)/shard_map/ppermute | solution.py:10
  53.1 6.6 %collective-permute-start.21 = (bf16[256,256]{1,0:T(8,128)(2,1)S(1)}, bf16[256,256]{1,0:T(8,128)(2,1)S(1)}, u32[]{:S(2)}, u32[]{:S(2)}) collective-permute-start(bf16[256,256]{1,0:T(8,128)(2,1)S(1)} %fusion.1), channel_id=1, source_target_pairs={{0,24},{8,16},{16,8},{24,0},{1,25},{9,17},{17,9},{25,1},{2,26},{10... | collective-permute-start | bytes 393224 | tf_op jit(solution)/shard_map/ppermute | solution.py:10

commit v9 on v7

--- a/solution.py
+++ b/solution.py
@@ -26,9 +26,10 @@
         local_mask = jnp.repeat(jnp.repeat(local_blocks, B, axis=0), B, axis=1)
         masked = matrix_in * local_mask.astype(jnp.bfloat16)
 
-        col_pieces = [masked] + [_swap(masked, "row", n_row, j) for j in range(1, n_row)]
+        first = _swap(masked, "row", n_row, 1)
+        late, _ = lax.optimization_barrier((masked, first))
+        col_pieces = [masked, first] + [_swap(late, "row", n_row, j) for j in range(2, n_row)]
 
-        late, _ = lax.optimization_barrier((masked, col_pieces[1]))
         row_pieces = [None] * n_col
         row_pieces[0] = masked
         row_pieces[1] = _swap(late, "col", n_col, 1)

time: 53.9 us -> 55.9 us (1.037)
  local copies, waits for them, and re-layouts: 4.07 us -> 7.27 us
  waiting for transfers between devices: 31.8 us -> 29.6 us
  starting transfers between devices: 12.2 us -> 13.2 us
    unnamed x12, local copies, waits for them, and re-layouts: 1.58 us -> 4.78 us
    ppermute x13, waiting for transfers between devices: 31.8 us -> 29.6 us  [_swap(): return lax.ppermute(x, axis, [(i, i ^ d) for i in range(size)])]
    ppermute x13, starting transfers between devices: 12.2 us -> 13.2 us  [_swap(): return lax.ppermute(x, axis, [(i, i ^ d) for i in range(size)])]
  transfers between devices with their start and end apart: 13 -> 13, of which waited for: 7 -> 5; matrix products, arithmetic and copies ran while one was open for 2% -> 5% of each run, Pallas kernels for 0% -> 0%
where the time goes in v9:
time: 55.9 us; the launch traced here: 55.6 us
  waiting for transfers between devices  29.6 us (53%)
  starting transfers between devices  13.2 us (24%)
  local copies, waits for them, and re-layouts  7.27 us (13%)
  other arithmetic  3.17 us (6%)
  matrix products  2.22 us (4%)
    ppermute x13, waiting for transfers between devices, _swap(): return lax.ppermute(x, axis, [(i, i ^ d) for i in range(size)])  29.6 us
    ppermute x13, starting transfers between devices, _swap(): return lax.ppermute(x, axis, [(i, i ^ d) for i in range(size)])  13.2 us
    unnamed x12, local copies, waits for them, and re-layouts  4.78 us
    unnamed x1, other arithmetic  1.79 us
    dot_general x1, matrix products, body(): cubic = jnp.dot(row_cat, f_slot, preferred_element_type=jnp.float32)  1.51 us
    broadcast_in_dim x4, local copies, waits for them, and re-layouts, body(): local_mask = jnp.repeat(jnp.repeat(local_blocks, B, axis=0), B, axis=1)  1.24 us
    gather x2, local copies, waits for them, and re-layouts, in_slot_order(): return jnp.take(stacked, sub_index, axis=0).reshape(n_col * cols, cols)  1.23 us
  transfers between devices with their start and end apart: 13, of which 5 were waited for; matrix products, arithmetic and copies ran while one was open for 5% of the time, Pallas kernels for 0%

profile of v9, /device:TPU:16, one launch (start us, length us, event | category | flops | bytes accessed | tf_op | source)
XLA Modules:
  0.0 55.6 jit_solution(10541232721292990730)
XLA Ops:
  0.0 0.8 %dynamic-slice_convert_fusion.1 = (f32[4,2]{1,0:T(4,128)S(1)}, bf16[4,2]{1,0:T(4,128)(2,1)S(1)}) fusion(s32[16,16]{1,0:T(8,128)} %param.5, s32[]{:T(128)S(6)} %select_n.24, s32[]{:T(128)S(6)} %select_n.25), kind=kLoop, calls=%fused_computation.26 | loop fusion | flops 16 | bytes 88 | tf_op jit(solution)/shard_map/convert_element_type | solution.py:50
  0.8 0.6 %broadcast_in_dim.22 = bf16[512,2,128]{2,1,0:T(2,128)(2,1)S(1)} broadcast(bf16[512,2]{1,0:T(8,128)(2,1)S(1)} %bitcast.33), dimensions={0,1} | broadcast | bytes 264192 | tf_op jit(solution)/shard_map/broadcast_in_dim | solution.py:26
  1.4 1.8 %constant_dynamic-update-slice_fusion.7 = (bf16[512,2048]{1,0:T(8,128)(2,1)}, bf16[512,256]{1,0:T(8,128)(2,1)S(1)}) fusion(bf16[512,256]{1,0:T(8,128)(2,1)} %param.4, bf16[64,8,2,128]{3,2,1,0:T(2,128)(2,1)S(1)} %bitcast.31), kind=kLoop, calls=%fused_computation.19 | loop fusion | flops 524287 | bytes 1048576
  3.2 1.5 %collective-permute-start = (bf16[512,256]{1,0:T(8,128)(2,1)S(1)}, bf16[512,256]{1,0:T(8,128)(2,1)S(1)}, u32[]{:S(2)}, u32[]{:S(2)}) collective-permute-start(bf16[512,256]{1,0:T(8,128)(2,1)S(1)} %get-tuple-element.7), channel_id=1, source_target_pairs={{0,8},{8,0},{16,24},{24,16},{1,9},{9,1},{17,25},{25,17},{2,10},{10... | collective-permute-start | bytes 786440 | tf_op jit(solution)/shard_map/ppermute | solution.py:10
  4.7 0.3 collective-permute-start.4
  5.0 2.7 %collective-permute-start.6 = (bf16[512,256]{1,0:T(8,128)(2,1)S(1)}, bf16[512,256]{1,0:T(8,128)(2,1)S(1)}, u32[]{:S(2)}, u32[]{:S(2)}) collective-permute-start(bf16[512,256]{1,0:T(8,128)(2,1)S(1)} %get-tuple-element.7), channel_id=1, source_target_pairs={{0,6},{1,7},{2,4},{3,5},{4,2},{5,3},{6,0},{7,1},{8,14},{9,15},{10,... | collective-permute-start | bytes 786440 | tf_op jit(solution)/shard_map/ppermute | solution.py:10
  7.7 3.5 %collective-permute-done = bf16[512,256]{1,0:T(8,128)(2,1)S(1)} collective-permute-done((bf16[512,256]{1,0:T(8,128)(2,1)S(1)}, bf16[512,256]{1,0:T(8,128)(2,1)S(1)}, u32[]{:S(2)}, u32[]{:S(2)}) %collective-permute-start) | collective-permute-done | bytes 262176 | tf_op jit(solution)/shard_map/ppermute | solution.py:10
  11.2 1.5 %collective-permute-start.8 = (bf16[512,256]{1,0:T(8,128)(2,1)S(1)}, bf16[512,256]{1,0:T(8,128)(2,1)S(1)}, u32[]{:S(2)}, u32[]{:S(2)}) collective-permute-start(bf16[512,256]{1,0:T(8,128)(2,1)S(1)} %get-tuple-element.7), channel_id=1, source_target_pairs={{0,16},{8,24},{16,0},{24,8},{1,17},{9,25},{17,1},{25,9},{2,18},{10... | collective-permute-start | bytes 786440 | tf_op jit(solution)/shard_map/ppermute | solution.py:10
  12.8 1.4 %collective-permute-start.9 = (bf16[512,256]{1,0:T(8,128)(2,1)S(1)}, bf16[512,256]{1,0:T(8,128)(2,1)S(1)}, u32[]{:S(2)}, u32[]{:S(2)}) collective-permute-start(bf16[512,256]{1,0:T(8,128)(2,1)S(1)} %get-tuple-element.7), channel_id=1, source_target_pairs={{0,24},{8,16},{16,8},{24,0},{1,25},{9,17},{17,9},{25,1},{2,26},{10... | collective-permute-start | bytes 786440 | tf_op jit(solution)/shard_map/ppermute | solution.py:10
  14.2 1.6 %collective-permute-start.2 = (bf16[512,256]{1,0:T(8,128)(2,1)S(1)}, bf16[512,256]{1,0:T(8,128)(2,1)S(1)}, u32[]{:S(2)}, u32[]{:S(2)}) collective-permute-start(bf16[512,256]{1,0:T(8,128)(2,1)S(1)} %get-tuple-element.7), channel_id=1, source_target_pairs={{0,2},{1,3},{2,0},{3,1},{4,6},{5,7},{6,4},{7,5},{8,10},{9,11},{10,... | collective-permute-start | bytes 786440 | tf_op jit(solution)/shard_map/ppermute | solution.py:10
  15.8 6.9 %collective-permute-done.4 = bf16[512,256]{1,0:T(8,128)(2,1)S(1)} collective-permute-done((bf16[512,256]{1,0:T(8,128)(2,1)S(1)}, bf16[512,256]{1,0:T(8,128)(2,1)S(1)}, u32[]{:S(2)}, u32[]{:S(2)}) %collective-permute-start.4) | collective-permute-done | bytes 262176 | tf_op jit(solution)/shard_map/ppermute | solution.py:10
  22.7 0.0 collective-permute-start.1
  22.7 7.5 %collective-permute-done.6 = bf16[512,256]{1,0:T(8,128)(2,1)S(1)} collective-permute-done((bf16[512,256]{1,0:T(8,128)(2,1)S(1)}, bf16[512,256]{1,0:T(8,128)(2,1)S(1)}, u32[]{:S(2)}, u32[]{:S(2)}) %collective-permute-start.6) | collective-permute-done | bytes 262176 | tf_op jit(solution)/shard_map/ppermute | solution.py:10
  30.2 0.0 collective-permute-start.5
  30.3 0.0 collective-permute-done.8
  30.3 0.5 collective-permute-start.7
  30.8 0.0 collective-permute-done.9
  30.8 0.1 pad_maximum_fusion
  30.9 0.6 %gather_fusion = bf16[8,256,256]{2,1,0:T(8,128)(2,1)S(1)} fusion(bf16[8,256,256]{2,1,0:T(8,128)(2,1)S(1)} %bitcast.27, s32[1024]{0:T(1024)S(1)} %pad_clamp_fusion), kind=kCustom, calls=%fused_computation.clone | custom fusion | bytes 2097184 | tf_op jit(solution)/shard_map/jit(_take)/gather | solution.py:46
  31.5 0.0 copy-start
  31.5 0.0 collective-permute-done.2
  31.5 0.1 collective-permute-start.3
  31.6 0.2 broadcast_select_fusion
  31.8 0.0 collective-permute-done.1
  31.8 1.3 %copy-done = bf16[512,2048]{1,0:T(8,128)(2,1)S(1)} copy-done((bf16[512,2048]{1,0:T(8,128)(2,1)S(1)}, bf16[512,2048]{1,0:T(8,128)(2,1)}, u32[]{:S(2)}) %copy-start) | copy-done | bytes 2097176
  33.1 1.0 %constant_dynamic-update-slice_fusion.6 = bf16[512,2048]{1,0:T(8,128)(2,1)S(1)} fusion(bf16[512,2048]{1,0:T(8,128)(2,1)S(1)} %copy-done, bf16[512,256]{1,0:T(8,128)(2,1)} %collective-permute-done.1), kind=kLoop, calls=%fused_computation.18 | loop fusion | bytes 524288
  34.1 0.0 collective-permute-done.3
  34.2 0.0 collective-permute-done.5
  34.2 1.0 %constant_dynamic-update-slice_fusion.2 = bf16[512,2048]{1,0:T(8,128)(2,1)S(1)} fusion(bf16[512,2048]{1,0:T(8,128)(2,1)S(1)} %constant_dynamic-update-slice_fusion.3, bf16[512,256]{1,0:T(8,128)(2,1)} %collective-permute-done.5), kind=kLoop, calls=%fused_computation.14 | loop fusion | bytes 524288
  35.2 0.0 collective-permute-done.7
  35.3 0.0 copy-start.1
  35.3 0.6 %broadcast_in_dim.20 = f32[512,2,128]{2,1,0:T(2,128)S(1)} broadcast(f32[512,2]{1,0:T(8,128)S(1)} %bitcast.30), dimensions={0,1} | broadcast | bytes 528384 | tf_op jit(solution)/shard_map/broadcast_in_dim | solution.py:26
  35.9 0.7 %fusion.2 = bf16[512,256]{1,0:T(8,128)(2,1)S(1)} fusion(bf16[512,2048]{1,0:T(8,128)(2,1)S(1)} %constant_dynamic-update-slice_fusion, bf16[2048,256]{1,0:T(8,128)(2,1)S(1)} %bitcast.28, f32[64,8,2,128]{3,2,1,0:T(2,128)S(1)} %bitcast.34), kind=kOutput, calls=%fused_computation.6 | convolution fusion | flops 537133056 | bytes 3932160 | tf_op jit(solution)/shard_map/dot_general | solution.py:49
  36.6 0.0 copy-done.1
  36.6 1.6 %collective-permute-start.11 = (bf16[512,256]{1,0:T(8,128)(2,1)S(1)}, bf16[512,256]{1,0:T(8,128)(2,1)S(1)}, u32[]{:S(2)}, u32[]{:S(2)}) collective-permute-start(bf16[512,256]{1,0:T(8,128)(2,1)S(1)} %fusion.2), channel_id=1, source_target_pairs={{0,16},{8,24},{16,0},{24,8},{1,17},{9,25},{17,1},{25,9},{2,18},{10... | collective-permute-start | bytes 786440 | tf_op jit(solution)/shard_map/ppermute | solution.py:10
  38.2 0.5 collective-permute-start.12
  38.7 1.5 %collective-permute-start.10 = (bf16[512,256]{1,0:T(8,128)(2,1)S(1)}, bf16[512,256]{1,0:T(8,128)(2,1)S(1)}, u32[]{:S(2)}, u32[]{:S(2)}) collective-permute-start(bf16[512,256]{1,0:T(8,128)(2,1)S(1)} %fusion.2), channel_id=1, source_target_pairs={{0,8},{8,0},{16,24},{24,16},{1,9},{9,1},{17,25},{25,17},{2,10},{10... | collective-permute-start | bytes 786440 | tf_op jit(solution)/shard_map/ppermute | solution.py:10
  40.2 10.4 %collective-permute-done.11 = bf16[512,256]{1,0:T(8,128)(2,1)S(1)} collective-permute-done((bf16[512,256]{1,0:T(8,128)(2,1)S(1)}, bf16[512,256]{1,0:T(8,128)(2,1)S(1)}, u32[]{:S(2)}, u32[]{:S(2)}) %collective-permute-start.11) | collective-permute-done | bytes 262176 | tf_op jit(solution)/shard_map/ppermute | solution.py:10
  50.5 0.0 collective-permute-done.12
  50.6 1.2 %collective-permute-done.10 = bf16[512,256]{1,0:T(8,128)(2,1)S(1)} collective-permute-done((bf16[512,256]{1,0:T(8,128)(2,1)S(1)}, bf16[512,256]{1,0:T(8,128)(2,1)S(1)}, u32[]{:S(2)}, u32[]{:S(2)}) %collective-permute-start.10) | collective-permute-done | bytes 262176 | tf_op jit(solution)/shard_map/ppermute | solution.py:10
  51.8 0.1 pad_maximum_fusion.1
  51.9 0.6 %gather_fusion.1 = bf16[8,256,256]{2,1,0:T(8,128)(2,1)S(1)} fusion(bf16[8,256,256]{2,1,0:T(8,128)(2,1)S(1)} %bitcast.26, s32[1024]{0:T(1024)S(1)} %pad_clamp_fusion), kind=kCustom, calls=%fused_computation.1.clone | custom fusion | bytes 2097184 | tf_op jit(solution)/shard_map/jit(_take)/gather | solution.py:46
  52.5 0.0 copy-start.2
  52.5 0.2 broadcast_select_fusion.1
  52.7 1.4 %copy-done.2 = bf16[512,2048]{1,0:T(8,128)(2,1)S(1)} copy-done((bf16[512,2048]{1,0:T(8,128)(2,1)S(1)}, bf16[512,2048]{1,0:T(8,128)(2,1)}, u32[]{:S(2)}) %copy-start.2) | copy-done | bytes 2097176
  54.1 1.5 %fusion.1 = f32[512,256]{1,0:T(8,128)} fusion(bf16[512,2048]{1,0:T(8,128)(2,1)S(1)} %copy-done.2, bf16[2048,256]{1,0:T(8,128)(2,1)S(1)} %bitcast.29, bf16[512,256]{1,0:T(8,128)(2,1)S(1)} %get-tuple-element.7, f32[64,8,2,128]{3,2,1,0:T(2,128)S(1)} %bitcast.35), kind=kOutput, calls=%fused_computation.5 | convolution fusion | flops 537526272 | bytes 4456448 | tf_op jit(solution)/shard_map/dot_general | solution.py:54
  (9 shorter events, 0.2 us)
Async XLA Ops:
  3.2 8.0 %collective-permute-start = (bf16[512,256]{1,0:T(8,128)(2,1)S(1)}, bf16[512,256]{1,0:T(8,128)(2,1)S(1)}, u32[]{:S(2)}, u32[]{:S(2)}) collective-permute-start(bf16[512,256]{1,0:T(8,128)(2,1)S(1)} %get-tuple-element.7), channel_id=1, source_target_pairs={{0,8},{8,0},{16,24},{24,16},{1,9},{9,1},{17,25},{25,17},{2,10},{10... | collective-permute-start | bytes 786440 | tf_op jit(solution)/shard_map/ppermute | solution.py:10
  4.7 18.1 %collective-permute-start.4 = (bf16[512,256]{1,0:T(8,128)(2,1)S(1)}, bf16[512,256]{1,0:T(8,128)(2,1)S(1)}, u32[]{:S(2)}, u32[]{:S(2)}) collective-permute-start(bf16[512,256]{1,0:T(8,128)(2,1)S(1)} %get-tuple-element.7), channel_id=1, source_target_pairs={{0,4},{1,5},{2,6},{3,7},{4,0},{5,1},{6,2},{7,3},{8,12},{9,13},{10,... | collective-permute-start | bytes 786440 | tf_op jit(solution)/shard_map/ppermute | solution.py:10
  5.0 25.2 %collective-permute-start.6 = (bf16[512,256]{1,0:T(8,128)(2,1)S(1)}, bf16[512,256]{1,0:T(8,128)(2,1)S(1)}, u32[]{:S(2)}, u32[]{:S(2)}) collective-permute-start(bf16[512,256]{1,0:T(8,128)(2,1)S(1)} %get-tuple-element.7), channel_id=1, source_target_pairs={{0,6},{1,7},{2,4},{3,5},{4,2},{5,3},{6,0},{7,1},{8,14},{9,15},{10,... | collective-permute-start | bytes 786440 | tf_op jit(solution)/shard_map/ppermute | solution.py:10
  11.2 19.0 %collective-permute-start.8 = (bf16[512,256]{1,0:T(8,128)(2,1)S(1)}, bf16[512,256]{1,0:T(8,128)(2,1)S(1)}, u32[]{:S(2)}, u32[]{:S(2)}) collective-permute-start(bf16[512,256]{1,0:T(8,128)(2,1)S(1)} %get-tuple-element.7), channel_id=1, source_target_pairs={{0,16},{8,24},{16,0},{24,8},{1,17},{9,25},{17,1},{25,9},{2,18},{10... | collective-permute-start | bytes 786440 | tf_op jit(solution)/shard_map/ppermute | solution.py:10
  12.8 18.0 %collective-permute-start.9 = (bf16[512,256]{1,0:T(8,128)(2,1)S(1)}, bf16[512,256]{1,0:T(8,128)(2,1)S(1)}, u32[]{:S(2)}, u32[]{:S(2)}) collective-permute-start(bf16[512,256]{1,0:T(8,128)(2,1)S(1)} %get-tuple-element.7), channel_id=1, source_target_pairs={{0,24},{8,16},{16,8},{24,0},{1,25},{9,17},{17,9},{25,1},{2,26},{10... | collective-permute-start | bytes 786440 | tf_op jit(solution)/shard_map/ppermute | solution.py:10
  14.2 17.3 %collective-permute-start.2 = (bf16[512,256]{1,0:T(8,128)(2,1)S(1)}, bf16[512,256]{1,0:T(8,128)(2,1)S(1)}, u32[]{:S(2)}, u32[]{:S(2)}) collective-permute-start(bf16[512,256]{1,0:T(8,128)(2,1)S(1)} %get-tuple-element.7), channel_id=1, source_target_pairs={{0,2},{1,3},{2,0},{3,1},{4,6},{5,7},{6,4},{7,5},{8,10},{9,11},{10,... | collective-permute-start | bytes 786440 | tf_op jit(solution)/shard_map/ppermute | solution.py:10
  22.7 9.0 %collective-permute-start.1 = (bf16[512,256]{1,0:T(8,128)(2,1)S(1)}, bf16[512,256]{1,0:T(8,128)(2,1)}, u32[]{:S(2)}, u32[]{:S(2)}) collective-permute-start(bf16[512,256]{1,0:T(8,128)(2,1)S(1)} %get-tuple-element.7), channel_id=1, source_target_pairs={{0,1},{1,0},{2,3},{3,2},{4,5},{5,4},{6,7},{7,6},{8,9},{9,8},{10,11... | collective-permute-start | bytes 786440 | tf_op jit(solution)/shard_map/ppermute | solution.py:10
  30.2 4.0 %collective-permute-start.5 = (bf16[512,256]{1,0:T(8,128)(2,1)S(1)}, bf16[512,256]{1,0:T(8,128)(2,1)}, u32[]{:S(2)}, u32[]{:S(2)}) collective-permute-start(bf16[512,256]{1,0:T(8,128)(2,1)S(1)} %collective-permute-done.4), channel_id=1, source_target_pairs={{0,1},{1,0},{2,3},{3,2},{4,5},{5,4},{6,7},{7,6},{8,9},{9,8},{10,11... | collective-permute-start | bytes 786440 | tf_op jit(solution)/shard_map/ppermute | solution.py:10
  30.3 5.0 %collective-permute-start.7 = (bf16[512,256]{1,0:T(8,128)(2,1)S(1)}, bf16[512,256]{1,0:T(8,128)(2,1)S(1)}, u32[]{:S(2)}, u32[]{:S(2)}) collective-permute-start(bf16[512,256]{1,0:T(8,128)(2,1)S(1)} %collective-permute-done.6), channel_id=1, source_target_pairs={{0,1},{1,0},{2,3},{3,2},{4,5},{5,4},{6,7},{7,6},{8,9},{9,8},{10,11... | collective-permute-start | bytes 786440 | tf_op jit(solution)/shard_map/ppermute | solution.py:10
  31.5 1.6 %copy-start = (bf16[512,2048]{1,0:T(8,128)(2,1)S(1)}, bf16[512,2048]{1,0:T(8,128)(2,1)}, u32[]{:S(2)}) copy-start(bf16[512,2048]{1,0:T(8,128)(2,1)} %get-tuple-element.10) | copy-start | bytes 6291460
  31.5 2.6 %collective-permute-start.3 = (bf16[512,256]{1,0:T(8,128)(2,1)S(1)}, bf16[512,256]{1,0:T(8,128)(2,1)S(1)}, u32[]{:S(2)}, u32[]{:S(2)}) collective-permute-start(bf16[512,256]{1,0:T(8,128)(2,1)S(1)} %collective-permute-done.2), channel_id=1, source_target_pairs={{0,1},{1,0},{2,3},{3,2},{4,5},{5,4},{6,7},{7,6},{8,9},{9,8},{10,11... | collective-permute-start | bytes 786440 | tf_op jit(solution)/shard_map/ppermute | solution.py:10
  35.3 1.4 %copy-start.1 = (bf16[512,2048]{1,0:T(8,128)(2,1)}, bf16[512,2048]{1,0:T(8,128)(2,1)S(1)}, u32[]{:S(2)}) copy-start(bf16[512,2048]{1,0:T(8,128)(2,1)S(1)} %constant_dynamic-update-slice_fusion) | copy-start | bytes 6291460
  36.6 13.9 %collective-permute-start.11 = (bf16[512,256]{1,0:T(8,128)(2,1)S(1)}, bf16[512,256]{1,0:T(8,128)(2,1)S(1)}, u32[]{:S(2)}, u32[]{:S(2)}) collective-permute-start(bf16[512,256]{1,0:T(8,128)(2,1)S(1)} %fusion.2), channel_id=1, source_target_pairs={{0,16},{8,24},{16,0},{24,8},{1,17},{9,25},{17,1},{25,9},{2,18},{10... | collective-permute-start | bytes 786440 | tf_op jit(solution)/shard_map/ppermute | solution.py:10
  38.2 12.3 %collective-permute-start.12 = (bf16[512,256]{1,0:T(8,128)(2,1)S(1)}, bf16[512,256]{1,0:T(8,128)(2,1)S(1)}, u32[]{:S(2)}, u32[]{:S(2)}) collective-permute-start(bf16[512,256]{1,0:T(8,128)(2,1)S(1)} %fusion.2), channel_id=1, source_target_pairs={{0,24},{8,16},{16,8},{24,0},{1,25},{9,17},{17,9},{25,1},{2,26},{10... | collective-permute-start | bytes 786440 | tf_op jit(solution)/shard_map/ppermute | solution.py:10
  38.7 13.1 %collective-permute-start.10 = (bf16[512,256]{1,0:T(8,128)(2,1)S(1)}, bf16[512,256]{1,0:T(8,128)(2,1)S(1)}, u32[]{:S(2)}, u32[]{:S(2)}) collective-permute-start(bf16[512,256]{1,0:T(8,128)(2,1)S(1)} %fusion.2), channel_id=1, source_target_pairs={{0,8},{8,0},{16,24},{24,16},{1,9},{9,1},{17,25},{25,17},{2,10},{10... | collective-permute-start | bytes 786440 | tf_op jit(solution)/shard_map/ppermute | solution.py:10
  52.5 1.6 %copy-start.2 = (bf16[512,2048]{1,0:T(8,128)(2,1)S(1)}, bf16[512,2048]{1,0:T(8,128)(2,1)}, u32[]{:S(2)}) copy-start(bf16[512,2048]{1,0:T(8,128)(2,1)} %copy-done.1) | copy-start | bytes 6291460

commit v10 on v7

--- a/solution.py
+++ b/solution.py
@@ -26,16 +26,18 @@
         local_mask = jnp.repeat(jnp.repeat(local_blocks, B, axis=0), B, axis=1)
         masked = matrix_in * local_mask.astype(jnp.bfloat16)
 
-        col_pieces = [masked] + [_swap(masked, "row", n_row, j) for j in range(1, n_row)]
-
-        late, _ = lax.optimization_barrier((masked, col_pieces[1]))
         row_pieces = [None] * n_col
         row_pieces[0] = masked
+        for k in range(1, n_z):
+            row_pieces[2 * k] = _swap(masked, "col", n_col, 2 * k)
+        late = masked
+        if n_z > 1:
+            late, _ = lax.optimization_barrier((masked, row_pieces[2]))
         row_pieces[1] = _swap(late, "col", n_col, 1)
         for k in range(1, n_z):
-            piece = _swap(late if k == 1 else masked, "col", n_col, 2 * k)
-            row_pieces[2 * k] = piece
-            row_pieces[2 * k + 1] = _swap(piece, "col", n_col, 1)
+            row_pieces[2 * k + 1] = _swap(row_pieces[2 * k], "col", n_col, 1)
+
+        col_pieces = [masked] + [_swap(late, "row", n_row, j) for j in range(1, n_row)]
 
         slots = jnp.arange(n_col, dtype=jnp.int32) ^ col_index
         sub_index = ((slots // ratio) ^ row_index) * ratio + slots % ratio

time: 53.9 us -> 63.8 us (1.18)
  the two profiles are of different devices: /device:TPU:16 before, /device:TPU:0 now
where the time goes in v10:
time: 63.8 us; the launch traced here: 63.5 us
  waiting for transfers between devices  31.6 us (50%)
  starting transfers between devices  15.4 us (24%)
  local copies, waits for them, and re-layouts  11.6 us (18%)
  other arithmetic  2.4 us (4%)
  matrix products  2.22 us (3%)
    ppermute x13, waiting for transfers between devices, _swap(): return lax.ppermute(x, axis, [(i, i ^ d) for i in range(size)])  31.6 us
    ppermute x13, starting transfers between devices, _swap(): return lax.ppermute(x, axis, [(i, i ^ d) for i in range(size)])  15.4 us
    unnamed x14, local copies, waits for them, and re-layouts  9.15 us
    dot_general x1, matrix products, body(): cubic = jnp.dot(row_cat, f_slot, preferred_element_type=jnp.float32)  1.51 us
  transfers between devices with their start and end apart: 13, of which 6 were waited for; matrix products, arithmetic and copies ran while one was open for 9% of the time, Pallas kernels for 0%

profile of v10, /device:TPU:0, one launch (start us, length us, event | category | flops | bytes accessed | tf_op | source)
XLA Modules:
  0.0 63.5 jit_solution(16368966683800868644)
XLA Ops:
  0.0 0.8 %dynamic-slice_convert_fusion.1 = (f32[4,2]{1,0:T(4,128)S(1)}, bf16[4,2]{1,0:T(4,128)(2,1)S(1)}) fusion(s32[16,16]{1,0:T(8,128)} %param.5, s32[]{:T(128)S(6)} %select_n.24, s32[]{:T(128)S(6)} %select_n.25), kind=kLoop, calls=%fused_computation.26 | loop fusion | flops 16 | bytes 88 | tf_op jit(solution)/shard_map/convert_element_type | solution.py:51
  0.8 0.6 broadcast_in_dim.22
  1.4 1.0 %constant_dynamic-update-slice_fusion.7 = (bf16[512,2048]{1,0:T(8,128)(2,1)S(1)}, bf16[512,256]{1,0:T(8,128)(2,1)S(1)}) fusion(bf16[512,256]{1,0:T(8,128)(2,1)} %param.4, bf16[64,8,2,128]{3,2,1,0:T(2,128)(2,1)S(1)} %bitcast.31), kind=kLoop, calls=%fused_computation.19 | loop fusion | flops 524287 | bytes 1048576
  2.4 3.1 %collective-permute-start = (bf16[512,256]{1,0:T(8,128)(2,1)S(1)}, bf16[512,256]{1,0:T(8,128)(2,1)S(1)}, u32[]{:S(2)}, u32[]{:S(2)}) collective-permute-start(bf16[512,256]{1,0:T(8,128)(2,1)S(1)} %get-tuple-element.7), channel_id=1, source_target_pairs={{0,2},{1,3},{2,0},{3,1},{4,6},{5,7},{6,4},{7,5},{8,10},{9,11},{10,... | collective-permute-start | bytes 786440 | tf_op jit(solution)/shard_map/ppermute | solution.py:10
  5.5 2.6 %collective-permute-start.3 = (bf16[512,256]{1,0:T(8,128)(2,1)S(1)}, bf16[512,256]{1,0:T(8,128)(2,1)S(1)}, u32[]{:S(2)}, u32[]{:S(2)}) collective-permute-start(bf16[512,256]{1,0:T(8,128)(2,1)S(1)} %get-tuple-element.7), channel_id=1, source_target_pairs={{0,4},{1,5},{2,6},{3,7},{4,0},{5,1},{6,2},{7,3},{8,12},{9,13},{10,... | collective-permute-start | bytes 786440 | tf_op jit(solution)/shard_map/ppermute | solution.py:10
  8.1 9.2 %collective-permute-done = bf16[512,256]{1,0:T(8,128)(2,1)S(1)} collective-permute-done((bf16[512,256]{1,0:T(8,128)(2,1)S(1)}, bf16[512,256]{1,0:T(8,128)(2,1)S(1)}, u32[]{:S(2)}, u32[]{:S(2)}) %collective-permute-start) | collective-permute-done | bytes 262176 | tf_op jit(solution)/shard_map/ppermute | solution.py:10
  17.3 0.0 collective-permute-start.1
  17.3 2.6 %collective-permute-start.5 = (bf16[512,256]{1,0:T(8,128)(2,1)S(1)}, bf16[512,256]{1,0:T(8,128)(2,1)S(1)}, u32[]{:S(2)}, u32[]{:S(2)}) collective-permute-start(bf16[512,256]{1,0:T(8,128)(2,1)S(1)} %get-tuple-element.7), channel_id=1, source_target_pairs={{0,6},{1,7},{2,4},{3,5},{4,2},{5,3},{6,0},{7,1},{8,14},{9,15},{10,... | collective-permute-start | bytes 786440 | tf_op jit(solution)/shard_map/ppermute | solution.py:10
  20.0 1.5 %collective-permute-start.7 = (bf16[512,256]{1,0:T(8,128)(2,1)S(1)}, bf16[512,256]{1,0:T(8,128)(2,1)S(1)}, u32[]{:S(2)}, u32[]{:S(2)}) collective-permute-start(bf16[512,256]{1,0:T(8,128)(2,1)S(1)} %get-tuple-element.7), channel_id=1, source_target_pairs={{0,8},{8,0},{16,24},{24,16},{1,9},{9,1},{17,25},{25,17},{2,10},{10... | collective-permute-start | bytes 786440 | tf_op jit(solution)/shard_map/ppermute | solution.py:10
  21.5 1.5 %collective-permute-start.8 = (bf16[512,256]{1,0:T(8,128)(2,1)S(1)}, bf16[512,256]{1,0:T(8,128)(2,1)S(1)}, u32[]{:S(2)}, u32[]{:S(2)}) collective-permute-start(bf16[512,256]{1,0:T(8,128)(2,1)S(1)} %get-tuple-element.7), channel_id=1, source_target_pairs={{0,16},{8,24},{16,0},{24,8},{1,17},{9,25},{17,1},{25,9},{2,18},{10... | collective-permute-start | bytes 786440 | tf_op jit(solution)/shard_map/ppermute | solution.py:10
  23.0 0.0 collective-permute-done.3
  23.0 0.5 collective-permute-start.9
  23.5 0.0 collective-permute-done.1
  23.5 0.1 collective-permute-start.2
  23.6 4.3 %collective-permute-done.5 = bf16[512,256]{1,0:T(8,128)(2,1)S(1)} collective-permute-done((bf16[512,256]{1,0:T(8,128)(2,1)S(1)}, bf16[512,256]{1,0:T(8,128)(2,1)S(1)}, u32[]{:S(2)}, u32[]{:S(2)}) %collective-permute-start.5) | collective-permute-done | bytes 262176 | tf_op jit(solution)/shard_map/ppermute | solution.py:10
  28.0 0.0 collective-permute-start.4
  28.0 1.2 %collective-permute-done.7 = bf16[512,256]{1,0:T(8,128)(2,1)S(1)} collective-permute-done((bf16[512,256]{1,0:T(8,128)(2,1)S(1)}, bf16[512,256]{1,0:T(8,128)(2,1)S(1)}, u32[]{:S(2)}, u32[]{:S(2)}) %collective-permute-start.7) | collective-permute-done | bytes 262176 | tf_op jit(solution)/shard_map/ppermute | solution.py:10
  29.1 0.0 collective-permute-start.6
  29.1 6.1 %collective-permute-done.8 = bf16[512,256]{1,0:T(8,128)(2,1)S(1)} collective-permute-done((bf16[512,256]{1,0:T(8,128)(2,1)S(1)}, bf16[512,256]{1,0:T(8,128)(2,1)S(1)}, u32[]{:S(2)}, u32[]{:S(2)}) %collective-permute-start.8) | collective-permute-done | bytes 262176 | tf_op jit(solution)/shard_map/ppermute | solution.py:10
  35.2 0.0 collective-permute-done.9
  35.2 0.1 pad_maximum_fusion
  35.4 0.0 copy-start
  35.4 1.3 %copy-done = bf16[512,2048]{1,0:T(8,128)(2,1)} copy-done((bf16[512,2048]{1,0:T(8,128)(2,1)}, bf16[512,2048]{1,0:T(8,128)(2,1)S(1)}, u32[]{:S(2)}) %copy-start) | copy-done | bytes 2097176
  36.8 0.6 gather_fusion
  37.4 0.0 collective-permute-done.2
  37.4 1.7 %constant_dynamic-update-slice_fusion.4 = bf16[512,2048]{1,0:T(8,128)(2,1)} fusion(bf16[512,2048]{1,0:T(8,128)(2,1)} %copy-done, bf16[512,256]{1,0:T(8,128)(2,1)} %collective-permute-done.2), kind=kLoop, calls=%fused_computation.16 | loop fusion | bytes 524288
  39.1 0.8 %constant_dynamic-update-slice_fusion.3 = bf16[512,2048]{1,0:T(8,128)(2,1)} fusion(bf16[512,2048]{1,0:T(8,128)(2,1)} %constant_dynamic-update-slice_fusion.4, bf16[512,256]{1,0:T(8,128)(2,1)S(1)} %collective-permute-done.3), kind=kLoop, calls=%fused_computation.15 | loop fusion | bytes 524288
  39.9 0.0 collective-permute-done.4
  39.9 1.7 %constant_dynamic-update-slice_fusion.2 = bf16[512,2048]{1,0:T(8,128)(2,1)} fusion(bf16[512,2048]{1,0:T(8,128)(2,1)} %constant_dynamic-update-slice_fusion.3, bf16[512,256]{1,0:T(8,128)(2,1)} %collective-permute-done.4), kind=kLoop, calls=%fused_computation.14 | loop fusion | bytes 524288
  41.6 0.7 %constant_dynamic-update-slice_fusion.1 = bf16[512,2048]{1,0:T(8,128)(2,1)} fusion(bf16[512,2048]{1,0:T(8,128)(2,1)} %constant_dynamic-update-slice_fusion.2, bf16[512,256]{1,0:T(8,128)(2,1)S(1)} %collective-permute-done.5), kind=kLoop, calls=%fused_computation.13 | loop fusion | bytes 524288
  42.3 0.0 copy-start.1
  42.3 0.2 broadcast_select_fusion
  42.5 0.0 collective-permute-done.6
  42.5 1.4 %copy-done.1 = bf16[512,2048]{1,0:T(8,128)(2,1)S(1)} copy-done((bf16[512,2048]{1,0:T(8,128)(2,1)S(1)}, bf16[512,2048]{1,0:T(8,128)(2,1)}, u32[]{:S(2)}) %copy-start.1) | copy-done | bytes 2097176
  43.9 0.0 copy-start.2
  44.0 0.6 broadcast_in_dim.20
  44.6 0.7 %fusion.2 = bf16[512,256]{1,0:T(8,128)(2,1)S(1)} fusion(bf16[512,2048]{1,0:T(8,128)(2,1)S(1)} %constant_dynamic-update-slice_fusion, bf16[2048,256]{1,0:T(8,128)(2,1)S(1)} %bitcast.28, f32[64,8,2,128]{3,2,1,0:T(2,128)S(1)} %bitcast.34), kind=kOutput, calls=%fused_computation.6 | convolution fusion | flops 537133056 | bytes 3932160 | tf_op jit(solution)/shard_map/dot_general | solution.py:50
  45.3 1.6 %collective-permute-start.11 = (bf16[512,256]{1,0:T(8,128)(2,1)S(1)}, bf16[512,256]{1,0:T(8,128)(2,1)S(1)}, u32[]{:S(2)}, u32[]{:S(2)}) collective-permute-start(bf16[512,256]{1,0:T(8,128)(2,1)S(1)} %fusion.2), channel_id=1, source_target_pairs={{0,16},{8,24},{16,0},{24,8},{1,17},{9,25},{17,1},{25,9},{2,18},{10... | collective-permute-start | bytes 786440 | tf_op jit(solution)/shard_map/ppermute | solution.py:10
  46.9 1.2 %collective-permute-start.12 = (bf16[512,256]{1,0:T(8,128)(2,1)S(1)}, bf16[512,256]{1,0:T(8,128)(2,1)S(1)}, u32[]{:S(2)}, u32[]{:S(2)}) collective-permute-start(bf16[512,256]{1,0:T(8,128)(2,1)S(1)} %fusion.2), channel_id=1, source_target_pairs={{0,24},{8,16},{16,8},{24,0},{1,25},{9,17},{17,9},{25,1},{2,26},{10... | collective-permute-start | bytes 786440 | tf_op jit(solution)/shard_map/ppermute | solution.py:10
  48.1 0.8 %collective-permute-start.10 = (bf16[512,256]{1,0:T(8,128)(2,1)S(1)}, bf16[512,256]{1,0:T(8,128)(2,1)S(1)}, u32[]{:S(2)}, u32[]{:S(2)}) collective-permute-start(bf16[512,256]{1,0:T(8,128)(2,1)S(1)} %fusion.2), channel_id=1, source_target_pairs={{0,8},{8,0},{16,24},{24,16},{1,9},{9,1},{17,25},{25,17},{2,10},{10... | collective-permute-start | bytes 786440 | tf_op jit(solution)/shard_map/ppermute | solution.py:10
  48.9 9.5 %collective-permute-done.11 = bf16[512,256]{1,0:T(8,128)(2,1)S(1)} collective-permute-done((bf16[512,256]{1,0:T(8,128)(2,1)S(1)}, bf16[512,256]{1,0:T(8,128)(2,1)S(1)}, u32[]{:S(2)}, u32[]{:S(2)}) %collective-permute-start.11) | collective-permute-done | bytes 262176 | tf_op jit(solution)/shard_map/ppermute | solution.py:10
  58.4 0.0 collective-permute-done.12
  58.4 1.2 %collective-permute-done.10 = bf16[512,256]{1,0:T(8,128)(2,1)S(1)} collective-permute-done((bf16[512,256]{1,0:T(8,128)(2,1)S(1)}, bf16[512,256]{1,0:T(8,128)(2,1)S(1)}, u32[]{:S(2)}, u32[]{:S(2)}) %collective-permute-start.10) | collective-permute-done | bytes 262176 | tf_op jit(solution)/shard_map/ppermute | solution.py:10
  59.6 0.1 pad_maximum_fusion.1
  59.8 0.0 copy-done.2
  59.8 0.6 gather_fusion.1
  60.4 0.0 copy-start.3
  60.4 0.2 broadcast_select_fusion.1
  60.6 1.4 %copy-done.3 = bf16[512,2048]{1,0:T(8,128)(2,1)S(1)} copy-done((bf16[512,2048]{1,0:T(8,128)(2,1)S(1)}, bf16[512,2048]{1,0:T(8,128)(2,1)}, u32[]{:S(2)}) %copy-start.3) | copy-done | bytes 2097176
  62.0 1.5 %fusion.1 = f32[512,256]{1,0:T(8,128)} fusion(bf16[512,2048]{1,0:T(8,128)(2,1)S(1)} %copy-done.3, bf16[2048,256]{1,0:T(8,128)(2,1)S(1)} %bitcast.29, bf16[512,256]{1,0:T(8,128)(2,1)S(1)} %get-tuple-element.7, f32[64,8,2,128]{3,2,1,0:T(2,128)S(1)} %bitcast.35), kind=kOutput, calls=%fused_computation.5 | convolution fusion | flops 537526272 | bytes 4456448 | tf_op jit(solution)/shard_map/dot_general | solution.py:55
  (7 shorter events, 0.1 us)
Async XLA Ops:
  2.4 14.9 %collective-permute-start = (bf16[512,256]{1,0:T(8,128)(2,1)S(1)}, bf16[512,256]{1,0:T(8,128)(2,1)S(1)}, u32[]{:S(2)}, u32[]{:S(2)}) collective-permute-start(bf16[512,256]{1,0:T(8,128)(2,1)S(1)} %get-tuple-element.7), channel_id=1, source_target_pairs={{0,2},{1,3},{2,0},{3,1},{4,6},{5,7},{6,4},{7,5},{8,10},{9,11},{10,... | collective-permute-start | bytes 786440 | tf_op jit(solution)/shard_map/ppermute | solution.py:10
  5.5 17.5 %collective-permute-start.3 = (bf16[512,256]{1,0:T(8,128)(2,1)S(1)}, bf16[512,256]{1,0:T(8,128)(2,1)S(1)}, u32[]{:S(2)}, u32[]{:S(2)}) collective-permute-start(bf16[512,256]{1,0:T(8,128)(2,1)S(1)} %get-tuple-element.7), channel_id=1, source_target_pairs={{0,4},{1,5},{2,6},{3,7},{4,0},{5,1},{6,2},{7,3},{8,12},{9,13},{10,... | collective-permute-start | bytes 786440 | tf_op jit(solution)/shard_map/ppermute | solution.py:10
  17.3 6.2 %collective-permute-start.1 = (bf16[512,256]{1,0:T(8,128)(2,1)S(1)}, bf16[512,256]{1,0:T(8,128)(2,1)S(1)}, u32[]{:S(2)}, u32[]{:S(2)}) collective-permute-start(bf16[512,256]{1,0:T(8,128)(2,1)S(1)} %get-tuple-element.7), channel_id=1, source_target_pairs={{0,1},{1,0},{2,3},{3,2},{4,5},{5,4},{6,7},{7,6},{8,9},{9,8},{10,11... | collective-permute-start | bytes 786440 | tf_op jit(solution)/shard_map/ppermute | solution.py:10
  17.3 10.6 %collective-permute-start.5 = (bf16[512,256]{1,0:T(8,128)(2,1)S(1)}, bf16[512,256]{1,0:T(8,128)(2,1)S(1)}, u32[]{:S(2)}, u32[]{:S(2)}) collective-permute-start(bf16[512,256]{1,0:T(8,128)(2,1)S(1)} %get-tuple-element.7), channel_id=1, source_target_pairs={{0,6},{1,7},{2,4},{3,5},{4,2},{5,3},{6,0},{7,1},{8,14},{9,15},{10,... | collective-permute-start | bytes 786440 | tf_op jit(solution)/shard_map/ppermute | solution.py:10
  20.0 9.1 %collective-permute-start.7 = (bf16[512,256]{1,0:T(8,128)(2,1)S(1)}, bf16[512,256]{1,0:T(8,128)(2,1)S(1)}, u32[]{:S(2)}, u32[]{:S(2)}) collective-permute-start(bf16[512,256]{1,0:T(8,128)(2,1)S(1)} %get-tuple-element.7), channel_id=1, source_target_pairs={{0,8},{8,0},{16,24},{24,16},{1,9},{9,1},{17,25},{25,17},{2,10},{10... | collective-permute-start | bytes 786440 | tf_op jit(solution)/shard_map/ppermute | solution.py:10
  21.5 13.8 %collective-permute-start.8 = (bf16[512,256]{1,0:T(8,128)(2,1)S(1)}, bf16[512,256]{1,0:T(8,128)(2,1)S(1)}, u32[]{:S(2)}, u32[]{:S(2)}) collective-permute-start(bf16[512,256]{1,0:T(8,128)(2,1)S(1)} %get-tuple-element.7), channel_id=1, source_target_pairs={{0,16},{8,24},{16,0},{24,8},{1,17},{9,25},{17,1},{25,9},{2,18},{10... | collective-permute-start | bytes 786440 | tf_op jit(solution)/shard_map/ppermute | solution.py:10
  23.0 12.3 %collective-permute-start.9 = (bf16[512,256]{1,0:T(8,128)(2,1)S(1)}, bf16[512,256]{1,0:T(8,128)(2,1)S(1)}, u32[]{:S(2)}, u32[]{:S(2)}) collective-permute-start(bf16[512,256]{1,0:T(8,128)(2,1)S(1)} %get-tuple-element.7), channel_id=1, source_target_pairs={{0,24},{8,16},{16,8},{24,0},{1,25},{9,17},{17,9},{25,1},{2,26},{10... | collective-permute-start | bytes 786440 | tf_op jit(solution)/shard_map/ppermute | solution.py:10
  23.5 13.9 %collective-permute-start.2 = (bf16[512,256]{1,0:T(8,128)(2,1)S(1)}, bf16[512,256]{1,0:T(8,128)(2,1)}, u32[]{:S(2)}, u32[]{:S(2)}) collective-permute-start(bf16[512,256]{1,0:T(8,128)(2,1)S(1)} %collective-permute-done), channel_id=1, source_target_pairs={{0,1},{1,0},{2,3},{3,2},{4,5},{5,4},{6,7},{7,6},{8,9},{9,8},{10,11... | collective-permute-start | bytes 786440 | tf_op jit(solution)/shard_map/ppermute | solution.py:10
  28.0 11.9 %collective-permute-start.4 = (bf16[512,256]{1,0:T(8,128)(2,1)S(1)}, bf16[512,256]{1,0:T(8,128)(2,1)}, u32[]{:S(2)}, u32[]{:S(2)}) collective-permute-start(bf16[512,256]{1,0:T(8,128)(2,1)S(1)} %collective-permute-done.3), channel_id=1, source_target_pairs={{0,1},{1,0},{2,3},{3,2},{4,5},{5,4},{6,7},{7,6},{8,9},{9,8},{10,11... | collective-permute-start | bytes 786440 | tf_op jit(solution)/shard_map/ppermute | solution.py:10
  29.1 13.4 %collective-permute-start.6 = (bf16[512,256]{1,0:T(8,128)(2,1)S(1)}, bf16[512,256]{1,0:T(8,128)(2,1)S(1)}, u32[]{:S(2)}, u32[]{:S(2)}) collective-permute-start(bf16[512,256]{1,0:T(8,128)(2,1)S(1)} %collective-permute-done.5), channel_id=1, source_target_pairs={{0,1},{1,0},{2,3},{3,2},{4,5},{5,4},{6,7},{7,6},{8,9},{9,8},{10,11... | collective-permute-start | bytes 786440 | tf_op jit(solution)/shard_map/ppermute | solution.py:10
  35.4 1.4 %copy-start = (bf16[512,2048]{1,0:T(8,128)(2,1)}, bf16[512,2048]{1,0:T(8,128)(2,1)S(1)}, u32[]{:S(2)}) copy-start(bf16[512,2048]{1,0:T(8,128)(2,1)S(1)} %constant_dynamic-update-slice_fusion.5) | copy-start | bytes 6291460
  42.3 1.6 %copy-start.1 = (bf16[512,2048]{1,0:T(8,128)(2,1)S(1)}, bf16[512,2048]{1,0:T(8,128)(2,1)}, u32[]{:S(2)}) copy-start(bf16[512,2048]{1,0:T(8,128)(2,1)} %constant_dynamic-update-slice_fusion.1) | copy-start | bytes 6291460
  43.9 15.8 %copy-start.2 = (bf16[512,2048]{1,0:T(8,128)(2,1)}, bf16[512,2048]{1,0:T(8,128)(2,1)S(1)}, u32[]{:S(2)}) copy-start(bf16[512,2048]{1,0:T(8,128)(2,1)S(1)} %constant_dynamic-update-slice_fusion) | copy-start | bytes 6291460
  45.3 13.1 %collective-permute-start.11 = (bf16[512,256]{1,0:T(8,128)(2,1)S(1)}, bf16[512,256]{1,0:T(8,128)(2,1)S(1)}, u32[]{:S(2)}, u32[]{:S(2)}) collective-permute-start(bf16[512,256]{1,0:T(8,128)(2,1)S(1)} %fusion.2), channel_id=1, source_target_pairs={{0,16},{8,24},{16,0},{24,8},{1,17},{9,25},{17,1},{25,9},{2,18},{10... | collective-permute-start | bytes 786440 | tf_op jit(solution)/shard_map/ppermute | solution.py:10
  46.9 11.5 %collective-permute-start.12 = (bf16[512,256]{1,0:T(8,128)(2,1)S(1)}, bf16[512,256]{1,0:T(8,128)(2,1)S(1)}, u32[]{:S(2)}, u32[]{:S(2)}) collective-permute-start(bf16[512,256]{1,0:T(8,128)(2,1)S(1)} %fusion.2), channel_id=1, source_target_pairs={{0,24},{8,16},{16,8},{24,0},{1,25},{9,17},{17,9},{25,1},{2,26},{10... | collective-permute-start | bytes 786440 | tf_op jit(solution)/shard_map/ppermute | solution.py:10
  48.1 11.6 %collective-permute-start.10 = (bf16[512,256]{1,0:T(8,128)(2,1)S(1)}, bf16[512,256]{1,0:T(8,128)(2,1)S(1)}, u32[]{:S(2)}, u32[]{:S(2)}) collective-permute-start(bf16[512,256]{1,0:T(8,128)(2,1)S(1)} %fusion.2), channel_id=1, source_target_pairs={{0,8},{8,0},{16,24},{24,16},{1,9},{9,1},{17,25},{25,17},{2,10},{10... | collective-permute-start | bytes 786440 | tf_op jit(solution)/shard_map/ppermute | solution.py:10
  60.4 1.6 %copy-start.3 = (bf16[512,2048]{1,0:T(8,128)(2,1)S(1)}, bf16[512,2048]{1,0:T(8,128)(2,1)}, u32[]{:S(2)}) copy-start(bf16[512,2048]{1,0:T(8,128)(2,1)} %copy-done.2) | copy-start | bytes 6291460

commit v11 on v7

--- a/solution.py
+++ b/solution.py
@@ -25,15 +25,16 @@
         )
         local_mask = jnp.repeat(jnp.repeat(local_blocks, B, axis=0), B, axis=1)
         masked = matrix_in * local_mask.astype(jnp.bfloat16)
+        sent = matrix_in
 
-        col_pieces = [masked] + [_swap(masked, "row", n_row, j) for j in range(1, n_row)]
+        col_pieces = [sent] + [_swap(sent, "row", n_row, j) for j in range(1, n_row)]
 
-        late, _ = lax.optimization_barrier((masked, col_pieces[1]))
+        late, _ = lax.optimization_barrier((sent, col_pieces[1]))
         row_pieces = [None] * n_col
-        row_pieces[0] = masked
+        row_pieces[0] = sent
         row_pieces[1] = _swap(late, "col", n_col, 1)
         for k in range(1, n_z):
-            piece = _swap(late if k == 1 else masked, "col", n_col, 2 * k)
+            piece = _swap(late if k == 1 else sent, "col", n_col, 2 * k)
             row_pieces[2 * k] = piece
             row_pieces[2 * k + 1] = _swap(piece, "col", n_col, 1)
 
@@ -45,7 +46,21 @@
             return jnp.take(stacked, sub_index, axis=0).reshape(n_col * cols, cols)
 
         row_cat = jnp.concatenate(row_pieces, axis=1)
-        square = jnp.dot(row_cat, in_slot_order(col_pieces), preferred_element_type=jnp.float32)
+        halves = jnp.arange(block_cols, dtype=jnp.int32)
+        slot_blocks = (slots[:, None] * block_cols + halves[None, :]).reshape(-1)
+        own_rows = lax.dynamic_slice_in_dim(pattern, row_index * block_rows, block_rows, 0)
+        row_keep = jnp.take(own_rows, slot_blocks, axis=1).astype(jnp.bfloat16)
+        own_cols = lax.dynamic_slice_in_dim(pattern, col_index * block_cols, block_cols, 1)
+        col_keep = jnp.take(own_cols, slot_blocks, axis=0).astype(jnp.bfloat16)
+        n_slot_blocks = n_col * block_cols
+        row_cat = (
+            row_cat.reshape(block_rows, B, n_slot_blocks, B) * row_keep[:, None, :, None]
+        ).reshape(rows, n_col * cols)
+        col_slot = in_slot_order(col_pieces)
+        col_slot = (
+            col_slot.reshape(n_slot_blocks, B, block_cols, B) * col_keep[:, None, :, None]
+        ).reshape(n_col * cols, cols)
+        square = jnp.dot(row_cat, col_slot, preferred_element_type=jnp.float32)
         mask_float = local_mask.astype(jnp.float32)
         filtered = (mask_float * square).astype(jnp.bfloat16)
         f_pieces = [filtered] + [_swap(filtered, "row", n_row, k) for k in range(1, n_row)]

time: 53.9 us -> 57 us (1.058)
  the two profiles are of different devices: /device:TPU:16 before, /device:TPU:0 now
where the time goes in v11:
time: 57 us; the launch traced here: 56.6 us
  waiting for transfers between devices  22.9 us (40%)
  starting transfers between devices  14.7 us (26%)
  local copies, waits for them, and re-layouts  13.5 us (24%)
  other arithmetic  2.97 us (5%)
  matrix products  2.24 us (4%)
    ppermute x13, waiting for transfers between devices, _swap(): return lax.ppermute(x, axis, [(i, i ^ d) for i in range(size)])  22.9 us
    ppermute x13, starting transfers between devices, _swap(): return lax.ppermute(x, axis, [(i, i ^ d) for i in range(size)])  14.7 us
    unnamed x21, local copies, waits for them, and re-layouts  6.88 us
    dot_general x1, matrix products, body(): cubic = jnp.dot(row_cat, f_slot, preferred_element_type=jnp.float32)  1.52 us
    another operation x2, other arithmetic, in_slot_order(): stacked = jnp.stack(pieces).reshape(n_row * ratio, cols, cols)  1.37 us
    mul x2, local copies, waits for them, and re-layouts, body(): col_slot.reshape(n_slot_blocks, B, block_cols, B)  1.31 us
    broadcast_in_dim x4, local copies, waits for them, and re-layouts, body(): local_mask = jnp.repeat(jnp.repeat(local_blocks, B, axis=0), B, axis=1)  1.24 us
    gather x2, local copies, waits for them, and re-layouts, in_slot_order(): return jnp.take(stacked, sub_index, axis=0).reshape(n_col * cols, cols)  1.23 us
  transfers between devices with their start and end apart: 13, of which 5 were waited for; matrix products, arithmetic and copies ran while one was open for 21% of the time, Pallas kernels for 0%

profile of v11, /device:TPU:0, one launch (start us, length us, event | category | flops | bytes accessed | tf_op | source)
XLA Modules:
  0.0 56.6 jit_solution(3857648414080201981)
XLA Ops:
  0.0 3.9 %collective-permute-start.9 = (bf16[512,256]{1,0:T(8,128)(2,1)}, bf16[512,256]{1,0:T(8,128)(2,1)S(1)}, u32[]{:S(2)}, u32[]{:S(2)}) collective-permute-start(bf16[512,256]{1,0:T(8,128)(2,1)} %param.4), channel_id=1, source_target_pairs={{0,24},{8,16},{16,8},{24,0},{1,25},{9,17},{17,9},{25,1},{2,26},{10... | collective-permute-start | bytes 786440 | tf_op jit(solution)/shard_map/ppermute | solution.py:10
  3.9 0.5 collective-permute-start.8
  4.4 0.1 collective-permute-start
  4.5 3.0 %collective-permute-start.4 = (bf16[512,256]{1,0:T(8,128)(2,1)}, bf16[512,256]{1,0:T(8,128)(2,1)}, u32[]{:S(2)}, u32[]{:S(2)}) collective-permute-start(bf16[512,256]{1,0:T(8,128)(2,1)} %param.4), channel_id=1, source_target_pairs={{0,4},{1,5},{2,6},{3,7},{4,0},{5,1},{6,2},{7,3},{8,12},{9,13},{10,... | collective-permute-start | bytes 786440 | tf_op jit(solution)/shard_map/ppermute | solution.py:10
  7.5 1.3 %collective-permute-start.6 = (bf16[512,256]{1,0:T(8,128)(2,1)}, bf16[512,256]{1,0:T(8,128)(2,1)}, u32[]{:S(2)}, u32[]{:S(2)}) collective-permute-start(bf16[512,256]{1,0:T(8,128)(2,1)} %param.4), channel_id=1, source_target_pairs={{0,6},{1,7},{2,4},{3,5},{4,2},{5,3},{6,0},{7,1},{8,14},{9,15},{10,... | collective-permute-start | bytes 786440 | tf_op jit(solution)/shard_map/ppermute | solution.py:10
  8.9 0.1 iota_add_fusion
  9.0 0.1 add.74
  9.0 0.1 add.72
  9.2 0.8 %constant_dynamic-slice_fusion = s32[16,2]{1,0:T(8,128)S(1)} fusion(s32[16,16]{1,0:T(8,128)} %param.5, s32[]{:T(128)S(6)} %select_n.61), kind=kLoop, calls=%fused_computation.51 | loop fusion | bytes 260 | tf_op jit(solution)/shard_map/dynamic_slice | solution.py:53
  10.0 0.6 gather_fusion.1
  10.5 0.1 select_convert_fusion.1
  10.6 0.7 %constant_dynamic-slice_fusion.1 = s32[4,16]{1,0:T(4,128)S(1)} fusion(s32[16,16]{1,0:T(8,128)} %param.5, s32[]{:T(128)S(6)} %select_n.60), kind=kLoop, calls=%fused_computation.52 | loop fusion | bytes 516 | tf_op jit(solution)/shard_map/dynamic_slice | solution.py:51
  11.3 0.1 copy.7
  11.4 0.6 gather_fusion
  11.9 0.1 fusion.21
  12.0 4.3 %collective-permute-done = bf16[512,256]{1,0:T(8,128)(2,1)S(1)} collective-permute-done((bf16[512,256]{1,0:T(8,128)(2,1)}, bf16[512,256]{1,0:T(8,128)(2,1)S(1)}, u32[]{:S(2)}, u32[]{:S(2)}) %collective-permute-start) | collective-permute-done | bytes 262176 | tf_op jit(solution)/shard_map/ppermute | solution.py:10
  16.3 1.6 %collective-permute-start.2 = (bf16[512,256]{1,0:T(8,128)(2,1)}, bf16[512,256]{1,0:T(8,128)(2,1)}, u32[]{:S(2)}, u32[]{:S(2)}) collective-permute-start(bf16[512,256]{1,0:T(8,128)(2,1)} %param.4), channel_id=1, source_target_pairs={{0,2},{1,3},{2,0},{3,1},{4,6},{5,7},{6,4},{7,5},{8,10},{9,11},{10,... | collective-permute-start | bytes 786440 | tf_op jit(solution)/shard_map/ppermute | solution.py:10
  17.9 0.8 %dynamic-slice_convert_fusion = (bf16[4,2]{1,0:T(4,128)(2,1)S(1)}, f32[4,2]{1,0:T(4,128)S(1)}) fusion(s32[16,16]{1,0:T(8,128)} %param.5, s32[]{:T(128)S(6)} %select_n.60, s32[]{:T(128)S(6)} %select_n.61), kind=kLoop, calls=%fused_computation.42 | loop fusion | flops 16 | bytes 88 | tf_op jit(solution)/shard_map/convert_element_type | solution.py:27
  18.7 0.6 %mul.86 = bf16[16,128,2,128]{3,2,1,0:T(2,128)(2,1)S(1)} broadcast(bf16[16,2]{1,0:T(8,128)(2,1)S(1)} %select_convert_fusion.1), dimensions={0,2} | broadcast | bytes 1048640 | tf_op jit(solution)/shard_map/mul | solution.py:61
  19.3 0.7 %mul.87 = bf16[8,256,256]{2,1,0:T(8,128)(2,1)S(1)} reshape(bf16[16,128,2,128]{3,2,1,0:T(2,128)(2,1)S(1)} %mul.86) | data formatting | bytes 2097152 | tf_op jit(solution)/shard_map/mul | solution.py:61
  20.0 0.1 copy.6
  20.1 0.0 copy-done.3
  20.1 0.7 %constant_dynamic-update-slice_fusion.7 = bf16[512,2048]{1,0:T(8,128)(2,1)} fusion(bf16[512,256]{1,0:T(8,128)(2,1)S(1)} %copy-done.3), kind=kLoop, calls=%fused_computation.28 | loop fusion | bytes 524288
  20.8 0.0 collective-permute-done.9
  20.8 0.0 collective-permute-start.1
  20.9 0.0 collective-permute-done.8
  20.9 0.0 copy-done.5
  20.9 0.7 %copy-done.4 = bf16[512,256]{1,0:T(8,128)(2,1)} copy-done((bf16[512,256]{1,0:T(8,128)(2,1)}, bf16[512,256]{1,0:T(8,128)(2,1)S(1)}, u32[]{:S(2)}) %copy-start.4) | copy-done | bytes 262168
  21.5 1.2 %pad_maximum_fusion = bf16[4,512,256]{2,1,0:T(8,128)(2,1)S(1)} fusion(bf16[1,512,256]{2,1,0:T(8,128)(2,1)} %bitcast.65, bf16[1,512,256]{2,1,0:T(8,128)(2,1)} %bitcast.6, bf16[1,512,256]{2,1,0:T(8,128)(2,1)} %bitcast.66, bf16[1,512,256]{2,1,0:T(8,128)(2,1)S(1)} %bitcast.60), kind=kLoop, calls=%fused_computation.16 | loop fusion | flops 1572864 | bytes 2097152 | tf_op jit(solution)/shard_map/stack | solution.py:45
  22.8 0.6 %gather_fusion.2 = bf16[8,256,256]{2,1,0:T(8,128)(2,1)S(1)} fusion(bf16[8,256,256]{2,1,0:T(8,128)(2,1)S(1)} %bitcast.53, s32[1024]{0:T(1024)S(1)} %get-tuple-element.12), kind=kCustom, calls=%fused_computation.clone | custom fusion | bytes 2097184 | tf_op jit(solution)/shard_map/jit(_take)/gather | solution.py:46
  23.4 0.0 copy-start
  23.4 6.8 %collective-permute-done.2 = bf16[512,256]{1,0:T(8,128)(2,1)} collective-permute-done((bf16[512,256]{1,0:T(8,128)(2,1)}, bf16[512,256]{1,0:T(8,128)(2,1)}, u32[]{:S(2)}, u32[]{:S(2)}) %collective-permute-start.2) | collective-permute-done | bytes 262176 | tf_op jit(solution)/shard_map/ppermute | solution.py:10
  30.2 0.0 collective-permute-start.3
  30.2 0.2 select_multiply_fusion
  30.4 0.0 collective-permute-done.4
  30.4 0.6 collective-permute-start.5
  31.0 0.0 collective-permute-done.6
  31.0 0.1 collective-permute-start.7
  31.1 0.0 collective-permute-done.1
  31.1 0.0 copy-done
  31.1 1.0 %constant_dynamic-update-slice_fusion.6 = bf16[512,2048]{1,0:T(8,128)(2,1)S(1)} fusion(bf16[512,2048]{1,0:T(8,128)(2,1)S(1)} %copy-done, bf16[512,256]{1,0:T(8,128)(2,1)} %collective-permute-done.1), kind=kLoop, calls=%fused_computation.27 | loop fusion | bytes 524288
  32.1 1.0 %constant_dynamic-update-slice_fusion.5 = bf16[512,2048]{1,0:T(8,128)(2,1)S(1)} fusion(bf16[512,2048]{1,0:T(8,128)(2,1)S(1)} %constant_dynamic-update-slice_fusion.6, bf16[512,256]{1,0:T(8,128)(2,1)} %collective-permute-done.2), kind=kLoop, calls=%fused_computation.26 | loop fusion | bytes 524288
  33.0 0.0 collective-permute-done.3
  33.1 1.0 %constant_dynamic-update-slice_fusion.3 = bf16[512,2048]{1,0:T(8,128)(2,1)S(1)} fusion(bf16[512,2048]{1,0:T(8,128)(2,1)S(1)} %constant_dynamic-update-slice_fusion.4, bf16[512,256]{1,0:T(8,128)(2,1)} %collective-permute-done.4), kind=kLoop, calls=%fused_computation.24 | loop fusion | bytes 524288
  34.1 0.0 collective-permute-done.5
  34.1 1.0 %constant_dynamic-update-slice_fusion.1 = bf16[512,2048]{1,0:T(8,128)(2,1)S(1)} fusion(bf16[512,2048]{1,0:T(8,128)(2,1)S(1)} %constant_dynamic-update-slice_fusion.2, bf16[512,256]{1,0:T(8,128)(2,1)} %collective-permute-done.6), kind=kLoop, calls=%fused_computation.22 | loop fusion | bytes 524288
  35.1 0.0 collective-permute-done.7
  35.1 0.6 %copy.10 = bf16[64,8,16,128]{3,2,1,0:T(8,128)(2,1)S(1)} copy(bf16[64,8,16,128]{3,1,2,0:T(8,128)(2,1)S(1)} %bitcast.54) | data formatting | bytes 4194304
  35.8 0.2 bitcast_multiply_fusion
  36.0 0.0 copy-start.1
  36.0 0.6 %broadcast_in_dim.44 = f32[512,2,128]{2,1,0:T(2,128)S(1)} broadcast(f32[512,2]{1,0:T(8,128)S(1)} %bitcast.58), dimensions={0,1} | broadcast | bytes 528384 | tf_op jit(solution)/shard_map/broadcast_in_dim | solution.py:26
  36.6 0.7 %fusion.18 = bf16[512,256]{1,0:T(8,128)(2,1)S(1)} fusion(bf16[2048,256]{1,0:T(8,128)(2,1)S(1)} %bitcast.59, bf16[64,8,16,128]{3,2,1,0:T(8,128)(2,1)S(1)} %bitcast.55, f32[64,8,2,128]{3,2,1,0:T(2,128)S(1)} %bitcast.62), kind=kOutput, calls=%fused_computation.15 | convolution fusion | flops 537133056 | bytes 3932160 | tf_op jit(solution)/shard_map/dot_general | solution.py:63
  37.4 2.6 %collective-permute-start.12 = (bf16[512,256]{1,0:T(8,128)(2,1)S(1)}, bf16[512,256]{1,0:T(8,128)(2,1)S(1)}, u32[]{:S(2)}, u32[]{:S(2)}) collective-permute-start(bf16[512,256]{1,0:T(8,128)(2,1)S(1)} %fusion.18), channel_id=1, source_target_pairs={{0,24},{8,16},{16,8},{24,0},{1,25},{9,17},{17,9},{25,1},{2,26},{10... | collective-permute-start | bytes 786440 | tf_op jit(solution)/shard_map/ppermute | solution.py:10
  39.9 0.5 collective-permute-start.11
  40.4 0.5 collective-permute-start.10
  40.9 6.6 %collective-permute-done.12 = bf16[512,256]{1,0:T(8,128)(2,1)S(1)} collective-permute-done((bf16[512,256]{1,0:T(8,128)(2,1)S(1)}, bf16[512,256]{1,0:T(8,128)(2,1)S(1)}, u32[]{:S(2)}, u32[]{:S(2)}) %collective-permute-start.12) | collective-permute-done | bytes 262176 | tf_op jit(solution)/shard_map/ppermute | solution.py:10
  47.5 5.1 %collective-permute-done.11 = bf16[512,256]{1,0:T(8,128)(2,1)S(1)} collective-permute-done((bf16[512,256]{1,0:T(8,128)(2,1)S(1)}, bf16[512,256]{1,0:T(8,128)(2,1)S(1)}, u32[]{:S(2)}, u32[]{:S(2)}) %collective-permute-start.11) | collective-permute-done | bytes 262176 | tf_op jit(solution)/shard_map/ppermute | solution.py:10
  52.6 0.1 collective-permute-done.10
  52.7 0.1 pad_maximum_fusion.1
  52.9 0.6 %gather_fusion.3 = bf16[8,256,256]{2,1,0:T(8,128)(2,1)S(1)} fusion(bf16[8,256,256]{2,1,0:T(8,128)(2,1)S(1)} %bitcast.52, s32[1024]{0:T(1024)S(1)} %get-tuple-element.12), kind=kCustom, calls=%fused_computation.1.clone | custom fusion | bytes 2097184 | tf_op jit(solution)/shard_map/jit(_take)/gather | solution.py:46
  53.5 0.2 broadcast_select_fusion
  53.7 0.6 %broadcast_in_dim.46 = bf16[512,2,128]{2,1,0:T(2,128)(2,1)S(1)} broadcast(bf16[512,2]{1,0:T(8,128)(2,1)S(1)} %bitcast.61), dimensions={0,1} | broadcast | bytes 264192 | tf_op jit(solution)/shard_map/broadcast_in_dim | solution.py:26
  54.3 0.8 %copy-done.2 = bf16[4,128,16,128]{3,2,1,0:T(8,128)(2,1)S(1)} copy-done((bf16[4,128,16,128]{3,2,1,0:T(8,128)(2,1)S(1)}, bf16[4,128,16,128]{3,2,1,0:T(8,128)(2,1)}, u32[]{:S(2)}) %copy-start.2) | copy-done | bytes 2097176
  55.1 1.5 %fusion.15 = f32[512,256]{1,0:T(8,128)} fusion(bf16[2048,256]{1,0:T(8,128)(2,1)S(1)} %bitcast.57, bf16[64,8,16,128]{3,2,1,0:T(8,128)(2,1)S(1)} %bitcast.56, f32[64,8,2,128]{3,2,1,0:T(2,128)S(1)} %bitcast.63, bf16[512,256]{1,0:T(8,128)(2,1)S(1)} %copy-done.3, bf16[64,8,2,128]{3,2,1,0:T(2,128)(2,1)S(1)} %bitcast.64), kind=kOutput, calls=%fused_computation.14 | convolution fusion | flops 537657344 | bytes 4718592 | tf_op jit(solution)/shard_map/dot_general | solution.py:68
  (15 shorter events, 0.2 us)
Async XLA Ops:
  0.0 20.1 %copy-start.3 = (bf16[512,256]{1,0:T(8,128)(2,1)S(1)}, bf16[512,256]{1,0:T(8,128)(2,1)}, u32[]{:S(2)}) copy-start(bf16[512,256]{1,0:T(8,128)(2,1)} %param.4) | copy-start | bytes 786436
  0.0 20.8 %collective-permute-start.9 = (bf16[512,256]{1,0:T(8,128)(2,1)}, bf16[512,256]{1,0:T(8,128)(2,1)S(1)}, u32[]{:S(2)}, u32[]{:S(2)}) collective-permute-start(bf16[512,256]{1,0:T(8,128)(2,1)} %param.4), channel_id=1, source_target_pairs={{0,24},{8,16},{16,8},{24,0},{1,25},{9,17},{17,9},{25,1},{2,26},{10... | collective-permute-start | bytes 786440 | tf_op jit(solution)/shard_map/ppermute | solution.py:10
  3.9 17.0 %collective-permute-start.8 = (bf16[512,256]{1,0:T(8,128)(2,1)}, bf16[512,256]{1,0:T(8,128)(2,1)}, u32[]{:S(2)}, u32[]{:S(2)}) collective-permute-start(bf16[512,256]{1,0:T(8,128)(2,1)} %param.4), channel_id=1, source_target_pairs={{0,16},{8,24},{16,0},{24,8},{1,17},{9,25},{17,1},{25,9},{2,18},{10... | collective-permute-start | bytes 786440 | tf_op jit(solution)/shard_map/ppermute | solution.py:10
  4.4 11.9 %collective-permute-start = (bf16[512,256]{1,0:T(8,128)(2,1)}, bf16[512,256]{1,0:T(8,128)(2,1)S(1)}, u32[]{:S(2)}, u32[]{:S(2)}) collective-permute-start(bf16[512,256]{1,0:T(8,128)(2,1)} %param.4), channel_id=1, source_target_pairs={{0,8},{8,0},{16,24},{24,16},{1,9},{9,1},{17,25},{25,17},{2,10},{10... | collective-permute-start | bytes 786440 | tf_op jit(solution)/shard_map/ppermute | solution.py:10
  4.5 25.9 %collective-permute-start.4 = (bf16[512,256]{1,0:T(8,128)(2,1)}, bf16[512,256]{1,0:T(8,128)(2,1)}, u32[]{:S(2)}, u32[]{:S(2)}) collective-permute-start(bf16[512,256]{1,0:T(8,128)(2,1)} %param.4), channel_id=1, source_target_pairs={{0,4},{1,5},{2,6},{3,7},{4,0},{5,1},{6,2},{7,3},{8,12},{9,13},{10,... | collective-permute-start | bytes 786440 | tf_op jit(solution)/shard_map/ppermute | solution.py:10
  7.5 23.5 %collective-permute-start.6 = (bf16[512,256]{1,0:T(8,128)(2,1)}, bf16[512,256]{1,0:T(8,128)(2,1)}, u32[]{:S(2)}, u32[]{:S(2)}) collective-permute-start(bf16[512,256]{1,0:T(8,128)(2,1)} %param.4), channel_id=1, source_target_pairs={{0,6},{1,7},{2,4},{3,5},{4,2},{5,3},{6,0},{7,1},{8,14},{9,15},{10,... | collective-permute-start | bytes 786440 | tf_op jit(solution)/shard_map/ppermute | solution.py:10
  16.3 4.5 %copy-start.5 = (bf16[512,256]{1,0:T(8,128)(2,1)}, bf16[512,256]{1,0:T(8,128)(2,1)S(1)}, u32[]{:S(2)}) copy-start(bf16[512,256]{1,0:T(8,128)(2,1)S(1)} %collective-permute-done) | copy-start | bytes 786436
  16.3 13.9 %collective-permute-start.2 = (bf16[512,256]{1,0:T(8,128)(2,1)}, bf16[512,256]{1,0:T(8,128)(2,1)}, u32[]{:S(2)}, u32[]{:S(2)}) collective-permute-start(bf16[512,256]{1,0:T(8,128)(2,1)} %param.4), channel_id=1, source_target_pairs={{0,2},{1,3},{2,0},{3,1},{4,6},{5,7},{6,4},{7,5},{8,10},{9,11},{10,... | collective-permute-start | bytes 786440 | tf_op jit(solution)/shard_map/ppermute | solution.py:10
  20.8 0.7 %copy-start.4 = (bf16[512,256]{1,0:T(8,128)(2,1)}, bf16[512,256]{1,0:T(8,128)(2,1)S(1)}, u32[]{:S(2)}) copy-start(bf16[512,256]{1,0:T(8,128)(2,1)S(1)} %collective-permute-done.9) | copy-start | bytes 786436
  20.8 10.2 %collective-permute-start.1 = (bf16[512,256]{1,0:T(8,128)(2,1)S(1)}, bf16[512,256]{1,0:T(8,128)(2,1)}, u32[]{:S(2)}, u32[]{:S(2)}) collective-permute-start(bf16[512,256]{1,0:T(8,128)(2,1)S(1)} %copy-done.3), channel_id=1, source_target_pairs={{0,1},{1,0},{2,3},{3,2},{4,5},{5,4},{6,7},{7,6},{8,9},{9,8},{10,11... | collective-permute-start | bytes 786440 | tf_op jit(solution)/shard_map/ppermute | solution.py:10
  23.4 7.7 %copy-start = (bf16[512,2048]{1,0:T(8,128)(2,1)S(1)}, bf16[512,2048]{1,0:T(8,128)(2,1)}, u32[]{:S(2)}) copy-start(bf16[512,2048]{1,0:T(8,128)(2,1)} %constant_dynamic-update-slice_fusion.7) | copy-start | bytes 6291460
  30.2 2.9 %collective-permute-start.3 = (bf16[512,256]{1,0:T(8,128)(2,1)}, bf16[512,256]{1,0:T(8,128)(2,1)S(1)}, u32[]{:S(2)}, u32[]{:S(2)}) collective-permute-start(bf16[512,256]{1,0:T(8,128)(2,1)} %collective-permute-done.2), channel_id=1, source_target_pairs={{0,1},{1,0},{2,3},{3,2},{4,5},{5,4},{6,7},{7,6},{8,9},{9,8},{10,11... | collective-permute-start | bytes 786440 | tf_op jit(solution)/shard_map/ppermute | solution.py:10
  30.4 3.6 %collective-permute-start.5 = (bf16[512,256]{1,0:T(8,128)(2,1)}, bf16[512,256]{1,0:T(8,128)(2,1)S(1)}, u32[]{:S(2)}, u32[]{:S(2)}) collective-permute-start(bf16[512,256]{1,0:T(8,128)(2,1)} %collective-permute-done.4), channel_id=1, source_target_pairs={{0,1},{1,0},{2,3},{3,2},{4,5},{5,4},{6,7},{7,6},{8,9},{9,8},{10,11... | collective-permute-start | bytes 786440 | tf_op jit(solution)/shard_map/ppermute | solution.py:10
  31.0 4.1 %collective-permute-start.7 = (bf16[512,256]{1,0:T(8,128)(2,1)}, bf16[512,256]{1,0:T(8,128)(2,1)S(1)}, u32[]{:S(2)}, u32[]{:S(2)}) collective-permute-start(bf16[512,256]{1,0:T(8,128)(2,1)} %collective-permute-done.6), channel_id=1, source_target_pairs={{0,1},{1,0},{2,3},{3,2},{4,5},{5,4},{6,7},{7,6},{8,9},{9,8},{10,11... | collective-permute-start | bytes 786440 | tf_op jit(solution)/shard_map/ppermute | solution.py:10
  36.0 1.4 %copy-start.1 = (bf16[4,128,16,128]{3,2,1,0:T(8,128)(2,1)}, bf16[4,128,16,128]{3,2,1,0:T(8,128)(2,1)S(1)}, u32[]{:S(2)}) copy-start(bf16[4,128,16,128]{3,2,1,0:T(8,128)(2,1)S(1)} %bitcast_multiply_fusion) | copy-start | bytes 6291460
  37.4 10.1 %collective-permute-start.12 = (bf16[512,256]{1,0:T(8,128)(2,1)S(1)}, bf16[512,256]{1,0:T(8,128)(2,1)S(1)}, u32[]{:S(2)}, u32[]{:S(2)}) collective-permute-start(bf16[512,256]{1,0:T(8,128)(2,1)S(1)} %fusion.18), channel_id=1, source_target_pairs={{0,24},{8,16},{16,8},{24,0},{1,25},{9,17},{17,9},{25,1},{2,26},{10... | collective-permute-start | bytes 786440 | tf_op jit(solution)/shard_map/ppermute | solution.py:10
  39.9 12.7 %collective-permute-start.11 = (bf16[512,256]{1,0:T(8,128)(2,1)S(1)}, bf16[512,256]{1,0:T(8,128)(2,1)S(1)}, u32[]{:S(2)}, u32[]{:S(2)}) collective-permute-start(bf16[512,256]{1,0:T(8,128)(2,1)S(1)} %fusion.18), channel_id=1, source_target_pairs={{0,16},{8,24},{16,0},{24,8},{1,17},{9,25},{17,1},{25,9},{2,18},{10... | collective-permute-start | bytes 786440 | tf_op jit(solution)/shard_map/ppermute | solution.py:10
  40.4 12.3 %collective-permute-start.10 = (bf16[512,256]{1,0:T(8,128)(2,1)S(1)}, bf16[512,256]{1,0:T(8,128)(2,1)S(1)}, u32[]{:S(2)}, u32[]{:S(2)}) collective-permute-start(bf16[512,256]{1,0:T(8,128)(2,1)S(1)} %fusion.18), channel_id=1, source_target_pairs={{0,8},{8,0},{16,24},{24,16},{1,9},{9,1},{17,25},{25,17},{2,10},{10... | collective-permute-start | bytes 786440 | tf_op jit(solution)/shard_map/ppermute | solution.py:10
  53.5 1.6 %copy-start.2 = (bf16[4,128,16,128]{3,2,1,0:T(8,128)(2,1)S(1)}, bf16[4,128,16,128]{3,2,1,0:T(8,128)(2,1)}, u32[]{:S(2)}) copy-start(bf16[4,128,16,128]{3,2,1,0:T(8,128)(2,1)} %copy-done.1) | copy-start | bytes 6291460

commit v12 on v8

--- a/solution.py
+++ b/solution.py
@@ -28,9 +28,10 @@
 
         col_pieces = [masked] + [_swap(masked, "row", n_row, j) for j in range(1, n_row)]
 
-        late, _ = lax.optimization_barrier((masked, col_pieces[1]))
+        col_pieces = [masked] + [_swap(masked, "row", n_row, j) for j in range(1, n_row)]
 
-        slots = jnp.arange(n_col, dtype=jnp.int32) ^ col_index
+        members = jnp.arange(n_z, dtype=jnp.int32) * 2
+        slots = jnp.concatenate([members, members + 1]) ^ col_index
         sub_index = ((slots // ratio) ^ row_index) * ratio + slots % ratio
 
         def in_slot_order(pieces):
@@ -45,18 +46,12 @@
         previous = None
         for w in range(waves):
             part = masked[w * half:(w + 1) * half]
-            early = late[w * half:(w + 1) * half]
             if previous is not None:
                 part, _ = lax.optimization_barrier((part, previous))
-                early = part
-            pieces = [None] * n_col
-            pieces[0] = part
-            pieces[1] = _swap(early, "col", n_col, 1)
-            for k in range(1, n_z):
-                piece = _swap(early if k == 1 else part, "col", n_col, 2 * k)
-                pieces[2 * k] = piece
-                pieces[2 * k + 1] = _swap(piece, "col", n_col, 1)
-            row_cat = jnp.concatenate(pieces, axis=1)
+            own = jnp.concatenate(
+                [part] + [_swap(part, "col", n_col, 2 * k) for k in range(1, n_z)], axis=1
+            )
+            row_cat = jnp.concatenate([own, _swap(own, "col", n_col, 1)], axis=1)
             row_cats.append(row_cat)
             if col_slot is None:
                 col_slot = in_slot_order(col_pieces)

time: 66.3 us -> 61.5 us (0.928)
  the two profiles are of different devices: /device:TPU:16 before, /device:TPU:0 now
where the time goes in v12:
time: 61.5 us; the launch traced here: 61.2 us
  waiting for transfers between devices  25.5 us (41%)
  starting transfers between devices  22.2 us (36%)
  local copies, waits for them, and re-layouts  7.08 us (12%)
  other arithmetic  4.39 us (7%)
  matrix products  1.76 us (3%)
    ppermute x16, waiting for transfers between devices, _swap(): return lax.ppermute(x, axis, [(i, i ^ d) for i in range(size)])  25.5 us
    ppermute x16, starting transfers between devices, _swap(): return lax.ppermute(x, axis, [(i, i ^ d) for i in range(size)])  22.2 us
    gather x2, local copies, waits for them, and re-layouts, in_slot_order(): return jnp.take(stacked, sub_index, axis=0).reshape(n_col * cols, cols)  2.45 us
    broadcast_in_dim x8, local copies, waits for them, and re-layouts, body(): local_mask = jnp.repeat(jnp.repeat(local_blocks, B, axis=0), B, axis=1)  1.92 us
    another operation x6, other arithmetic, in_slot_order(): stacked = jnp.stack(pieces).reshape(n_row * ratio, cols, cols)  1.33 us
  transfers between devices with their start and end apart: 16, of which 7 were waited for; matrix products, arithmetic and copies ran while one was open for 6% of the time, Pallas kernels for 0%

profile of v12, /device:TPU:0, one launch (start us, length us, event | category | flops | bytes accessed | tf_op | source)
XLA Modules:
  0.0 61.2 jit_solution(9883784184544347342)
XLA Ops:
  0.0 0.8 %dynamic-slice_convert_fusion = (bf16[4,2]{1,0:T(4,128)(2,1)S(1)}, f32[4,2]{1,0:T(4,128)S(1)}) fusion(s32[16,16]{1,0:T(8,128)} %param.5, s32[]{:T(128)S(6)} %select_n.24, s32[]{:T(128)S(6)} %select_n.25), kind=kLoop, calls=%fused_computation.38 | loop fusion | flops 16 | bytes 88 | tf_op jit(solution)/shard_map/convert_element_type | solution.py:27
  0.8 0.0 copy-start
  0.8 0.6 broadcast_in_dim.30
  1.4 0.3 copy-done
  1.8 3.1 %collective-permute-start = (bf16[256,256]{1,0:T(8,128)(2,1)S(1)}, bf16[256,256]{1,0:T(8,128)(2,1)S(1)}, u32[]{:S(2)}, u32[]{:S(2)}) collective-permute-start(bf16[256,256]{1,0:T(8,128)(2,1)S(1)} %get-tuple-element.12), channel_id=1, source_target_pairs={{0,2},{1,3},{2,0},{3,1},{4,6},{5,7},{6,4},{7,5},{8,10},{9,11},{10,... | collective-permute-start | bytes 393224 | tf_op jit(solution)/shard_map/ppermute | solution.py:10
  4.9 2.6 %collective-permute-start.1 = (bf16[256,256]{1,0:T(8,128)(2,1)S(1)}, bf16[256,256]{1,0:T(8,128)(2,1)S(1)}, u32[]{:S(2)}, u32[]{:S(2)}) collective-permute-start(bf16[256,256]{1,0:T(8,128)(2,1)S(1)} %get-tuple-element.12), channel_id=1, source_target_pairs={{0,4},{1,5},{2,6},{3,7},{4,0},{5,1},{6,2},{7,3},{8,12},{9,13},{10,... | collective-permute-start | bytes 393224 | tf_op jit(solution)/shard_map/ppermute | solution.py:10
  7.5 0.0 collective-permute-start.2
  7.5 1.7 %collective-permute-start.4 = (bf16[512,256]{1,0:T(8,128)(2,1)S(1)}, bf16[512,256]{1,0:T(8,128)(2,1)S(1)}, u32[]{:S(2)}, u32[]{:S(2)}) collective-permute-start(bf16[512,256]{1,0:T(8,128)(2,1)S(1)} %bitcast_multiply_fusion.1), channel_id=1, source_target_pairs={{0,8},{8,0},{16,24},{24,16},{1,9},{9,1},{17,25},{25,17},{2,10},{10... | collective-permute-start | bytes 786440 | tf_op jit(solution)/shard_map/ppermute | solution.py:10
  9.2 1.5 %collective-permute-start.5 = (bf16[512,256]{1,0:T(8,128)(2,1)S(1)}, bf16[512,256]{1,0:T(8,128)(2,1)S(1)}, u32[]{:S(2)}, u32[]{:S(2)}) collective-permute-start(bf16[512,256]{1,0:T(8,128)(2,1)S(1)} %bitcast_multiply_fusion.1), channel_id=1, source_target_pairs={{0,16},{8,24},{16,0},{24,8},{1,17},{9,25},{17,1},{25,9},{2,18},{10... | collective-permute-start | bytes 786440 | tf_op jit(solution)/shard_map/ppermute | solution.py:10
  10.7 0.5 fusion.5
  11.2 0.1 compare_and_fusion
  11.3 0.0 collective-permute-done
  11.4 1.2 %collective-permute-start.6 = (bf16[512,256]{1,0:T(8,128)(2,1)S(1)}, bf16[512,256]{1,0:T(8,128)(2,1)S(1)}, u32[]{:S(2)}, u32[]{:S(2)}) collective-permute-start(bf16[512,256]{1,0:T(8,128)(2,1)S(1)} %bitcast_multiply_fusion.1), channel_id=1, source_target_pairs={{0,24},{8,16},{16,8},{24,0},{1,25},{9,17},{17,9},{25,1},{2,26},{10... | collective-permute-start | bytes 786440 | tf_op jit(solution)/shard_map/ppermute | solution.py:10
  12.6 5.2 %collective-permute-done.1 = bf16[256,256]{1,0:T(8,128)(2,1)S(1)} collective-permute-done((bf16[256,256]{1,0:T(8,128)(2,1)S(1)}, bf16[256,256]{1,0:T(8,128)(2,1)S(1)}, u32[]{:S(2)}, u32[]{:S(2)}) %collective-permute-start.1) | collective-permute-done | bytes 131104 | tf_op jit(solution)/shard_map/ppermute | solution.py:10
  17.8 0.0 collective-permute-done.2
  17.8 0.9 %pad_maximum_fusion.2 = bf16[256,1024]{1,0:T(8,128)(2,1)} fusion(bf16[256,256]{1,0:T(8,128)(2,1)S(1)} %collective-permute-done.2, bf16[256,256]{1,0:T(8,128)(2,1)S(1)} %collective-permute-done.1, bf16[256,256]{1,0:T(8,128)(2,1)S(1)} %collective-permute-done, bf16[256,256]{1,0:T(8,128)(2,1)S(1)} %get-tuple-element.12), kind=kLoop, calls=%fused_computation.11 | loop fusion | flops 2097152 | bytes 1048576 | tf_op jit(solution)/shard_map/concatenate | solution.py:51
  18.7 0.0 collective-permute-start.3
  18.7 0.0 collective-permute-done.4
  18.7 3.1 %collective-permute-done.5 = bf16[512,256]{1,0:T(8,128)(2,1)S(1)} collective-permute-done((bf16[512,256]{1,0:T(8,128)(2,1)S(1)}, bf16[512,256]{1,0:T(8,128)(2,1)S(1)}, u32[]{:S(2)}, u32[]{:S(2)}) %collective-permute-start.5) | collective-permute-done | bytes 262176 | tf_op jit(solution)/shard_map/ppermute | solution.py:10
  21.8 0.0 collective-permute-done.6
  21.8 0.1 pad_maximum_fusion
  21.9 0.6 %gather_fusion = bf16[8,256,256]{2,1,0:T(8,128)(2,1)S(1)} fusion(bf16[8,256,256]{2,1,0:T(8,128)(2,1)S(1)} %bitcast.51, s32[1024]{0:T(1024)S(1)} %pad_clamp_fusion), kind=kCustom, calls=%fused_computation.clone | custom fusion | bytes 2097184 | tf_op jit(solution)/shard_map/jit(_take)/gather | solution.py:39
  22.5 0.2 broadcast_select_fusion
  22.7 0.0 collective-permute-done.3
  22.7 1.1 %constant_dynamic-update-slice_fusion = bf16[256,2048]{1,0:T(8,128)(2,1)S(1)} fusion(bf16[256,2048]{1,0:T(8,128)(2,1)S(1)} %constant_dynamic-update-slice_fusion.1, bf16[256,1024]{1,0:T(8,128)(2,1)} %collective-permute-done.3), kind=kLoop, calls=%fused_computation.23 | loop fusion | bytes 1048576 | tf_op jit(solution)/shard_map/concatenate | solution.py:54
  23.8 0.0 copy-start.1
  23.8 0.6 %copy-done.1 = f32[2,2]{1,0:T(2,128)S(1)} copy-done((f32[2,2]{1,0:T(2,128)S(1)}, f32[2,2]{1,0:T(2,128)}, u32[]{:S(2)}) %copy-start.1) | copy-done | bytes 40
  24.5 0.3 broadcast_in_dim.32
  24.8 0.4 fusion
  25.2 0.7 %collective-permute-start.7 = (bf16[256,256]{1,0:T(8,128)(2,1)S(1)}, bf16[256,256]{1,0:T(8,128)(2,1)S(1)}, u32[]{:S(2)}, u32[]{:S(2)}) collective-permute-start(bf16[256,256]{1,0:T(8,128)(2,1)S(1)} %get-tuple-element.7), channel_id=1, source_target_pairs={{0,2},{1,3},{2,0},{3,1},{4,6},{5,7},{6,4},{7,5},{8,10},{9,11},{10,... | collective-permute-start | bytes 393224 | tf_op jit(solution)/shard_map/ppermute | solution.py:10
  25.9 3.5 %collective-permute-start.8 = (bf16[256,256]{1,0:T(8,128)(2,1)S(1)}, bf16[256,256]{1,0:T(8,128)(2,1)S(1)}, u32[]{:S(2)}, u32[]{:S(2)}) collective-permute-start(bf16[256,256]{1,0:T(8,128)(2,1)S(1)} %get-tuple-element.7), channel_id=1, source_target_pairs={{0,4},{1,5},{2,6},{3,7},{4,0},{5,1},{6,2},{7,3},{8,12},{9,13},{10,... | collective-permute-start | bytes 393224 | tf_op jit(solution)/shard_map/ppermute | solution.py:10
  29.4 0.3 collective-permute-start.9
  29.7 1.2 %collective-permute-start.11 = (bf16[1,256,256]{2,1,0:T(8,128)(2,1)S(1)}, bf16[1,256,256]{2,1,0:T(8,128)(2,1)S(1)}, u32[]{:S(2)}, u32[]{:S(2)}) collective-permute-start(bf16[1,256,256]{2,1,0:T(8,128)(2,1)S(1)} %bitcast.54), channel_id=1, source_target_pairs={{0,8},{8,0},{16,24},{24,16},{1,9},{9,1},{17,25},{25,17},{2,10},{10... | collective-permute-start | bytes 393224 | tf_op jit(solution)/shard_map/ppermute | solution.py:10
  30.9 0.9 %collective-permute-done.7 = bf16[256,256]{1,0:T(8,128)(2,1)S(1)} collective-permute-done((bf16[256,256]{1,0:T(8,128)(2,1)S(1)}, bf16[256,256]{1,0:T(8,128)(2,1)S(1)}, u32[]{:S(2)}, u32[]{:S(2)}) %collective-permute-start.7) | collective-permute-done | bytes 131104 | tf_op jit(solution)/shard_map/ppermute | solution.py:10
  31.8 6.8 %collective-permute-done.8 = bf16[256,256]{1,0:T(8,128)(2,1)S(1)} collective-permute-done((bf16[256,256]{1,0:T(8,128)(2,1)S(1)}, bf16[256,256]{1,0:T(8,128)(2,1)S(1)}, u32[]{:S(2)}, u32[]{:S(2)}) %collective-permute-start.8) | collective-permute-done | bytes 131104 | tf_op jit(solution)/shard_map/ppermute | solution.py:10
  38.6 0.0 collective-permute-done.9
  38.6 0.1 pad_maximum_fusion.3
  38.7 0.1 collective-permute-start.10
  38.8 0.0 collective-permute-done.11
  38.9 1.6 %collective-permute-start.13 = (bf16[2,256,256]{2,1,0:T(8,128)(2,1)S(1)}, bf16[2,256,256]{2,1,0:T(8,128)(2,1)S(1)}, u32[]{:S(2)}, u32[]{:S(2)}) collective-permute-start(bf16[2,256,256]{2,1,0:T(8,128)(2,1)S(1)} %pad_maximum_fusion.4), channel_id=1, source_target_pairs={{0,16},{8,24},{16,0},{24,8},{1,17},{9,25},{17,1},{25,9},{2,18},{10... | collective-permute-start | bytes 786440 | tf_op jit(solution)/shard_map/ppermute | solution.py:10
  40.5 0.2 collective-permute-done.10
  40.7 0.3 broadcast_in_dim.34
  41.1 0.4 fusion.1
  41.5 1.6 %collective-permute-start.12 = (bf16[256,256]{1,0:T(8,128)(2,1)S(1)}, bf16[256,256]{1,0:T(8,128)(2,1)S(1)}, u32[]{:S(2)}, u32[]{:S(2)}) collective-permute-start(bf16[256,256]{1,0:T(8,128)(2,1)S(1)} %fusion.1), channel_id=1, source_target_pairs={{0,8},{8,0},{16,24},{24,16},{1,9},{9,1},{17,25},{25,17},{2,10},{10... | collective-permute-start | bytes 393224 | tf_op jit(solution)/shard_map/ppermute | solution.py:10
  43.1 4.5 %collective-permute-done.13 = bf16[2,256,256]{2,1,0:T(8,128)(2,1)S(1)} collective-permute-done((bf16[2,256,256]{2,1,0:T(8,128)(2,1)S(1)}, bf16[2,256,256]{2,1,0:T(8,128)(2,1)S(1)}, u32[]{:S(2)}, u32[]{:S(2)}) %collective-permute-start.13) | collective-permute-done | bytes 262176 | tf_op jit(solution)/shard_map/ppermute | solution.py:10
  47.6 1.6 %collective-permute-start.14 = (bf16[256,256]{1,0:T(8,128)(2,1)S(1)}, bf16[256,256]{1,0:T(8,128)(2,1)S(1)}, u32[]{:S(2)}, u32[]{:S(2)}) collective-permute-start(bf16[256,256]{1,0:T(8,128)(2,1)S(1)} %fusion.1), channel_id=1, source_target_pairs={{0,16},{8,24},{16,0},{24,8},{1,17},{9,25},{17,1},{25,9},{2,18},{10... | collective-permute-start | bytes 393224 | tf_op jit(solution)/shard_map/ppermute | solution.py:10
  49.2 1.5 %collective-permute-start.15 = (bf16[256,256]{1,0:T(8,128)(2,1)S(1)}, bf16[256,256]{1,0:T(8,128)(2,1)S(1)}, u32[]{:S(2)}, u32[]{:S(2)}) collective-permute-start(bf16[256,256]{1,0:T(8,128)(2,1)S(1)} %fusion.1), channel_id=1, source_target_pairs={{0,24},{8,16},{16,8},{24,0},{1,25},{9,17},{17,9},{25,1},{2,26},{10... | collective-permute-start | bytes 393224 | tf_op jit(solution)/shard_map/ppermute | solution.py:10
  50.8 0.0 collective-permute-done.12
  50.8 4.8 %collective-permute-done.14 = bf16[256,256]{1,0:T(8,128)(2,1)S(1)} collective-permute-done((bf16[256,256]{1,0:T(8,128)(2,1)S(1)}, bf16[256,256]{1,0:T(8,128)(2,1)S(1)}, u32[]{:S(2)}, u32[]{:S(2)}) %collective-permute-start.14) | collective-permute-done | bytes 131104 | tf_op jit(solution)/shard_map/ppermute | solution.py:10
  55.6 0.0 collective-permute-done.15
  55.7 1.1 %pad_maximum_fusion.1 = bf16[4,512,256]{2,1,0:T(8,128)(2,1)} fusion(bf16[1,512,256]{2,1,0:T(8,128)(2,1)S(1)} %maximum_bitcast_fusion.3, bf16[1,512,256]{2,1,0:T(8,128)(2,1)S(1)} %maximum_bitcast_fusion.2, bf16[1,512,256]{2,1,0:T(8,128)(2,1)S(1)} %maximum_bitcast_fusion.1, bf16[1,512,256]{2,1,0:T(8,128)(2,1)S(1)} %maximum_bitcast_fusion), kind=kLoop, calls=%fused_computation.7 | loop fusion | flops 1572864 | bytes 2097152 | tf_op jit(solution)/shard_map/stack | solution.py:38
  56.8 1.8 %gather_fusion.1 = bf16[8,256,256]{2,1,0:T(8,128)(2,1)S(1)} fusion(bf16[8,256,256]{2,1,0:T(8,128)(2,1)} %bitcast.50, s32[1024]{0:T(1024)S(1)} %pad_clamp_fusion), kind=kCustom, calls=%fused_computation.1.clone | custom fusion | bytes 2097184 | tf_op jit(solution)/shard_map/jit(_take)/gather | solution.py:39
  58.7 0.2 broadcast_select_fusion.1
  58.8 0.4 fusion.6
  59.3 0.4 fusion.7
  59.7 0.6 broadcast_in_dim.28
  60.3 0.9 %bitcast_multiply_fusion = f32[512,256]{1,0:T(8,128)} fusion(f32[64,8,2,128]{3,2,1,0:T(2,128)S(1)} %bitcast.53, f32[256,256]{1,0:T(8,128)S(1)} %fusion.7, f32[256,256]{1,0:T(8,128)S(1)} %fusion.6, bf16[512,256]{1,0:T(8,128)(2,1)S(1)} %bitcast_multiply_fusion.1), kind=kLoop, calls=%fused_computation.10 | loop fusion | flops 786432 | bytes 1835008 | tf_op jit(solution)/shard_map/mul | solution.py:79
  (22 shorter events, 0.4 us)
Async XLA Ops:
  0.8 0.9 %copy-start = (bf16[512,256]{1,0:T(8,128)(2,1)S(1)}, bf16[512,256]{1,0:T(8,128)(2,1)}, u32[]{:S(2)}) copy-start(bf16[512,256]{1,0:T(8,128)(2,1)} %param.4) | copy-start | bytes 786436
  1.8 9.6 %collective-permute-start = (bf16[256,256]{1,0:T(8,128)(2,1)S(1)}, bf16[256,256]{1,0:T(8,128)(2,1)S(1)}, u32[]{:S(2)}, u32[]{:S(2)}) collective-permute-start(bf16[256,256]{1,0:T(8,128)(2,1)S(1)} %get-tuple-element.12), channel_id=1, source_target_pairs={{0,2},{1,3},{2,0},{3,1},{4,6},{5,7},{6,4},{7,5},{8,10},{9,11},{10,... | collective-permute-start | bytes 393224 | tf_op jit(solution)/shard_map/ppermute | solution.py:10
  4.9 12.9 %collective-permute-start.1 = (bf16[256,256]{1,0:T(8,128)(2,1)S(1)}, bf16[256,256]{1,0:T(8,128)(2,1)S(1)}, u32[]{:S(2)}, u32[]{:S(2)}) collective-permute-start(bf16[256,256]{1,0:T(8,128)(2,1)S(1)} %get-tuple-element.12), channel_id=1, source_target_pairs={{0,4},{1,5},{2,6},{3,7},{4,0},{5,1},{6,2},{7,3},{8,12},{9,13},{10,... | collective-permute-start | bytes 393224 | tf_op jit(solution)/shard_map/ppermute | solution.py:10
  7.5 10.3 %collective-permute-start.2 = (bf16[256,256]{1,0:T(8,128)(2,1)S(1)}, bf16[256,256]{1,0:T(8,128)(2,1)S(1)}, u32[]{:S(2)}, u32[]{:S(2)}) collective-permute-start(bf16[256,256]{1,0:T(8,128)(2,1)S(1)} %get-tuple-element.12), channel_id=1, source_target_pairs={{0,6},{1,7},{2,4},{3,5},{4,2},{5,3},{6,0},{7,1},{8,14},{9,15},{10,... | collective-permute-start | bytes 393224 | tf_op jit(solution)/shard_map/ppermute | solution.py:10
  7.5 11.3 %collective-permute-start.4 = (bf16[512,256]{1,0:T(8,128)(2,1)S(1)}, bf16[512,256]{1,0:T(8,128)(2,1)S(1)}, u32[]{:S(2)}, u32[]{:S(2)}) collective-permute-start(bf16[512,256]{1,0:T(8,128)(2,1)S(1)} %bitcast_multiply_fusion.1), channel_id=1, source_target_pairs={{0,8},{8,0},{16,24},{24,16},{1,9},{9,1},{17,25},{25,17},{2,10},{10... | collective-permute-start | bytes 786440 | tf_op jit(solution)/shard_map/ppermute | solution.py:10
  9.2 12.6 %collective-permute-start.5 = (bf16[512,256]{1,0:T(8,128)(2,1)S(1)}, bf16[512,256]{1,0:T(8,128)(2,1)S(1)}, u32[]{:S(2)}, u32[]{:S(2)}) collective-permute-start(bf16[512,256]{1,0:T(8,128)(2,1)S(1)} %bitcast_multiply_fusion.1), channel_id=1, source_target_pairs={{0,16},{8,24},{16,0},{24,8},{1,17},{9,25},{17,1},{25,9},{2,18},{10... | collective-permute-start | bytes 786440 | tf_op jit(solution)/shard_map/ppermute | solution.py:10
  11.4 10.4 %collective-permute-start.6 = (bf16[512,256]{1,0:T(8,128)(2,1)S(1)}, bf16[512,256]{1,0:T(8,128)(2,1)S(1)}, u32[]{:S(2)}, u32[]{:S(2)}) collective-permute-start(bf16[512,256]{1,0:T(8,128)(2,1)S(1)} %bitcast_multiply_fusion.1), channel_id=1, source_target_pairs={{0,24},{8,16},{16,8},{24,0},{1,25},{9,17},{17,9},{25,1},{2,26},{10... | collective-permute-start | bytes 786440 | tf_op jit(solution)/shard_map/ppermute | solution.py:10
  18.7 4.1 %collective-permute-start.3 = (bf16[256,1024]{1,0:T(8,128)(2,1)}, bf16[256,1024]{1,0:T(8,128)(2,1)}, u32[]{:S(2)}, u32[]{:S(2)}) collective-permute-start(bf16[256,1024]{1,0:T(8,128)(2,1)} %pad_maximum_fusion.2), channel_id=1, source_target_pairs={{0,1},{1,0},{2,3},{3,2},{4,5},{5,4},{6,7},{7,6},{8,9},{9,8},{10,11... | collective-permute-start | bytes 1572872 | tf_op jit(solution)/shard_map/ppermute | solution.py:10
  23.8 0.6 %copy-start.1 = (f32[2,2]{1,0:T(2,128)S(1)}, f32[2,2]{1,0:T(2,128)}, u32[]{:S(2)}) copy-start(f32[2,2]{1,0:T(2,128)} %get-tuple-element.18) | copy-start | bytes 52
  25.2 6.6 %collective-permute-start.7 = (bf16[256,256]{1,0:T(8,128)(2,1)S(1)}, bf16[256,256]{1,0:T(8,128)(2,1)S(1)}, u32[]{:S(2)}, u32[]{:S(2)}) collective-permute-start(bf16[256,256]{1,0:T(8,128)(2,1)S(1)} %get-tuple-element.7), channel_id=1, source_target_pairs={{0,2},{1,3},{2,0},{3,1},{4,6},{5,7},{6,4},{7,5},{8,10},{9,11},{10,... | collective-permute-start | bytes 393224 | tf_op jit(solution)/shard_map/ppermute | solution.py:10
  25.9 12.7 %collective-permute-start.8 = (bf16[256,256]{1,0:T(8,128)(2,1)S(1)}, bf16[256,256]{1,0:T(8,128)(2,1)S(1)}, u32[]{:S(2)}, u32[]{:S(2)}) collective-permute-start(bf16[256,256]{1,0:T(8,128)(2,1)S(1)} %get-tuple-element.7), channel_id=1, source_target_pairs={{0,4},{1,5},{2,6},{3,7},{4,0},{5,1},{6,2},{7,3},{8,12},{9,13},{10,... | collective-permute-start | bytes 393224 | tf_op jit(solution)/shard_map/ppermute | solution.py:10
  29.4 9.2 %collective-permute-start.9 = (bf16[256,256]{1,0:T(8,128)(2,1)S(1)}, bf16[256,256]{1,0:T(8,128)(2,1)S(1)}, u32[]{:S(2)}, u32[]{:S(2)}) collective-permute-start(bf16[256,256]{1,0:T(8,128)(2,1)S(1)} %get-tuple-element.7), channel_id=1, source_target_pairs={{0,6},{1,7},{2,4},{3,5},{4,2},{5,3},{6,0},{7,1},{8,14},{9,15},{10,... | collective-permute-start | bytes 393224 | tf_op jit(solution)/shard_map/ppermute | solution.py:10
  29.7 9.1 %collective-permute-start.11 = (bf16[1,256,256]{2,1,0:T(8,128)(2,1)S(1)}, bf16[1,256,256]{2,1,0:T(8,128)(2,1)S(1)}, u32[]{:S(2)}, u32[]{:S(2)}) collective-permute-start(bf16[1,256,256]{2,1,0:T(8,128)(2,1)S(1)} %bitcast.54), channel_id=1, source_target_pairs={{0,8},{8,0},{16,24},{24,16},{1,9},{9,1},{17,25},{25,17},{2,10},{10... | collective-permute-start | bytes 393224 | tf_op jit(solution)/shard_map/ppermute | solution.py:10
  38.7 2.0 %collective-permute-start.10 = (bf16[256,1024]{1,0:T(8,128)(2,1)S(1)}, bf16[256,1024]{1,0:T(8,128)(2,1)S(1)}, u32[]{:S(2)}, u32[]{:S(2)}) collective-permute-start(bf16[256,1024]{1,0:T(8,128)(2,1)S(1)} %pad_maximum_fusion.3), channel_id=1, source_target_pairs={{0,1},{1,0},{2,3},{3,2},{4,5},{5,4},{6,7},{7,6},{8,9},{9,8},{10,11... | collective-permute-start | bytes 1572872 | tf_op jit(solution)/shard_map/ppermute | solution.py:10
  38.9 8.8 %collective-permute-start.13 = (bf16[2,256,256]{2,1,0:T(8,128)(2,1)S(1)}, bf16[2,256,256]{2,1,0:T(8,128)(2,1)S(1)}, u32[]{:S(2)}, u32[]{:S(2)}) collective-permute-start(bf16[2,256,256]{2,1,0:T(8,128)(2,1)S(1)} %pad_maximum_fusion.4), channel_id=1, source_target_pairs={{0,16},{8,24},{16,0},{24,8},{1,17},{9,25},{17,1},{25,9},{2,18},{10... | collective-permute-start | bytes 786440 | tf_op jit(solution)/shard_map/ppermute | solution.py:10
  41.5 9.3 %collective-permute-start.12 = (bf16[256,256]{1,0:T(8,128)(2,1)S(1)}, bf16[256,256]{1,0:T(8,128)(2,1)S(1)}, u32[]{:S(2)}, u32[]{:S(2)}) collective-permute-start(bf16[256,256]{1,0:T(8,128)(2,1)S(1)} %fusion.1), channel_id=1, source_target_pairs={{0,8},{8,0},{16,24},{24,16},{1,9},{9,1},{17,25},{25,17},{2,10},{10... | collective-permute-start | bytes 393224 | tf_op jit(solution)/shard_map/ppermute | solution.py:10
  47.6 8.0 %collective-permute-start.14 = (bf16[256,256]{1,0:T(8,128)(2,1)S(1)}, bf16[256,256]{1,0:T(8,128)(2,1)S(1)}, u32[]{:S(2)}, u32[]{:S(2)}) collective-permute-start(bf16[256,256]{1,0:T(8,128)(2,1)S(1)} %fusion.1), channel_id=1, source_target_pairs={{0,16},{8,24},{16,0},{24,8},{1,17},{9,25},{17,1},{25,9},{2,18},{10... | collective-permute-start | bytes 393224 | tf_op jit(solution)/shard_map/ppermute | solution.py:10
  49.2 6.4 %collective-permute-start.15 = (bf16[256,256]{1,0:T(8,128)(2,1)S(1)}, bf16[256,256]{1,0:T(8,128)(2,1)S(1)}, u32[]{:S(2)}, u32[]{:S(2)}) collective-permute-start(bf16[256,256]{1,0:T(8,128)(2,1)S(1)} %fusion.1), channel_id=1, source_target_pairs={{0,24},{8,16},{16,8},{24,0},{1,25},{9,17},{17,9},{25,1},{2,26},{10... | collective-permute-start | bytes 393224 | tf_op jit(solution)/shard_map/ppermute | solution.py:10

commit v13 on v7

--- a/solution.py
+++ b/solution.py
@@ -49,8 +49,15 @@
         mask_float = local_mask.astype(jnp.float32)
         filtered = (mask_float * square).astype(jnp.bfloat16)
         f_pieces = [filtered] + [_swap(filtered, "row", n_row, k) for k in range(1, n_row)]
-        f_slot = in_slot_order(f_pieces)
-        cubic = jnp.dot(row_cat, f_slot, preferred_element_type=jnp.float32)
+        cubic = None
+        for j, f_piece in enumerate(f_pieces):
+            for h in range(ratio):
+                member = (row_index ^ j) * ratio + h
+                window = lax.dynamic_slice_in_dim(row_cat, (member ^ col_index) * cols, cols, 1)
+                term = jnp.dot(
+                    window, f_piece[h * cols:(h + 1) * cols], preferred_element_type=jnp.float32
+                )
+                cubic = term if cubic is None else cubic + term
         return mask_float * (1.5 * masked.astype(jnp.float32) - 0.5 * cubic)
 
     return body

time: 53.9 us -> 56.2 us (1.043)
  the two profiles are of different devices: /device:TPU:16 before, /device:TPU:0 now
where the time goes in v13:
time: 56.2 us; the launch traced here: 55.8 us
  waiting for transfers between devices  23 us (41%)
  starting transfers between devices  15.7 us (28%)
  matrix products  7.81 us (14%)
  local copies, waits for them, and re-layouts  5.92 us (11%)
  other arithmetic  3.22 us (6%)
    ppermute x13, waiting for transfers between devices, _swap(): return lax.ppermute(x, axis, [(i, i ^ d) for i in range(size)])  23 us
    ppermute x13, starting transfers between devices, _swap(): return lax.ppermute(x, axis, [(i, i ^ d) for i in range(size)])  15.7 us
    dot_general x8, matrix products, body(): jnp.dot(window, f_piece[h * cols:(h + 1) * cols], preferred_element_type=...  6.4 us
    unnamed x8, local copies, waits for them, and re-layouts  3.95 us
    unnamed x1, other arithmetic  1.76 us
    dot_general x1, matrix products, body(): jnp.dot(row_cat, in_slot_order(col_pieces), preferred_element_type=jnp.fl...  1.42 us
    broadcast_in_dim x4, local copies, waits for them, and re-layouts, body(): local_mask = jnp.repeat(jnp.repeat(local_blocks, B, axis=0), B, axis=1)  1.24 us
  transfers between devices with their start and end apart: 13, of which 6 were waited for; matrix products, arithmetic and copies ran while one was open for 17% of the time, Pallas kernels for 0%

profile of v13, /device:TPU:0, one launch (start us, length us, event | category | flops | bytes accessed | tf_op | source)
XLA Modules:
  0.0 55.8 jit_solution(14826085571938905045)
XLA Ops:
  0.0 0.8 %dynamic-slice_convert_fusion.1 = (f32[4,2]{1,0:T(4,128)S(1)}, bf16[4,2]{1,0:T(4,128)(2,1)S(1)}) fusion(s32[16,16]{1,0:T(8,128)} %param.3, s32[]{:T(128)S(6)} %select_n.84, s32[]{:T(128)S(6)} %select_n.85), kind=kLoop, calls=%fused_computation.64 | loop fusion | flops 16 | bytes 88 | tf_op jit(solution)/shard_map/convert_element_type | solution.py:49
  0.8 0.6 %broadcast_in_dim.27 = bf16[512,2,128]{2,1,0:T(2,128)(2,1)S(1)} broadcast(bf16[512,2]{1,0:T(8,128)(2,1)S(1)} %bitcast.27), dimensions={0,1} | broadcast | bytes 264192 | tf_op jit(solution)/shard_map/broadcast_in_dim | solution.py:26
  1.4 1.8 %constant_dynamic-update-slice_fusion.7 = (bf16[512,2048]{1,0:T(8,128)(2,1)}, bf16[512,256]{1,0:T(8,128)(2,1)S(1)}) fusion(bf16[512,256]{1,0:T(8,128)(2,1)} %param.2, bf16[64,8,2,128]{3,2,1,0:T(2,128)(2,1)S(1)} %bitcast.26), kind=kLoop, calls=%fused_computation.46 | loop fusion | flops 524287 | bytes 1048576
  3.2 2.9 %collective-permute-start = (bf16[512,256]{1,0:T(8,128)(2,1)S(1)}, bf16[512,256]{1,0:T(8,128)(2,1)S(1)}, u32[]{:S(2)}, u32[]{:S(2)}) collective-permute-start(bf16[512,256]{1,0:T(8,128)(2,1)S(1)} %get-tuple-element.6), channel_id=1, source_target_pairs={{0,8},{8,0},{16,24},{24,16},{1,9},{9,1},{17,25},{25,17},{2,10},{10... | collective-permute-start | bytes 786440 | tf_op jit(solution)/shard_map/ppermute | solution.py:10
  6.1 2.6 %collective-permute-start.4 = (bf16[512,256]{1,0:T(8,128)(2,1)S(1)}, bf16[512,256]{1,0:T(8,128)(2,1)}, u32[]{:S(2)}, u32[]{:S(2)}) collective-permute-start(bf16[512,256]{1,0:T(8,128)(2,1)S(1)} %get-tuple-element.6), channel_id=1, source_target_pairs={{0,4},{1,5},{2,6},{3,7},{4,0},{5,1},{6,2},{7,3},{8,12},{9,13},{10,... | collective-permute-start | bytes 786440 | tf_op jit(solution)/shard_map/ppermute | solution.py:10
  8.7 1.3 %collective-permute-start.6 = (bf16[512,256]{1,0:T(8,128)(2,1)S(1)}, bf16[512,256]{1,0:T(8,128)(2,1)}, u32[]{:S(2)}, u32[]{:S(2)}) collective-permute-start(bf16[512,256]{1,0:T(8,128)(2,1)S(1)} %get-tuple-element.6), channel_id=1, source_target_pairs={{0,6},{1,7},{2,4},{3,5},{4,2},{5,3},{6,0},{7,1},{8,14},{9,15},{10,... | collective-permute-start | bytes 786440 | tf_op jit(solution)/shard_map/ppermute | solution.py:10
  10.0 1.5 %collective-permute-start.9 = (bf16[512,256]{1,0:T(8,128)(2,1)S(1)}, bf16[512,256]{1,0:T(8,128)(2,1)S(1)}, u32[]{:S(2)}, u32[]{:S(2)}) collective-permute-start(bf16[512,256]{1,0:T(8,128)(2,1)S(1)} %get-tuple-element.6), channel_id=1, source_target_pairs={{0,24},{8,16},{16,8},{24,0},{1,25},{9,17},{17,9},{25,1},{2,26},{10... | collective-permute-start | bytes 786440 | tf_op jit(solution)/shard_map/ppermute | solution.py:10
  11.5 0.5 collective-permute-start.8
  12.0 0.6 %collective-permute-done = bf16[512,256]{1,0:T(8,128)(2,1)S(1)} collective-permute-done((bf16[512,256]{1,0:T(8,128)(2,1)S(1)}, bf16[512,256]{1,0:T(8,128)(2,1)S(1)}, u32[]{:S(2)}, u32[]{:S(2)}) %collective-permute-start) | collective-permute-done | bytes 262176 | tf_op jit(solution)/shard_map/ppermute | solution.py:10
  12.6 2.7 %collective-permute-start.2 = (bf16[512,256]{1,0:T(8,128)(2,1)S(1)}, bf16[512,256]{1,0:T(8,128)(2,1)}, u32[]{:S(2)}, u32[]{:S(2)}) collective-permute-start(bf16[512,256]{1,0:T(8,128)(2,1)S(1)} %get-tuple-element.6), channel_id=1, source_target_pairs={{0,2},{1,3},{2,0},{3,1},{4,6},{5,7},{6,4},{7,5},{8,10},{9,11},{10,... | collective-permute-start | bytes 786440 | tf_op jit(solution)/shard_map/ppermute | solution.py:10
  15.3 0.1 broadcast_in_dim.28
  15.4 3.9 %collective-permute-done.9 = bf16[512,256]{1,0:T(8,128)(2,1)S(1)} collective-permute-done((bf16[512,256]{1,0:T(8,128)(2,1)S(1)}, bf16[512,256]{1,0:T(8,128)(2,1)S(1)}, u32[]{:S(2)}, u32[]{:S(2)}) %collective-permute-start.9) | collective-permute-done | bytes 262176 | tf_op jit(solution)/shard_map/ppermute | solution.py:10
  19.3 0.0 collective-permute-start.1
  19.3 4.6 %collective-permute-done.8 = bf16[512,256]{1,0:T(8,128)(2,1)S(1)} collective-permute-done((bf16[512,256]{1,0:T(8,128)(2,1)S(1)}, bf16[512,256]{1,0:T(8,128)(2,1)S(1)}, u32[]{:S(2)}, u32[]{:S(2)}) %collective-permute-start.8) | collective-permute-done | bytes 262176 | tf_op jit(solution)/shard_map/ppermute | solution.py:10
  23.9 0.1 pad_maximum_fusion
  24.1 0.6 %gather_fusion = bf16[8,256,256]{2,1,0:T(8,128)(2,1)S(1)} fusion(bf16[8,256,256]{2,1,0:T(8,128)(2,1)S(1)} %bitcast.21, s32[1024]{0:T(1024)S(1)} %pad_clamp_fusion), kind=kCustom, calls=%fused_computation | custom fusion | bytes 2097184 | tf_op jit(solution)/shard_map/jit(_take)/gather | solution.py:45
  24.7 0.0 copy-start
  24.7 5.4 %collective-permute-done.2 = bf16[512,256]{1,0:T(8,128)(2,1)} collective-permute-done((bf16[512,256]{1,0:T(8,128)(2,1)S(1)}, bf16[512,256]{1,0:T(8,128)(2,1)}, u32[]{:S(2)}, u32[]{:S(2)}) %collective-permute-start.2) | collective-permute-done | bytes 262176 | tf_op jit(solution)/shard_map/ppermute | solution.py:10
  30.1 0.0 collective-permute-start.3
  30.1 0.5 bitcast_select_fusion
  30.7 0.0 collective-permute-done.4
  30.7 0.6 %collective-permute-start.5 = (bf16[512,256]{1,0:T(8,128)(2,1)}, bf16[512,256]{1,0:T(8,128)(2,1)S(1)}, u32[]{:S(2)}, u32[]{:S(2)}) collective-permute-start(bf16[512,256]{1,0:T(8,128)(2,1)} %collective-permute-done.4), channel_id=1, source_target_pairs={{0,1},{1,0},{2,3},{3,2},{4,5},{5,4},{6,7},{7,6},{8,9},{9,8},{10,11... | collective-permute-start | bytes 786440 | tf_op jit(solution)/shard_map/ppermute | solution.py:10
  31.2 0.0 collective-permute-done.6
  31.2 0.1 collective-permute-start.7
  31.3 0.0 collective-permute-done.1
  31.3 0.0 copy-done
  31.3 1.0 %constant_dynamic-update-slice_fusion.6 = bf16[512,2048]{1,0:T(8,128)(2,1)S(1)} fusion(bf16[512,2048]{1,0:T(8,128)(2,1)S(1)} %copy-done, bf16[512,256]{1,0:T(8,128)(2,1)} %collective-permute-done.1), kind=kLoop, calls=%fused_computation.45 | loop fusion | bytes 524288
  32.3 1.0 %constant_dynamic-update-slice_fusion.5 = bf16[512,2048]{1,0:T(8,128)(2,1)S(1)} fusion(bf16[512,2048]{1,0:T(8,128)(2,1)S(1)} %constant_dynamic-update-slice_fusion.6, bf16[512,256]{1,0:T(8,128)(2,1)} %collective-permute-done.2), kind=kLoop, calls=%fused_computation.44 | loop fusion | bytes 524288
  33.3 0.0 collective-permute-done.3
  33.3 1.0 %constant_dynamic-update-slice_fusion.3 = bf16[512,2048]{1,0:T(8,128)(2,1)S(1)} fusion(bf16[512,2048]{1,0:T(8,128)(2,1)S(1)} %constant_dynamic-update-slice_fusion.4, bf16[512,256]{1,0:T(8,128)(2,1)} %collective-permute-done.4), kind=kLoop, calls=%fused_computation.42 | loop fusion | bytes 524288
  34.3 0.0 collective-permute-done.5
  34.4 1.0 %constant_dynamic-update-slice_fusion.1 = bf16[512,2048]{1,0:T(8,128)(2,1)S(1)} fusion(bf16[512,2048]{1,0:T(8,128)(2,1)S(1)} %constant_dynamic-update-slice_fusion.2, bf16[512,256]{1,0:T(8,128)(2,1)} %collective-permute-done.6), kind=kLoop, calls=%fused_computation.40 | loop fusion | bytes 524288
  35.4 0.0 collective-permute-done.7
  35.4 0.6 %broadcast_in_dim.25 = f32[512,2,128]{2,1,0:T(2,128)S(1)} broadcast(f32[512,2]{1,0:T(8,128)S(1)} %bitcast.25), dimensions={0,1} | broadcast | bytes 528384 | tf_op jit(solution)/shard_map/broadcast_in_dim | solution.py:26
  36.0 1.4 %fusion.9 = bf16[512,256]{1,0:T(8,128)(2,1)} fusion(bf16[512,2048]{1,0:T(8,128)(2,1)S(1)} %constant_dynamic-update-slice_fusion, bf16[2048,256]{1,0:T(8,128)(2,1)S(1)} %bitcast_select_fusion, f32[64,8,2,128]{3,2,1,0:T(2,128)S(1)} %bitcast.23), kind=kOutput, calls=%fused_computation.12 | convolution fusion | flops 537133056 | bytes 3932160 | tf_op jit(solution)/shard_map/dot_general | solution.py:48
  37.4 2.0 %collective-permute-start.12 = (bf16[512,256]{1,0:T(8,128)(2,1)}, bf16[512,256]{1,0:T(8,128)(2,1)}, u32[]{:S(2)}, u32[]{:S(2)}) collective-permute-start(bf16[512,256]{1,0:T(8,128)(2,1)} %fusion.9), channel_id=1, source_target_pairs={{0,24},{8,16},{16,8},{24,0},{1,25},{9,17},{17,9},{25,1},{2,26},{10... | collective-permute-start | bytes 786440 | tf_op jit(solution)/shard_map/ppermute | solution.py:10
  39.5 0.5 collective-permute-start.11
  40.0 1.0 %collective-permute-start.10 = (bf16[512,256]{1,0:T(8,128)(2,1)}, bf16[512,256]{1,0:T(8,128)(2,1)S(1)}, u32[]{:S(2)}, u32[]{:S(2)}) collective-permute-start(bf16[512,256]{1,0:T(8,128)(2,1)} %fusion.9), channel_id=1, source_target_pairs={{0,8},{8,0},{16,24},{24,16},{1,9},{9,1},{17,25},{25,17},{2,10},{10... | collective-permute-start | bytes 786440 | tf_op jit(solution)/shard_map/ppermute | solution.py:10
  40.9 1.2 %fusion.22 = f32[512,256]{1,0:T(8,128)S(1)} fusion(bf16[512,2048]{1,0:T(8,128)(2,1)S(1)} %constant_dynamic-update-slice_fusion, s32[]{:T(128)S(6)} %select_n.94, bf16[512,256]{1,0:T(8,128)(2,1)} %fusion.9), kind=kOutput, calls=%fused_computation.28 | convolution fusion | flops 67108864 | bytes 917508 | tf_op jit(solution)/shard_map/dot_general | solution.py:57
  42.1 5.7 %collective-permute-done.12 = bf16[512,256]{1,0:T(8,128)(2,1)} collective-permute-done((bf16[512,256]{1,0:T(8,128)(2,1)}, bf16[512,256]{1,0:T(8,128)(2,1)}, u32[]{:S(2)}, u32[]{:S(2)}) %collective-permute-start.12) | collective-permute-done | bytes 262176 | tf_op jit(solution)/shard_map/ppermute | solution.py:10
  47.8 1.1 %fusion.10 = f32[512,256]{1,0:T(8,128)S(1)} fusion(bf16[512,2048]{1,0:T(8,128)(2,1)S(1)} %constant_dynamic-update-slice_fusion, s32[]{:T(128)S(6)} %select_n.100, bf16[512,256]{1,0:T(8,128)(2,1)} %collective-permute-done.12), kind=kOutput, calls=%fused_computation.16 | convolution fusion | flops 67108864 | bytes 917508 | tf_op jit(solution)/shard_map/dot_general | solution.py:57
  48.9 1.1 %fusion.12 = f32[512,256]{1,0:T(8,128)S(1)} fusion(bf16[512,2048]{1,0:T(8,128)(2,1)S(1)} %constant_dynamic-update-slice_fusion, s32[]{:T(128)S(6)} %select_n.99, bf16[512,256]{1,0:T(8,128)(2,1)} %collective-permute-done.12), kind=kOutput, calls=%fused_computation.18 | convolution fusion | flops 67108864 | bytes 917508 | tf_op jit(solution)/shard_map/dot_general | solution.py:57
  50.1 2.7 %collective-permute-done.11 = bf16[512,256]{1,0:T(8,128)(2,1)S(1)} collective-permute-done((bf16[512,256]{1,0:T(8,128)(2,1)}, bf16[512,256]{1,0:T(8,128)(2,1)S(1)}, u32[]{:S(2)}, u32[]{:S(2)}) %collective-permute-start.11) | collective-permute-done | bytes 262176 | tf_op jit(solution)/shard_map/ppermute | solution.py:10
  52.8 0.2 fusion.14
  53.0 0.2 fusion.16
  53.3 0.0 collective-permute-done.10
  53.3 0.2 fusion.18
  53.5 0.2 fusion.20
  53.8 2.1 %fusion.8 = f32[512,256]{1,0:T(8,128)} fusion(f32[512,256]{1,0:T(8,128)S(1)} %fusion.10, f32[512,256]{1,0:T(8,128)S(1)} %fusion.12, f32[512,256]{1,0:T(8,128)S(1)} %fusion.14, f32[512,256]{1,0:T(8,128)S(1)} %fusion.16, f32[512,256]{1,0:T(8,128)S(1)} %fusion.18, f32[512,256]{1,0:T(8,128)S(1)} %fusion.20, f32[512,256]{1,0:T(8,128)S(1)} %fusion.22, ...), kind=kOutput, calls=%fused_computation.11 | convolution fusion | flops 68681728 | bytes 5373956 | tf_op jit(solution)/shard_map/dot_general | solution.py:57
  (9 shorter events, 0.2 us)
Async XLA Ops:
  3.2 9.5 %collective-permute-start = (bf16[512,256]{1,0:T(8,128)(2,1)S(1)}, bf16[512,256]{1,0:T(8,128)(2,1)S(1)}, u32[]{:S(2)}, u32[]{:S(2)}) collective-permute-start(bf16[512,256]{1,0:T(8,128)(2,1)S(1)} %get-tuple-element.6), channel_id=1, source_target_pairs={{0,8},{8,0},{16,24},{24,16},{1,9},{9,1},{17,25},{25,17},{2,10},{10... | collective-permute-start | bytes 786440 | tf_op jit(solution)/shard_map/ppermute | solution.py:10
  6.1 24.6 %collective-permute-start.4 = (bf16[512,256]{1,0:T(8,128)(2,1)S(1)}, bf16[512,256]{1,0:T(8,128)(2,1)}, u32[]{:S(2)}, u32[]{:S(2)}) collective-permute-start(bf16[512,256]{1,0:T(8,128)(2,1)S(1)} %get-tuple-element.6), channel_id=1, source_target_pairs={{0,4},{1,5},{2,6},{3,7},{4,0},{5,1},{6,2},{7,3},{8,12},{9,13},{10,... | collective-permute-start | bytes 786440 | tf_op jit(solution)/shard_map/ppermute | solution.py:10
  8.7 22.6 %collective-permute-start.6 = (bf16[512,256]{1,0:T(8,128)(2,1)S(1)}, bf16[512,256]{1,0:T(8,128)(2,1)}, u32[]{:S(2)}, u32[]{:S(2)}) collective-permute-start(bf16[512,256]{1,0:T(8,128)(2,1)S(1)} %get-tuple-element.6), channel_id=1, source_target_pairs={{0,6},{1,7},{2,4},{3,5},{4,2},{5,3},{6,0},{7,1},{8,14},{9,15},{10,... | collective-permute-start | bytes 786440 | tf_op jit(solution)/shard_map/ppermute | solution.py:10
  10.0 9.3 %collective-permute-start.9 = (bf16[512,256]{1,0:T(8,128)(2,1)S(1)}, bf16[512,256]{1,0:T(8,128)(2,1)S(1)}, u32[]{:S(2)}, u32[]{:S(2)}) collective-permute-start(bf16[512,256]{1,0:T(8,128)(2,1)S(1)} %get-tuple-element.6), channel_id=1, source_target_pairs={{0,24},{8,16},{16,8},{24,0},{1,25},{9,17},{17,9},{25,1},{2,26},{10... | collective-permute-start | bytes 786440 | tf_op jit(solution)/shard_map/ppermute | solution.py:10
  11.5 12.4 %collective-permute-start.8 = (bf16[512,256]{1,0:T(8,128)(2,1)S(1)}, bf16[512,256]{1,0:T(8,128)(2,1)S(1)}, u32[]{:S(2)}, u32[]{:S(2)}) collective-permute-start(bf16[512,256]{1,0:T(8,128)(2,1)S(1)} %get-tuple-element.6), channel_id=1, source_target_pairs={{0,16},{8,24},{16,0},{24,8},{1,17},{9,25},{17,1},{25,9},{2,18},{10... | collective-permute-start | bytes 786440 | tf_op jit(solution)/shard_map/ppermute | solution.py:10
  12.6 17.5 %collective-permute-start.2 = (bf16[512,256]{1,0:T(8,128)(2,1)S(1)}, bf16[512,256]{1,0:T(8,128)(2,1)}, u32[]{:S(2)}, u32[]{:S(2)}) collective-permute-start(bf16[512,256]{1,0:T(8,128)(2,1)S(1)} %get-tuple-element.6), channel_id=1, source_target_pairs={{0,2},{1,3},{2,0},{3,1},{4,6},{5,7},{6,4},{7,5},{8,10},{9,11},{10,... | collective-permute-start | bytes 786440 | tf_op jit(solution)/shard_map/ppermute | solution.py:10
  19.3 12.0 %collective-permute-start.1 = (bf16[512,256]{1,0:T(8,128)(2,1)S(1)}, bf16[512,256]{1,0:T(8,128)(2,1)}, u32[]{:S(2)}, u32[]{:S(2)}) collective-permute-start(bf16[512,256]{1,0:T(8,128)(2,1)S(1)} %get-tuple-element.6), channel_id=1, source_target_pairs={{0,1},{1,0},{2,3},{3,2},{4,5},{5,4},{6,7},{7,6},{8,9},{9,8},{10,11... | collective-permute-start | bytes 786440 | tf_op jit(solution)/shard_map/ppermute | solution.py:10
  24.7 6.6 %copy-start = (bf16[512,2048]{1,0:T(8,128)(2,1)S(1)}, bf16[512,2048]{1,0:T(8,128)(2,1)}, u32[]{:S(2)}) copy-start(bf16[512,2048]{1,0:T(8,128)(2,1)} %get-tuple-element.7) | copy-start | bytes 6291460
  30.1 3.2 %collective-permute-start.3 = (bf16[512,256]{1,0:T(8,128)(2,1)}, bf16[512,256]{1,0:T(8,128)(2,1)S(1)}, u32[]{:S(2)}, u32[]{:S(2)}) collective-permute-start(bf16[512,256]{1,0:T(8,128)(2,1)} %collective-permute-done.2), channel_id=1, source_target_pairs={{0,1},{1,0},{2,3},{3,2},{4,5},{5,4},{6,7},{7,6},{8,9},{9,8},{10,11... | collective-permute-start | bytes 786440 | tf_op jit(solution)/shard_map/ppermute | solution.py:10
  30.7 3.7 %collective-permute-start.5 = (bf16[512,256]{1,0:T(8,128)(2,1)}, bf16[512,256]{1,0:T(8,128)(2,1)S(1)}, u32[]{:S(2)}, u32[]{:S(2)}) collective-permute-start(bf16[512,256]{1,0:T(8,128)(2,1)} %collective-permute-done.4), channel_id=1, source_target_pairs={{0,1},{1,0},{2,3},{3,2},{4,5},{5,4},{6,7},{7,6},{8,9},{9,8},{10,11... | collective-permute-start | bytes 786440 | tf_op jit(solution)/shard_map/ppermute | solution.py:10
  31.2 4.1 %collective-permute-start.7 = (bf16[512,256]{1,0:T(8,128)(2,1)}, bf16[512,256]{1,0:T(8,128)(2,1)S(1)}, u32[]{:S(2)}, u32[]{:S(2)}) collective-permute-start(bf16[512,256]{1,0:T(8,128)(2,1)} %collective-permute-done.6), channel_id=1, source_target_pairs={{0,1},{1,0},{2,3},{3,2},{4,5},{5,4},{6,7},{7,6},{8,9},{9,8},{10,11... | collective-permute-start | bytes 786440 | tf_op jit(solution)/shard_map/ppermute | solution.py:10
  37.4 10.4 %collective-permute-start.12 = (bf16[512,256]{1,0:T(8,128)(2,1)}, bf16[512,256]{1,0:T(8,128)(2,1)}, u32[]{:S(2)}, u32[]{:S(2)}) collective-permute-start(bf16[512,256]{1,0:T(8,128)(2,1)} %fusion.9), channel_id=1, source_target_pairs={{0,24},{8,16},{16,8},{24,0},{1,25},{9,17},{17,9},{25,1},{2,26},{10... | collective-permute-start | bytes 786440 | tf_op jit(solution)/shard_map/ppermute | solution.py:10
  39.5 13.4 %collective-permute-start.11 = (bf16[512,256]{1,0:T(8,128)(2,1)}, bf16[512,256]{1,0:T(8,128)(2,1)S(1)}, u32[]{:S(2)}, u32[]{:S(2)}) collective-permute-start(bf16[512,256]{1,0:T(8,128)(2,1)} %fusion.9), channel_id=1, source_target_pairs={{0,16},{8,24},{16,0},{24,8},{1,17},{9,25},{17,1},{25,9},{2,18},{10... | collective-permute-start | bytes 786440 | tf_op jit(solution)/shard_map/ppermute | solution.py:10
  40.0 13.3 %collective-permute-start.10 = (bf16[512,256]{1,0:T(8,128)(2,1)}, bf16[512,256]{1,0:T(8,128)(2,1)S(1)}, u32[]{:S(2)}, u32[]{:S(2)}) collective-permute-start(bf16[512,256]{1,0:T(8,128)(2,1)} %fusion.9), channel_id=1, source_target_pairs={{0,8},{8,0},{16,24},{24,16},{1,9},{9,1},{17,25},{25,17},{2,10},{10... | collective-permute-start | bytes 786440 | tf_op jit(solution)/shard_map/ppermute | solution.py:10

commit v14 on v4

--- a/solution.py
+++ b/solution.py
@@ -25,16 +25,29 @@
         )
         local_mask = jnp.repeat(jnp.repeat(local_blocks, B, axis=0), B, axis=1)
         masked = matrix_in * local_mask.astype(jnp.bfloat16)
+        keep = pattern.astype(jnp.bfloat16)
 
-        row_pieces = [None] * n_col
-        row_pieces[0] = masked
-        row_pieces[1] = _swap(masked, "col", n_col, 1)
+        def mask_from(x, row_member, col_member):
+            blocks = lax.dynamic_slice(
+                keep, (row_member * block_rows, col_member * block_cols), (block_rows, block_cols)
+            )
+            x4 = x.reshape(block_rows, B, block_cols, B)
+            return (x4 * blocks[:, None, :, None]).reshape(rows, cols)
+
+
+        col_raw = [None] + [_swap(matrix_in, "row", n_row, j) for j in range(1, n_row)]
+        col_pieces = [masked] + [
+            mask_from(col_raw[j], row_index ^ j, col_index) for j in range(1, n_row)
+        ]
+
+        late, _ = lax.optimization_barrier((matrix_in, col_raw[1]))
+        raw = [None] * n_col
+        raw[1] = _swap(late, "col", n_col, 1)
         for k in range(1, n_z):
-            piece = _swap(masked, "col", n_col, 2 * k)
-            row_pieces[2 * k] = piece
-            row_pieces[2 * k + 1] = _swap(piece, "col", n_col, 1)
-
-        col_pieces = [masked] + [_swap(masked, "row", n_row, k) for k in range(1, n_row)]
+            piece = _swap(late if k == 1 else matrix_in, "col", n_col, 2 * k)
+            raw[2 * k] = piece
+            raw[2 * k + 1] = _swap(piece, "col", n_col, 1)
+        row_pieces = [masked] + [mask_from(raw[t], row_index, col_index ^ t) for t in range(1, n_col)]
 
         slots = jnp.arange(n_col, dtype=jnp.int32) ^ col_index
         sub_index = ((slots // ratio) ^ row_index) * ratio + slots % ratio

time: 58.6 us -> 53.4 us (0.911)
  the two profiles are of different devices: /device:TPU:16 before, /device:TPU:0 now
where the time goes in v14:
time: 53.4 us; the launch traced here: 53.1 us
  waiting for transfers between devices  24.5 us (46%)
  starting transfers between devices  14.6 us (27%)
  local copies, waits for them, and re-layouts  6.03 us (11%)
  other arithmetic  4.51 us (8%)
  matrix products  3.17 us (6%)
    ppermute x13, waiting for transfers between devices, _swap(): return lax.ppermute(x, axis, [(i, i ^ d) for i in range(size)])  24.5 us
    ppermute x13, starting transfers between devices, _swap(): return lax.ppermute(x, axis, [(i, i ^ d) for i in range(size)])  14.6 us
    dot_general x1, matrix products, body(): cubic = jnp.dot(row_cat, f_slot, preferred_element_type=jnp.float32)  2.46 us
    mul x10, local copies, waits for them, and re-layouts, mask_from(): return (x4 * blocks[:, None, :, None]).reshape(rows, cols)  2.05 us
    another operation x3, other arithmetic, in_slot_order(): stacked = jnp.stack(pieces).reshape(n_row * ratio, cols, cols)  2.01 us
    unnamed x6, local copies, waits for them, and re-layouts  1.42 us
    broadcast_in_dim x4, local copies, waits for them, and re-layouts, body(): local_mask = jnp.repeat(jnp.repeat(local_blocks, B, axis=0), B, axis=1)  1.24 us
    gather x2, local copies, waits for them, and re-layouts, in_slot_order(): return jnp.take(stacked, sub_index, axis=0).reshape(n_col * cols, cols)  1.23 us
  transfers between devices with their start and end apart: 13, of which 7 were waited for; matrix products, arithmetic and copies ran while one was open for 14% of the time, Pallas kernels for 0%

profile of v14, /device:TPU:0, one launch (start us, length us, event | category | flops | bytes accessed | tf_op | source)
XLA Modules:
  0.0 53.1 jit_solution(3069818571027239281)
XLA Ops:
  0.0 2.9 %collective-permute-start = (bf16[512,256]{1,0:T(8,128)(2,1)}, bf16[512,256]{1,0:T(8,128)(2,1)S(1)}, u32[]{:S(2)}, u32[]{:S(2)}) collective-permute-start(bf16[512,256]{1,0:T(8,128)(2,1)} %param.4), channel_id=1, source_target_pairs={{0,8},{8,0},{16,24},{24,16},{1,9},{9,1},{17,25},{25,17},{2,10},{10... | collective-permute-start | bytes 786440 | tf_op jit(solution)/shard_map/ppermute | solution.py:10
  2.9 2.6 %collective-permute-start.4 = (bf16[512,256]{1,0:T(8,128)(2,1)}, bf16[512,256]{1,0:T(8,128)(2,1)S(1)}, u32[]{:S(2)}, u32[]{:S(2)}) collective-permute-start(bf16[512,256]{1,0:T(8,128)(2,1)} %param.4), channel_id=1, source_target_pairs={{0,4},{1,5},{2,6},{3,7},{4,0},{5,1},{6,2},{7,3},{8,12},{9,13},{10,... | collective-permute-start | bytes 786440 | tf_op jit(solution)/shard_map/ppermute | solution.py:10
  5.5 1.3 %collective-permute-start.6 = (bf16[512,256]{1,0:T(8,128)(2,1)}, bf16[512,256]{1,0:T(8,128)(2,1)S(1)}, u32[]{:S(2)}, u32[]{:S(2)}) collective-permute-start(bf16[512,256]{1,0:T(8,128)(2,1)} %param.4), channel_id=1, source_target_pairs={{0,6},{1,7},{2,4},{3,5},{4,2},{5,3},{6,0},{7,1},{8,14},{9,15},{10,... | collective-permute-start | bytes 786440 | tf_op jit(solution)/shard_map/ppermute | solution.py:10
  6.9 1.5 %collective-permute-start.9 = (bf16[512,256]{1,0:T(8,128)(2,1)}, bf16[512,256]{1,0:T(8,128)(2,1)S(1)}, u32[]{:S(2)}, u32[]{:S(2)}) collective-permute-start(bf16[512,256]{1,0:T(8,128)(2,1)} %param.4), channel_id=1, source_target_pairs={{0,24},{8,16},{16,8},{24,0},{1,25},{9,17},{17,9},{25,1},{2,26},{10... | collective-permute-start | bytes 786440 | tf_op jit(solution)/shard_map/ppermute | solution.py:10
  8.4 0.5 collective-permute-start.8
  8.9 0.8 %dynamic-slice_convert_fusion.1 = (f32[4,2]{1,0:T(4,128)S(1)}, bf16[4,2]{1,0:T(4,128)(2,1)S(1)}) fusion(s32[16,16]{1,0:T(8,128)} %param.5, s32[]{:T(128)S(6)} %select_n.64, s32[]{:T(128)S(6)} %select_n.65), kind=kLoop, calls=%fused_computation.39 | loop fusion | flops 16 | bytes 88 | tf_op jit(solution)/shard_map/convert_element_type | solution.py:61
  9.7 0.6 %broadcast_in_dim.32 = bf16[512,2,128]{2,1,0:T(2,128)(2,1)S(1)} broadcast(bf16[512,2]{1,0:T(8,128)(2,1)S(1)} %bitcast.112), dimensions={0,1} | broadcast | bytes 264192 | tf_op jit(solution)/shard_map/broadcast_in_dim | solution.py:26
  10.3 1.7 %fusion.14 = (bf16[1,512,256]{2,1,0:T(8,128)(2,1)S(1)}, bf16[512,2048]{1,0:T(8,128)(2,1)}) fusion(bf16[512,256]{1,0:T(8,128)(2,1)} %param.4, bf16[64,8,2,128]{3,2,1,0:T(2,128)(2,1)S(1)} %bitcast.110), kind=kLoop, calls=%fused_computation.44 | loop fusion | flops 524287 | bytes 1048576 | tf_op jit(solution)/shard_map/stack | solution.py:56
  12.1 0.7 %convert_element_type.38 = bf16[16,16]{1,0:T(8,128)(2,1)S(1)} convert(s32[16,16]{1,0:T(8,128)} %param.5) | non-fusion elementwise | flops 256 | bytes 1536 | tf_op jit(solution)/shard_map/convert_element_type | solution.py:28
  12.8 0.1 fusion.15
  12.9 0.0 collective-permute-done
  12.9 0.1 collective-permute-start.1
  13.0 0.2 mul.223
  13.2 0.1 fusion.5
  13.3 3.1 %collective-permute-done.9 = bf16[512,256]{1,0:T(8,128)(2,1)S(1)} collective-permute-done((bf16[512,256]{1,0:T(8,128)(2,1)}, bf16[512,256]{1,0:T(8,128)(2,1)S(1)}, u32[]{:S(2)}, u32[]{:S(2)}) %collective-permute-start.9) | collective-permute-done | bytes 262176 | tf_op jit(solution)/shard_map/ppermute | solution.py:10
  16.4 1.6 %collective-permute-start.2 = (bf16[512,256]{1,0:T(8,128)(2,1)}, bf16[512,256]{1,0:T(8,128)(2,1)S(1)}, u32[]{:S(2)}, u32[]{:S(2)}) collective-permute-start(bf16[512,256]{1,0:T(8,128)(2,1)} %param.4), channel_id=1, source_target_pairs={{0,2},{1,3},{2,0},{3,1},{4,6},{5,7},{6,4},{7,5},{8,10},{9,11},{10,... | collective-permute-start | bytes 786440 | tf_op jit(solution)/shard_map/ppermute | solution.py:10
  18.0 0.2 mul.233
  18.2 0.1 fusion.3
  18.2 2.8 %collective-permute-done.8 = bf16[512,256]{1,0:T(8,128)(2,1)S(1)} collective-permute-done((bf16[512,256]{1,0:T(8,128)(2,1)}, bf16[512,256]{1,0:T(8,128)(2,1)S(1)}, u32[]{:S(2)}, u32[]{:S(2)}) %collective-permute-start.8) | collective-permute-done | bytes 262176 | tf_op jit(solution)/shard_map/ppermute | solution.py:10
  21.0 0.2 mul.228
  21.2 0.1 fusion.4
  21.3 0.1 pad_maximum_fusion
  21.4 0.6 %gather_fusion = bf16[8,256,256]{2,1,0:T(8,128)(2,1)S(1)} fusion(bf16[8,256,256]{2,1,0:T(8,128)(2,1)S(1)} %bitcast.96, s32[1024]{0:T(1024)S(1)} %pad_clamp_fusion), kind=kCustom, calls=%fused_computation.clone | custom fusion | bytes 2097184 | tf_op jit(solution)/shard_map/jit(_take)/gather | solution.py:57
  22.0 0.0 copy-start
  22.0 2.2 %collective-permute-done.4 = bf16[512,256]{1,0:T(8,128)(2,1)S(1)} collective-permute-done((bf16[512,256]{1,0:T(8,128)(2,1)}, bf16[512,256]{1,0:T(8,128)(2,1)S(1)}, u32[]{:S(2)}, u32[]{:S(2)}) %collective-permute-start.4) | collective-permute-done | bytes 262176 | tf_op jit(solution)/shard_map/ppermute | solution.py:10
  24.3 0.0 collective-permute-start.5
  24.3 0.0 collective-permute-done.6
  24.3 0.5 collective-permute-start.7
  24.8 0.2 broadcast_select_fusion
  25.0 3.7 %collective-permute-done.2 = bf16[512,256]{1,0:T(8,128)(2,1)S(1)} collective-permute-done((bf16[512,256]{1,0:T(8,128)(2,1)}, bf16[512,256]{1,0:T(8,128)(2,1)S(1)}, u32[]{:S(2)}, u32[]{:S(2)}) %collective-permute-start.2) | collective-permute-done | bytes 262176 | tf_op jit(solution)/shard_map/ppermute | solution.py:10
  28.7 0.0 collective-permute-start.3
  28.7 0.0 collective-permute-done.1
  28.7 0.2 mul.195
  28.9 0.0 copy-done
  28.9 0.1 fusion.12
  29.0 0.2 mul.199
  29.2 0.1 fusion.11
  29.3 0.9 %collective-permute-done.3 = bf16[512,256]{1,0:T(8,128)(2,1)S(1)} collective-permute-done((bf16[512,256]{1,0:T(8,128)(2,1)S(1)}, bf16[512,256]{1,0:T(8,128)(2,1)S(1)}, u32[]{:S(2)}, u32[]{:S(2)}) %collective-permute-start.3) | collective-permute-done | bytes 262176 | tf_op jit(solution)/shard_map/ppermute | solution.py:10
  30.2 0.2 mul.203
  30.4 0.1 fusion.10
  30.5 0.2 mul.207
  30.7 0.1 fusion.9
  30.8 0.0 collective-permute-done.5
  30.8 0.2 mul.211
  31.0 0.1 fusion.8
  31.1 0.2 mul.215
  31.3 0.1 fusion.7
  31.4 0.0 collective-permute-done.7
  31.4 0.2 mul.219
  31.6 0.1 fusion.6
  31.7 0.6 %broadcast_in_dim.30 = f32[512,2,128]{2,1,0:T(2,128)S(1)} broadcast(f32[512,2]{1,0:T(8,128)S(1)} %bitcast.109), dimensions={0,1} | broadcast | bytes 528384 | tf_op jit(solution)/shard_map/broadcast_in_dim | solution.py:26
  32.3 0.7 %fusion.2 = bf16[512,256]{1,0:T(8,128)(2,1)S(1)} fusion(bf16[512,2048]{1,0:T(8,128)(2,1)S(1)} %fusion.6, bf16[2048,256]{1,0:T(8,128)(2,1)S(1)} %bitcast.97, f32[64,8,2,128]{3,2,1,0:T(2,128)S(1)} %bitcast.113), kind=kOutput, calls=%fused_computation.6 | convolution fusion | flops 537133056 | bytes 3932160 | tf_op jit(solution)/shard_map/dot_general | solution.py:60
  33.1 0.0 copy-done.1
  33.1 1.6 %collective-permute-start.11 = (bf16[512,256]{1,0:T(8,128)(2,1)S(1)}, bf16[512,256]{1,0:T(8,128)(2,1)S(1)}, u32[]{:S(2)}, u32[]{:S(2)}) collective-permute-start(bf16[512,256]{1,0:T(8,128)(2,1)S(1)} %fusion.2), channel_id=1, source_target_pairs={{0,16},{8,24},{16,0},{24,8},{1,17},{9,25},{17,1},{25,9},{2,18},{10... | collective-permute-start | bytes 786440 | tf_op jit(solution)/shard_map/ppermute | solution.py:10
  34.7 0.4 collective-permute-start.12
  35.1 1.5 %collective-permute-start.10 = (bf16[512,256]{1,0:T(8,128)(2,1)S(1)}, bf16[512,256]{1,0:T(8,128)(2,1)S(1)}, u32[]{:S(2)}, u32[]{:S(2)}) collective-permute-start(bf16[512,256]{1,0:T(8,128)(2,1)S(1)} %fusion.2), channel_id=1, source_target_pairs={{0,8},{8,0},{16,24},{24,16},{1,9},{9,1},{17,25},{25,17},{2,10},{10... | collective-permute-start | bytes 786440 | tf_op jit(solution)/shard_map/ppermute | solution.py:10
  36.6 10.5 %collective-permute-done.11 = bf16[512,256]{1,0:T(8,128)(2,1)S(1)} collective-permute-done((bf16[512,256]{1,0:T(8,128)(2,1)S(1)}, bf16[512,256]{1,0:T(8,128)(2,1)S(1)}, u32[]{:S(2)}, u32[]{:S(2)}) %collective-permute-start.11) | collective-permute-done | bytes 262176 | tf_op jit(solution)/shard_map/ppermute | solution.py:10
  47.1 0.0 collective-permute-done.12
  47.1 1.2 %collective-permute-done.10 = bf16[512,256]{1,0:T(8,128)(2,1)S(1)} collective-permute-done((bf16[512,256]{1,0:T(8,128)(2,1)S(1)}, bf16[512,256]{1,0:T(8,128)(2,1)S(1)}, u32[]{:S(2)}, u32[]{:S(2)}) %collective-permute-start.10) | collective-permute-done | bytes 262176 | tf_op jit(solution)/shard_map/ppermute | solution.py:10
  48.3 0.1 pad_maximum_fusion.1
  48.5 0.6 %gather_fusion.1 = bf16[8,256,256]{2,1,0:T(8,128)(2,1)S(1)} fusion(bf16[8,256,256]{2,1,0:T(8,128)(2,1)S(1)} %bitcast.95, s32[1024]{0:T(1024)S(1)} %pad_clamp_fusion), kind=kCustom, calls=%fused_computation.1.clone | custom fusion | bytes 2097184 | tf_op jit(solution)/shard_map/jit(_take)/gather | solution.py:57
  49.1 0.2 broadcast_select_fusion.1
  49.3 1.4 %copy-done.2 = bf16[512,2048]{1,0:T(8,128)(2,1)S(1)} copy-done((bf16[512,2048]{1,0:T(8,128)(2,1)S(1)}, bf16[512,2048]{1,0:T(8,128)(2,1)}, u32[]{:S(2)}) %copy-start.2) | copy-done | bytes 2097176
  50.7 2.5 %fusion.1 = f32[512,256]{1,0:T(8,128)} fusion(bf16[512,2048]{1,0:T(8,128)(2,1)S(1)} %copy-done.2, bf16[2048,256]{1,0:T(8,128)(2,1)S(1)} %bitcast.98, f32[64,8,2,128]{3,2,1,0:T(2,128)S(1)} %bitcast.114, bf16[512,256]{1,0:T(8,128)(2,1)} %param.4, bf16[64,8,2,128]{3,2,1,0:T(2,128)(2,1)S(1)} %bitcast.111), kind=kOutput, calls=%fused_computation.5 | convolution fusion | flops 537657344 | bytes 4718592 | tf_op jit(solution)/shard_map/dot_general | solution.py:65
  (6 shorter events, 0.1 us)
Async XLA Ops:
  0.0 12.9 %collective-permute-start = (bf16[512,256]{1,0:T(8,128)(2,1)}, bf16[512,256]{1,0:T(8,128)(2,1)S(1)}, u32[]{:S(2)}, u32[]{:S(2)}) collective-permute-start(bf16[512,256]{1,0:T(8,128)(2,1)} %param.4), channel_id=1, source_target_pairs={{0,8},{8,0},{16,24},{24,16},{1,9},{9,1},{17,25},{25,17},{2,10},{10... | collective-permute-start | bytes 786440 | tf_op jit(solution)/shard_map/ppermute | solution.py:10
  2.9 21.3 %collective-permute-start.4 = (bf16[512,256]{1,0:T(8,128)(2,1)}, bf16[512,256]{1,0:T(8,128)(2,1)S(1)}, u32[]{:S(2)}, u32[]{:S(2)}) collective-permute-start(bf16[512,256]{1,0:T(8,128)(2,1)} %param.4), channel_id=1, source_target_pairs={{0,4},{1,5},{2,6},{3,7},{4,0},{5,1},{6,2},{7,3},{8,12},{9,13},{10,... | collective-permute-start | bytes 786440 | tf_op jit(solution)/shard_map/ppermute | solution.py:10
  5.5 18.8 %collective-permute-start.6 = (bf16[512,256]{1,0:T(8,128)(2,1)}, bf16[512,256]{1,0:T(8,128)(2,1)S(1)}, u32[]{:S(2)}, u32[]{:S(2)}) collective-permute-start(bf16[512,256]{1,0:T(8,128)(2,1)} %param.4), channel_id=1, source_target_pairs={{0,6},{1,7},{2,4},{3,5},{4,2},{5,3},{6,0},{7,1},{8,14},{9,15},{10,... | collective-permute-start | bytes 786440 | tf_op jit(solution)/shard_map/ppermute | solution.py:10
  6.9 9.5 %collective-permute-start.9 = (bf16[512,256]{1,0:T(8,128)(2,1)}, bf16[512,256]{1,0:T(8,128)(2,1)S(1)}, u32[]{:S(2)}, u32[]{:S(2)}) collective-permute-start(bf16[512,256]{1,0:T(8,128)(2,1)} %param.4), channel_id=1, source_target_pairs={{0,24},{8,16},{16,8},{24,0},{1,25},{9,17},{17,9},{25,1},{2,26},{10... | collective-permute-start | bytes 786440 | tf_op jit(solution)/shard_map/ppermute | solution.py:10
  8.4 12.6 %collective-permute-start.8 = (bf16[512,256]{1,0:T(8,128)(2,1)}, bf16[512,256]{1,0:T(8,128)(2,1)S(1)}, u32[]{:S(2)}, u32[]{:S(2)}) collective-permute-start(bf16[512,256]{1,0:T(8,128)(2,1)} %param.4), channel_id=1, source_target_pairs={{0,16},{8,24},{16,0},{24,8},{1,17},{9,25},{17,1},{25,9},{2,18},{10... | collective-permute-start | bytes 786440 | tf_op jit(solution)/shard_map/ppermute | solution.py:10
  12.9 15.8 %collective-permute-start.1 = (bf16[512,256]{1,0:T(8,128)(2,1)}, bf16[512,256]{1,0:T(8,128)(2,1)S(1)}, u32[]{:S(2)}, u32[]{:S(2)}) collective-permute-start(bf16[512,256]{1,0:T(8,128)(2,1)} %param.4), channel_id=1, source_target_pairs={{0,1},{1,0},{2,3},{3,2},{4,5},{5,4},{6,7},{7,6},{8,9},{9,8},{10,11... | collective-permute-start | bytes 786440 | tf_op jit(solution)/shard_map/ppermute | solution.py:10
  16.4 12.3 %collective-permute-start.2 = (bf16[512,256]{1,0:T(8,128)(2,1)}, bf16[512,256]{1,0:T(8,128)(2,1)S(1)}, u32[]{:S(2)}, u32[]{:S(2)}) collective-permute-start(bf16[512,256]{1,0:T(8,128)(2,1)} %param.4), channel_id=1, source_target_pairs={{0,2},{1,3},{2,0},{3,1},{4,6},{5,7},{6,4},{7,5},{8,10},{9,11},{10,... | collective-permute-start | bytes 786440 | tf_op jit(solution)/shard_map/ppermute | solution.py:10
  22.0 6.9 %copy-start = (bf16[512,2048]{1,0:T(8,128)(2,1)S(1)}, bf16[512,2048]{1,0:T(8,128)(2,1)}, u32[]{:S(2)}) copy-start(bf16[512,2048]{1,0:T(8,128)(2,1)} %get-tuple-element.11) | copy-start | bytes 6291460
  24.3 6.5 %collective-permute-start.5 = (bf16[512,256]{1,0:T(8,128)(2,1)S(1)}, bf16[512,256]{1,0:T(8,128)(2,1)S(1)}, u32[]{:S(2)}, u32[]{:S(2)}) collective-permute-start(bf16[512,256]{1,0:T(8,128)(2,1)S(1)} %collective-permute-done.4), channel_id=1, source_target_pairs={{0,1},{1,0},{2,3},{3,2},{4,5},{5,4},{6,7},{7,6},{8,9},{9,8},{10,11... | collective-permute-start | bytes 786440 | tf_op jit(solution)/shard_map/ppermute | solution.py:10
  24.3 7.1 %collective-permute-start.7 = (bf16[512,256]{1,0:T(8,128)(2,1)S(1)}, bf16[512,256]{1,0:T(8,128)(2,1)S(1)}, u32[]{:S(2)}, u32[]{:S(2)}) collective-permute-start(bf16[512,256]{1,0:T(8,128)(2,1)S(1)} %collective-permute-done.6), channel_id=1, source_target_pairs={{0,1},{1,0},{2,3},{3,2},{4,5},{5,4},{6,7},{7,6},{8,9},{9,8},{10,11... | collective-permute-start | bytes 786440 | tf_op jit(solution)/shard_map/ppermute | solution.py:10
  28.7 1.5 %collective-permute-start.3 = (bf16[512,256]{1,0:T(8,128)(2,1)S(1)}, bf16[512,256]{1,0:T(8,128)(2,1)S(1)}, u32[]{:S(2)}, u32[]{:S(2)}) collective-permute-start(bf16[512,256]{1,0:T(8,128)(2,1)S(1)} %collective-permute-done.2), channel_id=1, source_target_pairs={{0,1},{1,0},{2,3},{3,2},{4,5},{5,4},{6,7},{7,6},{8,9},{9,8},{10,11... | collective-permute-start | bytes 786440 | tf_op jit(solution)/shard_map/ppermute | solution.py:10
  31.7 1.4 %copy-start.1 = (bf16[512,2048]{1,0:T(8,128)(2,1)}, bf16[512,2048]{1,0:T(8,128)(2,1)S(1)}, u32[]{:S(2)}) copy-start(bf16[512,2048]{1,0:T(8,128)(2,1)S(1)} %fusion.6) | copy-start | bytes 6291460
  33.1 14.0 %collective-permute-start.11 = (bf16[512,256]{1,0:T(8,128)(2,1)S(1)}, bf16[512,256]{1,0:T(8,128)(2,1)S(1)}, u32[]{:S(2)}, u32[]{:S(2)}) collective-permute-start(bf16[512,256]{1,0:T(8,128)(2,1)S(1)} %fusion.2), channel_id=1, source_target_pairs={{0,16},{8,24},{16,0},{24,8},{1,17},{9,25},{17,1},{25,9},{2,18},{10... | collective-permute-start | bytes 786440 | tf_op jit(solution)/shard_map/ppermute | solution.py:10
  34.7 12.4 %collective-permute-start.12 = (bf16[512,256]{1,0:T(8,128)(2,1)S(1)}, bf16[512,256]{1,0:T(8,128)(2,1)S(1)}, u32[]{:S(2)}, u32[]{:S(2)}) collective-permute-start(bf16[512,256]{1,0:T(8,128)(2,1)S(1)} %fusion.2), channel_id=1, source_target_pairs={{0,24},{8,16},{16,8},{24,0},{1,25},{9,17},{17,9},{25,1},{2,26},{10... | collective-permute-start | bytes 786440 | tf_op jit(solution)/shard_map/ppermute | solution.py:10
  35.1 13.2 %collective-permute-start.10 = (bf16[512,256]{1,0:T(8,128)(2,1)S(1)}, bf16[512,256]{1,0:T(8,128)(2,1)S(1)}, u32[]{:S(2)}, u32[]{:S(2)}) collective-permute-start(bf16[512,256]{1,0:T(8,128)(2,1)S(1)} %fusion.2), channel_id=1, source_target_pairs={{0,8},{8,0},{16,24},{24,16},{1,9},{9,1},{17,25},{25,17},{2,10},{10... | collective-permute-start | bytes 786440 | tf_op jit(solution)/shard_map/ppermute | solution.py:10
  49.1 1.6 %copy-start.2 = (bf16[512,2048]{1,0:T(8,128)(2,1)S(1)}, bf16[512,2048]{1,0:T(8,128)(2,1)}, u32[]{:S(2)}) copy-start(bf16[512,2048]{1,0:T(8,128)(2,1)} %copy-done.1) | copy-start | bytes 6291460

commit v15 on v14

--- a/solution.py
+++ b/solution.py
@@ -44,7 +44,7 @@
         raw = [None] * n_col
         raw[1] = _swap(late, "col", n_col, 1)
         for k in range(1, n_z):
-            piece = _swap(late if k == 1 else matrix_in, "col", n_col, 2 * k)
+            piece = _swap(matrix_in, "col", n_col, 2 * k)
             raw[2 * k] = piece
             raw[2 * k + 1] = _swap(piece, "col", n_col, 1)
         row_pieces = [masked] + [mask_from(raw[t], row_index, col_index ^ t) for t in range(1, n_col)]

time: 53.4 us -> 51.9 us (0.972)
  the two profiles are of different devices: /device:TPU:0 before, /device:TPU:16 now
where the time goes in v15:
time: 51.9 us; the launch traced here: 51.6 us
  waiting for transfers between devices  26.5 us (51%)
  starting transfers between devices  11 us (21%)
  local copies, waits for them, and re-layouts  6.03 us (12%)
  other arithmetic  4.51 us (9%)
  matrix products  3.17 us (6%)
    ppermute x13, waiting for transfers between devices, _swap(): return lax.ppermute(x, axis, [(i, i ^ d) for i in range(size)])  26.5 us
    ppermute x13, starting transfers between devices, _swap(): return lax.ppermute(x, axis, [(i, i ^ d) for i in range(size)])  11 us
    dot_general x1, matrix products, body(): cubic = jnp.dot(row_cat, f_slot, preferred_element_type=jnp.float32)  2.46 us
    mul x10, local copies, waits for them, and re-layouts, mask_from(): return (x4 * blocks[:, None, :, None]).reshape(rows, cols)  2.05 us
    another operation x3, other arithmetic, in_slot_order(): stacked = jnp.stack(pieces).reshape(n_row * ratio, cols, cols)  2.01 us
    unnamed x6, local copies, waits for them, and re-layouts  1.42 us
    broadcast_in_dim x4, local copies, waits for them, and re-layouts, body(): local_mask = jnp.repeat(jnp.repeat(local_blocks, B, axis=0), B, axis=1)  1.24 us
    gather x2, local copies, waits for them, and re-layouts, in_slot_order(): return jnp.take(stacked, sub_index, axis=0).reshape(n_col * cols, cols)  1.23 us
  transfers between devices with their start and end apart: 13, of which 6 were waited for; matrix products, arithmetic and copies ran while one was open for 14% of the time, Pallas kernels for 0%

profile of v15, /device:TPU:16, one launch (start us, length us, event | category | flops | bytes accessed | tf_op | source)
XLA Modules:
  0.0 51.6 jit_solution(11161261643045097164)
XLA Ops:
  0.0 1.5 %collective-permute-start = (bf16[512,256]{1,0:T(8,128)(2,1)}, bf16[512,256]{1,0:T(8,128)(2,1)S(1)}, u32[]{:S(2)}, u32[]{:S(2)}) collective-permute-start(bf16[512,256]{1,0:T(8,128)(2,1)} %param.4), channel_id=1, source_target_pairs={{0,8},{8,0},{16,24},{24,16},{1,9},{9,1},{17,25},{25,17},{2,10},{10... | collective-permute-start | bytes 786440 | tf_op jit(solution)/shard_map/ppermute | solution.py:10
  1.5 1.6 %collective-permute-start.2 = (bf16[512,256]{1,0:T(8,128)(2,1)}, bf16[512,256]{1,0:T(8,128)(2,1)S(1)}, u32[]{:S(2)}, u32[]{:S(2)}) collective-permute-start(bf16[512,256]{1,0:T(8,128)(2,1)} %param.4), channel_id=1, source_target_pairs={{0,2},{1,3},{2,0},{3,1},{4,6},{5,7},{6,4},{7,5},{8,10},{9,11},{10,... | collective-permute-start | bytes 786440 | tf_op jit(solution)/shard_map/ppermute | solution.py:10
  3.1 0.3 collective-permute-start.4
  3.4 1.6 %collective-permute-start.6 = (bf16[512,256]{1,0:T(8,128)(2,1)}, bf16[512,256]{1,0:T(8,128)(2,1)S(1)}, u32[]{:S(2)}, u32[]{:S(2)}) collective-permute-start(bf16[512,256]{1,0:T(8,128)(2,1)} %param.4), channel_id=1, source_target_pairs={{0,6},{1,7},{2,4},{3,5},{4,2},{5,3},{6,0},{7,1},{8,14},{9,15},{10,... | collective-permute-start | bytes 786440 | tf_op jit(solution)/shard_map/ppermute | solution.py:10
  5.0 1.5 %collective-permute-start.9 = (bf16[512,256]{1,0:T(8,128)(2,1)}, bf16[512,256]{1,0:T(8,128)(2,1)S(1)}, u32[]{:S(2)}, u32[]{:S(2)}) collective-permute-start(bf16[512,256]{1,0:T(8,128)(2,1)} %param.4), channel_id=1, source_target_pairs={{0,24},{8,16},{16,8},{24,0},{1,25},{9,17},{17,9},{25,1},{2,26},{10... | collective-permute-start | bytes 786440 | tf_op jit(solution)/shard_map/ppermute | solution.py:10
  6.5 0.8 %dynamic-slice_convert_fusion.1 = (f32[4,2]{1,0:T(4,128)S(1)}, bf16[4,2]{1,0:T(4,128)(2,1)S(1)}) fusion(s32[16,16]{1,0:T(8,128)} %param.5, s32[]{:T(128)S(6)} %select_n.64, s32[]{:T(128)S(6)} %select_n.65), kind=kLoop, calls=%fused_computation.39 | loop fusion | flops 16 | bytes 88 | tf_op jit(solution)/shard_map/convert_element_type | solution.py:61
  7.3 0.6 %broadcast_in_dim.32 = bf16[512,2,128]{2,1,0:T(2,128)(2,1)S(1)} broadcast(bf16[512,2]{1,0:T(8,128)(2,1)S(1)} %bitcast.112), dimensions={0,1} | broadcast | bytes 264192 | tf_op jit(solution)/shard_map/broadcast_in_dim | solution.py:26
  7.9 1.7 %fusion.14 = (bf16[1,512,256]{2,1,0:T(8,128)(2,1)S(1)}, bf16[512,2048]{1,0:T(8,128)(2,1)}) fusion(bf16[512,256]{1,0:T(8,128)(2,1)} %param.4, bf16[64,8,2,128]{3,2,1,0:T(2,128)(2,1)S(1)} %bitcast.110), kind=kLoop, calls=%fused_computation.44 | loop fusion | flops 524287 | bytes 1048576 | tf_op jit(solution)/shard_map/stack | solution.py:56
  9.7 0.7 %convert_element_type.38 = bf16[16,16]{1,0:T(8,128)(2,1)S(1)} convert(s32[16,16]{1,0:T(8,128)} %param.5) | non-fusion elementwise | flops 256 | bytes 1536 | tf_op jit(solution)/shard_map/convert_element_type | solution.py:28
  10.4 0.1 fusion.15
  10.5 0.0 collective-permute-done
  10.5 0.6 %collective-permute-start.8 = (bf16[512,256]{1,0:T(8,128)(2,1)}, bf16[512,256]{1,0:T(8,128)(2,1)S(1)}, u32[]{:S(2)}, u32[]{:S(2)}) collective-permute-start(bf16[512,256]{1,0:T(8,128)(2,1)} %param.4), channel_id=1, source_target_pairs={{0,16},{8,24},{16,0},{24,8},{1,17},{9,25},{17,1},{25,9},{2,18},{10... | collective-permute-start | bytes 786440 | tf_op jit(solution)/shard_map/ppermute | solution.py:10
  11.1 0.2 mul.223
  11.3 0.1 fusion.5
  11.3 3.6 %collective-permute-done.9 = bf16[512,256]{1,0:T(8,128)(2,1)S(1)} collective-permute-done((bf16[512,256]{1,0:T(8,128)(2,1)}, bf16[512,256]{1,0:T(8,128)(2,1)S(1)}, u32[]{:S(2)}, u32[]{:S(2)}) %collective-permute-start.9) | collective-permute-done | bytes 262176 | tf_op jit(solution)/shard_map/ppermute | solution.py:10
  14.9 0.0 collective-permute-start.1
  14.9 0.2 mul.233
  15.1 0.1 fusion.3
  15.2 5.2 %collective-permute-done.8 = bf16[512,256]{1,0:T(8,128)(2,1)S(1)} collective-permute-done((bf16[512,256]{1,0:T(8,128)(2,1)}, bf16[512,256]{1,0:T(8,128)(2,1)S(1)}, u32[]{:S(2)}, u32[]{:S(2)}) %collective-permute-start.8) | collective-permute-done | bytes 262176 | tf_op jit(solution)/shard_map/ppermute | solution.py:10
  20.4 0.2 mul.228
  20.7 0.1 fusion.4
  20.7 0.1 pad_maximum_fusion
  20.9 0.6 %gather_fusion = bf16[8,256,256]{2,1,0:T(8,128)(2,1)S(1)} fusion(bf16[8,256,256]{2,1,0:T(8,128)(2,1)S(1)} %bitcast.96, s32[1024]{0:T(1024)S(1)} %pad_clamp_fusion), kind=kCustom, calls=%fused_computation.clone | custom fusion | bytes 2097184 | tf_op jit(solution)/shard_map/jit(_take)/gather | solution.py:57
  21.5 0.0 copy-start
  21.5 0.0 collective-permute-done.2
  21.5 0.1 collective-permute-start.3
  21.6 0.1 collective-permute-done.4
  21.7 0.4 collective-permute-start.5
  22.1 5.5 %collective-permute-done.6 = bf16[512,256]{1,0:T(8,128)(2,1)S(1)} collective-permute-done((bf16[512,256]{1,0:T(8,128)(2,1)}, bf16[512,256]{1,0:T(8,128)(2,1)S(1)}, u32[]{:S(2)}, u32[]{:S(2)}) %collective-permute-start.6) | collective-permute-done | bytes 262176 | tf_op jit(solution)/shard_map/ppermute | solution.py:10
  27.5 0.0 collective-permute-start.7
  27.6 0.2 broadcast_select_fusion
  27.7 0.0 collective-permute-done.1
  27.7 0.2 mul.195
  27.9 0.0 copy-done
  28.0 0.1 fusion.12
  28.0 0.2 mul.199
  28.2 0.1 fusion.11
  28.3 0.0 collective-permute-done.3
  28.3 0.2 mul.203
  28.5 0.1 fusion.10
  28.6 0.2 mul.207
  28.8 0.1 fusion.9
  28.9 0.0 collective-permute-done.5
  28.9 0.2 mul.211
  29.1 0.1 fusion.8
  29.2 0.2 mul.215
  29.4 0.1 fusion.7
  29.5 0.0 collective-permute-done.7
  29.5 0.2 mul.219
  29.7 0.1 fusion.6
  29.9 0.6 %broadcast_in_dim.30 = f32[512,2,128]{2,1,0:T(2,128)S(1)} broadcast(f32[512,2]{1,0:T(8,128)S(1)} %bitcast.109), dimensions={0,1} | broadcast | bytes 528384 | tf_op jit(solution)/shard_map/broadcast_in_dim | solution.py:26
  30.5 0.7 %fusion.2 = bf16[512,256]{1,0:T(8,128)(2,1)S(1)} fusion(bf16[512,2048]{1,0:T(8,128)(2,1)S(1)} %fusion.6, bf16[2048,256]{1,0:T(8,128)(2,1)S(1)} %bitcast.97, f32[64,8,2,128]{3,2,1,0:T(2,128)S(1)} %bitcast.113), kind=kOutput, calls=%fused_computation.6 | convolution fusion | flops 537133056 | bytes 3932160 | tf_op jit(solution)/shard_map/dot_general | solution.py:60
  31.2 0.0 copy-done.1
  31.2 1.6 %collective-permute-start.11 = (bf16[512,256]{1,0:T(8,128)(2,1)S(1)}, bf16[512,256]{1,0:T(8,128)(2,1)S(1)}, u32[]{:S(2)}, u32[]{:S(2)}) collective-permute-start(bf16[512,256]{1,0:T(8,128)(2,1)S(1)} %fusion.2), channel_id=1, source_target_pairs={{0,16},{8,24},{16,0},{24,8},{1,17},{9,25},{17,1},{25,9},{2,18},{10... | collective-permute-start | bytes 786440 | tf_op jit(solution)/shard_map/ppermute | solution.py:10
  32.8 0.5 collective-permute-start.12
  33.3 1.5 %collective-permute-start.10 = (bf16[512,256]{1,0:T(8,128)(2,1)S(1)}, bf16[512,256]{1,0:T(8,128)(2,1)S(1)}, u32[]{:S(2)}, u32[]{:S(2)}) collective-permute-start(bf16[512,256]{1,0:T(8,128)(2,1)S(1)} %fusion.2), channel_id=1, source_target_pairs={{0,8},{8,0},{16,24},{24,16},{1,9},{9,1},{17,25},{25,17},{2,10},{10... | collective-permute-start | bytes 786440 | tf_op jit(solution)/shard_map/ppermute | solution.py:10
  34.7 10.8 %collective-permute-done.11 = bf16[512,256]{1,0:T(8,128)(2,1)S(1)} collective-permute-done((bf16[512,256]{1,0:T(8,128)(2,1)S(1)}, bf16[512,256]{1,0:T(8,128)(2,1)S(1)}, u32[]{:S(2)}, u32[]{:S(2)}) %collective-permute-start.11) | collective-permute-done | bytes 262176 | tf_op jit(solution)/shard_map/ppermute | solution.py:10
  45.6 0.0 collective-permute-done.12
  45.6 1.2 %collective-permute-done.10 = bf16[512,256]{1,0:T(8,128)(2,1)S(1)} collective-permute-done((bf16[512,256]{1,0:T(8,128)(2,1)S(1)}, bf16[512,256]{1,0:T(8,128)(2,1)S(1)}, u32[]{:S(2)}, u32[]{:S(2)}) %collective-permute-start.10) | collective-permute-done | bytes 262176 | tf_op jit(solution)/shard_map/ppermute | solution.py:10
  46.8 0.1 pad_maximum_fusion.1
  47.0 0.6 %gather_fusion.1 = bf16[8,256,256]{2,1,0:T(8,128)(2,1)S(1)} fusion(bf16[8,256,256]{2,1,0:T(8,128)(2,1)S(1)} %bitcast.95, s32[1024]{0:T(1024)S(1)} %pad_clamp_fusion), kind=kCustom, calls=%fused_computation.1.clone | custom fusion | bytes 2097184 | tf_op jit(solution)/shard_map/jit(_take)/gather | solution.py:57
  47.6 0.2 broadcast_select_fusion.1
  47.8 1.4 %copy-done.2 = bf16[512,2048]{1,0:T(8,128)(2,1)S(1)} copy-done((bf16[512,2048]{1,0:T(8,128)(2,1)S(1)}, bf16[512,2048]{1,0:T(8,128)(2,1)}, u32[]{:S(2)}) %copy-start.2) | copy-done | bytes 2097176
  49.2 2.5 %fusion.1 = f32[512,256]{1,0:T(8,128)} fusion(bf16[512,2048]{1,0:T(8,128)(2,1)S(1)} %copy-done.2, bf16[2048,256]{1,0:T(8,128)(2,1)S(1)} %bitcast.98, f32[64,8,2,128]{3,2,1,0:T(2,128)S(1)} %bitcast.114, bf16[512,256]{1,0:T(8,128)(2,1)} %param.4, bf16[64,8,2,128]{3,2,1,0:T(2,128)(2,1)S(1)} %bitcast.111), kind=kOutput, calls=%fused_computation.5 | convolution fusion | flops 537657344 | bytes 4718592 | tf_op jit(solution)/shard_map/dot_general | solution.py:65
  (6 shorter events, 0.1 us)
Async XLA Ops:
  0.0 10.5 %collective-permute-start = (bf16[512,256]{1,0:T(8,128)(2,1)}, bf16[512,256]{1,0:T(8,128)(2,1)S(1)}, u32[]{:S(2)}, u32[]{:S(2)}) collective-permute-start(bf16[512,256]{1,0:T(8,128)(2,1)} %param.4), channel_id=1, source_target_pairs={{0,8},{8,0},{16,24},{24,16},{1,9},{9,1},{17,25},{25,17},{2,10},{10... | collective-permute-start | bytes 786440 | tf_op jit(solution)/shard_map/ppermute | solution.py:10
  1.5 20.0 %collective-permute-start.2 = (bf16[512,256]{1,0:T(8,128)(2,1)}, bf16[512,256]{1,0:T(8,128)(2,1)S(1)}, u32[]{:S(2)}, u32[]{:S(2)}) collective-permute-start(bf16[512,256]{1,0:T(8,128)(2,1)} %param.4), channel_id=1, source_target_pairs={{0,2},{1,3},{2,0},{3,1},{4,6},{5,7},{6,4},{7,5},{8,10},{9,11},{10,... | collective-permute-start | bytes 786440 | tf_op jit(solution)/shard_map/ppermute | solution.py:10
  3.1 18.7 %collective-permute-start.4 = (bf16[512,256]{1,0:T(8,128)(2,1)}, bf16[512,256]{1,0:T(8,128)(2,1)S(1)}, u32[]{:S(2)}, u32[]{:S(2)}) collective-permute-start(bf16[512,256]{1,0:T(8,128)(2,1)} %param.4), channel_id=1, source_target_pairs={{0,4},{1,5},{2,6},{3,7},{4,0},{5,1},{6,2},{7,3},{8,12},{9,13},{10,... | collective-permute-start | bytes 786440 | tf_op jit(solution)/shard_map/ppermute | solution.py:10
  3.4 24.1 %collective-permute-start.6 = (bf16[512,256]{1,0:T(8,128)(2,1)}, bf16[512,256]{1,0:T(8,128)(2,1)S(1)}, u32[]{:S(2)}, u32[]{:S(2)}) collective-permute-start(bf16[512,256]{1,0:T(8,128)(2,1)} %param.4), channel_id=1, source_target_pairs={{0,6},{1,7},{2,4},{3,5},{4,2},{5,3},{6,0},{7,1},{8,14},{9,15},{10,... | collective-permute-start | bytes 786440 | tf_op jit(solution)/shard_map/ppermute | solution.py:10
  5.0 10.0 %collective-permute-start.9 = (bf16[512,256]{1,0:T(8,128)(2,1)}, bf16[512,256]{1,0:T(8,128)(2,1)S(1)}, u32[]{:S(2)}, u32[]{:S(2)}) collective-permute-start(bf16[512,256]{1,0:T(8,128)(2,1)} %param.4), channel_id=1, source_target_pairs={{0,24},{8,16},{16,8},{24,0},{1,25},{9,17},{17,9},{25,1},{2,26},{10... | collective-permute-start | bytes 786440 | tf_op jit(solution)/shard_map/ppermute | solution.py:10
  10.5 9.9 %collective-permute-start.8 = (bf16[512,256]{1,0:T(8,128)(2,1)}, bf16[512,256]{1,0:T(8,128)(2,1)S(1)}, u32[]{:S(2)}, u32[]{:S(2)}) collective-permute-start(bf16[512,256]{1,0:T(8,128)(2,1)} %param.4), channel_id=1, source_target_pairs={{0,16},{8,24},{16,0},{24,8},{1,17},{9,25},{17,1},{25,9},{2,18},{10... | collective-permute-start | bytes 786440 | tf_op jit(solution)/shard_map/ppermute | solution.py:10
  14.9 12.8 %collective-permute-start.1 = (bf16[512,256]{1,0:T(8,128)(2,1)}, bf16[512,256]{1,0:T(8,128)(2,1)S(1)}, u32[]{:S(2)}, u32[]{:S(2)}) collective-permute-start(bf16[512,256]{1,0:T(8,128)(2,1)} %param.4), channel_id=1, source_target_pairs={{0,1},{1,0},{2,3},{3,2},{4,5},{5,4},{6,7},{7,6},{8,9},{9,8},{10,11... | collective-permute-start | bytes 786440 | tf_op jit(solution)/shard_map/ppermute | solution.py:10
  21.5 6.5 %copy-start = (bf16[512,2048]{1,0:T(8,128)(2,1)S(1)}, bf16[512,2048]{1,0:T(8,128)(2,1)}, u32[]{:S(2)}) copy-start(bf16[512,2048]{1,0:T(8,128)(2,1)} %get-tuple-element.11) | copy-start | bytes 6291460
  21.5 6.8 %collective-permute-start.3 = (bf16[512,256]{1,0:T(8,128)(2,1)S(1)}, bf16[512,256]{1,0:T(8,128)(2,1)S(1)}, u32[]{:S(2)}, u32[]{:S(2)}) collective-permute-start(bf16[512,256]{1,0:T(8,128)(2,1)S(1)} %collective-permute-done.2), channel_id=1, source_target_pairs={{0,1},{1,0},{2,3},{3,2},{4,5},{5,4},{6,7},{7,6},{8,9},{9,8},{10,11... | collective-permute-start | bytes 786440 | tf_op jit(solution)/shard_map/ppermute | solution.py:10
  21.7 7.2 %collective-permute-start.5 = (bf16[512,256]{1,0:T(8,128)(2,1)S(1)}, bf16[512,256]{1,0:T(8,128)(2,1)S(1)}, u32[]{:S(2)}, u32[]{:S(2)}) collective-permute-start(bf16[512,256]{1,0:T(8,128)(2,1)S(1)} %collective-permute-done.4), channel_id=1, source_target_pairs={{0,1},{1,0},{2,3},{3,2},{4,5},{5,4},{6,7},{7,6},{8,9},{9,8},{10,11... | collective-permute-start | bytes 786440 | tf_op jit(solution)/shard_map/ppermute | solution.py:10
  27.5 2.0 %collective-permute-start.7 = (bf16[512,256]{1,0:T(8,128)(2,1)S(1)}, bf16[512,256]{1,0:T(8,128)(2,1)S(1)}, u32[]{:S(2)}, u32[]{:S(2)}) collective-permute-start(bf16[512,256]{1,0:T(8,128)(2,1)S(1)} %collective-permute-done.6), channel_id=1, source_target_pairs={{0,1},{1,0},{2,3},{3,2},{4,5},{5,4},{6,7},{7,6},{8,9},{9,8},{10,11... | collective-permute-start | bytes 786440 | tf_op jit(solution)/shard_map/ppermute | solution.py:10
  29.8 1.4 %copy-start.1 = (bf16[512,2048]{1,0:T(8,128)(2,1)}, bf16[512,2048]{1,0:T(8,128)(2,1)S(1)}, u32[]{:S(2)}) copy-start(bf16[512,2048]{1,0:T(8,128)(2,1)S(1)} %fusion.6) | copy-start | bytes 6291460
  31.2 14.4 %collective-permute-start.11 = (bf16[512,256]{1,0:T(8,128)(2,1)S(1)}, bf16[512,256]{1,0:T(8,128)(2,1)S(1)}, u32[]{:S(2)}, u32[]{:S(2)}) collective-permute-start(bf16[512,256]{1,0:T(8,128)(2,1)S(1)} %fusion.2), channel_id=1, source_target_pairs={{0,16},{8,24},{16,0},{24,8},{1,17},{9,25},{17,1},{25,9},{2,18},{10... | collective-permute-start | bytes 786440 | tf_op jit(solution)/shard_map/ppermute | solution.py:10
  32.8 12.8 %collective-permute-start.12 = (bf16[512,256]{1,0:T(8,128)(2,1)S(1)}, bf16[512,256]{1,0:T(8,128)(2,1)S(1)}, u32[]{:S(2)}, u32[]{:S(2)}) collective-permute-start(bf16[512,256]{1,0:T(8,128)(2,1)S(1)} %fusion.2), channel_id=1, source_target_pairs={{0,24},{8,16},{16,8},{24,0},{1,25},{9,17},{17,9},{25,1},{2,26},{10... | collective-permute-start | bytes 786440 | tf_op jit(solution)/shard_map/ppermute | solution.py:10
  33.3 13.6 %collective-permute-start.10 = (bf16[512,256]{1,0:T(8,128)(2,1)S(1)}, bf16[512,256]{1,0:T(8,128)(2,1)S(1)}, u32[]{:S(2)}, u32[]{:S(2)}) collective-permute-start(bf16[512,256]{1,0:T(8,128)(2,1)S(1)} %fusion.2), channel_id=1, source_target_pairs={{0,8},{8,0},{16,24},{24,16},{1,9},{9,1},{17,25},{25,17},{2,10},{10... | collective-permute-start | bytes 786440 | tf_op jit(solution)/shard_map/ppermute | solution.py:10
  47.6 1.6 %copy-start.2 = (bf16[512,2048]{1,0:T(8,128)(2,1)S(1)}, bf16[512,2048]{1,0:T(8,128)(2,1)}, u32[]{:S(2)}) copy-start(bf16[512,2048]{1,0:T(8,128)(2,1)} %copy-done.1) | copy-start | bytes 6291460

commit v16 on v15

--- a/solution.py
+++ b/solution.py
@@ -35,18 +35,20 @@
             return (x4 * blocks[:, None, :, None]).reshape(rows, cols)
 
 
-        col_raw = [None] + [_swap(matrix_in, "row", n_row, j) for j in range(1, n_row)]
+        raw = [None] * n_col
+        for k in range(1, n_z):
+            raw[2 * k] = _swap(matrix_in, "col", n_col, 2 * k)
+        first_src = lax.optimization_barrier((matrix_in, raw[2]))[0] if n_z > 1 else matrix_in
+        col_raw = [None] + [
+            _swap(first_src if j == 1 else matrix_in, "row", n_row, j) for j in range(1, n_row)
+        ]
+        late = lax.optimization_barrier((matrix_in, col_raw[1]))[0] if n_row > 1 else matrix_in
         col_pieces = [masked] + [
             mask_from(col_raw[j], row_index ^ j, col_index) for j in range(1, n_row)
         ]
-
-        late, _ = lax.optimization_barrier((matrix_in, col_raw[1]))
-        raw = [None] * n_col
         raw[1] = _swap(late, "col", n_col, 1)
         for k in range(1, n_z):
-            piece = _swap(matrix_in, "col", n_col, 2 * k)
-            raw[2 * k] = piece
-            raw[2 * k + 1] = _swap(piece, "col", n_col, 1)
+            raw[2 * k + 1] = _swap(raw[2 * k], "col", n_col, 1)
         row_pieces = [masked] + [mask_from(raw[t], row_index, col_index ^ t) for t in range(1, n_col)]
 
         slots = jnp.arange(n_col, dtype=jnp.int32) ^ col_index

time: 51.9 us -> 57 us (1.098)
  other arithmetic: 4.51 us -> 7.36 us
  starting transfers between devices: 11 us -> 12.1 us
  waiting for transfers between devices: 26.5 us -> 27.1 us
    unnamed x6, other arithmetic: 0.45 us -> 3.3 us
    ppermute x13, starting transfers between devices: 11 us -> 12.1 us  [_swap(): return lax.ppermute(x, axis, [(i, i ^ d) for i in range(size)])]
  transfers between devices with their start and end apart: 13 -> 13, of which waited for: 6 -> 6; matrix products, arithmetic and copies ran while one was open for 14% -> 18% of each run, Pallas kernels for 0% -> 0%
where the time goes in v16:
time: 57 us; the launch traced here: 56.6 us
  waiting for transfers between devices  27.1 us (48%)
  starting transfers between devices  12.1 us (21%)
  other arithmetic  7.36 us (13%)
  local copies, waits for them, and re-layouts  6.58 us (12%)
  matrix products  3.17 us (6%)
    ppermute x13, waiting for transfers between devices, _swap(): return lax.ppermute(x, axis, [(i, i ^ d) for i in range(size)])  27.1 us
    ppermute x13, starting transfers between devices, _swap(): return lax.ppermute(x, axis, [(i, i ^ d) for i in range(size)])  12.1 us
    unnamed x6, other arithmetic  3.3 us
    dot_general x1, matrix products, body(): cubic = jnp.dot(row_cat, f_slot, preferred_element_type=jnp.float32)  2.46 us
    mul x10, local copies, waits for them, and re-layouts, mask_from(): return (x4 * blocks[:, None, :, None]).reshape(rows, cols)  2.05 us
    another operation x3, other arithmetic, in_slot_order(): stacked = jnp.stack(pieces).reshape(n_row * ratio, cols, cols)  2.01 us
    unnamed x6, local copies, waits for them, and re-layouts  1.97 us
    broadcast_in_dim x4, local copies, waits for them, and re-layouts, body(): local_mask = jnp.repeat(jnp.repeat(local_blocks, B, axis=0), B, axis=1)  1.24 us
  transfers between devices with their start and end apart: 13, of which 6 were waited for; matrix products, arithmetic and copies ran while one was open for 18% of the time, Pallas kernels for 0%

profile of v16, /device:TPU:16, one launch (start us, length us, event | category | flops | bytes accessed | tf_op | source)
XLA Modules:
  0.0 56.6 jit_solution(6202016554104173578)
XLA Ops:
  0.0 1.6 %collective-permute-start = (bf16[512,256]{1,0:T(8,128)(2,1)}, bf16[512,256]{1,0:T(8,128)(2,1)S(1)}, u32[]{:S(2)}, u32[]{:S(2)}) collective-permute-start(bf16[512,256]{1,0:T(8,128)(2,1)} %param.4), channel_id=1, source_target_pairs={{0,2},{1,3},{2,0},{3,1},{4,6},{5,7},{6,4},{7,5},{8,10},{9,11},{10,... | collective-permute-start | bytes 786440 | tf_op jit(solution)/shard_map/ppermute | solution.py:10
  1.6 0.3 collective-permute-start.4
  1.9 1.6 %collective-permute-start.6 = (bf16[512,256]{1,0:T(8,128)(2,1)}, bf16[512,256]{1,0:T(8,128)(2,1)S(1)}, u32[]{:S(2)}, u32[]{:S(2)}) collective-permute-start(bf16[512,256]{1,0:T(8,128)(2,1)} %param.4), channel_id=1, source_target_pairs={{0,6},{1,7},{2,4},{3,5},{4,2},{5,3},{6,0},{7,1},{8,14},{9,15},{10,... | collective-permute-start | bytes 786440 | tf_op jit(solution)/shard_map/ppermute | solution.py:10
  3.5 2.4 %collective-permute-start.9 = (bf16[512,256]{1,0:T(8,128)(2,1)}, bf16[512,256]{1,0:T(8,128)(2,1)S(1)}, u32[]{:S(2)}, u32[]{:S(2)}) collective-permute-start(bf16[512,256]{1,0:T(8,128)(2,1)} %param.4), channel_id=1, source_target_pairs={{0,24},{8,16},{16,8},{24,0},{1,25},{9,17},{17,9},{25,1},{2,26},{10... | collective-permute-start | bytes 786440 | tf_op jit(solution)/shard_map/ppermute | solution.py:10
  5.9 0.5 collective-permute-start.8
  6.4 0.8 %dynamic-slice_convert_fusion.1 = (f32[4,2]{1,0:T(4,128)S(1)}, bf16[4,2]{1,0:T(4,128)(2,1)S(1)}) fusion(s32[16,16]{1,0:T(8,128)} %param.5, s32[]{:T(128)S(6)} %select_n.64, s32[]{:T(128)S(6)} %select_n.65), kind=kLoop, calls=%fused_computation.39 | loop fusion | flops 16 | bytes 88 | tf_op jit(solution)/shard_map/convert_element_type | solution.py:63
  7.2 0.6 %broadcast_in_dim.32 = bf16[512,2,128]{2,1,0:T(2,128)(2,1)S(1)} broadcast(bf16[512,2]{1,0:T(8,128)(2,1)S(1)} %bitcast.112), dimensions={0,1} | broadcast | bytes 264192 | tf_op jit(solution)/shard_map/broadcast_in_dim | solution.py:26
  7.8 1.7 %fusion.14 = (bf16[1,512,256]{2,1,0:T(8,128)(2,1)S(1)}, bf16[512,2048]{1,0:T(8,128)(2,1)}) fusion(bf16[512,256]{1,0:T(8,128)(2,1)} %param.4, bf16[64,8,2,128]{3,2,1,0:T(2,128)(2,1)S(1)} %bitcast.110), kind=kLoop, calls=%fused_computation.44 | loop fusion | flops 524287 | bytes 1048576 | tf_op jit(solution)/shard_map/stack | solution.py:58
  9.7 0.7 %convert_element_type.38 = bf16[16,16]{1,0:T(8,128)(2,1)S(1)} convert(s32[16,16]{1,0:T(8,128)} %param.5) | non-fusion elementwise | flops 256 | bytes 1536 | tf_op jit(solution)/shard_map/convert_element_type | solution.py:28
  10.4 0.1 fusion.15
  10.5 1.3 %collective-permute-done = bf16[512,256]{1,0:T(8,128)(2,1)S(1)} collective-permute-done((bf16[512,256]{1,0:T(8,128)(2,1)}, bf16[512,256]{1,0:T(8,128)(2,1)S(1)}, u32[]{:S(2)}, u32[]{:S(2)}) %collective-permute-start) | collective-permute-done | bytes 262176 | tf_op jit(solution)/shard_map/ppermute | solution.py:10
  11.7 1.5 %collective-permute-start.1 = (bf16[512,256]{1,0:T(8,128)(2,1)}, bf16[512,256]{1,0:T(8,128)(2,1)S(1)}, u32[]{:S(2)}, u32[]{:S(2)}) collective-permute-start(bf16[512,256]{1,0:T(8,128)(2,1)} %param.4), channel_id=1, source_target_pairs={{0,8},{8,0},{16,24},{24,16},{1,9},{9,1},{17,25},{25,17},{2,10},{10... | collective-permute-start | bytes 786440 | tf_op jit(solution)/shard_map/ppermute | solution.py:10
  13.2 7.0 %collective-permute-done.4 = bf16[512,256]{1,0:T(8,128)(2,1)S(1)} collective-permute-done((bf16[512,256]{1,0:T(8,128)(2,1)}, bf16[512,256]{1,0:T(8,128)(2,1)S(1)}, u32[]{:S(2)}, u32[]{:S(2)}) %collective-permute-start.4) | collective-permute-done | bytes 262176 | tf_op jit(solution)/shard_map/ppermute | solution.py:10
  20.2 0.0 collective-permute-start.3
  20.2 6.1 %collective-permute-done.6 = bf16[512,256]{1,0:T(8,128)(2,1)S(1)} collective-permute-done((bf16[512,256]{1,0:T(8,128)(2,1)}, bf16[512,256]{1,0:T(8,128)(2,1)S(1)}, u32[]{:S(2)}, u32[]{:S(2)}) %collective-permute-start.6) | collective-permute-done | bytes 262176 | tf_op jit(solution)/shard_map/ppermute | solution.py:10
  26.3 0.0 collective-permute-start.5
  26.3 0.0 collective-permute-done.9
  26.3 0.5 collective-permute-start.7
  26.9 0.2 mul.233
  27.1 0.1 fusion.3
  27.1 0.0 collective-permute-done.8
  27.1 0.2 mul.228
  27.3 0.1 fusion.4
  27.4 0.0 collective-permute-done.1
  27.4 0.1 collective-permute-start.2
  27.5 0.2 mul.223
  27.7 0.1 fusion.5
  27.7 0.1 pad_maximum_fusion
  27.9 0.6 %gather_fusion = bf16[8,256,256]{2,1,0:T(8,128)(2,1)S(1)} fusion(bf16[8,256,256]{2,1,0:T(8,128)(2,1)S(1)} %bitcast.96, s32[1024]{0:T(1024)S(1)} %pad_clamp_fusion), kind=kCustom, calls=%fused_computation.clone | custom fusion | bytes 2097184 | tf_op jit(solution)/shard_map/jit(_take)/gather | solution.py:59
  28.5 0.0 copy-start
  28.5 0.2 broadcast_select_fusion
  28.7 0.7 %collective-permute-done.2 = bf16[512,256]{1,0:T(8,128)(2,1)} collective-permute-done((bf16[512,256]{1,0:T(8,128)(2,1)}, bf16[512,256]{1,0:T(8,128)(2,1)}, u32[]{:S(2)}, u32[]{:S(2)}) %collective-permute-start.2) | collective-permute-done | bytes 262176 | tf_op jit(solution)/shard_map/ppermute | solution.py:10
  29.3 0.2 mul.195
  29.6 0.6 copy-done
  30.1 1.0 %fusion.12 = bf16[512,2048]{1,0:T(8,128)(2,1)S(1)} fusion(bf16[512,2048]{1,0:T(8,128)(2,1)S(1)} %copy-done, bf16[512,256]{1,0:T(8,128)(2,1)} %collective-permute-done.2, bf16[64,8,2,128]{3,2,1,0:T(2,128)(2,1)S(1)} %bitcast.99), kind=kLoop, calls=%fused_computation.30 | loop fusion | flops 524288 | bytes 786432
  31.1 0.2 mul.199
  31.3 0.1 fusion.11
  31.4 0.0 collective-permute-done.3
  31.4 0.2 mul.203
  31.6 1.0 %fusion.10 = bf16[512,2048]{1,0:T(8,128)(2,1)S(1)} fusion(bf16[512,2048]{1,0:T(8,128)(2,1)S(1)} %fusion.11, bf16[512,256]{1,0:T(8,128)(2,1)} %collective-permute-done.3, bf16[64,8,2,128]{3,2,1,0:T(2,128)(2,1)S(1)} %bitcast.100), kind=kLoop, calls=%fused_computation.26 | loop fusion | flops 524288 | bytes 786432
  32.7 0.2 mul.207
  32.9 0.1 fusion.9
  33.0 0.0 collective-permute-done.5
  33.0 0.2 mul.211
  33.2 1.0 %fusion.8 = bf16[512,2048]{1,0:T(8,128)(2,1)S(1)} fusion(bf16[512,2048]{1,0:T(8,128)(2,1)S(1)} %fusion.9, bf16[512,256]{1,0:T(8,128)(2,1)} %collective-permute-done.5, bf16[64,8,2,128]{3,2,1,0:T(2,128)(2,1)S(1)} %bitcast.101), kind=kLoop, calls=%fused_computation.22 | loop fusion | flops 524288 | bytes 786432
  34.2 0.2 mul.215
  34.4 0.1 fusion.7
  34.5 0.0 collective-permute-done.7
  34.5 0.2 mul.219
  34.7 0.1 fusion.6
  34.8 0.0 copy-start.1
  34.9 0.6 %broadcast_in_dim.30 = f32[512,2,128]{2,1,0:T(2,128)S(1)} broadcast(f32[512,2]{1,0:T(8,128)S(1)} %bitcast.109), dimensions={0,1} | broadcast | bytes 528384 | tf_op jit(solution)/shard_map/broadcast_in_dim | solution.py:26
  35.5 0.7 %fusion.2 = bf16[512,256]{1,0:T(8,128)(2,1)S(1)} fusion(bf16[512,2048]{1,0:T(8,128)(2,1)S(1)} %fusion.6, bf16[2048,256]{1,0:T(8,128)(2,1)S(1)} %bitcast.97, f32[64,8,2,128]{3,2,1,0:T(2,128)S(1)} %bitcast.113), kind=kOutput, calls=%fused_computation.6 | convolution fusion | flops 537133056 | bytes 3932160 | tf_op jit(solution)/shard_map/dot_general | solution.py:62
  36.2 1.6 %collective-permute-start.11 = (bf16[512,256]{1,0:T(8,128)(2,1)S(1)}, bf16[512,256]{1,0:T(8,128)(2,1)S(1)}, u32[]{:S(2)}, u32[]{:S(2)}) collective-permute-start(bf16[512,256]{1,0:T(8,128)(2,1)S(1)} %fusion.2), channel_id=1, source_target_pairs={{0,16},{8,24},{16,0},{24,8},{1,17},{9,25},{17,1},{25,9},{2,18},{10... | collective-permute-start | bytes 786440 | tf_op jit(solution)/shard_map/ppermute | solution.py:10
  37.8 1.4 %collective-permute-start.12 = (bf16[512,256]{1,0:T(8,128)(2,1)S(1)}, bf16[512,256]{1,0:T(8,128)(2,1)S(1)}, u32[]{:S(2)}, u32[]{:S(2)}) collective-permute-start(bf16[512,256]{1,0:T(8,128)(2,1)S(1)} %fusion.2), channel_id=1, source_target_pairs={{0,24},{8,16},{16,8},{24,0},{1,25},{9,17},{17,9},{25,1},{2,26},{10... | collective-permute-start | bytes 786440 | tf_op jit(solution)/shard_map/ppermute | solution.py:10
  39.2 0.5 collective-permute-start.10
  39.7 10.8 %collective-permute-done.11 = bf16[512,256]{1,0:T(8,128)(2,1)S(1)} collective-permute-done((bf16[512,256]{1,0:T(8,128)(2,1)S(1)}, bf16[512,256]{1,0:T(8,128)(2,1)S(1)}, u32[]{:S(2)}, u32[]{:S(2)}) %collective-permute-start.11) | collective-permute-done | bytes 262176 | tf_op jit(solution)/shard_map/ppermute | solution.py:10
  50.6 0.0 collective-permute-done.12
  50.6 1.2 %collective-permute-done.10 = bf16[512,256]{1,0:T(8,128)(2,1)S(1)} collective-permute-done((bf16[512,256]{1,0:T(8,128)(2,1)S(1)}, bf16[512,256]{1,0:T(8,128)(2,1)S(1)}, u32[]{:S(2)}, u32[]{:S(2)}) %collective-permute-start.10) | collective-permute-done | bytes 262176 | tf_op jit(solution)/shard_map/ppermute | solution.py:10
  51.8 0.1 pad_maximum_fusion.1
  51.9 0.6 %gather_fusion.1 = bf16[8,256,256]{2,1,0:T(8,128)(2,1)S(1)} fusion(bf16[8,256,256]{2,1,0:T(8,128)(2,1)S(1)} %bitcast.95, s32[1024]{0:T(1024)S(1)} %pad_clamp_fusion), kind=kCustom, calls=%fused_computation.1.clone | custom fusion | bytes 2097184 | tf_op jit(solution)/shard_map/jit(_take)/gather | solution.py:59
  52.6 0.2 broadcast_select_fusion.1
  52.7 1.4 %copy-done.2 = bf16[512,2048]{1,0:T(8,128)(2,1)S(1)} copy-done((bf16[512,2048]{1,0:T(8,128)(2,1)S(1)}, bf16[512,2048]{1,0:T(8,128)(2,1)}, u32[]{:S(2)}) %copy-start.2) | copy-done | bytes 2097176
  54.2 2.5 %fusion.1 = f32[512,256]{1,0:T(8,128)} fusion(bf16[512,2048]{1,0:T(8,128)(2,1)S(1)} %copy-done.2, bf16[2048,256]{1,0:T(8,128)(2,1)S(1)} %bitcast.98, f32[64,8,2,128]{3,2,1,0:T(2,128)S(1)} %bitcast.114, bf16[512,256]{1,0:T(8,128)(2,1)} %param.4, bf16[64,8,2,128]{3,2,1,0:T(2,128)(2,1)S(1)} %bitcast.111), kind=kOutput, calls=%fused_computation.5 | convolution fusion | flops 537657344 | bytes 4718592 | tf_op jit(solution)/shard_map/dot_general | solution.py:67
  (6 shorter events, 0.1 us)
Async XLA Ops:
  0.0 11.7 %collective-permute-start = (bf16[512,256]{1,0:T(8,128)(2,1)}, bf16[512,256]{1,0:T(8,128)(2,1)S(1)}, u32[]{:S(2)}, u32[]{:S(2)}) collective-permute-start(bf16[512,256]{1,0:T(8,128)(2,1)} %param.4), channel_id=1, source_target_pairs={{0,2},{1,3},{2,0},{3,1},{4,6},{5,7},{6,4},{7,5},{8,10},{9,11},{10,... | collective-permute-start | bytes 786440 | tf_op jit(solution)/shard_map/ppermute | solution.py:10
  1.6 18.6 %collective-permute-start.4 = (bf16[512,256]{1,0:T(8,128)(2,1)}, bf16[512,256]{1,0:T(8,128)(2,1)S(1)}, u32[]{:S(2)}, u32[]{:S(2)}) collective-permute-start(bf16[512,256]{1,0:T(8,128)(2,1)} %param.4), channel_id=1, source_target_pairs={{0,4},{1,5},{2,6},{3,7},{4,0},{5,1},{6,2},{7,3},{8,12},{9,13},{10,... | collective-permute-start | bytes 786440 | tf_op jit(solution)/shard_map/ppermute | solution.py:10
  1.9 24.4 %collective-permute-start.6 = (bf16[512,256]{1,0:T(8,128)(2,1)}, bf16[512,256]{1,0:T(8,128)(2,1)S(1)}, u32[]{:S(2)}, u32[]{:S(2)}) collective-permute-start(bf16[512,256]{1,0:T(8,128)(2,1)} %param.4), channel_id=1, source_target_pairs={{0,6},{1,7},{2,4},{3,5},{4,2},{5,3},{6,0},{7,1},{8,14},{9,15},{10,... | collective-permute-start | bytes 786440 | tf_op jit(solution)/shard_map/ppermute | solution.py:10
  3.5 22.9 %collective-permute-start.9 = (bf16[512,256]{1,0:T(8,128)(2,1)}, bf16[512,256]{1,0:T(8,128)(2,1)S(1)}, u32[]{:S(2)}, u32[]{:S(2)}) collective-permute-start(bf16[512,256]{1,0:T(8,128)(2,1)} %param.4), channel_id=1, source_target_pairs={{0,24},{8,16},{16,8},{24,0},{1,25},{9,17},{17,9},{25,1},{2,26},{10... | collective-permute-start | bytes 786440 | tf_op jit(solution)/shard_map/ppermute | solution.py:10
  5.9 21.2 %collective-permute-start.8 = (bf16[512,256]{1,0:T(8,128)(2,1)}, bf16[512,256]{1,0:T(8,128)(2,1)S(1)}, u32[]{:S(2)}, u32[]{:S(2)}) collective-permute-start(bf16[512,256]{1,0:T(8,128)(2,1)} %param.4), channel_id=1, source_target_pairs={{0,16},{8,24},{16,0},{24,8},{1,17},{9,25},{17,1},{25,9},{2,18},{10... | collective-permute-start | bytes 786440 | tf_op jit(solution)/shard_map/ppermute | solution.py:10
  11.7 15.7 %collective-permute-start.1 = (bf16[512,256]{1,0:T(8,128)(2,1)}, bf16[512,256]{1,0:T(8,128)(2,1)S(1)}, u32[]{:S(2)}, u32[]{:S(2)}) collective-permute-start(bf16[512,256]{1,0:T(8,128)(2,1)} %param.4), channel_id=1, source_target_pairs={{0,8},{8,0},{16,24},{24,16},{1,9},{9,1},{17,25},{25,17},{2,10},{10... | collective-permute-start | bytes 786440 | tf_op jit(solution)/shard_map/ppermute | solution.py:10
  20.2 11.2 %collective-permute-start.3 = (bf16[512,256]{1,0:T(8,128)(2,1)S(1)}, bf16[512,256]{1,0:T(8,128)(2,1)}, u32[]{:S(2)}, u32[]{:S(2)}) collective-permute-start(bf16[512,256]{1,0:T(8,128)(2,1)S(1)} %collective-permute-done), channel_id=1, source_target_pairs={{0,1},{1,0},{2,3},{3,2},{4,5},{5,4},{6,7},{7,6},{8,9},{9,8},{10,11... | collective-permute-start | bytes 786440 | tf_op jit(solution)/shard_map/ppermute | solution.py:10
  26.3 6.6 %collective-permute-start.5 = (bf16[512,256]{1,0:T(8,128)(2,1)S(1)}, bf16[512,256]{1,0:T(8,128)(2,1)}, u32[]{:S(2)}, u32[]{:S(2)}) collective-permute-start(bf16[512,256]{1,0:T(8,128)(2,1)S(1)} %collective-permute-done.4), channel_id=1, source_target_pairs={{0,1},{1,0},{2,3},{3,2},{4,5},{5,4},{6,7},{7,6},{8,9},{9,8},{10,11... | collective-permute-start | bytes 786440 | tf_op jit(solution)/shard_map/ppermute | solution.py:10
  26.3 8.2 %collective-permute-start.7 = (bf16[512,256]{1,0:T(8,128)(2,1)S(1)}, bf16[512,256]{1,0:T(8,128)(2,1)S(1)}, u32[]{:S(2)}, u32[]{:S(2)}) collective-permute-start(bf16[512,256]{1,0:T(8,128)(2,1)S(1)} %collective-permute-done.6), channel_id=1, source_target_pairs={{0,1},{1,0},{2,3},{3,2},{4,5},{5,4},{6,7},{7,6},{8,9},{9,8},{10,11... | collective-permute-start | bytes 786440 | tf_op jit(solution)/shard_map/ppermute | solution.py:10
  27.4 1.9 %collective-permute-start.2 = (bf16[512,256]{1,0:T(8,128)(2,1)}, bf16[512,256]{1,0:T(8,128)(2,1)}, u32[]{:S(2)}, u32[]{:S(2)}) collective-permute-start(bf16[512,256]{1,0:T(8,128)(2,1)} %param.4), channel_id=1, source_target_pairs={{0,1},{1,0},{2,3},{3,2},{4,5},{5,4},{6,7},{7,6},{8,9},{9,8},{10,11... | collective-permute-start | bytes 786440 | tf_op jit(solution)/shard_map/ppermute | solution.py:10
  28.5 1.6 %copy-start = (bf16[512,2048]{1,0:T(8,128)(2,1)S(1)}, bf16[512,2048]{1,0:T(8,128)(2,1)}, u32[]{:S(2)}) copy-start(bf16[512,2048]{1,0:T(8,128)(2,1)} %get-tuple-element.13) | copy-start | bytes 6291460
  34.8 1.4 %copy-start.1 = (bf16[512,2048]{1,0:T(8,128)(2,1)}, bf16[512,2048]{1,0:T(8,128)(2,1)S(1)}, u32[]{:S(2)}) copy-start(bf16[512,2048]{1,0:T(8,128)(2,1)S(1)} %fusion.6) | copy-start | bytes 6291460
  36.2 14.4 %collective-permute-start.11 = (bf16[512,256]{1,0:T(8,128)(2,1)S(1)}, bf16[512,256]{1,0:T(8,128)(2,1)S(1)}, u32[]{:S(2)}, u32[]{:S(2)}) collective-permute-start(bf16[512,256]{1,0:T(8,128)(2,1)S(1)} %fusion.2), channel_id=1, source_target_pairs={{0,16},{8,24},{16,0},{24,8},{1,17},{9,25},{17,1},{25,9},{2,18},{10... | collective-permute-start | bytes 786440 | tf_op jit(solution)/shard_map/ppermute | solution.py:10
  37.8 12.8 %collective-permute-start.12 = (bf16[512,256]{1,0:T(8,128)(2,1)S(1)}, bf16[512,256]{1,0:T(8,128)(2,1)S(1)}, u32[]{:S(2)}, u32[]{:S(2)}) collective-permute-start(bf16[512,256]{1,0:T(8,128)(2,1)S(1)} %fusion.2), channel_id=1, source_target_pairs={{0,24},{8,16},{16,8},{24,0},{1,25},{9,17},{17,9},{25,1},{2,26},{10... | collective-permute-start | bytes 786440 | tf_op jit(solution)/shard_map/ppermute | solution.py:10
  39.2 12.6 %collective-permute-start.10 = (bf16[512,256]{1,0:T(8,128)(2,1)S(1)}, bf16[512,256]{1,0:T(8,128)(2,1)S(1)}, u32[]{:S(2)}, u32[]{:S(2)}) collective-permute-start(bf16[512,256]{1,0:T(8,128)(2,1)S(1)} %fusion.2), channel_id=1, source_target_pairs={{0,8},{8,0},{16,24},{24,16},{1,9},{9,1},{17,25},{25,17},{2,10},{10... | collective-permute-start | bytes 786440 | tf_op jit(solution)/shard_map/ppermute | solution.py:10
  52.6 1.6 %copy-start.2 = (bf16[512,2048]{1,0:T(8,128)(2,1)S(1)}, bf16[512,2048]{1,0:T(8,128)(2,1)}, u32[]{:S(2)}) copy-start(bf16[512,2048]{1,0:T(8,128)(2,1)} %copy-done.1) | copy-start | bytes 6291460

commit v17 on v15

--- a/solution.py
+++ b/solution.py
@@ -61,8 +61,14 @@
         mask_float = local_mask.astype(jnp.float32)
         filtered = (mask_float * square).astype(jnp.bfloat16)
         f_pieces = [filtered] + [_swap(filtered, "row", n_row, k) for k in range(1, n_row)]
-        f_slot = in_slot_order(f_pieces)
-        cubic = jnp.dot(row_cat, f_slot, preferred_element_type=jnp.float32)
+        f_members = (
+            (jnp.arange(n_row, dtype=jnp.int32)[:, None] ^ row_index) * ratio
+            + jnp.arange(ratio, dtype=jnp.int32)[None, :]
+        ).reshape(-1)
+        row_f = jnp.take(row_cat.reshape(rows, n_col, cols), f_members ^ col_index, axis=1)
+        row_f = row_f.reshape(rows, n_col * cols)
+        f_cat = jnp.concatenate(f_pieces, axis=0)
+        cubic = jnp.dot(row_f, f_cat, preferred_element_type=jnp.float32)
         return mask_float * (1.5 * masked.astype(jnp.float32) - 0.5 * cubic)
 
     return body

time: 51.9 us -> 50.8 us (0.979)
  waiting for transfers between devices: 26.5 us -> 14.1 us
  other arithmetic: 4.51 us -> 11.1 us
  local copies, waits for them, and re-layouts: 6.03 us -> 9.78 us
  matrix products: 3.17 us -> 4.14 us
    ppermute x13, waiting for transfers between devices: 26.5 us -> 14.1 us  [_swap(): return lax.ppermute(x, axis, [(i, i ^ d) for i in range(size)])]
    unnamed x6 -> x13, other arithmetic: 0.45 us -> 6.74 us
    gather x0 -> x2, local copies, waits for them, and re-layouts: none -> 4.7 us  [body(): jnp.take(row_cat.reshape(rows, n_col, cols), f_members ^ col_index, axis=1)]
    another operation x3 -> x1, other arithmetic: 2.01 us -> 0.13 us  [in_slot_order(): stacked = jnp.stack(pieces).reshape(n_row * ratio, cols, cols)]
    select_n x0 -> x2, other arithmetic: none -> 1.83 us  [body(): jnp.take(row_cat.reshape(rows, n_col, cols), f_members ^ col_index, axis=1)]
    concatenate x1 -> x2, other arithmetic: 0.08 us -> 0.85 us  [body(): row_cat = jnp.concatenate(row_pieces, axis=1)]
    unnamed x6 -> x9, local copies, waits for them, and re-layouts: 1.42 us -> 0.72 us
    convert_element_type x1, other arithmetic: 0.7 us -> 0.01 us  [body(): keep = pattern.astype(jnp.bfloat16)]
  transfers between devices with their start and end apart: 13 -> 13, of which waited for: 6 -> 5; matrix products, arithmetic and copies ran while one was open for 14% -> 40% of each run, Pallas kernels for 0% -> 0%
where the time goes in v17:
time: 50.8 us; the launch traced here: 50.5 us
  waiting for transfers between devices  14.1 us (28%)
  other arithmetic  11.1 us (22%)
  starting transfers between devices  11 us (22%)
  local copies, waits for them, and re-layouts  9.78 us (19%)
  matrix products  4.14 us (8%)
    ppermute x13, waiting for transfers between devices, _swap(): return lax.ppermute(x, axis, [(i, i ^ d) for i in range(size)])  14.1 us
    ppermute x13, starting transfers between devices, _swap(): return lax.ppermute(x, axis, [(i, i ^ d) for i in range(size)])  11 us
    unnamed x13, other arithmetic  6.74 us
    gather x2, local copies, waits for them, and re-layouts, body(): jnp.take(row_cat.reshape(rows, n_col, cols), f_members ^ col_index, axis=1)  4.7 us
    dot_general x1, matrix products, body(): cubic = jnp.dot(row_f, f_cat, preferred_element_type=jnp.float32)  2.73 us
    mul x10, local copies, waits for them, and re-layouts, mask_from(): return (x4 * blocks[:, None, :, None]).reshape(rows, cols)  2.05 us
    select_n x2, other arithmetic, body(): jnp.take(row_cat.reshape(rows, n_col, cols), f_members ^ col_index, axis=1)  1.83 us
    dot_general x1, matrix products, body(): jnp.dot(row_cat, in_slot_order(col_pieces), preferred_element_type=jnp.fl...  1.41 us
  transfers between devices with their start and end apart: 13, of which 5 were waited for; matrix products, arithmetic and copies ran while one was open for 40% of the time, Pallas kernels for 0%

profile of v17, /device:TPU:16, one launch (start us, length us, event | category | flops | bytes accessed | tf_op | source)
XLA Modules:
  0.0 50.5 jit_solution(12355883651772361448)
XLA Ops:
  0.0 1.5 %collective-permute-start = (bf16[512,256]{1,0:T(8,128)(2,1)}, bf16[512,256]{1,0:T(8,128)(2,1)S(1)}, u32[]{:S(2)}, u32[]{:S(2)}) collective-permute-start(bf16[512,256]{1,0:T(8,128)(2,1)} %param.2), channel_id=1, source_target_pairs={{0,8},{8,0},{16,24},{24,16},{1,9},{9,1},{17,25},{25,17},{2,10},{10... | collective-permute-start | bytes 786440 | tf_op jit(solution)/shard_map/ppermute | solution.py:10
  1.5 1.6 %collective-permute-start.2 = (bf16[512,256]{1,0:T(8,128)(2,1)}, bf16[512,256]{1,0:T(8,128)(2,1)S(1)}, u32[]{:S(2)}, u32[]{:S(2)}) collective-permute-start(bf16[512,256]{1,0:T(8,128)(2,1)} %param.2), channel_id=1, source_target_pairs={{0,2},{1,3},{2,0},{3,1},{4,6},{5,7},{6,4},{7,5},{8,10},{9,11},{10,... | collective-permute-start | bytes 786440 | tf_op jit(solution)/shard_map/ppermute | solution.py:10
  3.1 0.3 collective-permute-start.4
  3.4 1.6 %collective-permute-start.6 = (bf16[512,256]{1,0:T(8,128)(2,1)}, bf16[512,256]{1,0:T(8,128)(2,1)S(1)}, u32[]{:S(2)}, u32[]{:S(2)}) collective-permute-start(bf16[512,256]{1,0:T(8,128)(2,1)} %param.2), channel_id=1, source_target_pairs={{0,6},{1,7},{2,4},{3,5},{4,2},{5,3},{6,0},{7,1},{8,14},{9,15},{10,... | collective-permute-start | bytes 786440 | tf_op jit(solution)/shard_map/ppermute | solution.py:10
  5.0 1.5 %collective-permute-start.9 = (bf16[512,256]{1,0:T(8,128)(2,1)}, bf16[512,256]{1,0:T(8,128)(2,1)S(1)}, u32[]{:S(2)}, u32[]{:S(2)}) collective-permute-start(bf16[512,256]{1,0:T(8,128)(2,1)} %param.2), channel_id=1, source_target_pairs={{0,24},{8,16},{16,8},{24,0},{1,25},{9,17},{17,9},{25,1},{2,26},{10... | collective-permute-start | bytes 786440 | tf_op jit(solution)/shard_map/ppermute | solution.py:10
  6.5 0.1 add_xor_fusion
  6.6 0.1 xor.112
  6.7 0.1 xor.104
  6.7 0.8 %dynamic-slice_convert_fusion.1 = (f32[4,2]{1,0:T(4,128)S(1)}, bf16[4,2]{1,0:T(4,128)(2,1)S(1)}) fusion(s32[16,16]{1,0:T(8,128)} %param.3, s32[]{:T(128)S(6)} %select_n.120, s32[]{:T(128)S(6)} %select_n.121), kind=kLoop, calls=%fused_computation.61 | loop fusion | flops 16 | bytes 88 | tf_op jit(solution)/shard_map/convert_element_type | solution.py:61
  7.5 0.6 %broadcast_in_dim.53 = bf16[512,2,128]{2,1,0:T(2,128)(2,1)S(1)} broadcast(bf16[512,2]{1,0:T(8,128)(2,1)S(1)} %bitcast.142), dimensions={0,1} | broadcast | bytes 264192 | tf_op jit(solution)/shard_map/broadcast_in_dim | solution.py:26
  8.1 1.7 %constant_dynamic-update-slice_fusion = (bf16[512,2048]{1,0:T(8,128)(2,1)}, bf16[512,256]{1,0:T(8,128)(2,1)S(1)}) fusion(bf16[512,256]{1,0:T(8,128)(2,1)} %param.2, bf16[64,8,2,128]{3,2,1,0:T(2,128)(2,1)S(1)} %bitcast.141), kind=kLoop, calls=%fused_computation.46 | loop fusion | flops 524287 | bytes 1048576
  9.9 0.7 %bitcast_dynamic-update-slice_fusion.7 = bf16[512,8,256]{2,0,1:T(8,128)(2,1)} fusion(bf16[512,256]{1,0:T(8,128)(2,1)S(1)} %get-tuple-element.8), kind=kLoop, calls=%fused_computation.38 | loop fusion | bytes 524288
  10.8 0.1 fusion.25
  10.9 0.1 broadcast_in_dim.58
  11.0 0.1 broadcast_in_dim.54
  11.1 0.6 %collective-permute-start.8 = (bf16[512,256]{1,0:T(8,128)(2,1)}, bf16[512,256]{1,0:T(8,128)(2,1)S(1)}, u32[]{:S(2)}, u32[]{:S(2)}) collective-permute-start(bf16[512,256]{1,0:T(8,128)(2,1)} %param.2), channel_id=1, source_target_pairs={{0,16},{8,24},{16,0},{24,8},{1,17},{9,25},{17,1},{25,9},{2,18},{10... | collective-permute-start | bytes 786440 | tf_op jit(solution)/shard_map/ppermute | solution.py:10
  11.6 0.2 mul.244
  11.9 0.1 fusion.12
  11.9 3.0 %collective-permute-done.9 = bf16[512,256]{1,0:T(8,128)(2,1)S(1)} collective-permute-done((bf16[512,256]{1,0:T(8,128)(2,1)}, bf16[512,256]{1,0:T(8,128)(2,1)S(1)}, u32[]{:S(2)}, u32[]{:S(2)}) %collective-permute-start.9) | collective-permute-done | bytes 262176 | tf_op jit(solution)/shard_map/ppermute | solution.py:10
  14.9 0.0 collective-permute-start.1
  14.9 0.2 mul.254
  15.2 0.1 fusion.10
  15.2 5.2 %collective-permute-done.8 = bf16[512,256]{1,0:T(8,128)(2,1)S(1)} collective-permute-done((bf16[512,256]{1,0:T(8,128)(2,1)}, bf16[512,256]{1,0:T(8,128)(2,1)S(1)}, u32[]{:S(2)}, u32[]{:S(2)}) %collective-permute-start.8) | collective-permute-done | bytes 262176 | tf_op jit(solution)/shard_map/ppermute | solution.py:10
  20.5 0.2 mul.249
  20.7 0.1 fusion.11
  20.7 0.1 pad_maximum_fusion
  20.9 0.6 %gather_fusion.1 = bf16[8,256,256]{2,1,0:T(8,128)(2,1)S(1)} fusion(bf16[8,256,256]{2,1,0:T(8,128)(2,1)S(1)} %bitcast.121, s32[1024]{0:T(1024)S(1)} %pad_clamp_fusion), kind=kCustom, calls=%fused_computation.1 | custom fusion | bytes 2097184 | tf_op jit(solution)/shard_map/jit(_take)/gather | solution.py:57
  21.5 0.1 collective-permute-start.3
  21.6 0.1 collective-permute-done.4
  21.7 0.4 collective-permute-start.5
  22.1 5.5 %collective-permute-done.6 = bf16[512,256]{1,0:T(8,128)(2,1)S(1)} collective-permute-done((bf16[512,256]{1,0:T(8,128)(2,1)}, bf16[512,256]{1,0:T(8,128)(2,1)S(1)}, u32[]{:S(2)}, u32[]{:S(2)}) %collective-permute-start.6) | collective-permute-done | bytes 262176 | tf_op jit(solution)/shard_map/ppermute | solution.py:10
  27.6 0.5 %bitcast_select_fusion.1 = bf16[2048,256]{1,0:T(8,128)(2,1)S(1)} fusion(bf16[8,256,256]{2,1,0:T(8,128)(2,1)S(1)} %gather_fusion.1, pred[2048]{0:T(1024)(128)(4,1)S(1)} %broadcast_in_dim.59), kind=kLoop, calls=%fused_computation.16 | loop fusion | flops 524288 | bytes 2099200 | tf_op jit(solution)/shard_map/jit(_take)/select_n | solution.py:57
  28.1 0.2 mul.215
  28.3 0.1 fusion.13
  28.4 0.2 mul.219
  28.6 0.1 fusion.14
  28.7 0.2 mul.223
  28.9 0.1 fusion.15
  29.0 0.2 mul.227
  29.2 0.1 fusion.16
  29.3 0.2 mul.231
  29.5 0.1 fusion.17
  29.6 0.2 mul.235
  29.8 0.1 fusion.18
  29.8 0.2 mul.239
  30.1 0.1 fusion.19
  30.2 0.6 %broadcast_in_dim.51 = f32[512,2,128]{2,1,0:T(2,128)S(1)} broadcast(f32[512,2]{1,0:T(8,128)S(1)} %bitcast.140), dimensions={0,1} | broadcast | bytes 528384 | tf_op jit(solution)/shard_map/broadcast_in_dim | solution.py:26
  30.8 0.0 copy-start
  30.8 1.4 %fusion.2 = bf16[512,256]{1,0:T(8,128)(2,1)} fusion(bf16[512,2048]{1,0:T(8,128)(2,1)S(1)} %fusion.19, bf16[2048,256]{1,0:T(8,128)(2,1)S(1)} %bitcast_select_fusion.1, f32[64,8,2,128]{3,2,1,0:T(2,128)S(1)} %bitcast.143), kind=kOutput, calls=%fused_computation.7 | convolution fusion | flops 537133056 | bytes 3932160 | tf_op jit(solution)/shard_map/dot_general | solution.py:60
  32.2 0.5 %collective-permute-start.10 = (bf16[512,256]{1,0:T(8,128)(2,1)}, bf16[512,256]{1,0:T(8,128)(2,1)}, u32[]{:S(2)}, u32[]{:S(2)}) collective-permute-start(bf16[512,256]{1,0:T(8,128)(2,1)} %fusion.2), channel_id=1, source_target_pairs={{0,8},{8,0},{16,24},{24,16},{1,9},{9,1},{17,25},{25,17},{2,10},{10... | collective-permute-start | bytes 786440 | tf_op jit(solution)/shard_map/ppermute | solution.py:10
  32.7 1.5 %collective-permute-start.11 = (bf16[512,256]{1,0:T(8,128)(2,1)}, bf16[512,256]{1,0:T(8,128)(2,1)}, u32[]{:S(2)}, u32[]{:S(2)}) collective-permute-start(bf16[512,256]{1,0:T(8,128)(2,1)} %fusion.2), channel_id=1, source_target_pairs={{0,16},{8,24},{16,0},{24,8},{1,17},{9,25},{17,1},{25,9},{2,18},{10... | collective-permute-start | bytes 786440 | tf_op jit(solution)/shard_map/ppermute | solution.py:10
  34.2 1.4 %collective-permute-start.12 = (bf16[512,256]{1,0:T(8,128)(2,1)}, bf16[512,256]{1,0:T(8,128)(2,1)}, u32[]{:S(2)}, u32[]{:S(2)}) collective-permute-start(bf16[512,256]{1,0:T(8,128)(2,1)} %fusion.2), channel_id=1, source_target_pairs={{0,24},{8,16},{16,8},{24,0},{1,25},{9,17},{17,9},{25,1},{2,26},{10... | collective-permute-start | bytes 786440 | tf_op jit(solution)/shard_map/ppermute | solution.py:10
  35.7 0.8 %bitcast_dynamic-update-slice_fusion.6 = bf16[512,8,256]{2,0,1:T(8,128)(2,1)} fusion(bf16[512,8,256]{2,0,1:T(8,128)(2,1)} %bitcast_dynamic-update-slice_fusion.7, bf16[512,256]{1,0:T(8,128)(2,1)S(1)} %collective-permute-done.1, bf16[64,8,2,128]{3,2,1,0:T(2,128)(2,1)S(1)} %bitcast.123), kind=kLoop, calls=%fused_computation.37 | loop fusion | flops 524288 | bytes 786432
  36.4 0.8 %bitcast_dynamic-update-slice_fusion.5 = bf16[512,8,256]{2,0,1:T(8,128)(2,1)} fusion(bf16[512,8,256]{2,0,1:T(8,128)(2,1)} %bitcast_dynamic-update-slice_fusion.6, bf16[512,256]{1,0:T(8,128)(2,1)S(1)} %collective-permute-done.2, bf16[64,8,2,128]{3,2,1,0:T(2,128)(2,1)S(1)} %bitcast.125), kind=kLoop, calls=%fused_computation.36 | loop fusion | flops 524288 | bytes 786432
  37.2 0.8 %bitcast_dynamic-update-slice_fusion.4 = bf16[512,8,256]{2,0,1:T(8,128)(2,1)} fusion(bf16[512,8,256]{2,0,1:T(8,128)(2,1)} %bitcast_dynamic-update-slice_fusion.5, bf16[512,256]{1,0:T(8,128)(2,1)S(1)} %collective-permute-done.3, bf16[64,8,2,128]{3,2,1,0:T(2,128)(2,1)S(1)} %bitcast.127), kind=kLoop, calls=%fused_computation.35 | loop fusion | flops 524288 | bytes 786432
  38.0 0.8 %bitcast_dynamic-update-slice_fusion.3 = bf16[512,8,256]{2,0,1:T(8,128)(2,1)} fusion(bf16[512,8,256]{2,0,1:T(8,128)(2,1)} %bitcast_dynamic-update-slice_fusion.4, bf16[512,256]{1,0:T(8,128)(2,1)S(1)} %collective-permute-done.4, bf16[64,8,2,128]{3,2,1,0:T(2,128)(2,1)S(1)} %bitcast.129), kind=kLoop, calls=%fused_computation.34 | loop fusion | flops 524288 | bytes 786432
  38.7 0.8 %bitcast_dynamic-update-slice_fusion.2 = bf16[512,8,256]{2,0,1:T(8,128)(2,1)} fusion(bf16[512,8,256]{2,0,1:T(8,128)(2,1)} %bitcast_dynamic-update-slice_fusion.3, bf16[512,256]{1,0:T(8,128)(2,1)S(1)} %collective-permute-done.5, bf16[64,8,2,128]{3,2,1,0:T(2,128)(2,1)S(1)} %bitcast.131), kind=kLoop, calls=%fused_computation.33 | loop fusion | flops 524288 | bytes 786432
  39.5 0.8 %bitcast_dynamic-update-slice_fusion.1 = bf16[512,8,256]{2,0,1:T(8,128)(2,1)} fusion(bf16[512,8,256]{2,0,1:T(8,128)(2,1)} %bitcast_dynamic-update-slice_fusion.2, bf16[512,256]{1,0:T(8,128)(2,1)S(1)} %collective-permute-done.6, bf16[64,8,2,128]{3,2,1,0:T(2,128)(2,1)S(1)} %bitcast.133), kind=kLoop, calls=%fused_computation.32 | loop fusion | flops 524288 | bytes 786432
  40.3 0.8 %bitcast_dynamic-update-slice_fusion = bf16[512,8,256]{2,0,1:T(8,128)(2,1)} fusion(bf16[512,8,256]{2,0,1:T(8,128)(2,1)} %bitcast_dynamic-update-slice_fusion.1, bf16[512,256]{1,0:T(8,128)(2,1)S(1)} %collective-permute-done.7, bf16[64,8,2,128]{3,2,1,0:T(2,128)(2,1)S(1)} %bitcast.135), kind=kLoop, calls=%fused_computation.31 | loop fusion | flops 524288 | bytes 786432 | tf_op jit(solution)/shard_map/concatenate | solution.py:59
  41.1 2.3 %gather_fusion = bf16[8,512,256]{2,1,0:T(8,128)(2,1)S(1)} fusion(bf16[512,8,256]{2,0,1:T(8,128)(2,1)} %bitcast_dynamic-update-slice_fusion, s32[1024]{0:T(1024)S(1)} %pad_clamp_fusion.1), kind=kCustom, calls=%fused_computation | custom fusion | bytes 4194336 | tf_op jit(solution)/shard_map/jit(_take)/gather | solution.py:68
  43.3 2.4 %copy.3 = bf16[512,8,256]{0,2,1:T(8,128)(2,1)} copy(bf16[512,8,256]{2,0,1:T(8,128)(2,1)S(1)} %bitcast.120) | data formatting | bytes 4194304 | tf_op jit(solution)/shard_map/jit(_take)/gather | solution.py:68
  45.8 1.8 %bitcast_select_fusion = bf16[512,2048]{0,1:T(8,128)(2,1)S(1)} fusion(bf16[512,8,256]{0,2,1:T(8,128)(2,1)} %copy.3, pred[2048]{0:T(1024)(128)(4,1)S(1)} %broadcast_in_dim.55), kind=kLoop, calls=%fused_computation.2 | loop fusion | flops 1048576 | bytes 4196352 | tf_op jit(solution)/shard_map/jit(_take)/select_n | solution.py:68
  47.6 0.2 collective-permute-done.12
  47.8 2.7 %fusion.1 = f32[512,256]{1,0:T(8,128)} fusion(bf16[512,2048]{0,1:T(8,128)(2,1)S(1)} %bitcast_select_fusion, bf16[512,256]{1,0:T(8,128)(2,1)} %collective-permute-done.12, bf16[512,256]{1,0:T(8,128)(2,1)} %collective-permute-done.11, bf16[512,256]{1,0:T(8,128)(2,1)} %collective-permute-done.10, bf16[512,256]{1,0:T(8,128)(2,1)} %fusion.2, ...), kind=kOutput, calls=%fused_computation.6 | convolution fusion | flops 541720576 | bytes 4456448 | tf_op jit(solution)/shard_map/dot_general | solution.py:71
  (28 shorter events, 0.2 us)
Async XLA Ops:
  0.0 10.7 %copy-start.3 = (s32[16,16]{1,0:T(8,128)S(1)}, s32[16,16]{1,0:T(8,128)}, u32[]{:S(2)}) copy-start(s32[16,16]{1,0:T(8,128)} %param.3) | copy-start | bytes 3076
  0.0 11.1 %collective-permute-start = (bf16[512,256]{1,0:T(8,128)(2,1)}, bf16[512,256]{1,0:T(8,128)(2,1)S(1)}, u32[]{:S(2)}, u32[]{:S(2)}) collective-permute-start(bf16[512,256]{1,0:T(8,128)(2,1)} %param.2), channel_id=1, source_target_pairs={{0,8},{8,0},{16,24},{24,16},{1,9},{9,1},{17,25},{25,17},{2,10},{10... | collective-permute-start | bytes 786440 | tf_op jit(solution)/shard_map/ppermute | solution.py:10
  1.5 20.0 %collective-permute-start.2 = (bf16[512,256]{1,0:T(8,128)(2,1)}, bf16[512,256]{1,0:T(8,128)(2,1)S(1)}, u32[]{:S(2)}, u32[]{:S(2)}) collective-permute-start(bf16[512,256]{1,0:T(8,128)(2,1)} %param.2), channel_id=1, source_target_pairs={{0,2},{1,3},{2,0},{3,1},{4,6},{5,7},{6,4},{7,5},{8,10},{9,11},{10,... | collective-permute-start | bytes 786440 | tf_op jit(solution)/shard_map/ppermute | solution.py:10
  3.1 18.7 %collective-permute-start.4 = (bf16[512,256]{1,0:T(8,128)(2,1)}, bf16[512,256]{1,0:T(8,128)(2,1)S(1)}, u32[]{:S(2)}, u32[]{:S(2)}) collective-permute-start(bf16[512,256]{1,0:T(8,128)(2,1)} %param.2), channel_id=1, source_target_pairs={{0,4},{1,5},{2,6},{3,7},{4,0},{5,1},{6,2},{7,3},{8,12},{9,13},{10,... | collective-permute-start | bytes 786440 | tf_op jit(solution)/shard_map/ppermute | solution.py:10
  3.4 24.1 %collective-permute-start.6 = (bf16[512,256]{1,0:T(8,128)(2,1)}, bf16[512,256]{1,0:T(8,128)(2,1)S(1)}, u32[]{:S(2)}, u32[]{:S(2)}) collective-permute-start(bf16[512,256]{1,0:T(8,128)(2,1)} %param.2), channel_id=1, source_target_pairs={{0,6},{1,7},{2,4},{3,5},{4,2},{5,3},{6,0},{7,1},{8,14},{9,15},{10,... | collective-permute-start | bytes 786440 | tf_op jit(solution)/shard_map/ppermute | solution.py:10
  5.0 10.0 %collective-permute-start.9 = (bf16[512,256]{1,0:T(8,128)(2,1)}, bf16[512,256]{1,0:T(8,128)(2,1)S(1)}, u32[]{:S(2)}, u32[]{:S(2)}) collective-permute-start(bf16[512,256]{1,0:T(8,128)(2,1)} %param.2), channel_id=1, source_target_pairs={{0,24},{8,16},{16,8},{24,0},{1,25},{9,17},{17,9},{25,1},{2,26},{10... | collective-permute-start | bytes 786440 | tf_op jit(solution)/shard_map/ppermute | solution.py:10
  11.1 9.4 %collective-permute-start.8 = (bf16[512,256]{1,0:T(8,128)(2,1)}, bf16[512,256]{1,0:T(8,128)(2,1)S(1)}, u32[]{:S(2)}, u32[]{:S(2)}) collective-permute-start(bf16[512,256]{1,0:T(8,128)(2,1)} %param.2), channel_id=1, source_target_pairs={{0,16},{8,24},{16,0},{24,8},{1,17},{9,25},{17,1},{25,9},{2,18},{10... | collective-permute-start | bytes 786440 | tf_op jit(solution)/shard_map/ppermute | solution.py:10
  14.9 13.2 %collective-permute-start.1 = (bf16[512,256]{1,0:T(8,128)(2,1)}, bf16[512,256]{1,0:T(8,128)(2,1)S(1)}, u32[]{:S(2)}, u32[]{:S(2)}) collective-permute-start(bf16[512,256]{1,0:T(8,128)(2,1)} %param.2), channel_id=1, source_target_pairs={{0,1},{1,0},{2,3},{3,2},{4,5},{5,4},{6,7},{7,6},{8,9},{9,8},{10,11... | collective-permute-start | bytes 786440 | tf_op jit(solution)/shard_map/ppermute | solution.py:10
  21.5 6.8 %copy-start.2 = (bf16[512,2048]{1,0:T(8,128)(2,1)S(1)}, bf16[512,2048]{1,0:T(8,128)(2,1)}, u32[]{:S(2)}) copy-start(bf16[512,2048]{1,0:T(8,128)(2,1)} %get-tuple-element.7) | copy-start | bytes 6291460
  21.5 7.2 %collective-permute-start.3 = (bf16[512,256]{1,0:T(8,128)(2,1)S(1)}, bf16[512,256]{1,0:T(8,128)(2,1)S(1)}, u32[]{:S(2)}, u32[]{:S(2)}) collective-permute-start(bf16[512,256]{1,0:T(8,128)(2,1)S(1)} %collective-permute-done.2), channel_id=1, source_target_pairs={{0,1},{1,0},{2,3},{3,2},{4,5},{5,4},{6,7},{7,6},{8,9},{9,8},{10,11... | collective-permute-start | bytes 786440 | tf_op jit(solution)/shard_map/ppermute | solution.py:10
  21.7 7.5 %collective-permute-start.5 = (bf16[512,256]{1,0:T(8,128)(2,1)S(1)}, bf16[512,256]{1,0:T(8,128)(2,1)S(1)}, u32[]{:S(2)}, u32[]{:S(2)}) collective-permute-start(bf16[512,256]{1,0:T(8,128)(2,1)S(1)} %collective-permute-done.4), channel_id=1, source_target_pairs={{0,1},{1,0},{2,3},{3,2},{4,5},{5,4},{6,7},{7,6},{8,9},{9,8},{10,11... | collective-permute-start | bytes 786440 | tf_op jit(solution)/shard_map/ppermute | solution.py:10
  27.6 2.3 %collective-permute-start.7 = (bf16[512,256]{1,0:T(8,128)(2,1)S(1)}, bf16[512,256]{1,0:T(8,128)(2,1)S(1)}, u32[]{:S(2)}, u32[]{:S(2)}) collective-permute-start(bf16[512,256]{1,0:T(8,128)(2,1)S(1)} %collective-permute-done.6), channel_id=1, source_target_pairs={{0,1},{1,0},{2,3},{3,2},{4,5},{5,4},{6,7},{7,6},{8,9},{9,8},{10,11... | collective-permute-start | bytes 786440 | tf_op jit(solution)/shard_map/ppermute | solution.py:10
  30.8 1.4 %copy-start = (f32[512,2,128]{2,1,0:T(2,128)}, f32[512,2,128]{2,1,0:T(2,128)S(1)}, u32[]{:S(2)}) copy-start(f32[512,2,128]{2,1,0:T(2,128)S(1)} %broadcast_in_dim.51) | copy-start | bytes 1572868
  32.2 15.4 %collective-permute-start.10 = (bf16[512,256]{1,0:T(8,128)(2,1)}, bf16[512,256]{1,0:T(8,128)(2,1)}, u32[]{:S(2)}, u32[]{:S(2)}) collective-permute-start(bf16[512,256]{1,0:T(8,128)(2,1)} %fusion.2), channel_id=1, source_target_pairs={{0,8},{8,0},{16,24},{24,16},{1,9},{9,1},{17,25},{25,17},{2,10},{10... | collective-permute-start | bytes 786440 | tf_op jit(solution)/shard_map/ppermute | solution.py:10
  32.7 14.9 %collective-permute-start.11 = (bf16[512,256]{1,0:T(8,128)(2,1)}, bf16[512,256]{1,0:T(8,128)(2,1)}, u32[]{:S(2)}, u32[]{:S(2)}) collective-permute-start(bf16[512,256]{1,0:T(8,128)(2,1)} %fusion.2), channel_id=1, source_target_pairs={{0,16},{8,24},{16,0},{24,8},{1,17},{9,25},{17,1},{25,9},{2,18},{10... | collective-permute-start | bytes 786440 | tf_op jit(solution)/shard_map/ppermute | solution.py:10
  34.2 13.6 %collective-permute-start.12 = (bf16[512,256]{1,0:T(8,128)(2,1)}, bf16[512,256]{1,0:T(8,128)(2,1)}, u32[]{:S(2)}, u32[]{:S(2)}) collective-permute-start(bf16[512,256]{1,0:T(8,128)(2,1)} %fusion.2), channel_id=1, source_target_pairs={{0,24},{8,16},{16,8},{24,0},{1,25},{9,17},{17,9},{25,1},{2,26},{10... | collective-permute-start | bytes 786440 | tf_op jit(solution)/shard_map/ppermute | solution.py:10
  45.8 2.0 %copy-start.1 = (f32[512,2,128]{2,1,0:T(2,128)S(1)}, f32[512,2,128]{2,1,0:T(2,128)}, u32[]{:S(2)}) copy-start(f32[512,2,128]{2,1,0:T(2,128)} %copy-done) | copy-start | bytes 1572868

commit v18 on v17

--- a/solution.py
+++ b/solution.py
@@ -54,7 +54,8 @@
 
         def in_slot_order(pieces):
             stacked = jnp.stack(pieces).reshape(n_row * ratio, cols, cols)
-            return jnp.take(stacked, sub_index, axis=0).reshape(n_col * cols, cols)
+            picked = jnp.take(stacked, sub_index, axis=0, mode="clip")
+            return picked.reshape(n_col * cols, cols)
 
         row_cat = jnp.concatenate(row_pieces, axis=1)
         square = jnp.dot(row_cat, in_slot_order(col_pieces), preferred_element_type=jnp.float32)
@@ -65,7 +66,10 @@
             (jnp.arange(n_row, dtype=jnp.int32)[:, None] ^ row_index) * ratio
             + jnp.arange(ratio, dtype=jnp.int32)[None, :]
         ).reshape(-1)
-        row_f = jnp.take(row_cat.reshape(rows, n_col, cols), f_members ^ col_index, axis=1)
+        row_f = jnp.take(
+            row_cat.reshape(rows, n_col, cols), f_members ^ col_index, axis=1,
+            mode="clip",
+        )
         row_f = row_f.reshape(rows, n_col * cols)
         f_cat = jnp.concatenate(f_pieces, axis=0)
         cubic = jnp.dot(row_f, f_cat, preferred_element_type=jnp.float32)

time: 50.8 us -> 57.5 us (1.13)
  other arithmetic: 11.1 us -> 13.8 us
  waiting for transfers between devices: 14.1 us -> 16.4 us
  matrix products: 4.14 us -> 6.4 us
    unnamed x13, other arithmetic: 6.74 us -> 11.1 us
    select_n x4 -> x0, other arithmetic: 2.37 us -> none  [the longest x2 1.83 us: body(): jnp.take(row_cat.reshape(rows, n_col, cols), f_members ^ col_index, axis=1)]
    ppermute x13, waiting for transfers between devices: 14.1 us -> 16.4 us  [_swap(): return lax.ppermute(x, axis, [(i, i ^ d) for i in range(size)])]
    dot_general x1, matrix products: 1.41 us -> 3.2 us  [body(): jnp.dot(row_cat, in_slot_order(col_pieces), preferred_element_type=jnp.fl...]
    concatenate x2, other arithmetic: 0.85 us -> 1.58 us  [body(): row_cat = jnp.concatenate(row_pieces, axis=1)]
  transfers between devices with their start and end apart: 13 -> 13, of which waited for: 5 -> 6; matrix products, arithmetic and copies ran while one was open for 40% -> 38% of each run, Pallas kernels for 0% -> 0%
where the time goes in v18:
time: 57.5 us; the launch traced here: 57.2 us
  waiting for transfers between devices  16.4 us (29%)
  other arithmetic  13.8 us (24%)
  starting transfers between devices  11 us (19%)
  local copies, waits for them, and re-layouts  9.51 us (17%)
  matrix products  6.4 us (11%)
    ppermute x13, waiting for transfers between devices, _swap(): return lax.ppermute(x, axis, [(i, i ^ d) for i in range(size)])  16.4 us
    unnamed x13, other arithmetic  11.1 us
    ppermute x13, starting transfers between devices, _swap(): return lax.ppermute(x, axis, [(i, i ^ d) for i in range(size)])  11 us
    gather x2, local copies, waits for them, and re-layouts, body(): jnp.take(row_cat.reshape(rows, n_col, cols), f_members ^ col_index, axis=...  4.7 us
    dot_general x1, matrix products, body(): cubic = jnp.dot(row_f, f_cat, preferred_element_type=jnp.float32)  3.2 us
    dot_general x1, matrix products, body(): jnp.dot(row_cat, in_slot_order(col_pieces), preferred_element_type=jnp.fl...  3.2 us
    mul x10, local copies, waits for them, and re-layouts, mask_from(): return (x4 * blocks[:, None, :, None]).reshape(rows, cols)  2.04 us
    concatenate x2, other arithmetic, body(): row_cat = jnp.concatenate(row_pieces, axis=1)  1.58 us
  transfers between devices with their start and end apart: 13, of which 6 were waited for; matrix products, arithmetic and copies ran while one was open for 38% of the time, Pallas kernels for 0%

profile of v18, /device:TPU:16, one launch (start us, length us, event | category | flops | bytes accessed | tf_op | source)
XLA Modules:
  0.0 57.2 jit_solution(12955713666270465269)
XLA Ops:
  0.0 1.5 %collective-permute-start = (bf16[512,256]{1,0:T(8,128)(2,1)}, bf16[512,256]{1,0:T(8,128)(2,1)S(1)}, u32[]{:S(2)}, u32[]{:S(2)}) collective-permute-start(bf16[512,256]{1,0:T(8,128)(2,1)} %param.2), channel_id=1, source_target_pairs={{0,8},{8,0},{16,24},{24,16},{1,9},{9,1},{17,25},{25,17},{2,10},{10... | collective-permute-start | bytes 786440 | tf_op jit(solution)/shard_map/ppermute | solution.py:10
  1.5 1.6 %collective-permute-start.2 = (bf16[512,256]{1,0:T(8,128)(2,1)}, bf16[512,256]{1,0:T(8,128)(2,1)S(1)}, u32[]{:S(2)}, u32[]{:S(2)}) collective-permute-start(bf16[512,256]{1,0:T(8,128)(2,1)} %param.2), channel_id=1, source_target_pairs={{0,2},{1,3},{2,0},{3,1},{4,6},{5,7},{6,4},{7,5},{8,10},{9,11},{10,... | collective-permute-start | bytes 786440 | tf_op jit(solution)/shard_map/ppermute | solution.py:10
  3.1 0.3 collective-permute-start.4
  3.4 1.6 %collective-permute-start.6 = (bf16[512,256]{1,0:T(8,128)(2,1)}, bf16[512,256]{1,0:T(8,128)(2,1)S(1)}, u32[]{:S(2)}, u32[]{:S(2)}) collective-permute-start(bf16[512,256]{1,0:T(8,128)(2,1)} %param.2), channel_id=1, source_target_pairs={{0,6},{1,7},{2,4},{3,5},{4,2},{5,3},{6,0},{7,1},{8,14},{9,15},{10,... | collective-permute-start | bytes 786440 | tf_op jit(solution)/shard_map/ppermute | solution.py:10
  5.0 1.5 %collective-permute-start.9 = (bf16[512,256]{1,0:T(8,128)(2,1)}, bf16[512,256]{1,0:T(8,128)(2,1)S(1)}, u32[]{:S(2)}, u32[]{:S(2)}) collective-permute-start(bf16[512,256]{1,0:T(8,128)(2,1)} %param.2), channel_id=1, source_target_pairs={{0,24},{8,16},{16,8},{24,0},{1,25},{9,17},{17,9},{25,1},{2,26},{10... | collective-permute-start | bytes 786440 | tf_op jit(solution)/shard_map/ppermute | solution.py:10
  6.5 0.8 %dynamic-slice_convert_fusion.1 = (f32[4,2]{1,0:T(4,128)S(1)}, bf16[4,2]{1,0:T(4,128)(2,1)S(1)}) fusion(s32[16,16]{1,0:T(8,128)} %param.3, s32[]{:T(128)S(6)} %select_n.72, s32[]{:T(128)S(6)} %select_n.73), kind=kLoop, calls=%fused_computation.51 | loop fusion | flops 16 | bytes 88 | tf_op jit(solution)/shard_map/convert_element_type | solution.py:62
  7.3 0.6 %broadcast_in_dim.14 = bf16[512,2,128]{2,1,0:T(2,128)(2,1)S(1)} broadcast(bf16[512,2]{1,0:T(8,128)(2,1)S(1)} %bitcast.140), dimensions={0,1} | broadcast | bytes 264192 | tf_op jit(solution)/shard_map/broadcast_in_dim | solution.py:26
  7.9 1.7 %constant_dynamic-update-slice_fusion = (bf16[512,2048]{1,0:T(8,128)(2,1)}, bf16[512,256]{1,0:T(8,128)(2,1)S(1)}) fusion(bf16[512,256]{1,0:T(8,128)(2,1)} %param.2, bf16[64,8,2,128]{3,2,1,0:T(2,128)(2,1)S(1)} %bitcast.139), kind=kLoop, calls=%fused_computation.44 | loop fusion | flops 524287 | bytes 1048576
  9.6 0.7 %bitcast_dynamic-update-slice_fusion.7 = bf16[512,8,256]{2,0,1:T(8,128)(2,1)} fusion(bf16[512,256]{1,0:T(8,128)(2,1)S(1)} %get-tuple-element.8), kind=kLoop, calls=%fused_computation.36 | loop fusion | bytes 524288
  10.4 0.1 add_xor_fusion
  10.5 0.1 reshape.194
  10.6 0.1 fusion.23
  10.7 0.0 collective-permute-done
  10.7 0.6 collective-permute-start.8
  11.2 0.2 mul.239
  11.5 0.1 fusion.12
  11.5 3.4 %collective-permute-done.9 = bf16[512,256]{1,0:T(8,128)(2,1)S(1)} collective-permute-done((bf16[512,256]{1,0:T(8,128)(2,1)}, bf16[512,256]{1,0:T(8,128)(2,1)S(1)}, u32[]{:S(2)}, u32[]{:S(2)}) %collective-permute-start.9) | collective-permute-done | bytes 262176 | tf_op jit(solution)/shard_map/ppermute | solution.py:10
  14.9 0.0 collective-permute-start.1
  14.9 0.2 mul.249
  15.2 0.1 fusion.10
  15.2 5.2 %collective-permute-done.8 = bf16[512,256]{1,0:T(8,128)(2,1)S(1)} collective-permute-done((bf16[512,256]{1,0:T(8,128)(2,1)}, bf16[512,256]{1,0:T(8,128)(2,1)S(1)}, u32[]{:S(2)}, u32[]{:S(2)}) %collective-permute-start.8) | collective-permute-done | bytes 262176 | tf_op jit(solution)/shard_map/ppermute | solution.py:10
  20.5 0.2 mul.244
  20.7 0.1 fusion.11
  20.7 0.1 pad_maximum_fusion
  20.9 0.6 %gather_fusion.1 = bf16[8,256,256]{2,1,0:T(8,128)(2,1)S(1)} fusion(bf16[8,256,256]{2,1,0:T(8,128)(2,1)S(1)} %bitcast.117, s32[1024]{0:T(1024)S(1)} %pad_clamp_fusion), kind=kCustom, calls=%fused_computation.1 | custom fusion | bytes 2097184 | tf_op jit(solution)/shard_map/jit(_take)/gather | solution.py:57
  21.5 0.0 collective-permute-done.2
  21.5 0.1 collective-permute-start.3
  21.6 0.1 collective-permute-done.4
  21.7 0.3 collective-permute-start.5
  22.1 5.5 %collective-permute-done.6 = bf16[512,256]{1,0:T(8,128)(2,1)S(1)} collective-permute-done((bf16[512,256]{1,0:T(8,128)(2,1)}, bf16[512,256]{1,0:T(8,128)(2,1)S(1)}, u32[]{:S(2)}, u32[]{:S(2)}) %collective-permute-start.6) | collective-permute-done | bytes 262176 | tf_op jit(solution)/shard_map/ppermute | solution.py:10
  27.6 0.0 collective-permute-start.7
  27.6 0.2 mul.210
  27.8 0.8 %fusion.13 = bf16[512,2048]{1,0:T(8,128)(2,1)} fusion(bf16[512,2048]{1,0:T(8,128)(2,1)} %get-tuple-element.7, bf16[512,256]{1,0:T(8,128)(2,1)S(1)} %collective-permute-done.1, bf16[64,8,2,128]{3,2,1,0:T(2,128)(2,1)S(1)} %bitcast.118), kind=kLoop, calls=%fused_computation.37 | loop fusion | flops 524288 | bytes 786432
  28.6 0.2 mul.214
  28.8 0.8 %fusion.14 = bf16[512,2048]{1,0:T(8,128)(2,1)} fusion(bf16[512,2048]{1,0:T(8,128)(2,1)} %fusion.13, bf16[512,256]{1,0:T(8,128)(2,1)S(1)} %collective-permute-done.2, bf16[64,8,2,128]{3,2,1,0:T(2,128)(2,1)S(1)} %bitcast.120), kind=kLoop, calls=%fused_computation.38 | loop fusion | flops 524288 | bytes 786432
  29.6 0.2 mul.218
  29.8 0.8 %fusion.15 = bf16[512,2048]{1,0:T(8,128)(2,1)} fusion(bf16[512,2048]{1,0:T(8,128)(2,1)} %fusion.14, bf16[512,256]{1,0:T(8,128)(2,1)S(1)} %collective-permute-done.3, bf16[64,8,2,128]{3,2,1,0:T(2,128)(2,1)S(1)} %bitcast.122), kind=kLoop, calls=%fused_computation.39 | loop fusion | flops 524288 | bytes 786432
  30.6 0.2 mul.222
  30.8 0.8 %fusion.16 = bf16[512,2048]{1,0:T(8,128)(2,1)} fusion(bf16[512,2048]{1,0:T(8,128)(2,1)} %fusion.15, bf16[512,256]{1,0:T(8,128)(2,1)S(1)} %collective-permute-done.4, bf16[64,8,2,128]{3,2,1,0:T(2,128)(2,1)S(1)} %bitcast.124), kind=kLoop, calls=%fused_computation.40 | loop fusion | flops 524288 | bytes 786432
  31.6 0.2 mul.226
  31.8 0.8 %fusion.17 = bf16[512,2048]{1,0:T(8,128)(2,1)} fusion(bf16[512,2048]{1,0:T(8,128)(2,1)} %fusion.16, bf16[512,256]{1,0:T(8,128)(2,1)S(1)} %collective-permute-done.5, bf16[64,8,2,128]{3,2,1,0:T(2,128)(2,1)S(1)} %bitcast.126), kind=kLoop, calls=%fused_computation.41 | loop fusion | flops 524288 | bytes 786432
  32.6 0.2 mul.230
  32.8 0.8 %fusion.18 = bf16[512,2048]{1,0:T(8,128)(2,1)} fusion(bf16[512,2048]{1,0:T(8,128)(2,1)} %fusion.17, bf16[512,256]{1,0:T(8,128)(2,1)S(1)} %collective-permute-done.6, bf16[64,8,2,128]{3,2,1,0:T(2,128)(2,1)S(1)} %bitcast.128), kind=kLoop, calls=%fused_computation.42 | loop fusion | flops 524288 | bytes 786432
  33.6 0.2 mul.234
  33.8 0.8 %fusion.19 = bf16[512,2048]{1,0:T(8,128)(2,1)} fusion(bf16[512,2048]{1,0:T(8,128)(2,1)} %fusion.18, bf16[512,256]{1,0:T(8,128)(2,1)S(1)} %collective-permute-done.7, bf16[64,8,2,128]{3,2,1,0:T(2,128)(2,1)S(1)} %bitcast.130), kind=kLoop, calls=%fused_computation.43 | loop fusion | flops 524288 | bytes 786432 | tf_op jit(solution)/shard_map/concatenate | solution.py:60
  34.6 0.6 %broadcast_in_dim.11 = f32[512,2,128]{2,1,0:T(2,128)S(1)} broadcast(f32[512,2]{1,0:T(8,128)S(1)} %bitcast.138), dimensions={0,1} | broadcast | bytes 528384 | tf_op jit(solution)/shard_map/broadcast_in_dim | solution.py:26
  35.2 0.0 copy-start
  35.2 3.2 %fusion.2 = bf16[512,256]{1,0:T(8,128)(2,1)} fusion(bf16[512,2048]{1,0:T(8,128)(2,1)} %fusion.19, bf16[2048,256]{1,0:T(8,128)(2,1)S(1)} %bitcast.134, f32[64,8,2,128]{3,2,1,0:T(2,128)S(1)} %bitcast.141), kind=kOutput, calls=%fused_computation.6 | convolution fusion | flops 537133056 | bytes 3932160 | tf_op jit(solution)/shard_map/dot_general | solution.py:61
  38.4 0.5 collective-permute-start.10
  39.0 1.5 %collective-permute-start.11 = (bf16[512,256]{1,0:T(8,128)(2,1)}, bf16[512,256]{1,0:T(8,128)(2,1)S(1)}, u32[]{:S(2)}, u32[]{:S(2)}) collective-permute-start(bf16[512,256]{1,0:T(8,128)(2,1)} %fusion.2), channel_id=1, source_target_pairs={{0,16},{8,24},{16,0},{24,8},{1,17},{9,25},{17,1},{25,9},{2,18},{10... | collective-permute-start | bytes 786440 | tf_op jit(solution)/shard_map/ppermute | solution.py:10
  40.5 1.4 %collective-permute-start.12 = (bf16[512,256]{1,0:T(8,128)(2,1)}, bf16[512,256]{1,0:T(8,128)(2,1)}, u32[]{:S(2)}, u32[]{:S(2)}) collective-permute-start(bf16[512,256]{1,0:T(8,128)(2,1)} %fusion.2), channel_id=1, source_target_pairs={{0,24},{8,16},{16,8},{24,0},{1,25},{9,17},{17,9},{25,1},{2,26},{10... | collective-permute-start | bytes 786440 | tf_op jit(solution)/shard_map/ppermute | solution.py:10
  41.9 0.8 %bitcast_dynamic-update-slice_fusion.6 = bf16[512,8,256]{2,0,1:T(8,128)(2,1)} fusion(bf16[512,8,256]{2,0,1:T(8,128)(2,1)} %bitcast_dynamic-update-slice_fusion.7, bf16[512,256]{1,0:T(8,128)(2,1)S(1)} %collective-permute-done.1, bf16[64,8,2,128]{3,2,1,0:T(2,128)(2,1)S(1)} %bitcast.119), kind=kLoop, calls=%fused_computation.35 | loop fusion | flops 524288 | bytes 786432
  42.7 0.8 %bitcast_dynamic-update-slice_fusion.5 = bf16[512,8,256]{2,0,1:T(8,128)(2,1)} fusion(bf16[512,8,256]{2,0,1:T(8,128)(2,1)} %bitcast_dynamic-update-slice_fusion.6, bf16[512,256]{1,0:T(8,128)(2,1)S(1)} %collective-permute-done.2, bf16[64,8,2,128]{3,2,1,0:T(2,128)(2,1)S(1)} %bitcast.121), kind=kLoop, calls=%fused_computation.34 | loop fusion | flops 524288 | bytes 786432
  43.4 0.8 %bitcast_dynamic-update-slice_fusion.4 = bf16[512,8,256]{2,0,1:T(8,128)(2,1)} fusion(bf16[512,8,256]{2,0,1:T(8,128)(2,1)} %bitcast_dynamic-update-slice_fusion.5, bf16[512,256]{1,0:T(8,128)(2,1)S(1)} %collective-permute-done.3, bf16[64,8,2,128]{3,2,1,0:T(2,128)(2,1)S(1)} %bitcast.123), kind=kLoop, calls=%fused_computation.33 | loop fusion | flops 524288 | bytes 786432
  44.2 0.8 %bitcast_dynamic-update-slice_fusion.3 = bf16[512,8,256]{2,0,1:T(8,128)(2,1)} fusion(bf16[512,8,256]{2,0,1:T(8,128)(2,1)} %bitcast_dynamic-update-slice_fusion.4, bf16[512,256]{1,0:T(8,128)(2,1)S(1)} %collective-permute-done.4, bf16[64,8,2,128]{3,2,1,0:T(2,128)(2,1)S(1)} %bitcast.125), kind=kLoop, calls=%fused_computation.32 | loop fusion | flops 524288 | bytes 786432
  45.0 0.8 %bitcast_dynamic-update-slice_fusion.2 = bf16[512,8,256]{2,0,1:T(8,128)(2,1)} fusion(bf16[512,8,256]{2,0,1:T(8,128)(2,1)} %bitcast_dynamic-update-slice_fusion.3, bf16[512,256]{1,0:T(8,128)(2,1)S(1)} %collective-permute-done.5, bf16[64,8,2,128]{3,2,1,0:T(2,128)(2,1)S(1)} %bitcast.127), kind=kLoop, calls=%fused_computation.31 | loop fusion | flops 524288 | bytes 786432
  45.7 0.8 %bitcast_dynamic-update-slice_fusion.1 = bf16[512,8,256]{2,0,1:T(8,128)(2,1)} fusion(bf16[512,8,256]{2,0,1:T(8,128)(2,1)} %bitcast_dynamic-update-slice_fusion.2, bf16[512,256]{1,0:T(8,128)(2,1)S(1)} %collective-permute-done.6, bf16[64,8,2,128]{3,2,1,0:T(2,128)(2,1)S(1)} %bitcast.129), kind=kLoop, calls=%fused_computation.30 | loop fusion | flops 524288 | bytes 786432
  46.5 0.8 %bitcast_dynamic-update-slice_fusion = bf16[512,8,256]{2,0,1:T(8,128)(2,1)} fusion(bf16[512,8,256]{2,0,1:T(8,128)(2,1)} %bitcast_dynamic-update-slice_fusion.1, bf16[512,256]{1,0:T(8,128)(2,1)S(1)} %collective-permute-done.7, bf16[64,8,2,128]{3,2,1,0:T(2,128)(2,1)S(1)} %bitcast.131), kind=kLoop, calls=%fused_computation.29 | loop fusion | flops 524288 | bytes 786432 | tf_op jit(solution)/shard_map/concatenate | solution.py:60
  47.3 2.3 %gather_fusion = bf16[8,512,256]{2,1,0:T(8,128)(2,1)S(1)} fusion(bf16[512,8,256]{2,0,1:T(8,128)(2,1)} %bitcast_dynamic-update-slice_fusion, s32[1024]{0:T(1024)S(1)} %pad_clamp_fusion.1), kind=kCustom, calls=%fused_computation | custom fusion | bytes 4194336 | tf_op jit(solution)/shard_map/jit(_take)/gather | solution.py:69
  49.6 0.0 copy-start.1
  49.6 2.4 %copy.3 = bf16[512,8,256]{0,2,1:T(8,128)(2,1)} copy(bf16[512,8,256]{2,0,1:T(8,128)(2,1)S(1)} %bitcast.116) | data formatting | bytes 4194304 | tf_op jit(solution)/shard_map/jit(_take)/gather | solution.py:69
  52.0 0.4 collective-permute-done.11
  52.4 1.6 %collective-permute-done.12 = bf16[512,256]{1,0:T(8,128)(2,1)} collective-permute-done((bf16[512,256]{1,0:T(8,128)(2,1)}, bf16[512,256]{1,0:T(8,128)(2,1)}, u32[]{:S(2)}, u32[]{:S(2)}) %collective-permute-start.12) | collective-permute-done | bytes 262176 | tf_op jit(solution)/shard_map/ppermute | solution.py:10
  54.0 3.2 %fusion.1 = f32[512,256]{1,0:T(8,128)} fusion(bf16[512,2048]{0,1:T(8,128)(2,1)} %bitcast.133, bf16[512,256]{1,0:T(8,128)(2,1)} %collective-permute-done.12, bf16[512,256]{1,0:T(8,128)(2,1)S(1)} %collective-permute-done.11, bf16[512,256]{1,0:T(8,128)(2,1)S(1)} %collective-permute-done.10, bf16[512,256]{1,0:T(8,128)(2,1)} %fusion.2, ...), kind=kOutput, calls=%fused_computation.5 | convolution fusion | flops 541720576 | bytes 4456448 | tf_op jit(solution)/shard_map/dot_general | solution.py:75
  (16 shorter events, 0.1 us)
Async XLA Ops:
  0.0 10.5 %copy-start.2 = (s32[16,16]{1,0:T(8,128)S(1)}, s32[16,16]{1,0:T(8,128)}, u32[]{:S(2)}) copy-start(s32[16,16]{1,0:T(8,128)} %param.3) | copy-start | bytes 3076
  0.0 10.7 %collective-permute-start = (bf16[512,256]{1,0:T(8,128)(2,1)}, bf16[512,256]{1,0:T(8,128)(2,1)S(1)}, u32[]{:S(2)}, u32[]{:S(2)}) collective-permute-start(bf16[512,256]{1,0:T(8,128)(2,1)} %param.2), channel_id=1, source_target_pairs={{0,8},{8,0},{16,24},{24,16},{1,9},{9,1},{17,25},{25,17},{2,10},{10... | collective-permute-start | bytes 786440 | tf_op jit(solution)/shard_map/ppermute | solution.py:10
  1.5 20.0 %collective-permute-start.2 = (bf16[512,256]{1,0:T(8,128)(2,1)}, bf16[512,256]{1,0:T(8,128)(2,1)S(1)}, u32[]{:S(2)}, u32[]{:S(2)}) collective-permute-start(bf16[512,256]{1,0:T(8,128)(2,1)} %param.2), channel_id=1, source_target_pairs={{0,2},{1,3},{2,0},{3,1},{4,6},{5,7},{6,4},{7,5},{8,10},{9,11},{10,... | collective-permute-start | bytes 786440 | tf_op jit(solution)/shard_map/ppermute | solution.py:10
  3.1 18.7 %collective-permute-start.4 = (bf16[512,256]{1,0:T(8,128)(2,1)}, bf16[512,256]{1,0:T(8,128)(2,1)S(1)}, u32[]{:S(2)}, u32[]{:S(2)}) collective-permute-start(bf16[512,256]{1,0:T(8,128)(2,1)} %param.2), channel_id=1, source_target_pairs={{0,4},{1,5},{2,6},{3,7},{4,0},{5,1},{6,2},{7,3},{8,12},{9,13},{10,... | collective-permute-start | bytes 786440 | tf_op jit(solution)/shard_map/ppermute | solution.py:10
  3.4 24.1 %collective-permute-start.6 = (bf16[512,256]{1,0:T(8,128)(2,1)}, bf16[512,256]{1,0:T(8,128)(2,1)S(1)}, u32[]{:S(2)}, u32[]{:S(2)}) collective-permute-start(bf16[512,256]{1,0:T(8,128)(2,1)} %param.2), channel_id=1, source_target_pairs={{0,6},{1,7},{2,4},{3,5},{4,2},{5,3},{6,0},{7,1},{8,14},{9,15},{10,... | collective-permute-start | bytes 786440 | tf_op jit(solution)/shard_map/ppermute | solution.py:10
  5.0 10.0 %collective-permute-start.9 = (bf16[512,256]{1,0:T(8,128)(2,1)}, bf16[512,256]{1,0:T(8,128)(2,1)S(1)}, u32[]{:S(2)}, u32[]{:S(2)}) collective-permute-start(bf16[512,256]{1,0:T(8,128)(2,1)} %param.2), channel_id=1, source_target_pairs={{0,24},{8,16},{16,8},{24,0},{1,25},{9,17},{17,9},{25,1},{2,26},{10... | collective-permute-start | bytes 786440 | tf_op jit(solution)/shard_map/ppermute | solution.py:10
  10.7 9.8 %collective-permute-start.8 = (bf16[512,256]{1,0:T(8,128)(2,1)}, bf16[512,256]{1,0:T(8,128)(2,1)S(1)}, u32[]{:S(2)}, u32[]{:S(2)}) collective-permute-start(bf16[512,256]{1,0:T(8,128)(2,1)} %param.2), channel_id=1, source_target_pairs={{0,16},{8,24},{16,0},{24,8},{1,17},{9,25},{17,1},{25,9},{2,18},{10... | collective-permute-start | bytes 786440 | tf_op jit(solution)/shard_map/ppermute | solution.py:10
  14.9 12.6 %collective-permute-start.1 = (bf16[512,256]{1,0:T(8,128)(2,1)}, bf16[512,256]{1,0:T(8,128)(2,1)S(1)}, u32[]{:S(2)}, u32[]{:S(2)}) collective-permute-start(bf16[512,256]{1,0:T(8,128)(2,1)} %param.2), channel_id=1, source_target_pairs={{0,1},{1,0},{2,3},{3,2},{4,5},{5,4},{6,7},{7,6},{8,9},{9,8},{10,11... | collective-permute-start | bytes 786440 | tf_op jit(solution)/shard_map/ppermute | solution.py:10
  21.5 8.1 %collective-permute-start.3 = (bf16[512,256]{1,0:T(8,128)(2,1)S(1)}, bf16[512,256]{1,0:T(8,128)(2,1)S(1)}, u32[]{:S(2)}, u32[]{:S(2)}) collective-permute-start(bf16[512,256]{1,0:T(8,128)(2,1)S(1)} %collective-permute-done.2), channel_id=1, source_target_pairs={{0,1},{1,0},{2,3},{3,2},{4,5},{5,4},{6,7},{7,6},{8,9},{9,8},{10,11... | collective-permute-start | bytes 786440 | tf_op jit(solution)/shard_map/ppermute | solution.py:10
  21.7 9.8 %collective-permute-start.5 = (bf16[512,256]{1,0:T(8,128)(2,1)S(1)}, bf16[512,256]{1,0:T(8,128)(2,1)S(1)}, u32[]{:S(2)}, u32[]{:S(2)}) collective-permute-start(bf16[512,256]{1,0:T(8,128)(2,1)S(1)} %collective-permute-done.4), channel_id=1, source_target_pairs={{0,1},{1,0},{2,3},{3,2},{4,5},{5,4},{6,7},{7,6},{8,9},{9,8},{10,11... | collective-permute-start | bytes 786440 | tf_op jit(solution)/shard_map/ppermute | solution.py:10
  27.6 6.0 %collective-permute-start.7 = (bf16[512,256]{1,0:T(8,128)(2,1)S(1)}, bf16[512,256]{1,0:T(8,128)(2,1)S(1)}, u32[]{:S(2)}, u32[]{:S(2)}) collective-permute-start(bf16[512,256]{1,0:T(8,128)(2,1)S(1)} %collective-permute-done.6), channel_id=1, source_target_pairs={{0,1},{1,0},{2,3},{3,2},{4,5},{5,4},{6,7},{7,6},{8,9},{9,8},{10,11... | collective-permute-start | bytes 786440 | tf_op jit(solution)/shard_map/ppermute | solution.py:10
  35.2 3.2 %copy-start = (f32[512,2,128]{2,1,0:T(2,128)}, f32[512,2,128]{2,1,0:T(2,128)S(1)}, u32[]{:S(2)}) copy-start(f32[512,2,128]{2,1,0:T(2,128)S(1)} %broadcast_in_dim.11) | copy-start | bytes 1572868
  38.4 13.6 %collective-permute-start.10 = (bf16[512,256]{1,0:T(8,128)(2,1)}, bf16[512,256]{1,0:T(8,128)(2,1)S(1)}, u32[]{:S(2)}, u32[]{:S(2)}) collective-permute-start(bf16[512,256]{1,0:T(8,128)(2,1)} %fusion.2), channel_id=1, source_target_pairs={{0,8},{8,0},{16,24},{24,16},{1,9},{9,1},{17,25},{25,17},{2,10},{10... | collective-permute-start | bytes 786440 | tf_op jit(solution)/shard_map/ppermute | solution.py:10
  39.0 13.4 %collective-permute-start.11 = (bf16[512,256]{1,0:T(8,128)(2,1)}, bf16[512,256]{1,0:T(8,128)(2,1)S(1)}, u32[]{:S(2)}, u32[]{:S(2)}) collective-permute-start(bf16[512,256]{1,0:T(8,128)(2,1)} %fusion.2), channel_id=1, source_target_pairs={{0,16},{8,24},{16,0},{24,8},{1,17},{9,25},{17,1},{25,9},{2,18},{10... | collective-permute-start | bytes 786440 | tf_op jit(solution)/shard_map/ppermute | solution.py:10
  40.5 13.6 %collective-permute-start.12 = (bf16[512,256]{1,0:T(8,128)(2,1)}, bf16[512,256]{1,0:T(8,128)(2,1)}, u32[]{:S(2)}, u32[]{:S(2)}) collective-permute-start(bf16[512,256]{1,0:T(8,128)(2,1)} %fusion.2), channel_id=1, source_target_pairs={{0,24},{8,16},{16,8},{24,0},{1,25},{9,17},{17,9},{25,1},{2,26},{10... | collective-permute-start | bytes 786440 | tf_op jit(solution)/shard_map/ppermute | solution.py:10
  49.6 4.5 %copy-start.1 = (f32[512,2,128]{2,1,0:T(2,128)S(1)}, f32[512,2,128]{2,1,0:T(2,128)}, u32[]{:S(2)}) copy-start(f32[512,2,128]{2,1,0:T(2,128)} %copy-done) | copy-start | bytes 1572868

commit v19 on v17

--- a/solution.py
+++ b/solution.py
@@ -65,10 +65,9 @@
             (jnp.arange(n_row, dtype=jnp.int32)[:, None] ^ row_index) * ratio
             + jnp.arange(ratio, dtype=jnp.int32)[None, :]
         ).reshape(-1)
-        row_f = jnp.take(row_cat.reshape(rows, n_col, cols), f_members ^ col_index, axis=1)
-        row_f = row_f.reshape(rows, n_col * cols)
-        f_cat = jnp.concatenate(f_pieces, axis=0)
-        cubic = jnp.dot(row_f, f_cat, preferred_element_type=jnp.float32)
+        row_fs = jnp.take(jnp.stack(row_pieces), f_members ^ col_index, axis=0, mode="clip")
+        f_stack = jnp.concatenate(f_pieces, axis=0).reshape(n_col, cols, cols)
+        cubic = jnp.einsum("qmj,qjn->mn", row_fs, f_stack, preferred_element_type=jnp.float32)
         return mask_float * (1.5 * masked.astype(jnp.float32) - 0.5 * cubic)
 
     return body

time: 50.8 us -> 50.8 us (level)
  waiting for transfers between devices: 14.1 us -> 23.7 us
  other arithmetic: 11.1 us -> 5.64 us
  local copies, waits for them, and re-layouts: 9.78 us -> 6.93 us
  matrix products: 4.14 us -> 2.92 us
    ppermute x13, waiting for transfers between devices: 14.1 us -> 23.7 us  [_swap(): return lax.ppermute(x, axis, [(i, i ^ d) for i in range(size)])]
    unnamed x13, other arithmetic: 6.74 us -> 2.54 us
    gather x2 -> x1, local copies, waits for them, and re-layouts: 4.7 us -> 2.01 us  [body(): jnp.take(jnp.stack(row_pieces), f_members ^ col_index, axis=0, mode='clip')]
    select_n x2 -> x0, other arithmetic: 1.83 us -> none  [body(): jnp.take(row_cat.reshape(rows, n_col, cols), f_members ^ col_index, axis=1)]
    concatenate x0 -> x1, other arithmetic: none -> 1.26 us  [body(): f_stack = jnp.concatenate(f_pieces, axis=0).reshape(n_col, cols, cols)]
    dot_general x1, matrix products: 2.73 us -> 1.51 us  [body(): jnp.einsum('qmj,qjn->mn', row_fs, f_stack, preferred_element_type=jnp.flo...]
    concatenate x2 -> x1, other arithmetic: 0.85 us -> 0.07 us  [body(): row_cat = jnp.concatenate(row_pieces, axis=1)]
  transfers between devices with their start and end apart: 13 -> 13, of which waited for: 5 -> 7; matrix products, arithmetic and copies ran while one was open for 40% -> 21% of each run, Pallas kernels for 0% -> 0%
where the time goes in v19:
time: 50.8 us; the launch traced here: 50.6 us
  waiting for transfers between devices  23.7 us (47%)
  starting transfers between devices  11 us (22%)
  local copies, waits for them, and re-layouts  6.93 us (14%)
  other arithmetic  5.64 us (11%)
  matrix products  2.92 us (6%)
    ppermute x13, waiting for transfers between devices, _swap(): return lax.ppermute(x, axis, [(i, i ^ d) for i in range(size)])  23.7 us
    ppermute x13, starting transfers between devices, _swap(): return lax.ppermute(x, axis, [(i, i ^ d) for i in range(size)])  11 us
    unnamed x13, other arithmetic  2.54 us
    mul x10, local copies, waits for them, and re-layouts, mask_from(): return (x4 * blocks[:, None, :, None]).reshape(rows, cols)  2.05 us
    gather x1, local copies, waits for them, and re-layouts, body(): jnp.take(jnp.stack(row_pieces), f_members ^ col_index, axis=0, mode='clip')  2.01 us
    dot_general x1, matrix products, body(): jnp.einsum('qmj,qjn->mn', row_fs, f_stack, preferred_element_type=jnp.flo...  1.51 us
    dot_general x1, matrix products, body(): jnp.dot(row_cat, in_slot_order(col_pieces), preferred_element_type=jnp.fl...  1.41 us
    concatenate x1, other arithmetic, body(): f_stack = jnp.concatenate(f_pieces, axis=0).reshape(n_col, cols, cols)  1.26 us
  transfers between devices with their start and end apart: 13, of which 7 were waited for; matrix products, arithmetic and copies ran while one was open for 21% of the time, Pallas kernels for 0%

profile of v19, /device:TPU:16, one launch (start us, length us, event | category | flops | bytes accessed | tf_op | source)
XLA Modules:
  0.0 50.6 jit_solution(11714490060075679343)
XLA Ops:
  0.0 1.5 %collective-permute-start = (bf16[512,256]{1,0:T(8,128)(2,1)}, bf16[512,256]{1,0:T(8,128)(2,1)S(1)}, u32[]{:S(2)}, u32[]{:S(2)}) collective-permute-start(bf16[512,256]{1,0:T(8,128)(2,1)} %param.2), channel_id=1, source_target_pairs={{0,8},{8,0},{16,24},{24,16},{1,9},{9,1},{17,25},{25,17},{2,10},{10... | collective-permute-start | bytes 786440 | tf_op jit(solution)/shard_map/ppermute | solution.py:10
  1.5 1.6 %collective-permute-start.2 = (bf16[512,256]{1,0:T(8,128)(2,1)}, bf16[512,256]{1,0:T(8,128)(2,1)S(1)}, u32[]{:S(2)}, u32[]{:S(2)}) collective-permute-start(bf16[512,256]{1,0:T(8,128)(2,1)} %param.2), channel_id=1, source_target_pairs={{0,2},{1,3},{2,0},{3,1},{4,6},{5,7},{6,4},{7,5},{8,10},{9,11},{10,... | collective-permute-start | bytes 786440 | tf_op jit(solution)/shard_map/ppermute | solution.py:10
  3.1 0.3 collective-permute-start.4
  3.4 1.6 %collective-permute-start.6 = (bf16[512,256]{1,0:T(8,128)(2,1)}, bf16[512,256]{1,0:T(8,128)(2,1)S(1)}, u32[]{:S(2)}, u32[]{:S(2)}) collective-permute-start(bf16[512,256]{1,0:T(8,128)(2,1)} %param.2), channel_id=1, source_target_pairs={{0,6},{1,7},{2,4},{3,5},{4,2},{5,3},{6,0},{7,1},{8,14},{9,15},{10,... | collective-permute-start | bytes 786440 | tf_op jit(solution)/shard_map/ppermute | solution.py:10
  5.0 1.5 %collective-permute-start.9 = (bf16[512,256]{1,0:T(8,128)(2,1)}, bf16[512,256]{1,0:T(8,128)(2,1)S(1)}, u32[]{:S(2)}, u32[]{:S(2)}) collective-permute-start(bf16[512,256]{1,0:T(8,128)(2,1)} %param.2), channel_id=1, source_target_pairs={{0,24},{8,16},{16,8},{24,0},{1,25},{9,17},{17,9},{25,1},{2,26},{10... | collective-permute-start | bytes 786440 | tf_op jit(solution)/shard_map/ppermute | solution.py:10
  6.5 0.8 %dynamic-slice_convert_fusion.1 = (f32[4,2]{1,0:T(4,128)S(1)}, bf16[4,2]{1,0:T(4,128)(2,1)S(1)}) fusion(s32[16,16]{1,0:T(8,128)} %param.3, s32[]{:T(128)S(6)} %select_n.100, s32[]{:T(128)S(6)} %select_n.101), kind=kLoop, calls=%fused_computation.52 | loop fusion | flops 16 | bytes 88 | tf_op jit(solution)/shard_map/convert_element_type | solution.py:61
  7.3 0.6 %broadcast_in_dim.41 = bf16[512,2,128]{2,1,0:T(2,128)(2,1)S(1)} broadcast(bf16[512,2]{1,0:T(8,128)(2,1)S(1)} %bitcast.146), dimensions={0,1} | broadcast | bytes 264192 | tf_op jit(solution)/shard_map/broadcast_in_dim | solution.py:26
  7.9 1.7 %constant_dynamic-update-slice_fusion.1 = (bf16[512,2048]{1,0:T(8,128)(2,1)}, bf16[512,256]{1,0:T(8,128)(2,1)S(1)}) fusion(bf16[512,256]{1,0:T(8,128)(2,1)} %param.2, bf16[64,8,2,128]{3,2,1,0:T(2,128)(2,1)S(1)} %bitcast.145), kind=kLoop, calls=%fused_computation.40 | loop fusion | flops 524287 | bytes 1048576
  9.7 0.7 %constant_dynamic-update-slice_fusion = bf16[8,512,256]{2,1,0:T(8,128)(2,1)} fusion(bf16[512,256]{1,0:T(8,128)(2,1)S(1)} %get-tuple-element.8), kind=kLoop, calls=%fused_computation.39 | loop fusion | bytes 524288
  10.4 0.1 add_xor_fusion
  10.4 0.1 reshape.240
  10.6 0.1 fusion.17
  10.8 0.1 broadcast_in_dim.42
  10.9 0.6 %collective-permute-start.8 = (bf16[512,256]{1,0:T(8,128)(2,1)}, bf16[512,256]{1,0:T(8,128)(2,1)S(1)}, u32[]{:S(2)}, u32[]{:S(2)}) collective-permute-start(bf16[512,256]{1,0:T(8,128)(2,1)} %param.2), channel_id=1, source_target_pairs={{0,16},{8,24},{16,0},{24,8},{1,17},{9,25},{17,1},{25,9},{2,18},{10... | collective-permute-start | bytes 786440 | tf_op jit(solution)/shard_map/ppermute | solution.py:10
  11.4 0.2 mul.279
  11.7 0.1 fusion.6
  11.7 3.2 %collective-permute-done.9 = bf16[512,256]{1,0:T(8,128)(2,1)S(1)} collective-permute-done((bf16[512,256]{1,0:T(8,128)(2,1)}, bf16[512,256]{1,0:T(8,128)(2,1)S(1)}, u32[]{:S(2)}, u32[]{:S(2)}) %collective-permute-start.9) | collective-permute-done | bytes 262176 | tf_op jit(solution)/shard_map/ppermute | solution.py:10
  14.9 0.0 collective-permute-start.1
  14.9 0.2 mul.289
  15.2 0.1 fusion.4
  15.2 5.2 %collective-permute-done.8 = bf16[512,256]{1,0:T(8,128)(2,1)S(1)} collective-permute-done((bf16[512,256]{1,0:T(8,128)(2,1)}, bf16[512,256]{1,0:T(8,128)(2,1)S(1)}, u32[]{:S(2)}, u32[]{:S(2)}) %collective-permute-start.8) | collective-permute-done | bytes 262176 | tf_op jit(solution)/shard_map/ppermute | solution.py:10
  20.5 0.2 mul.284
  20.7 0.1 fusion.5
  20.7 0.1 pad_maximum_fusion
  20.9 0.6 %gather_fusion.1 = bf16[8,256,256]{2,1,0:T(8,128)(2,1)S(1)} fusion(bf16[8,256,256]{2,1,0:T(8,128)(2,1)S(1)} %bitcast.124, s32[1024]{0:T(1024)S(1)} %pad_clamp_fusion), kind=kCustom, calls=%fused_computation.1 | custom fusion | bytes 2097184 | tf_op jit(solution)/shard_map/jit(_take)/gather | solution.py:57
  21.5 0.1 collective-permute-start.3
  21.6 0.1 collective-permute-done.4
  21.7 0.4 collective-permute-start.5
  22.1 5.5 %collective-permute-done.6 = bf16[512,256]{1,0:T(8,128)(2,1)S(1)} collective-permute-done((bf16[512,256]{1,0:T(8,128)(2,1)}, bf16[512,256]{1,0:T(8,128)(2,1)S(1)}, u32[]{:S(2)}, u32[]{:S(2)}) %collective-permute-start.6) | collective-permute-done | bytes 262176 | tf_op jit(solution)/shard_map/ppermute | solution.py:10
  27.6 0.5 %bitcast_select_fusion = bf16[2048,256]{1,0:T(8,128)(2,1)S(1)} fusion(bf16[8,256,256]{2,1,0:T(8,128)(2,1)S(1)} %gather_fusion.1, pred[2048]{0:T(1024)(128)(4,1)S(1)} %broadcast_in_dim.43), kind=kLoop, calls=%fused_computation.10 | loop fusion | flops 524288 | bytes 2099200 | tf_op jit(solution)/shard_map/jit(_take)/select_n | solution.py:57
  28.1 0.2 mul.242
  28.3 0.1 fusion.7
  28.4 0.2 mul.247
  28.6 0.1 fusion.8
  28.7 0.2 mul.252
  28.9 0.1 fusion.9
  29.0 0.2 mul.257
  29.2 0.1 fusion.10
  29.3 0.2 mul.262
  29.5 0.1 fusion.11
  29.6 0.2 mul.267
  29.8 0.1 fusion.12
  29.8 0.2 mul.272
  30.1 0.1 fusion.13
  30.2 0.6 %broadcast_in_dim.39 = f32[512,2,128]{2,1,0:T(2,128)S(1)} broadcast(f32[512,2]{1,0:T(8,128)S(1)} %bitcast.143), dimensions={0,1} | broadcast | bytes 528384 | tf_op jit(solution)/shard_map/broadcast_in_dim | solution.py:26
  30.8 0.0 copy-start.2
  30.8 1.4 %fusion.3 = bf16[512,256]{1,0:T(8,128)(2,1)} fusion(bf16[512,2048]{1,0:T(8,128)(2,1)S(1)} %fusion.13, bf16[2048,256]{1,0:T(8,128)(2,1)S(1)} %bitcast_select_fusion, f32[64,8,2,128]{3,2,1,0:T(2,128)S(1)} %bitcast.147), kind=kOutput, calls=%fused_computation.7 | convolution fusion | flops 537133056 | bytes 3932160 | tf_op jit(solution)/shard_map/dot_general | solution.py:60
  32.2 0.5 %collective-permute-start.10 = (bf16[512,256]{1,0:T(8,128)(2,1)}, bf16[512,256]{1,0:T(8,128)(2,1)}, u32[]{:S(2)}, u32[]{:S(2)}) collective-permute-start(bf16[512,256]{1,0:T(8,128)(2,1)} %fusion.3), channel_id=1, source_target_pairs={{0,8},{8,0},{16,24},{24,16},{1,9},{9,1},{17,25},{25,17},{2,10},{10... | collective-permute-start | bytes 786440 | tf_op jit(solution)/shard_map/ppermute | solution.py:10
  32.7 1.5 %collective-permute-start.11 = (bf16[512,256]{1,0:T(8,128)(2,1)}, bf16[512,256]{1,0:T(8,128)(2,1)}, u32[]{:S(2)}, u32[]{:S(2)}) collective-permute-start(bf16[512,256]{1,0:T(8,128)(2,1)} %fusion.3), channel_id=1, source_target_pairs={{0,16},{8,24},{16,0},{24,8},{1,17},{9,25},{17,1},{25,9},{2,18},{10... | collective-permute-start | bytes 786440 | tf_op jit(solution)/shard_map/ppermute | solution.py:10
  34.3 1.4 %collective-permute-start.12 = (bf16[512,256]{1,0:T(8,128)(2,1)}, bf16[512,256]{1,0:T(8,128)(2,1)}, u32[]{:S(2)}, u32[]{:S(2)}) collective-permute-start(bf16[512,256]{1,0:T(8,128)(2,1)} %fusion.3), channel_id=1, source_target_pairs={{0,24},{8,16},{16,8},{24,0},{1,25},{9,17},{17,9},{25,1},{2,26},{10... | collective-permute-start | bytes 786440 | tf_op jit(solution)/shard_map/ppermute | solution.py:10
  35.7 0.1 bitcast_dynamic-update-slice_fusion.6
  35.8 0.1 bitcast_dynamic-update-slice_fusion.5
  35.8 0.1 bitcast_dynamic-update-slice_fusion.4
  35.9 0.1 bitcast_dynamic-update-slice_fusion.3
  36.0 0.1 bitcast_dynamic-update-slice_fusion.2
  36.0 0.1 bitcast_dynamic-update-slice_fusion.1
  36.1 0.1 bitcast_dynamic-update-slice_fusion
  36.2 0.0 copy-start.3
  36.2 2.0 %gather_fusion = bf16[8,512,256]{2,1,0:T(8,128)(2,1)} fusion(bf16[8,512,256]{2,1,0:T(8,128)(2,1)S(1)} %bitcast_dynamic-update-slice_fusion, s32[1024]{0:T(1024)S(1)} %pad_clamp_fusion.1), kind=kCustom, calls=%fused_computation | custom fusion | bytes 4194336 | tf_op jit(solution)/shard_map/jit(_take)/gather | solution.py:68
  38.2 3.4 %collective-permute-done.10 = bf16[512,256]{1,0:T(8,128)(2,1)} collective-permute-done((bf16[512,256]{1,0:T(8,128)(2,1)}, bf16[512,256]{1,0:T(8,128)(2,1)}, u32[]{:S(2)}, u32[]{:S(2)}) %collective-permute-start.10) | collective-permute-done | bytes 262176 | tf_op jit(solution)/shard_map/ppermute | solution.py:10
  41.6 4.6 %collective-permute-done.11 = bf16[512,256]{1,0:T(8,128)(2,1)} collective-permute-done((bf16[512,256]{1,0:T(8,128)(2,1)}, bf16[512,256]{1,0:T(8,128)(2,1)}, u32[]{:S(2)}, u32[]{:S(2)}) %collective-permute-start.11) | collective-permute-done | bytes 262176 | tf_op jit(solution)/shard_map/ppermute | solution.py:10
  46.2 1.6 %collective-permute-done.12 = bf16[512,256]{1,0:T(8,128)(2,1)} collective-permute-done((bf16[512,256]{1,0:T(8,128)(2,1)}, bf16[512,256]{1,0:T(8,128)(2,1)}, u32[]{:S(2)}, u32[]{:S(2)}) %collective-permute-start.12) | collective-permute-done | bytes 262176 | tf_op jit(solution)/shard_map/ppermute | solution.py:10
  47.8 1.3 %pad_maximum_fusion.1 = bf16[2048,256]{1,0:T(8,128)(2,1)S(1)} fusion(bf16[512,256]{1,0:T(8,128)(2,1)} %collective-permute-done.12, bf16[512,256]{1,0:T(8,128)(2,1)} %collective-permute-done.11, bf16[512,256]{1,0:T(8,128)(2,1)} %collective-permute-done.10, bf16[512,256]{1,0:T(8,128)(2,1)} %fusion.3), kind=kLoop, calls=%fused_computation.9 | loop fusion | flops 4194304 | bytes 2097152 | tf_op jit(solution)/shard_map/concatenate | solution.py:69
  49.1 1.5 %fusion.2 = f32[512,256]{1,0:T(8,128)} fusion(bf16[8,512,256]{2,1,0:T(8,128)(2,1)S(1)} %copy-done.1, bf16[8,256,256]{2,1,0:T(8,128)(2,1)S(1)} %bitcast.144, bf16[512,256]{1,0:T(8,128)(2,1)S(1)} %get-tuple-element.8, f32[64,8,2,128]{3,2,1,0:T(2,128)S(1)} %bitcast.148), kind=kOutput, calls=%fused_computation.6 | convolution fusion | flops 537526272 | bytes 4456448 | tf_op jit(solution)/shard_map/qmj,qjn->mn/dot_general | solution.py:70
  (26 shorter events, 0.2 us)
Async XLA Ops:
  0.0 10.6 %copy-start.5 = (s32[16,16]{1,0:T(8,128)S(1)}, s32[16,16]{1,0:T(8,128)}, u32[]{:S(2)}) copy-start(s32[16,16]{1,0:T(8,128)} %param.3) | copy-start | bytes 3076
  0.0 10.9 %collective-permute-start = (bf16[512,256]{1,0:T(8,128)(2,1)}, bf16[512,256]{1,0:T(8,128)(2,1)S(1)}, u32[]{:S(2)}, u32[]{:S(2)}) collective-permute-start(bf16[512,256]{1,0:T(8,128)(2,1)} %param.2), channel_id=1, source_target_pairs={{0,8},{8,0},{16,24},{24,16},{1,9},{9,1},{17,25},{25,17},{2,10},{10... | collective-permute-start | bytes 786440 | tf_op jit(solution)/shard_map/ppermute | solution.py:10
  1.5 20.0 %collective-permute-start.2 = (bf16[512,256]{1,0:T(8,128)(2,1)}, bf16[512,256]{1,0:T(8,128)(2,1)S(1)}, u32[]{:S(2)}, u32[]{:S(2)}) collective-permute-start(bf16[512,256]{1,0:T(8,128)(2,1)} %param.2), channel_id=1, source_target_pairs={{0,2},{1,3},{2,0},{3,1},{4,6},{5,7},{6,4},{7,5},{8,10},{9,11},{10,... | collective-permute-start | bytes 786440 | tf_op jit(solution)/shard_map/ppermute | solution.py:10
  3.1 18.7 %collective-permute-start.4 = (bf16[512,256]{1,0:T(8,128)(2,1)}, bf16[512,256]{1,0:T(8,128)(2,1)S(1)}, u32[]{:S(2)}, u32[]{:S(2)}) collective-permute-start(bf16[512,256]{1,0:T(8,128)(2,1)} %param.2), channel_id=1, source_target_pairs={{0,4},{1,5},{2,6},{3,7},{4,0},{5,1},{6,2},{7,3},{8,12},{9,13},{10,... | collective-permute-start | bytes 786440 | tf_op jit(solution)/shard_map/ppermute | solution.py:10
  3.4 24.1 %collective-permute-start.6 = (bf16[512,256]{1,0:T(8,128)(2,1)}, bf16[512,256]{1,0:T(8,128)(2,1)S(1)}, u32[]{:S(2)}, u32[]{:S(2)}) collective-permute-start(bf16[512,256]{1,0:T(8,128)(2,1)} %param.2), channel_id=1, source_target_pairs={{0,6},{1,7},{2,4},{3,5},{4,2},{5,3},{6,0},{7,1},{8,14},{9,15},{10,... | collective-permute-start | bytes 786440 | tf_op jit(solution)/shard_map/ppermute | solution.py:10
  5.0 10.0 %collective-permute-start.9 = (bf16[512,256]{1,0:T(8,128)(2,1)}, bf16[512,256]{1,0:T(8,128)(2,1)S(1)}, u32[]{:S(2)}, u32[]{:S(2)}) collective-permute-start(bf16[512,256]{1,0:T(8,128)(2,1)} %param.2), channel_id=1, source_target_pairs={{0,24},{8,16},{16,8},{24,0},{1,25},{9,17},{17,9},{25,1},{2,26},{10... | collective-permute-start | bytes 786440 | tf_op jit(solution)/shard_map/ppermute | solution.py:10
  10.9 9.6 %collective-permute-start.8 = (bf16[512,256]{1,0:T(8,128)(2,1)}, bf16[512,256]{1,0:T(8,128)(2,1)S(1)}, u32[]{:S(2)}, u32[]{:S(2)}) collective-permute-start(bf16[512,256]{1,0:T(8,128)(2,1)} %param.2), channel_id=1, source_target_pairs={{0,16},{8,24},{16,0},{24,8},{1,17},{9,25},{17,1},{25,9},{2,18},{10... | collective-permute-start | bytes 786440 | tf_op jit(solution)/shard_map/ppermute | solution.py:10
  14.9 13.2 %collective-permute-start.1 = (bf16[512,256]{1,0:T(8,128)(2,1)}, bf16[512,256]{1,0:T(8,128)(2,1)S(1)}, u32[]{:S(2)}, u32[]{:S(2)}) collective-permute-start(bf16[512,256]{1,0:T(8,128)(2,1)} %param.2), channel_id=1, source_target_pairs={{0,1},{1,0},{2,3},{3,2},{4,5},{5,4},{6,7},{7,6},{8,9},{9,8},{10,11... | collective-permute-start | bytes 786440 | tf_op jit(solution)/shard_map/ppermute | solution.py:10
  21.5 6.8 %copy-start.4 = (bf16[512,2048]{1,0:T(8,128)(2,1)S(1)}, bf16[512,2048]{1,0:T(8,128)(2,1)}, u32[]{:S(2)}) copy-start(bf16[512,2048]{1,0:T(8,128)(2,1)} %get-tuple-element.7) | copy-start | bytes 6291460
  21.5 7.2 %collective-permute-start.3 = (bf16[512,256]{1,0:T(8,128)(2,1)S(1)}, bf16[512,256]{1,0:T(8,128)(2,1)S(1)}, u32[]{:S(2)}, u32[]{:S(2)}) collective-permute-start(bf16[512,256]{1,0:T(8,128)(2,1)S(1)} %collective-permute-done.2), channel_id=1, source_target_pairs={{0,1},{1,0},{2,3},{3,2},{4,5},{5,4},{6,7},{7,6},{8,9},{9,8},{10,11... | collective-permute-start | bytes 786440 | tf_op jit(solution)/shard_map/ppermute | solution.py:10
  21.7 7.5 %collective-permute-start.5 = (bf16[512,256]{1,0:T(8,128)(2,1)S(1)}, bf16[512,256]{1,0:T(8,128)(2,1)S(1)}, u32[]{:S(2)}, u32[]{:S(2)}) collective-permute-start(bf16[512,256]{1,0:T(8,128)(2,1)S(1)} %collective-permute-done.4), channel_id=1, source_target_pairs={{0,1},{1,0},{2,3},{3,2},{4,5},{5,4},{6,7},{7,6},{8,9},{9,8},{10,11... | collective-permute-start | bytes 786440 | tf_op jit(solution)/shard_map/ppermute | solution.py:10
  27.6 2.3 %collective-permute-start.7 = (bf16[512,256]{1,0:T(8,128)(2,1)S(1)}, bf16[512,256]{1,0:T(8,128)(2,1)S(1)}, u32[]{:S(2)}, u32[]{:S(2)}) collective-permute-start(bf16[512,256]{1,0:T(8,128)(2,1)S(1)} %collective-permute-done.6), channel_id=1, source_target_pairs={{0,1},{1,0},{2,3},{3,2},{4,5},{5,4},{6,7},{7,6},{8,9},{9,8},{10,11... | collective-permute-start | bytes 786440 | tf_op jit(solution)/shard_map/ppermute | solution.py:10
  30.8 1.4 %copy-start.2 = (f32[512,2,128]{2,1,0:T(2,128)}, f32[512,2,128]{2,1,0:T(2,128)S(1)}, u32[]{:S(2)}) copy-start(f32[512,2,128]{2,1,0:T(2,128)S(1)} %broadcast_in_dim.39) | copy-start | bytes 1572868
  30.8 4.9 %copy-start = (bf16[8,512,256]{2,1,0:T(8,128)(2,1)S(1)}, bf16[8,512,256]{2,1,0:T(8,128)(2,1)}, u32[]{:S(2)}) copy-start(bf16[8,512,256]{2,1,0:T(8,128)(2,1)} %constant_dynamic-update-slice_fusion) | copy-start | bytes 6291460
  32.2 9.4 %collective-permute-start.10 = (bf16[512,256]{1,0:T(8,128)(2,1)}, bf16[512,256]{1,0:T(8,128)(2,1)}, u32[]{:S(2)}, u32[]{:S(2)}) collective-permute-start(bf16[512,256]{1,0:T(8,128)(2,1)} %fusion.3), channel_id=1, source_target_pairs={{0,8},{8,0},{16,24},{24,16},{1,9},{9,1},{17,25},{25,17},{2,10},{10... | collective-permute-start | bytes 786440 | tf_op jit(solution)/shard_map/ppermute | solution.py:10
  32.7 13.4 %collective-permute-start.11 = (bf16[512,256]{1,0:T(8,128)(2,1)}, bf16[512,256]{1,0:T(8,128)(2,1)}, u32[]{:S(2)}, u32[]{:S(2)}) collective-permute-start(bf16[512,256]{1,0:T(8,128)(2,1)} %fusion.3), channel_id=1, source_target_pairs={{0,16},{8,24},{16,0},{24,8},{1,17},{9,25},{17,1},{25,9},{2,18},{10... | collective-permute-start | bytes 786440 | tf_op jit(solution)/shard_map/ppermute | solution.py:10
  34.3 13.6 %collective-permute-start.12 = (bf16[512,256]{1,0:T(8,128)(2,1)}, bf16[512,256]{1,0:T(8,128)(2,1)}, u32[]{:S(2)}, u32[]{:S(2)}) collective-permute-start(bf16[512,256]{1,0:T(8,128)(2,1)} %fusion.3), channel_id=1, source_target_pairs={{0,24},{8,16},{16,8},{24,0},{1,25},{9,17},{17,9},{25,1},{2,26},{10... | collective-permute-start | bytes 786440 | tf_op jit(solution)/shard_map/ppermute | solution.py:10
  36.2 12.9 %copy-start.3 = (f32[512,2,128]{2,1,0:T(2,128)S(1)}, f32[512,2,128]{2,1,0:T(2,128)}, u32[]{:S(2)}) copy-start(f32[512,2,128]{2,1,0:T(2,128)} %copy-done.2) | copy-start | bytes 1572868
  38.2 10.9 %copy-start.1 = (bf16[8,512,256]{2,1,0:T(8,128)(2,1)S(1)}, bf16[8,512,256]{2,1,0:T(8,128)(2,1)}, u32[]{:S(2)}) copy-start(bf16[8,512,256]{2,1,0:T(8,128)(2,1)} %gather_fusion) | copy-start | bytes 6291460

commit v20 on v19

--- a/solution.py
+++ b/solution.py
@@ -66,8 +66,13 @@
             + jnp.arange(ratio, dtype=jnp.int32)[None, :]
         ).reshape(-1)
         row_fs = jnp.take(jnp.stack(row_pieces), f_members ^ col_index, axis=0, mode="clip")
-        f_stack = jnp.concatenate(f_pieces, axis=0).reshape(n_col, cols, cols)
-        cubic = jnp.einsum("qmj,qjn->mn", row_fs, f_stack, preferred_element_type=jnp.float32)
+        cubic = None
+        for j, f_piece in enumerate(f_pieces):
+            term = jnp.einsum(
+                "qmj,qjn->mn", row_fs[j * ratio:(j + 1) * ratio],
+                f_piece.reshape(ratio, cols, cols), preferred_element_type=jnp.float32,
+            )
+            cubic = term if cubic is None else cubic + term
         return mask_float * (1.5 * masked.astype(jnp.float32) - 0.5 * cubic)
 
     return body

time: 50.8 us -> 52 us (1.024); the launches traced: 50.6 us -> 51.1 us
  waiting for transfers between devices: 23.7 us -> 16.1 us
  matrix products: 2.92 us -> 7.19 us
  other arithmetic: 5.64 us -> 9.24 us
    ppermute x13, waiting for transfers between devices: 23.7 us -> 16.1 us  [_swap(): return lax.ppermute(x, axis, [(i, i ^ d) for i in range(size)])]
    dot_general x1 -> x4, matrix products: 1.51 us -> 5.78 us  [body(): jnp.einsum('qmj,qjn->mn', row_fs[j * ratio:(j + 1) * ratio], f_piece.resh...]
    unnamed x13, other arithmetic: 2.54 us -> 6.7 us
    concatenate x1 -> x0, other arithmetic: 1.26 us -> none  [body(): f_stack = jnp.concatenate(f_pieces, axis=0).reshape(n_col, cols, cols)]
    another operation x1, other arithmetic: 0.06 us -> 0.77 us  [body(): jnp.stack(row_pieces)]
  transfers between devices with their start and end apart: 13 -> 13, of which waited for: 7 -> 6; matrix products, arithmetic and copies ran while one was open for 21% -> 35% of each run, Pallas kernels for 0% -> 0%
where the time goes in v20:
time: 52 us; the launch traced here: 51.1 us
  waiting for transfers between devices  16.1 us (31%)
  starting transfers between devices  11 us (21%)
  other arithmetic  9.24 us (18%)
  local copies, waits for them, and re-layouts  7.19 us (14%)
  matrix products  7.19 us (14%)
    ppermute x13, waiting for transfers between devices, _swap(): return lax.ppermute(x, axis, [(i, i ^ d) for i in range(size)])  16.1 us
    ppermute x13, starting transfers between devices, _swap(): return lax.ppermute(x, axis, [(i, i ^ d) for i in range(size)])  11 us
    unnamed x13, other arithmetic  6.7 us
    dot_general x4, matrix products, body(): jnp.einsum('qmj,qjn->mn', row_fs[j * ratio:(j + 1) * ratio], f_piece.resh...  5.78 us
    gather x1, local copies, waits for them, and re-layouts, body(): jnp.take(jnp.stack(row_pieces), f_members ^ col_index, axis=0, mode='clip')  2.27 us
    mul x10, local copies, waits for them, and re-layouts, mask_from(): return (x4 * blocks[:, None, :, None]).reshape(rows, cols)  2.05 us
    dot_general x1, matrix products, body(): jnp.dot(row_cat, in_slot_order(col_pieces), preferred_element_type=jnp.fl...  1.41 us
    broadcast_in_dim x4, local copies, waits for them, and re-layouts, body(): local_mask = jnp.repeat(jnp.repeat(local_blocks, B, axis=0), B, axis=1)  1.24 us
  transfers between devices with their start and end apart: 13, of which 6 were waited for; matrix products, arithmetic and copies ran while one was open for 35% of the time, Pallas kernels for 0%

profile of v20, /device:TPU:16, one launch (start us, length us, event | category | flops | bytes accessed | tf_op | source)
XLA Modules:
  0.0 51.1 jit_solution(14344193892837349574)
XLA Ops:
  0.0 1.5 %collective-permute-start = (bf16[512,256]{1,0:T(8,128)(2,1)}, bf16[512,256]{1,0:T(8,128)(2,1)S(1)}, u32[]{:S(2)}, u32[]{:S(2)}) collective-permute-start(bf16[512,256]{1,0:T(8,128)(2,1)} %param.2), channel_id=1, source_target_pairs={{0,8},{8,0},{16,24},{24,16},{1,9},{9,1},{17,25},{25,17},{2,10},{10... | collective-permute-start | bytes 786440 | tf_op jit(solution)/shard_map/ppermute | solution.py:10
  1.5 1.6 %collective-permute-start.2 = (bf16[512,256]{1,0:T(8,128)(2,1)}, bf16[512,256]{1,0:T(8,128)(2,1)S(1)}, u32[]{:S(2)}, u32[]{:S(2)}) collective-permute-start(bf16[512,256]{1,0:T(8,128)(2,1)} %param.2), channel_id=1, source_target_pairs={{0,2},{1,3},{2,0},{3,1},{4,6},{5,7},{6,4},{7,5},{8,10},{9,11},{10,... | collective-permute-start | bytes 786440 | tf_op jit(solution)/shard_map/ppermute | solution.py:10
  3.1 0.3 collective-permute-start.4
  3.4 1.6 %collective-permute-start.6 = (bf16[512,256]{1,0:T(8,128)(2,1)}, bf16[512,256]{1,0:T(8,128)(2,1)S(1)}, u32[]{:S(2)}, u32[]{:S(2)}) collective-permute-start(bf16[512,256]{1,0:T(8,128)(2,1)} %param.2), channel_id=1, source_target_pairs={{0,6},{1,7},{2,4},{3,5},{4,2},{5,3},{6,0},{7,1},{8,14},{9,15},{10,... | collective-permute-start | bytes 786440 | tf_op jit(solution)/shard_map/ppermute | solution.py:10
  5.0 1.5 %collective-permute-start.9 = (bf16[512,256]{1,0:T(8,128)(2,1)}, bf16[512,256]{1,0:T(8,128)(2,1)S(1)}, u32[]{:S(2)}, u32[]{:S(2)}) collective-permute-start(bf16[512,256]{1,0:T(8,128)(2,1)} %param.2), channel_id=1, source_target_pairs={{0,24},{8,16},{16,8},{24,0},{1,25},{9,17},{17,9},{25,1},{2,26},{10... | collective-permute-start | bytes 786440 | tf_op jit(solution)/shard_map/ppermute | solution.py:10
  6.5 0.8 %dynamic-slice_convert_fusion.1 = (f32[4,2]{1,0:T(4,128)S(1)}, bf16[4,2]{1,0:T(4,128)(2,1)S(1)}) fusion(s32[16,16]{1,0:T(8,128)} %param.3, s32[]{:T(128)S(6)} %select_n.100, s32[]{:T(128)S(6)} %select_n.101), kind=kLoop, calls=%fused_computation.57 | loop fusion | flops 16 | bytes 88 | tf_op jit(solution)/shard_map/convert_element_type | solution.py:61
  7.3 0.6 %broadcast_in_dim.41 = bf16[512,2,128]{2,1,0:T(2,128)(2,1)S(1)} broadcast(bf16[512,2]{1,0:T(8,128)(2,1)S(1)} %bitcast.168), dimensions={0,1} | broadcast | bytes 264192 | tf_op jit(solution)/shard_map/broadcast_in_dim | solution.py:26
  7.9 1.7 %constant_dynamic-update-slice_fusion.1 = (bf16[512,2048]{1,0:T(8,128)(2,1)}, bf16[512,256]{1,0:T(8,128)(2,1)S(1)}) fusion(bf16[512,256]{1,0:T(8,128)(2,1)} %param.2, bf16[64,8,2,128]{3,2,1,0:T(2,128)(2,1)S(1)} %bitcast.167), kind=kLoop, calls=%fused_computation.45 | loop fusion | flops 524287 | bytes 1048576
  9.7 0.7 %constant_dynamic-update-slice_fusion = bf16[8,512,256]{2,1,0:T(8,128)(2,1)} fusion(bf16[512,256]{1,0:T(8,128)(2,1)S(1)} %get-tuple-element.8), kind=kLoop, calls=%fused_computation.44 | loop fusion | bytes 524288
  10.4 0.1 add_xor_fusion
  10.4 0.1 reshape.252
  10.6 0.1 fusion.20
  10.8 0.1 broadcast_in_dim.42
  10.9 0.6 %collective-permute-start.8 = (bf16[512,256]{1,0:T(8,128)(2,1)}, bf16[512,256]{1,0:T(8,128)(2,1)S(1)}, u32[]{:S(2)}, u32[]{:S(2)}) collective-permute-start(bf16[512,256]{1,0:T(8,128)(2,1)} %param.2), channel_id=1, source_target_pairs={{0,16},{8,24},{16,0},{24,8},{1,17},{9,25},{17,1},{25,9},{2,18},{10... | collective-permute-start | bytes 786440 | tf_op jit(solution)/shard_map/ppermute | solution.py:10
  11.4 0.2 mul.279
  11.7 3.2 %collective-permute-done.9 = bf16[512,256]{1,0:T(8,128)(2,1)S(1)} collective-permute-done((bf16[512,256]{1,0:T(8,128)(2,1)}, bf16[512,256]{1,0:T(8,128)(2,1)S(1)}, u32[]{:S(2)}, u32[]{:S(2)}) %collective-permute-start.9) | collective-permute-done | bytes 262176 | tf_op jit(solution)/shard_map/ppermute | solution.py:10
  14.9 0.0 collective-permute-start.1
  14.9 0.2 mul.289
  15.2 0.1 fusion.7
  15.2 5.2 %collective-permute-done.8 = bf16[512,256]{1,0:T(8,128)(2,1)S(1)} collective-permute-done((bf16[512,256]{1,0:T(8,128)(2,1)}, bf16[512,256]{1,0:T(8,128)(2,1)S(1)}, u32[]{:S(2)}, u32[]{:S(2)}) %collective-permute-start.8) | collective-permute-done | bytes 262176 | tf_op jit(solution)/shard_map/ppermute | solution.py:10
  20.5 0.2 mul.284
  20.7 0.1 fusion.8
  20.7 0.1 pad_maximum_fusion
  20.9 0.6 %gather_fusion.1 = bf16[8,256,256]{2,1,0:T(8,128)(2,1)S(1)} fusion(bf16[8,256,256]{2,1,0:T(8,128)(2,1)S(1)} %bitcast.145, s32[1024]{0:T(1024)S(1)} %pad_clamp_fusion), kind=kCustom, calls=%fused_computation.1 | custom fusion | bytes 2097184 | tf_op jit(solution)/shard_map/jit(_take)/gather | solution.py:57
  21.5 0.1 collective-permute-start.3
  21.6 0.1 collective-permute-done.4
  21.7 0.4 collective-permute-start.5
  22.1 5.5 %collective-permute-done.6 = bf16[512,256]{1,0:T(8,128)(2,1)S(1)} collective-permute-done((bf16[512,256]{1,0:T(8,128)(2,1)}, bf16[512,256]{1,0:T(8,128)(2,1)S(1)}, u32[]{:S(2)}, u32[]{:S(2)}) %collective-permute-start.6) | collective-permute-done | bytes 262176 | tf_op jit(solution)/shard_map/ppermute | solution.py:10
  27.6 0.5 %bitcast_select_fusion = bf16[2048,256]{1,0:T(8,128)(2,1)S(1)} fusion(bf16[8,256,256]{2,1,0:T(8,128)(2,1)S(1)} %gather_fusion.1, pred[2048]{0:T(1024)(128)(4,1)S(1)} %broadcast_in_dim.43), kind=kLoop, calls=%fused_computation.15 | loop fusion | flops 524288 | bytes 2099200 | tf_op jit(solution)/shard_map/jit(_take)/select_n | solution.py:57
  28.1 0.0 copy-start.2
  28.1 0.2 mul.242
  28.3 0.1 fusion.10
  28.4 0.2 mul.247
  28.6 0.1 fusion.11
  28.7 0.2 mul.252
  28.9 0.1 fusion.12
  29.0 0.2 mul.257
  29.2 0.1 fusion.13
  29.3 0.2 mul.262
  29.5 0.1 fusion.14
  29.6 0.2 mul.267
  29.8 0.1 fusion.15
  29.9 0.2 mul.272
  30.1 0.1 fusion.16
  30.2 0.6 %broadcast_in_dim.39 = f32[512,2,128]{2,1,0:T(2,128)S(1)} broadcast(f32[512,2]{1,0:T(8,128)S(1)} %bitcast.166), dimensions={0,1} | broadcast | bytes 528384 | tf_op jit(solution)/shard_map/broadcast_in_dim | solution.py:26
  30.8 0.0 copy-start.3
  30.8 1.4 %fusion.6 = bf16[512,256]{1,0:T(8,128)(2,1)} fusion(bf16[512,2048]{1,0:T(8,128)(2,1)S(1)} %fusion.16, bf16[2048,256]{1,0:T(8,128)(2,1)S(1)} %bitcast_select_fusion, f32[64,8,2,128]{3,2,1,0:T(2,128)S(1)} %bitcast.161), kind=kOutput, calls=%fused_computation.13 | convolution fusion | flops 537133056 | bytes 3932160 | tf_op jit(solution)/shard_map/dot_general | solution.py:60
  32.2 0.5 %collective-permute-start.10 = (bf16[512,256]{1,0:T(8,128)(2,1)}, bf16[512,256]{1,0:T(8,128)(2,1)}, u32[]{:S(2)}, u32[]{:S(2)}) collective-permute-start(bf16[512,256]{1,0:T(8,128)(2,1)} %fusion.6), channel_id=1, source_target_pairs={{0,8},{8,0},{16,24},{24,16},{1,9},{9,1},{17,25},{25,17},{2,10},{10... | collective-permute-start | bytes 786440 | tf_op jit(solution)/shard_map/ppermute | solution.py:10
  32.8 1.5 %collective-permute-start.11 = (bf16[512,256]{1,0:T(8,128)(2,1)}, bf16[512,256]{1,0:T(8,128)(2,1)}, u32[]{:S(2)}, u32[]{:S(2)}) collective-permute-start(bf16[512,256]{1,0:T(8,128)(2,1)} %fusion.6), channel_id=1, source_target_pairs={{0,16},{8,24},{16,0},{24,8},{1,17},{9,25},{17,1},{25,9},{2,18},{10... | collective-permute-start | bytes 786440 | tf_op jit(solution)/shard_map/ppermute | solution.py:10
  34.3 1.4 %collective-permute-start.12 = (bf16[512,256]{1,0:T(8,128)(2,1)}, bf16[512,256]{1,0:T(8,128)(2,1)}, u32[]{:S(2)}, u32[]{:S(2)}) collective-permute-start(bf16[512,256]{1,0:T(8,128)(2,1)} %fusion.6), channel_id=1, source_target_pairs={{0,24},{8,16},{16,8},{24,0},{1,25},{9,17},{17,9},{25,1},{2,26},{10... | collective-permute-start | bytes 786440 | tf_op jit(solution)/shard_map/ppermute | solution.py:10
  35.7 0.8 %bitcast_dynamic-update-slice_fusion.6 = bf16[8,512,256]{2,1,0:T(8,128)(2,1)} fusion(bf16[8,512,256]{2,1,0:T(8,128)(2,1)} %constant_dynamic-update-slice_fusion, bf16[512,256]{1,0:T(8,128)(2,1)S(1)} %copy-done.3, bf16[64,8,2,128]{3,2,1,0:T(2,128)(2,1)S(1)} %bitcast.148), kind=kLoop, calls=%fused_computation.36 | loop fusion | flops 524288 | bytes 786432
  36.5 0.8 %bitcast_dynamic-update-slice_fusion.5 = bf16[8,512,256]{2,1,0:T(8,128)(2,1)} fusion(bf16[8,512,256]{2,1,0:T(8,128)(2,1)} %bitcast_dynamic-update-slice_fusion.6, bf16[512,256]{1,0:T(8,128)(2,1)S(1)} %copy-done.1, bf16[64,8,2,128]{3,2,1,0:T(2,128)(2,1)S(1)} %bitcast.150), kind=kLoop, calls=%fused_computation.35 | loop fusion | flops 524288 | bytes 786432
  37.2 0.8 %bitcast_dynamic-update-slice_fusion.4 = bf16[8,512,256]{2,1,0:T(8,128)(2,1)} fusion(bf16[8,512,256]{2,1,0:T(8,128)(2,1)} %bitcast_dynamic-update-slice_fusion.5, bf16[512,256]{1,0:T(8,128)(2,1)S(1)} %collective-permute-done.3, bf16[64,8,2,128]{3,2,1,0:T(2,128)(2,1)S(1)} %bitcast.152), kind=kLoop, calls=%fused_computation.34 | loop fusion | flops 524288 | bytes 786432
  38.0 0.8 %bitcast_dynamic-update-slice_fusion.3 = bf16[8,512,256]{2,1,0:T(8,128)(2,1)} fusion(bf16[8,512,256]{2,1,0:T(8,128)(2,1)} %bitcast_dynamic-update-slice_fusion.4, bf16[512,256]{1,0:T(8,128)(2,1)S(1)} %collective-permute-done.4, bf16[64,8,2,128]{3,2,1,0:T(2,128)(2,1)S(1)} %bitcast.154), kind=kLoop, calls=%fused_computation.33 | loop fusion | flops 524288 | bytes 786432
  38.8 0.8 %bitcast_dynamic-update-slice_fusion.2 = bf16[8,512,256]{2,1,0:T(8,128)(2,1)} fusion(bf16[8,512,256]{2,1,0:T(8,128)(2,1)} %bitcast_dynamic-update-slice_fusion.3, bf16[512,256]{1,0:T(8,128)(2,1)S(1)} %collective-permute-done.5, bf16[64,8,2,128]{3,2,1,0:T(2,128)(2,1)S(1)} %bitcast.156), kind=kLoop, calls=%fused_computation.32 | loop fusion | flops 524288 | bytes 786432
  39.5 0.8 %bitcast_dynamic-update-slice_fusion.1 = bf16[8,512,256]{2,1,0:T(8,128)(2,1)} fusion(bf16[8,512,256]{2,1,0:T(8,128)(2,1)} %bitcast_dynamic-update-slice_fusion.2, bf16[512,256]{1,0:T(8,128)(2,1)S(1)} %collective-permute-done.6, bf16[64,8,2,128]{3,2,1,0:T(2,128)(2,1)S(1)} %bitcast.158), kind=kLoop, calls=%fused_computation.31 | loop fusion | flops 524288 | bytes 786432
  40.3 0.8 %bitcast_dynamic-update-slice_fusion = bf16[8,512,256]{2,1,0:T(8,128)(2,1)} fusion(bf16[8,512,256]{2,1,0:T(8,128)(2,1)} %bitcast_dynamic-update-slice_fusion.1, bf16[512,256]{1,0:T(8,128)(2,1)S(1)} %collective-permute-done.7, bf16[64,8,2,128]{3,2,1,0:T(2,128)(2,1)S(1)} %bitcast.160), kind=kLoop, calls=%fused_computation.30 | loop fusion | flops 524288 | bytes 786432 | tf_op jit(solution)/shard_map/stack | solution.py:68
  41.0 2.3 %gather_fusion = bf16[8,512,256]{2,1,0:T(8,128)(2,1)S(1)} fusion(bf16[8,512,256]{2,1,0:T(8,128)(2,1)} %bitcast_dynamic-update-slice_fusion, s32[1024]{0:T(1024)S(1)} %pad_clamp_fusion.1), kind=kCustom, calls=%fused_computation | custom fusion | bytes 4194336 | tf_op jit(solution)/shard_map/jit(_take)/gather | solution.py:68
  43.3 1.2 %convolution_bitcast_fusion.2 = f32[512,256]{1,0:T(8,128)S(1)} fusion(bf16[8,512,256]{2,1,0:T(8,128)(2,1)S(1)} %gather_fusion, bf16[2,256,256]{2,1,0:T(8,128)(2,1)} %bitcast.18), kind=kOutput, calls=%fused_computation.5 | convolution fusion | flops 134217728 | bytes 2883584 | tf_op jit(solution)/shard_map/qmj,qjn->mn/dot_general | solution.py:71
  44.6 1.6 %collective-permute-done.11 = bf16[512,256]{1,0:T(8,128)(2,1)} collective-permute-done((bf16[512,256]{1,0:T(8,128)(2,1)}, bf16[512,256]{1,0:T(8,128)(2,1)}, u32[]{:S(2)}, u32[]{:S(2)}) %collective-permute-start.11) | collective-permute-done | bytes 262176 | tf_op jit(solution)/shard_map/ppermute | solution.py:10
  46.2 1.2 %convolution_bitcast_fusion.1 = f32[512,256]{1,0:T(8,128)S(1)} fusion(bf16[8,512,256]{2,1,0:T(8,128)(2,1)S(1)} %gather_fusion, bf16[2,256,256]{2,1,0:T(8,128)(2,1)} %bitcast.20), kind=kOutput, calls=%fused_computation.4 | convolution fusion | flops 134217728 | bytes 2883584 | tf_op jit(solution)/shard_map/qmj,qjn->mn/dot_general | solution.py:71
  47.5 0.4 collective-permute-done.12
  47.8 1.2 %convolution_bitcast_fusion = f32[512,256]{1,0:T(8,128)S(1)} fusion(bf16[8,512,256]{2,1,0:T(8,128)(2,1)S(1)} %gather_fusion, bf16[2,256,256]{2,1,0:T(8,128)(2,1)} %bitcast.22), kind=kOutput, calls=%fused_computation.3 | convolution fusion | flops 134217728 | bytes 2883584 | tf_op jit(solution)/shard_map/qmj,qjn->mn/dot_general | solution.py:71
  49.1 2.1 %fusion.5 = f32[512,256]{1,0:T(8,128)} fusion(f32[512,256]{1,0:T(8,128)S(1)} %convolution_bitcast_fusion, f32[512,256]{1,0:T(8,128)S(1)} %convolution_bitcast_fusion.1, f32[512,256]{1,0:T(8,128)S(1)} %convolution_bitcast_fusion.2, bf16[8,512,256]{2,1,0:T(8,128)(2,1)S(1)} %gather_fusion, bf16[2,256,256]{2,1,0:T(8,128)(2,1)} %bitcast.16, ...), kind=kOutput, calls=%fused_computation.12 | convolution fusion | flops 135266304 | bytes 5242880 | tf_op jit(solution)/shard_map/qmj,qjn->mn/dot_general | solution.py:71
  (28 shorter events, 0.2 us)
Async XLA Ops:
  0.0 10.6 %copy-start.5 = (s32[16,16]{1,0:T(8,128)S(1)}, s32[16,16]{1,0:T(8,128)}, u32[]{:S(2)}) copy-start(s32[16,16]{1,0:T(8,128)} %param.3) | copy-start | bytes 3076
  0.0 10.9 %collective-permute-start = (bf16[512,256]{1,0:T(8,128)(2,1)}, bf16[512,256]{1,0:T(8,128)(2,1)S(1)}, u32[]{:S(2)}, u32[]{:S(2)}) collective-permute-start(bf16[512,256]{1,0:T(8,128)(2,1)} %param.2), channel_id=1, source_target_pairs={{0,8},{8,0},{16,24},{24,16},{1,9},{9,1},{17,25},{25,17},{2,10},{10... | collective-permute-start | bytes 786440 | tf_op jit(solution)/shard_map/ppermute | solution.py:10
  1.5 20.0 %collective-permute-start.2 = (bf16[512,256]{1,0:T(8,128)(2,1)}, bf16[512,256]{1,0:T(8,128)(2,1)S(1)}, u32[]{:S(2)}, u32[]{:S(2)}) collective-permute-start(bf16[512,256]{1,0:T(8,128)(2,1)} %param.2), channel_id=1, source_target_pairs={{0,2},{1,3},{2,0},{3,1},{4,6},{5,7},{6,4},{7,5},{8,10},{9,11},{10,... | collective-permute-start | bytes 786440 | tf_op jit(solution)/shard_map/ppermute | solution.py:10
  3.1 18.7 %collective-permute-start.4 = (bf16[512,256]{1,0:T(8,128)(2,1)}, bf16[512,256]{1,0:T(8,128)(2,1)S(1)}, u32[]{:S(2)}, u32[]{:S(2)}) collective-permute-start(bf16[512,256]{1,0:T(8,128)(2,1)} %param.2), channel_id=1, source_target_pairs={{0,4},{1,5},{2,6},{3,7},{4,0},{5,1},{6,2},{7,3},{8,12},{9,13},{10,... | collective-permute-start | bytes 786440 | tf_op jit(solution)/shard_map/ppermute | solution.py:10
  3.4 24.1 %collective-permute-start.6 = (bf16[512,256]{1,0:T(8,128)(2,1)}, bf16[512,256]{1,0:T(8,128)(2,1)S(1)}, u32[]{:S(2)}, u32[]{:S(2)}) collective-permute-start(bf16[512,256]{1,0:T(8,128)(2,1)} %param.2), channel_id=1, source_target_pairs={{0,6},{1,7},{2,4},{3,5},{4,2},{5,3},{6,0},{7,1},{8,14},{9,15},{10,... | collective-permute-start | bytes 786440 | tf_op jit(solution)/shard_map/ppermute | solution.py:10
  5.0 10.0 %collective-permute-start.9 = (bf16[512,256]{1,0:T(8,128)(2,1)}, bf16[512,256]{1,0:T(8,128)(2,1)S(1)}, u32[]{:S(2)}, u32[]{:S(2)}) collective-permute-start(bf16[512,256]{1,0:T(8,128)(2,1)} %param.2), channel_id=1, source_target_pairs={{0,24},{8,16},{16,8},{24,0},{1,25},{9,17},{17,9},{25,1},{2,26},{10... | collective-permute-start | bytes 786440 | tf_op jit(solution)/shard_map/ppermute | solution.py:10
  10.9 9.6 %collective-permute-start.8 = (bf16[512,256]{1,0:T(8,128)(2,1)}, bf16[512,256]{1,0:T(8,128)(2,1)S(1)}, u32[]{:S(2)}, u32[]{:S(2)}) collective-permute-start(bf16[512,256]{1,0:T(8,128)(2,1)} %param.2), channel_id=1, source_target_pairs={{0,16},{8,24},{16,0},{24,8},{1,17},{9,25},{17,1},{25,9},{2,18},{10... | collective-permute-start | bytes 786440 | tf_op jit(solution)/shard_map/ppermute | solution.py:10
  14.9 13.2 %collective-permute-start.1 = (bf16[512,256]{1,0:T(8,128)(2,1)}, bf16[512,256]{1,0:T(8,128)(2,1)S(1)}, u32[]{:S(2)}, u32[]{:S(2)}) collective-permute-start(bf16[512,256]{1,0:T(8,128)(2,1)} %param.2), channel_id=1, source_target_pairs={{0,1},{1,0},{2,3},{3,2},{4,5},{5,4},{6,7},{7,6},{8,9},{9,8},{10,11... | collective-permute-start | bytes 786440 | tf_op jit(solution)/shard_map/ppermute | solution.py:10
  21.5 6.8 %copy-start.4 = (bf16[512,2048]{1,0:T(8,128)(2,1)S(1)}, bf16[512,2048]{1,0:T(8,128)(2,1)}, u32[]{:S(2)}) copy-start(bf16[512,2048]{1,0:T(8,128)(2,1)} %get-tuple-element.7) | copy-start | bytes 6291460
  21.5 7.2 %copy-start = (bf16[512,256]{1,0:T(8,128)(2,1)}, bf16[512,256]{1,0:T(8,128)(2,1)S(1)}, u32[]{:S(2)}) copy-start(bf16[512,256]{1,0:T(8,128)(2,1)S(1)} %collective-permute-done.2) | copy-start | bytes 786436
  21.5 7.2 %collective-permute-start.3 = (bf16[512,256]{1,0:T(8,128)(2,1)S(1)}, bf16[512,256]{1,0:T(8,128)(2,1)S(1)}, u32[]{:S(2)}, u32[]{:S(2)}) collective-permute-start(bf16[512,256]{1,0:T(8,128)(2,1)S(1)} %collective-permute-done.2), channel_id=1, source_target_pairs={{0,1},{1,0},{2,3},{3,2},{4,5},{5,4},{6,7},{7,6},{8,9},{9,8},{10,11... | collective-permute-start | bytes 786440 | tf_op jit(solution)/shard_map/ppermute | solution.py:10
  21.7 7.6 %collective-permute-start.5 = (bf16[512,256]{1,0:T(8,128)(2,1)S(1)}, bf16[512,256]{1,0:T(8,128)(2,1)S(1)}, u32[]{:S(2)}, u32[]{:S(2)}) collective-permute-start(bf16[512,256]{1,0:T(8,128)(2,1)S(1)} %collective-permute-done.4), channel_id=1, source_target_pairs={{0,1},{1,0},{2,3},{3,2},{4,5},{5,4},{6,7},{7,6},{8,9},{9,8},{10,11... | collective-permute-start | bytes 786440 | tf_op jit(solution)/shard_map/ppermute | solution.py:10
  27.6 2.3 %collective-permute-start.7 = (bf16[512,256]{1,0:T(8,128)(2,1)S(1)}, bf16[512,256]{1,0:T(8,128)(2,1)S(1)}, u32[]{:S(2)}, u32[]{:S(2)}) collective-permute-start(bf16[512,256]{1,0:T(8,128)(2,1)S(1)} %collective-permute-done.6), channel_id=1, source_target_pairs={{0,1},{1,0},{2,3},{3,2},{4,5},{5,4},{6,7},{7,6},{8,9},{9,8},{10,11... | collective-permute-start | bytes 786440 | tf_op jit(solution)/shard_map/ppermute | solution.py:10
  28.1 1.2 %copy-start.2 = (bf16[512,256]{1,0:T(8,128)(2,1)}, bf16[512,256]{1,0:T(8,128)(2,1)S(1)}, u32[]{:S(2)}) copy-start(bf16[512,256]{1,0:T(8,128)(2,1)S(1)} %collective-permute-done.1) | copy-start | bytes 786436
  30.8 4.9 %copy-start.3 = (bf16[512,256]{1,0:T(8,128)(2,1)S(1)}, bf16[512,256]{1,0:T(8,128)(2,1)}, u32[]{:S(2)}) copy-start(bf16[512,256]{1,0:T(8,128)(2,1)} %copy-done.2) | copy-start | bytes 786436
  30.8 5.7 %copy-start.1 = (bf16[512,256]{1,0:T(8,128)(2,1)S(1)}, bf16[512,256]{1,0:T(8,128)(2,1)}, u32[]{:S(2)}) copy-start(bf16[512,256]{1,0:T(8,128)(2,1)} %copy-done) | copy-start | bytes 786436
  32.2 11.1 %collective-permute-start.10 = (bf16[512,256]{1,0:T(8,128)(2,1)}, bf16[512,256]{1,0:T(8,128)(2,1)}, u32[]{:S(2)}, u32[]{:S(2)}) collective-permute-start(bf16[512,256]{1,0:T(8,128)(2,1)} %fusion.6), channel_id=1, source_target_pairs={{0,8},{8,0},{16,24},{24,16},{1,9},{9,1},{17,25},{25,17},{2,10},{10... | collective-permute-start | bytes 786440 | tf_op jit(solution)/shard_map/ppermute | solution.py:10
  32.8 13.4 %collective-permute-start.11 = (bf16[512,256]{1,0:T(8,128)(2,1)}, bf16[512,256]{1,0:T(8,128)(2,1)}, u32[]{:S(2)}, u32[]{:S(2)}) collective-permute-start(bf16[512,256]{1,0:T(8,128)(2,1)} %fusion.6), channel_id=1, source_target_pairs={{0,16},{8,24},{16,0},{24,8},{1,17},{9,25},{17,1},{25,9},{2,18},{10... | collective-permute-start | bytes 786440 | tf_op jit(solution)/shard_map/ppermute | solution.py:10
  34.3 13.6 %collective-permute-start.12 = (bf16[512,256]{1,0:T(8,128)(2,1)}, bf16[512,256]{1,0:T(8,128)(2,1)}, u32[]{:S(2)}, u32[]{:S(2)}) collective-permute-start(bf16[512,256]{1,0:T(8,128)(2,1)} %fusion.6), channel_id=1, source_target_pairs={{0,24},{8,16},{16,8},{24,0},{1,25},{9,17},{17,9},{25,1},{2,26},{10... | collective-permute-start | bytes 786440 | tf_op jit(solution)/shard_map/ppermute | solution.py:10

commit v21 on v17

--- a/solution.py
+++ b/solution.py
@@ -65,8 +65,8 @@
             (jnp.arange(n_row, dtype=jnp.int32)[:, None] ^ row_index) * ratio
             + jnp.arange(ratio, dtype=jnp.int32)[None, :]
         ).reshape(-1)
-        row_f = jnp.take(row_cat.reshape(rows, n_col, cols), f_members ^ col_index, axis=1)
-        row_f = row_f.reshape(rows, n_col * cols)
+        row_fs = jnp.take(jnp.stack(row_pieces), f_members ^ col_index, axis=0, mode="clip")
+        row_f = jnp.transpose(row_fs, (1, 0, 2)).reshape(rows, n_col * cols)
         f_cat = jnp.concatenate(f_pieces, axis=0)
         cubic = jnp.dot(row_f, f_cat, preferred_element_type=jnp.float32)
         return mask_float * (1.5 * masked.astype(jnp.float32) - 0.5 * cubic)

time: 50.8 us -> 51.4 us (1.012)
  waiting for transfers between devices: 14.1 us -> 16.1 us
  other arithmetic: 11.1 us -> 9.31 us
  matrix products: 4.14 us -> 4.77 us
    gather x2 -> x1, local copies, waits for them, and re-layouts: 4.7 us -> 2.27 us  [body(): jnp.take(jnp.stack(row_pieces), f_members ^ col_index, axis=0, mode='clip')]
    transpose x0 -> x1, local copies, waits for them, and re-layouts: none -> 2.43 us  [body(): row_f = jnp.transpose(row_fs, (1, 0, 2)).reshape(rows, n_col * cols)]
    ppermute x13, waiting for transfers between devices: 14.1 us -> 16.1 us  [_swap(): return lax.ppermute(x, axis, [(i, i ^ d) for i in range(size)])]
    select_n x2 -> x0, other arithmetic: 1.83 us -> none  [body(): jnp.take(row_cat.reshape(rows, n_col, cols), f_members ^ col_index, axis=1)]
    concatenate x2 -> x1, other arithmetic: 0.85 us -> 0.07 us  [body(): row_cat = jnp.concatenate(row_pieces, axis=1)]
    another operation x0 -> x1, other arithmetic: none -> 0.78 us  [body(): jnp.stack(row_pieces)]
    dot_general x1, matrix products: 2.73 us -> 3.36 us  [body(): cubic = jnp.dot(row_f, f_cat, preferred_element_type=jnp.float32)]
  transfers between devices with their start and end apart: 13 -> 13, of which waited for: 5 -> 6; matrix products, arithmetic and copies ran while one was open for 40% -> 35% of each run, Pallas kernels for 0% -> 0%
where the time goes in v21:
time: 51.4 us; the launch traced here: 51.2 us
  waiting for transfers between devices  16.1 us (31%)
  starting transfers between devices  11 us (21%)
  local copies, waits for them, and re-layouts  9.61 us (19%)
  other arithmetic  9.31 us (18%)
  matrix products  4.77 us (9%)
    ppermute x13, waiting for transfers between devices, _swap(): return lax.ppermute(x, axis, [(i, i ^ d) for i in range(size)])  16.1 us
    ppermute x13, starting transfers between devices, _swap(): return lax.ppermute(x, axis, [(i, i ^ d) for i in range(size)])  11 us
    unnamed x13, other arithmetic  6.74 us
    dot_general x1, matrix products, body(): cubic = jnp.dot(row_f, f_cat, preferred_element_type=jnp.float32)  3.36 us
    transpose x1, local copies, waits for them, and re-layouts, body(): row_f = jnp.transpose(row_fs, (1, 0, 2)).reshape(rows, n_col * cols)  2.43 us
    gather x1, local copies, waits for them, and re-layouts, body(): jnp.take(jnp.stack(row_pieces), f_members ^ col_index, axis=0, mode='clip')  2.27 us
    mul x10, local copies, waits for them, and re-layouts, mask_from(): return (x4 * blocks[:, None, :, None]).reshape(rows, cols)  2.05 us
    dot_general x1, matrix products, body(): jnp.dot(row_cat, in_slot_order(col_pieces), preferred_element_type=jnp.fl...  1.41 us
  transfers between devices with their start and end apart: 13, of which 6 were waited for; matrix products, arithmetic and copies ran while one was open for 35% of the time, Pallas kernels for 0%

profile of v21, /device:TPU:16, one launch (start us, length us, event | category | flops | bytes accessed | tf_op | source)
XLA Modules:
  0.0 51.2 jit_solution(11002891462346567410)
XLA Ops:
  0.0 1.5 %collective-permute-start = (bf16[512,256]{1,0:T(8,128)(2,1)}, bf16[512,256]{1,0:T(8,128)(2,1)S(1)}, u32[]{:S(2)}, u32[]{:S(2)}) collective-permute-start(bf16[512,256]{1,0:T(8,128)(2,1)} %param.2), channel_id=1, source_target_pairs={{0,8},{8,0},{16,24},{24,16},{1,9},{9,1},{17,25},{25,17},{2,10},{10... | collective-permute-start | bytes 786440 | tf_op jit(solution)/shard_map/ppermute | solution.py:10
  1.5 1.6 %collective-permute-start.2 = (bf16[512,256]{1,0:T(8,128)(2,1)}, bf16[512,256]{1,0:T(8,128)(2,1)S(1)}, u32[]{:S(2)}, u32[]{:S(2)}) collective-permute-start(bf16[512,256]{1,0:T(8,128)(2,1)} %param.2), channel_id=1, source_target_pairs={{0,2},{1,3},{2,0},{3,1},{4,6},{5,7},{6,4},{7,5},{8,10},{9,11},{10,... | collective-permute-start | bytes 786440 | tf_op jit(solution)/shard_map/ppermute | solution.py:10
  3.1 0.3 collective-permute-start.4
  3.4 1.6 %collective-permute-start.6 = (bf16[512,256]{1,0:T(8,128)(2,1)}, bf16[512,256]{1,0:T(8,128)(2,1)S(1)}, u32[]{:S(2)}, u32[]{:S(2)}) collective-permute-start(bf16[512,256]{1,0:T(8,128)(2,1)} %param.2), channel_id=1, source_target_pairs={{0,6},{1,7},{2,4},{3,5},{4,2},{5,3},{6,0},{7,1},{8,14},{9,15},{10,... | collective-permute-start | bytes 786440 | tf_op jit(solution)/shard_map/ppermute | solution.py:10
  5.0 1.5 %collective-permute-start.9 = (bf16[512,256]{1,0:T(8,128)(2,1)}, bf16[512,256]{1,0:T(8,128)(2,1)S(1)}, u32[]{:S(2)}, u32[]{:S(2)}) collective-permute-start(bf16[512,256]{1,0:T(8,128)(2,1)} %param.2), channel_id=1, source_target_pairs={{0,24},{8,16},{16,8},{24,0},{1,25},{9,17},{17,9},{25,1},{2,26},{10... | collective-permute-start | bytes 786440 | tf_op jit(solution)/shard_map/ppermute | solution.py:10
  6.5 0.8 %dynamic-slice_convert_fusion.1 = (f32[4,2]{1,0:T(4,128)S(1)}, bf16[4,2]{1,0:T(4,128)(2,1)S(1)}) fusion(s32[16,16]{1,0:T(8,128)} %param.3, s32[]{:T(128)S(6)} %select_n.100, s32[]{:T(128)S(6)} %select_n.101), kind=kLoop, calls=%fused_computation.57 | loop fusion | flops 16 | bytes 88 | tf_op jit(solution)/shard_map/convert_element_type | solution.py:61
  7.3 0.6 %broadcast_in_dim.41 = bf16[512,2,128]{2,1,0:T(2,128)(2,1)S(1)} broadcast(bf16[512,2]{1,0:T(8,128)(2,1)S(1)} %bitcast.139), dimensions={0,1} | broadcast | bytes 264192 | tf_op jit(solution)/shard_map/broadcast_in_dim | solution.py:26
  7.9 1.7 %constant_dynamic-update-slice_fusion.1 = (bf16[512,2048]{1,0:T(8,128)(2,1)}, bf16[512,256]{1,0:T(8,128)(2,1)S(1)}) fusion(bf16[512,256]{1,0:T(8,128)(2,1)} %param.2, bf16[64,8,2,128]{3,2,1,0:T(2,128)(2,1)S(1)} %bitcast.138), kind=kLoop, calls=%fused_computation.45 | loop fusion | flops 524287 | bytes 1048576
  9.7 0.7 %constant_dynamic-update-slice_fusion = bf16[8,512,256]{2,1,0:T(8,128)(2,1)} fusion(bf16[512,256]{1,0:T(8,128)(2,1)S(1)} %get-tuple-element.8), kind=kLoop, calls=%fused_computation.44 | loop fusion | bytes 524288
  10.4 0.1 add_xor_fusion
  10.4 0.1 reshape.240
  10.6 0.1 fusion.24
  10.8 0.1 broadcast_in_dim.42
  10.9 0.6 %collective-permute-start.8 = (bf16[512,256]{1,0:T(8,128)(2,1)}, bf16[512,256]{1,0:T(8,128)(2,1)S(1)}, u32[]{:S(2)}, u32[]{:S(2)}) collective-permute-start(bf16[512,256]{1,0:T(8,128)(2,1)} %param.2), channel_id=1, source_target_pairs={{0,16},{8,24},{16,0},{24,8},{1,17},{9,25},{17,1},{25,9},{2,18},{10... | collective-permute-start | bytes 786440 | tf_op jit(solution)/shard_map/ppermute | solution.py:10
  11.4 0.2 mul.279
  11.6 0.1 fusion.12
  11.7 3.2 %collective-permute-done.9 = bf16[512,256]{1,0:T(8,128)(2,1)S(1)} collective-permute-done((bf16[512,256]{1,0:T(8,128)(2,1)}, bf16[512,256]{1,0:T(8,128)(2,1)S(1)}, u32[]{:S(2)}, u32[]{:S(2)}) %collective-permute-start.9) | collective-permute-done | bytes 262176 | tf_op jit(solution)/shard_map/ppermute | solution.py:10
  14.9 0.2 mul.289
  15.2 0.1 fusion.10
  15.2 5.2 %collective-permute-done.8 = bf16[512,256]{1,0:T(8,128)(2,1)S(1)} collective-permute-done((bf16[512,256]{1,0:T(8,128)(2,1)}, bf16[512,256]{1,0:T(8,128)(2,1)S(1)}, u32[]{:S(2)}, u32[]{:S(2)}) %collective-permute-start.8) | collective-permute-done | bytes 262176 | tf_op jit(solution)/shard_map/ppermute | solution.py:10
  20.5 0.2 mul.284
  20.7 0.1 fusion.11
  20.7 0.1 pad_maximum_fusion
  20.9 0.6 %gather_fusion.1 = bf16[8,256,256]{2,1,0:T(8,128)(2,1)S(1)} fusion(bf16[8,256,256]{2,1,0:T(8,128)(2,1)S(1)} %bitcast.117, s32[1024]{0:T(1024)S(1)} %pad_clamp_fusion), kind=kCustom, calls=%fused_computation.1 | custom fusion | bytes 2097184 | tf_op jit(solution)/shard_map/jit(_take)/gather | solution.py:57
  21.5 0.1 collective-permute-start.3
  21.6 0.1 collective-permute-done.4
  21.7 0.4 collective-permute-start.5
  22.1 5.5 %collective-permute-done.6 = bf16[512,256]{1,0:T(8,128)(2,1)S(1)} collective-permute-done((bf16[512,256]{1,0:T(8,128)(2,1)}, bf16[512,256]{1,0:T(8,128)(2,1)S(1)}, u32[]{:S(2)}, u32[]{:S(2)}) %collective-permute-start.6) | collective-permute-done | bytes 262176 | tf_op jit(solution)/shard_map/ppermute | solution.py:10
  27.6 0.0 collective-permute-start.7
  27.6 0.5 %bitcast_select_fusion = bf16[2048,256]{1,0:T(8,128)(2,1)S(1)} fusion(bf16[8,256,256]{2,1,0:T(8,128)(2,1)S(1)} %gather_fusion.1, pred[2048]{0:T(1024)(128)(4,1)S(1)} %broadcast_in_dim.43), kind=kLoop, calls=%fused_computation.15 | loop fusion | flops 524288 | bytes 2099200 | tf_op jit(solution)/shard_map/jit(_take)/select_n | solution.py:57
  28.1 0.0 collective-permute-done.1
  28.1 0.2 mul.242
  28.3 0.1 fusion.13
  28.4 0.2 mul.247
  28.6 0.1 fusion.14
  28.7 0.2 mul.252
  28.9 0.1 fusion.15
  29.0 0.2 mul.257
  29.2 0.1 fusion.16
  29.3 0.2 mul.262
  29.5 0.1 fusion.17
  29.6 0.2 mul.267
  29.8 0.1 fusion.18
  29.8 0.2 mul.272
  30.1 0.1 fusion.19
  30.2 0.6 %broadcast_in_dim.39 = f32[512,2,128]{2,1,0:T(2,128)S(1)} broadcast(f32[512,2]{1,0:T(8,128)S(1)} %bitcast.137), dimensions={0,1} | broadcast | bytes 528384 | tf_op jit(solution)/shard_map/broadcast_in_dim | solution.py:26
  30.8 0.0 copy-start
  30.8 1.4 %fusion.2 = bf16[512,256]{1,0:T(8,128)(2,1)} fusion(bf16[512,2048]{1,0:T(8,128)(2,1)S(1)} %fusion.19, bf16[2048,256]{1,0:T(8,128)(2,1)S(1)} %bitcast_select_fusion, f32[64,8,2,128]{3,2,1,0:T(2,128)S(1)} %bitcast.140), kind=kOutput, calls=%fused_computation.6 | convolution fusion | flops 537133056 | bytes 3932160 | tf_op jit(solution)/shard_map/dot_general | solution.py:60
  32.2 0.5 %collective-permute-start.10 = (bf16[512,256]{1,0:T(8,128)(2,1)}, bf16[512,256]{1,0:T(8,128)(2,1)}, u32[]{:S(2)}, u32[]{:S(2)}) collective-permute-start(bf16[512,256]{1,0:T(8,128)(2,1)} %fusion.2), channel_id=1, source_target_pairs={{0,8},{8,0},{16,24},{24,16},{1,9},{9,1},{17,25},{25,17},{2,10},{10... | collective-permute-start | bytes 786440 | tf_op jit(solution)/shard_map/ppermute | solution.py:10
  32.7 1.5 %collective-permute-start.11 = (bf16[512,256]{1,0:T(8,128)(2,1)}, bf16[512,256]{1,0:T(8,128)(2,1)}, u32[]{:S(2)}, u32[]{:S(2)}) collective-permute-start(bf16[512,256]{1,0:T(8,128)(2,1)} %fusion.2), channel_id=1, source_target_pairs={{0,16},{8,24},{16,0},{24,8},{1,17},{9,25},{17,1},{25,9},{2,18},{10... | collective-permute-start | bytes 786440 | tf_op jit(solution)/shard_map/ppermute | solution.py:10
  34.2 1.4 %collective-permute-start.12 = (bf16[512,256]{1,0:T(8,128)(2,1)}, bf16[512,256]{1,0:T(8,128)(2,1)}, u32[]{:S(2)}, u32[]{:S(2)}) collective-permute-start(bf16[512,256]{1,0:T(8,128)(2,1)} %fusion.2), channel_id=1, source_target_pairs={{0,24},{8,16},{16,8},{24,0},{1,25},{9,17},{17,9},{25,1},{2,26},{10... | collective-permute-start | bytes 786440 | tf_op jit(solution)/shard_map/ppermute | solution.py:10
  35.7 0.8 %bitcast_dynamic-update-slice_fusion.6 = bf16[8,512,256]{2,1,0:T(8,128)(2,1)} fusion(bf16[8,512,256]{2,1,0:T(8,128)(2,1)} %constant_dynamic-update-slice_fusion, bf16[512,256]{1,0:T(8,128)(2,1)S(1)} %collective-permute-done.1, bf16[64,8,2,128]{3,2,1,0:T(2,128)(2,1)S(1)} %bitcast.119), kind=kLoop, calls=%fused_computation.36 | loop fusion | flops 524288 | bytes 786432
  36.4 0.8 %bitcast_dynamic-update-slice_fusion.5 = bf16[8,512,256]{2,1,0:T(8,128)(2,1)} fusion(bf16[8,512,256]{2,1,0:T(8,128)(2,1)} %bitcast_dynamic-update-slice_fusion.6, bf16[512,256]{1,0:T(8,128)(2,1)S(1)} %collective-permute-done.2, bf16[64,8,2,128]{3,2,1,0:T(2,128)(2,1)S(1)} %bitcast.121), kind=kLoop, calls=%fused_computation.35 | loop fusion | flops 524288 | bytes 786432
  37.2 0.8 %bitcast_dynamic-update-slice_fusion.4 = bf16[8,512,256]{2,1,0:T(8,128)(2,1)} fusion(bf16[8,512,256]{2,1,0:T(8,128)(2,1)} %bitcast_dynamic-update-slice_fusion.5, bf16[512,256]{1,0:T(8,128)(2,1)S(1)} %collective-permute-done.3, bf16[64,8,2,128]{3,2,1,0:T(2,128)(2,1)S(1)} %bitcast.123), kind=kLoop, calls=%fused_computation.34 | loop fusion | flops 524288 | bytes 786432
  38.0 0.8 %bitcast_dynamic-update-slice_fusion.3 = bf16[8,512,256]{2,1,0:T(8,128)(2,1)} fusion(bf16[8,512,256]{2,1,0:T(8,128)(2,1)} %bitcast_dynamic-update-slice_fusion.4, bf16[512,256]{1,0:T(8,128)(2,1)S(1)} %collective-permute-done.4, bf16[64,8,2,128]{3,2,1,0:T(2,128)(2,1)S(1)} %bitcast.125), kind=kLoop, calls=%fused_computation.33 | loop fusion | flops 524288 | bytes 786432
  38.7 0.8 %bitcast_dynamic-update-slice_fusion.2 = bf16[8,512,256]{2,1,0:T(8,128)(2,1)} fusion(bf16[8,512,256]{2,1,0:T(8,128)(2,1)} %bitcast_dynamic-update-slice_fusion.3, bf16[512,256]{1,0:T(8,128)(2,1)S(1)} %collective-permute-done.5, bf16[64,8,2,128]{3,2,1,0:T(2,128)(2,1)S(1)} %bitcast.127), kind=kLoop, calls=%fused_computation.32 | loop fusion | flops 524288 | bytes 786432
  39.5 0.8 %bitcast_dynamic-update-slice_fusion.1 = bf16[8,512,256]{2,1,0:T(8,128)(2,1)} fusion(bf16[8,512,256]{2,1,0:T(8,128)(2,1)} %bitcast_dynamic-update-slice_fusion.2, bf16[512,256]{1,0:T(8,128)(2,1)S(1)} %collective-permute-done.6, bf16[64,8,2,128]{3,2,1,0:T(2,128)(2,1)S(1)} %bitcast.129), kind=kLoop, calls=%fused_computation.31 | loop fusion | flops 524288 | bytes 786432
  40.3 0.8 %bitcast_dynamic-update-slice_fusion = bf16[8,512,256]{2,1,0:T(8,128)(2,1)} fusion(bf16[8,512,256]{2,1,0:T(8,128)(2,1)} %bitcast_dynamic-update-slice_fusion.1, bf16[512,256]{1,0:T(8,128)(2,1)S(1)} %collective-permute-done.7, bf16[64,8,2,128]{3,2,1,0:T(2,128)(2,1)S(1)} %bitcast.131), kind=kLoop, calls=%fused_computation.30 | loop fusion | flops 524288 | bytes 786432 | tf_op jit(solution)/shard_map/stack | solution.py:68
  41.1 2.3 %gather_fusion = bf16[8,512,256]{2,1,0:T(8,128)(2,1)S(1)} fusion(bf16[8,512,256]{2,1,0:T(8,128)(2,1)} %bitcast_dynamic-update-slice_fusion, s32[1024]{0:T(1024)S(1)} %pad_clamp_fusion.1), kind=kCustom, calls=%fused_computation | custom fusion | bytes 4194336 | tf_op jit(solution)/shard_map/jit(_take)/gather | solution.py:68
  43.3 0.0 copy-start.1
  43.3 2.4 %copy.3 = bf16[512,8,256]{0,2,1:T(8,128)(2,1)} copy(bf16[512,8,256]{2,0,1:T(8,128)(2,1)S(1)} %bitcast.116) | data formatting | bytes 4194304 | tf_op jit(solution)/shard_map/transpose | solution.py:69
  45.8 0.4 collective-permute-done.11
  46.2 1.6 %collective-permute-done.12 = bf16[512,256]{1,0:T(8,128)(2,1)} collective-permute-done((bf16[512,256]{1,0:T(8,128)(2,1)}, bf16[512,256]{1,0:T(8,128)(2,1)}, u32[]{:S(2)}, u32[]{:S(2)}) %collective-permute-start.12) | collective-permute-done | bytes 262176 | tf_op jit(solution)/shard_map/ppermute | solution.py:10
  47.8 3.4 %fusion.1 = f32[512,256]{1,0:T(8,128)} fusion(bf16[512,2048]{0,1:T(8,128)(2,1)} %bitcast.133, bf16[512,256]{1,0:T(8,128)(2,1)} %collective-permute-done.12, bf16[512,256]{1,0:T(8,128)(2,1)} %collective-permute-done.11, bf16[512,256]{1,0:T(8,128)(2,1)} %collective-permute-done.10, bf16[512,256]{1,0:T(8,128)(2,1)} %fusion.2, ...), kind=kOutput, calls=%fused_computation.5 | convolution fusion | flops 541720576 | bytes 4456448 | tf_op jit(solution)/shard_map/dot_general | solution.py:71
  (22 shorter events, 0.1 us)
Async XLA Ops:
  0.0 10.6 %copy-start.3 = (s32[16,16]{1,0:T(8,128)S(1)}, s32[16,16]{1,0:T(8,128)}, u32[]{:S(2)}) copy-start(s32[16,16]{1,0:T(8,128)} %param.3) | copy-start | bytes 3076
  0.0 10.9 %collective-permute-start = (bf16[512,256]{1,0:T(8,128)(2,1)}, bf16[512,256]{1,0:T(8,128)(2,1)S(1)}, u32[]{:S(2)}, u32[]{:S(2)}) collective-permute-start(bf16[512,256]{1,0:T(8,128)(2,1)} %param.2), channel_id=1, source_target_pairs={{0,8},{8,0},{16,24},{24,16},{1,9},{9,1},{17,25},{25,17},{2,10},{10... | collective-permute-start | bytes 786440 | tf_op jit(solution)/shard_map/ppermute | solution.py:10
  1.5 20.0 %collective-permute-start.2 = (bf16[512,256]{1,0:T(8,128)(2,1)}, bf16[512,256]{1,0:T(8,128)(2,1)S(1)}, u32[]{:S(2)}, u32[]{:S(2)}) collective-permute-start(bf16[512,256]{1,0:T(8,128)(2,1)} %param.2), channel_id=1, source_target_pairs={{0,2},{1,3},{2,0},{3,1},{4,6},{5,7},{6,4},{7,5},{8,10},{9,11},{10,... | collective-permute-start | bytes 786440 | tf_op jit(solution)/shard_map/ppermute | solution.py:10
  3.1 18.7 %collective-permute-start.4 = (bf16[512,256]{1,0:T(8,128)(2,1)}, bf16[512,256]{1,0:T(8,128)(2,1)S(1)}, u32[]{:S(2)}, u32[]{:S(2)}) collective-permute-start(bf16[512,256]{1,0:T(8,128)(2,1)} %param.2), channel_id=1, source_target_pairs={{0,4},{1,5},{2,6},{3,7},{4,0},{5,1},{6,2},{7,3},{8,12},{9,13},{10,... | collective-permute-start | bytes 786440 | tf_op jit(solution)/shard_map/ppermute | solution.py:10
  3.4 24.1 %collective-permute-start.6 = (bf16[512,256]{1,0:T(8,128)(2,1)}, bf16[512,256]{1,0:T(8,128)(2,1)S(1)}, u32[]{:S(2)}, u32[]{:S(2)}) collective-permute-start(bf16[512,256]{1,0:T(8,128)(2,1)} %param.2), channel_id=1, source_target_pairs={{0,6},{1,7},{2,4},{3,5},{4,2},{5,3},{6,0},{7,1},{8,14},{9,15},{10,... | collective-permute-start | bytes 786440 | tf_op jit(solution)/shard_map/ppermute | solution.py:10
  5.0 10.0 %collective-permute-start.9 = (bf16[512,256]{1,0:T(8,128)(2,1)}, bf16[512,256]{1,0:T(8,128)(2,1)S(1)}, u32[]{:S(2)}, u32[]{:S(2)}) collective-permute-start(bf16[512,256]{1,0:T(8,128)(2,1)} %param.2), channel_id=1, source_target_pairs={{0,24},{8,16},{16,8},{24,0},{1,25},{9,17},{17,9},{25,1},{2,26},{10... | collective-permute-start | bytes 786440 | tf_op jit(solution)/shard_map/ppermute | solution.py:10
  10.9 9.6 %collective-permute-start.8 = (bf16[512,256]{1,0:T(8,128)(2,1)}, bf16[512,256]{1,0:T(8,128)(2,1)S(1)}, u32[]{:S(2)}, u32[]{:S(2)}) collective-permute-start(bf16[512,256]{1,0:T(8,128)(2,1)} %param.2), channel_id=1, source_target_pairs={{0,16},{8,24},{16,0},{24,8},{1,17},{9,25},{17,1},{25,9},{2,18},{10... | collective-permute-start | bytes 786440 | tf_op jit(solution)/shard_map/ppermute | solution.py:10
  14.9 13.2 %collective-permute-start.1 = (bf16[512,256]{1,0:T(8,128)(2,1)}, bf16[512,256]{1,0:T(8,128)(2,1)S(1)}, u32[]{:S(2)}, u32[]{:S(2)}) collective-permute-start(bf16[512,256]{1,0:T(8,128)(2,1)} %param.2), channel_id=1, source_target_pairs={{0,1},{1,0},{2,3},{3,2},{4,5},{5,4},{6,7},{7,6},{8,9},{9,8},{10,11... | collective-permute-start | bytes 786440 | tf_op jit(solution)/shard_map/ppermute | solution.py:10
  21.5 6.8 %copy-start.2 = (bf16[512,2048]{1,0:T(8,128)(2,1)S(1)}, bf16[512,2048]{1,0:T(8,128)(2,1)}, u32[]{:S(2)}) copy-start(bf16[512,2048]{1,0:T(8,128)(2,1)} %get-tuple-element.7) | copy-start | bytes 6291460
  21.5 7.2 %collective-permute-start.3 = (bf16[512,256]{1,0:T(8,128)(2,1)S(1)}, bf16[512,256]{1,0:T(8,128)(2,1)S(1)}, u32[]{:S(2)}, u32[]{:S(2)}) collective-permute-start(bf16[512,256]{1,0:T(8,128)(2,1)S(1)} %collective-permute-done.2), channel_id=1, source_target_pairs={{0,1},{1,0},{2,3},{3,2},{4,5},{5,4},{6,7},{7,6},{8,9},{9,8},{10,11... | collective-permute-start | bytes 786440 | tf_op jit(solution)/shard_map/ppermute | solution.py:10
  21.7 7.5 %collective-permute-start.5 = (bf16[512,256]{1,0:T(8,128)(2,1)S(1)}, bf16[512,256]{1,0:T(8,128)(2,1)S(1)}, u32[]{:S(2)}, u32[]{:S(2)}) collective-permute-start(bf16[512,256]{1,0:T(8,128)(2,1)S(1)} %collective-permute-done.4), channel_id=1, source_target_pairs={{0,1},{1,0},{2,3},{3,2},{4,5},{5,4},{6,7},{7,6},{8,9},{9,8},{10,11... | collective-permute-start | bytes 786440 | tf_op jit(solution)/shard_map/ppermute | solution.py:10
  27.6 2.3 %collective-permute-start.7 = (bf16[512,256]{1,0:T(8,128)(2,1)S(1)}, bf16[512,256]{1,0:T(8,128)(2,1)S(1)}, u32[]{:S(2)}, u32[]{:S(2)}) collective-permute-start(bf16[512,256]{1,0:T(8,128)(2,1)S(1)} %collective-permute-done.6), channel_id=1, source_target_pairs={{0,1},{1,0},{2,3},{3,2},{4,5},{5,4},{6,7},{7,6},{8,9},{9,8},{10,11... | collective-permute-start | bytes 786440 | tf_op jit(solution)/shard_map/ppermute | solution.py:10
  30.8 1.4 %copy-start = (f32[512,2,128]{2,1,0:T(2,128)}, f32[512,2,128]{2,1,0:T(2,128)S(1)}, u32[]{:S(2)}) copy-start(f32[512,2,128]{2,1,0:T(2,128)S(1)} %broadcast_in_dim.39) | copy-start | bytes 1572868
  32.2 13.6 %collective-permute-start.10 = (bf16[512,256]{1,0:T(8,128)(2,1)}, bf16[512,256]{1,0:T(8,128)(2,1)}, u32[]{:S(2)}, u32[]{:S(2)}) collective-permute-start(bf16[512,256]{1,0:T(8,128)(2,1)} %fusion.2), channel_id=1, source_target_pairs={{0,8},{8,0},{16,24},{24,16},{1,9},{9,1},{17,25},{25,17},{2,10},{10... | collective-permute-start | bytes 786440 | tf_op jit(solution)/shard_map/ppermute | solution.py:10
  32.7 13.4 %collective-permute-start.11 = (bf16[512,256]{1,0:T(8,128)(2,1)}, bf16[512,256]{1,0:T(8,128)(2,1)}, u32[]{:S(2)}, u32[]{:S(2)}) collective-permute-start(bf16[512,256]{1,0:T(8,128)(2,1)} %fusion.2), channel_id=1, source_target_pairs={{0,16},{8,24},{16,0},{24,8},{1,17},{9,25},{17,1},{25,9},{2,18},{10... | collective-permute-start | bytes 786440 | tf_op jit(solution)/shard_map/ppermute | solution.py:10
  34.2 13.6 %collective-permute-start.12 = (bf16[512,256]{1,0:T(8,128)(2,1)}, bf16[512,256]{1,0:T(8,128)(2,1)}, u32[]{:S(2)}, u32[]{:S(2)}) collective-permute-start(bf16[512,256]{1,0:T(8,128)(2,1)} %fusion.2), channel_id=1, source_target_pairs={{0,24},{8,16},{16,8},{24,0},{1,25},{9,17},{17,9},{25,1},{2,26},{10... | collective-permute-start | bytes 786440 | tf_op jit(solution)/shard_map/ppermute | solution.py:10
  43.3 4.5 %copy-start.1 = (f32[512,2,128]{2,1,0:T(2,128)S(1)}, f32[512,2,128]{2,1,0:T(2,128)}, u32[]{:S(2)}) copy-start(f32[512,2,128]{2,1,0:T(2,128)} %copy-done) | copy-start | bytes 1572868

commit v22 on v15

--- a/solution.py
+++ b/solution.py
@@ -49,20 +49,17 @@
             raw[2 * k + 1] = _swap(piece, "col", n_col, 1)
         row_pieces = [masked] + [mask_from(raw[t], row_index, col_index ^ t) for t in range(1, n_col)]
 
-        slots = jnp.arange(n_col, dtype=jnp.int32) ^ col_index
-        sub_index = ((slots // ratio) ^ row_index) * ratio + slots % ratio
-
-        def in_slot_order(pieces):
-            stacked = jnp.stack(pieces).reshape(n_row * ratio, cols, cols)
-            return jnp.take(stacked, sub_index, axis=0).reshape(n_col * cols, cols)
-
-        row_cat = jnp.concatenate(row_pieces, axis=1)
-        square = jnp.dot(row_cat, in_slot_order(col_pieces), preferred_element_type=jnp.float32)
+        shift = col_index ^ (row_index * ratio)
+        row_f = jnp.zeros((rows, n_col * cols), matrix_in.dtype)
+        for t, piece in enumerate(row_pieces):
+            row_f = lax.dynamic_update_slice_in_dim(row_f, piece, (t ^ shift) * cols, 1)
+        square = jnp.dot(
+            row_f, jnp.concatenate(col_pieces, axis=0), preferred_element_type=jnp.float32
+        )
         mask_float = local_mask.astype(jnp.float32)
         filtered = (mask_float * square).astype(jnp.bfloat16)
         f_pieces = [filtered] + [_swap(filtered, "row", n_row, k) for k in range(1, n_row)]
-        f_slot = in_slot_order(f_pieces)
-        cubic = jnp.dot(row_cat, f_slot, preferred_element_type=jnp.float32)
+        cubic = jnp.dot(row_f, jnp.concatenate(f_pieces, axis=0), preferred_element_type=jnp.float32)
         return mask_float * (1.5 * masked.astype(jnp.float32) - 0.5 * cubic)
 
     return body

time: 51.9 us -> 49.7 us (0.958)
  local copies, waits for them, and re-layouts: 6.03 us -> 3.64 us
  waiting for transfers between devices: 26.5 us -> 27.7 us
  matrix products: 3.17 us -> 2.24 us
  starting transfers between devices: 11 us -> 11.7 us
  other arithmetic: 4.51 us -> 3.89 us
    dynamic_update_slice x0 -> x8, other arithmetic: none -> 2.29 us  [body(): row_f = lax.dynamic_update_slice_in_dim(row_f, piece, (t ^ shift) * cols, 1)]
    another operation x3 -> x0, other arithmetic: 2.01 us -> none  [in_slot_order(): stacked = jnp.stack(pieces).reshape(n_row * ratio, cols, cols)]
    unnamed x6 -> x4, local copies, waits for them, and re-layouts: 1.42 us -> 0.01 us
    gather x2 -> x0, local copies, waits for them, and re-layouts: 1.23 us -> none  [in_slot_order(): return jnp.take(stacked, sub_index, axis=0).reshape(n_col * cols, cols)]
    ppermute x13, waiting for transfers between devices: 26.5 us -> 27.7 us  [_swap(): return lax.ppermute(x, axis, [(i, i ^ d) for i in range(size)])]
    dot_general x2, matrix products: 3.17 us -> 2.24 us  [the longest x1 1.52 us: body(): jnp.dot(row_f, jnp.concatenate(f_pieces, axis=0), preferred_element_type=...]
    ppermute x13, starting transfers between devices: 11 us -> 11.7 us  [_swap(): return lax.ppermute(x, axis, [(i, i ^ d) for i in range(size)])]
  transfers between devices with their start and end apart: 13 -> 13, of which waited for: 6 -> 6; matrix products, arithmetic and copies ran while one was open for 14% -> 13% of each run, Pallas kernels for 0% -> 0%
where the time goes in v22:
time: 49.7 us; the launch traced here: 49.4 us
  waiting for transfers between devices  27.7 us (56%)
  starting transfers between devices  11.7 us (24%)
  other arithmetic  3.89 us (8%)
  local copies, waits for them, and re-layouts  3.64 us (7%)
  matrix products  2.24 us (5%)
    ppermute x13, waiting for transfers between devices, _swap(): return lax.ppermute(x, axis, [(i, i ^ d) for i in range(size)])  27.7 us
    ppermute x13, starting transfers between devices, _swap(): return lax.ppermute(x, axis, [(i, i ^ d) for i in range(size)])  11.7 us
    dynamic_update_slice x8, other arithmetic, body(): row_f = lax.dynamic_update_slice_in_dim(row_f, piece, (t ^ shift) * cols, 1)  2.29 us
    mul x10, local copies, waits for them, and re-layouts, mask_from(): return (x4 * blocks[:, None, :, None]).reshape(rows, cols)  2.05 us
    dot_general x1, matrix products, body(): jnp.dot(row_f, jnp.concatenate(f_pieces, axis=0), preferred_element_type=...  1.52 us
    broadcast_in_dim x4, local copies, waits for them, and re-layouts, body(): local_mask = jnp.repeat(jnp.repeat(local_blocks, B, axis=0), B, axis=1)  1.24 us
  transfers between devices with their start and end apart: 13, of which 6 were waited for; matrix products, arithmetic and copies ran while one was open for 13% of the time, Pallas kernels for 0%

profile of v22, /device:TPU:16, one launch (start us, length us, event | category | flops | bytes accessed | tf_op | source)
XLA Modules:
  0.0 49.4 jit_solution(17840156247865508593)
XLA Ops:
  0.0 0.0 copy-start
  0.0 1.5 %collective-permute-start = (bf16[512,256]{1,0:T(8,128)(2,1)}, bf16[512,256]{1,0:T(8,128)(2,1)S(1)}, u32[]{:S(2)}, u32[]{:S(2)}) collective-permute-start(bf16[512,256]{1,0:T(8,128)(2,1)} %param.2), channel_id=1, source_target_pairs={{0,8},{8,0},{16,24},{24,16},{1,9},{9,1},{17,25},{25,17},{2,10},{10... | collective-permute-start | bytes 786440 | tf_op jit(solution)/shard_map/ppermute | solution.py:10
  1.5 1.6 %collective-permute-start.2 = (bf16[512,256]{1,0:T(8,128)(2,1)}, bf16[512,256]{1,0:T(8,128)(2,1)}, u32[]{:S(2)}, u32[]{:S(2)}) collective-permute-start(bf16[512,256]{1,0:T(8,128)(2,1)} %param.2), channel_id=1, source_target_pairs={{0,2},{1,3},{2,0},{3,1},{4,6},{5,7},{6,4},{7,5},{8,10},{9,11},{10,... | collective-permute-start | bytes 786440 | tf_op jit(solution)/shard_map/ppermute | solution.py:10
  3.1 0.3 collective-permute-start.4
  3.4 1.6 %collective-permute-start.6 = (bf16[512,256]{1,0:T(8,128)(2,1)}, bf16[512,256]{1,0:T(8,128)(2,1)S(1)}, u32[]{:S(2)}, u32[]{:S(2)}) collective-permute-start(bf16[512,256]{1,0:T(8,128)(2,1)} %param.2), channel_id=1, source_target_pairs={{0,6},{1,7},{2,4},{3,5},{4,2},{5,3},{6,0},{7,1},{8,14},{9,15},{10,... | collective-permute-start | bytes 786440 | tf_op jit(solution)/shard_map/ppermute | solution.py:10
  5.0 1.5 %collective-permute-start.9 = (bf16[512,256]{1,0:T(8,128)(2,1)}, bf16[512,256]{1,0:T(8,128)(2,1)S(1)}, u32[]{:S(2)}, u32[]{:S(2)}) collective-permute-start(bf16[512,256]{1,0:T(8,128)(2,1)} %param.2), channel_id=1, source_target_pairs={{0,24},{8,16},{16,8},{24,0},{1,25},{9,17},{17,9},{25,1},{2,26},{10... | collective-permute-start | bytes 786440 | tf_op jit(solution)/shard_map/ppermute | solution.py:10
  6.5 0.7 %convert_element_type.38 = bf16[16,16]{1,0:T(8,128)(2,1)S(1)} convert(s32[16,16]{1,0:T(8,128)} %param.3) | non-fusion elementwise | flops 256 | bytes 1536 | tf_op jit(solution)/shard_map/convert_element_type | solution.py:28
  7.2 0.8 %dynamic-slice_convert_fusion.1 = (f32[4,2]{1,0:T(4,128)S(1)}, bf16[4,2]{1,0:T(4,128)(2,1)S(1)}) fusion(s32[16,16]{1,0:T(8,128)} %param.3, s32[]{:T(128)S(6)} %select_n.70, s32[]{:T(128)S(6)} %select_n.71), kind=kLoop, calls=%fused_computation.39 | loop fusion | flops 16 | bytes 88 | tf_op jit(solution)/shard_map/convert_element_type | solution.py:59
  8.0 0.6 %broadcast_in_dim.26 = bf16[512,2,128]{2,1,0:T(2,128)(2,1)S(1)} broadcast(bf16[512,2]{1,0:T(8,128)(2,1)S(1)} %bitcast.78), dimensions={0,1} | broadcast | bytes 264192 | tf_op jit(solution)/shard_map/broadcast_in_dim | solution.py:26
  8.6 0.2 broadcast_in_dim.27
  8.8 0.0 copy-done
  8.8 0.8 %constant_dynamic-update-slice_fusion = (bf16[512,2048]{1,0:T(8,128)(2,1)S(1)}, bf16[512,256]{1,0:T(8,128)(2,1)}) fusion(bf16[512,2048]{1,0:T(8,128)(2,1)S(1)} %broadcast_in_dim.27, s32[]{:T(128)S(6)} %select_n.72, bf16[512,256]{1,0:T(8,128)(2,1)S(1)} %copy-done, bf16[64,8,2,128]{3,2,1,0:T(2,128)(2,1)S(1)} %bitcast.70), kind=kLoop, calls=%fused_computation.37 | loop fusion | flops 524288 | bytes 1048580 | tf_op jit(solution)/shard_map/dynamic_update_slice | solution.py:55
  9.6 0.1 fusion.26
  9.8 0.0 collective-permute-done
  9.8 1.1 %collective-permute-start.8 = (bf16[512,256]{1,0:T(8,128)(2,1)S(1)}, bf16[512,256]{1,0:T(8,128)(2,1)S(1)}, u32[]{:S(2)}, u32[]{:S(2)}) collective-permute-start(bf16[512,256]{1,0:T(8,128)(2,1)S(1)} %copy-done), channel_id=1, source_target_pairs={{0,16},{8,24},{16,0},{24,8},{1,17},{9,25},{17,1},{25,9},{2,18},{10... | collective-permute-start | bytes 786440 | tf_op jit(solution)/shard_map/ppermute | solution.py:10
  10.9 0.2 mul.247
  11.1 0.1 bitcast_multiply_fusion.2
  11.2 1.7 %collective-permute-done.2 = bf16[512,256]{1,0:T(8,128)(2,1)} collective-permute-done((bf16[512,256]{1,0:T(8,128)(2,1)}, bf16[512,256]{1,0:T(8,128)(2,1)}, u32[]{:S(2)}, u32[]{:S(2)}) %collective-permute-start.2) | collective-permute-done | bytes 262176 | tf_op jit(solution)/shard_map/ppermute | solution.py:10
  12.9 0.0 collective-permute-start.1
  12.9 8.8 %collective-permute-done.4 = bf16[512,256]{1,0:T(8,128)(2,1)S(1)} collective-permute-done((bf16[512,256]{1,0:T(8,128)(2,1)}, bf16[512,256]{1,0:T(8,128)(2,1)S(1)}, u32[]{:S(2)}, u32[]{:S(2)}) %collective-permute-start.4) | collective-permute-done | bytes 262176 | tf_op jit(solution)/shard_map/ppermute | solution.py:10
  21.7 0.0 collective-permute-start.3
  21.7 5.8 %collective-permute-done.6 = bf16[512,256]{1,0:T(8,128)(2,1)S(1)} collective-permute-done((bf16[512,256]{1,0:T(8,128)(2,1)}, bf16[512,256]{1,0:T(8,128)(2,1)S(1)}, u32[]{:S(2)}, u32[]{:S(2)}) %collective-permute-start.6) | collective-permute-done | bytes 262176 | tf_op jit(solution)/shard_map/ppermute | solution.py:10
  27.6 0.0 collective-permute-start.5
  27.6 0.0 collective-permute-done.9
  27.6 0.5 %collective-permute-start.7 = (bf16[512,256]{1,0:T(8,128)(2,1)S(1)}, bf16[512,256]{1,0:T(8,128)(2,1)S(1)}, u32[]{:S(2)}, u32[]{:S(2)}) collective-permute-start(bf16[512,256]{1,0:T(8,128)(2,1)S(1)} %collective-permute-done.6), channel_id=1, source_target_pairs={{0,1},{1,0},{2,3},{3,2},{4,5},{5,4},{6,7},{7,6},{8,9},{9,8},{10,11... | collective-permute-start | bytes 786440 | tf_op jit(solution)/shard_map/ppermute | solution.py:10
  28.1 0.2 mul.255
  28.3 0.1 bitcast_multiply_fusion
  28.3 0.0 collective-permute-done.8
  28.3 0.2 mul.251
  28.6 0.0 collective-permute-done.1
  28.6 0.2 mul.212
  28.8 0.1 fusion.23
  28.9 0.2 mul.217
  29.1 1.0 %fusion.22 = bf16[512,2048]{1,0:T(8,128)(2,1)S(1)} fusion(bf16[512,2048]{1,0:T(8,128)(2,1)S(1)} %fusion.23, s32[]{:T(128)S(6)} %select_n.76, bf16[512,256]{1,0:T(8,128)(2,1)} %collective-permute-done.2, bf16[64,8,2,128]{3,2,1,0:T(2,128)(2,1)S(1)} %bitcast.75), kind=kLoop, calls=%fused_computation.33 | loop fusion | flops 524288 | bytes 786436 | tf_op jit(solution)/shard_map/dynamic_update_slice | solution.py:55
  30.1 0.0 collective-permute-done.3
  30.2 0.2 mul.222
  30.4 0.1 fusion.21
  30.4 0.2 mul.227
  30.7 0.1 fusion.20
  30.7 0.0 collective-permute-done.5
  30.8 0.0 copy-start.1
  30.8 0.2 mul.232
  31.0 0.1 fusion.19
  31.1 0.2 mul.237
  31.3 0.1 fusion.18
  31.4 0.0 collective-permute-done.7
  31.4 0.2 mul.242
  31.6 0.1 fusion.17
  31.7 0.6 %broadcast_in_dim.11 = f32[512,2,128]{2,1,0:T(2,128)S(1)} broadcast(f32[512,2]{1,0:T(8,128)S(1)} %bitcast.69), dimensions={0,1} | broadcast | bytes 528384 | tf_op jit(solution)/shard_map/broadcast_in_dim | solution.py:26
  32.3 0.0 copy-done.1
  32.3 0.7 %fusion.2 = bf16[512,256]{1,0:T(8,128)(2,1)S(1)} fusion(bf16[512,2048]{1,0:T(8,128)(2,1)S(1)} %fusion.17, bf16[512,256]{1,0:T(8,128)(2,1)S(1)} %bitcast_multiply_fusion, bf16[512,256]{1,0:T(8,128)(2,1)S(1)} %bitcast_multiply_fusion.1, bf16[512,256]{1,0:T(8,128)(2,1)S(1)} %bitcast_multiply_fusion.2, bf16[512,256]{1,0:T(8,128)(2,1)S(1)} %copy-done.1, ...), kind=kOutput, calls=%fused_computation.4 | convolution fusion | flops 541327360 | bytes 3932160 | tf_op jit(solution)/shard_map/dot_general | solution.py:56
  33.0 0.6 %collective-permute-start.10 = (bf16[512,256]{1,0:T(8,128)(2,1)S(1)}, bf16[512,256]{1,0:T(8,128)(2,1)S(1)}, u32[]{:S(2)}, u32[]{:S(2)}) collective-permute-start(bf16[512,256]{1,0:T(8,128)(2,1)S(1)} %fusion.2), channel_id=1, source_target_pairs={{0,8},{8,0},{16,24},{24,16},{1,9},{9,1},{17,25},{25,17},{2,10},{10... | collective-permute-start | bytes 786440 | tf_op jit(solution)/shard_map/ppermute | solution.py:10
  33.6 1.5 %collective-permute-start.11 = (bf16[512,256]{1,0:T(8,128)(2,1)S(1)}, bf16[512,256]{1,0:T(8,128)(2,1)S(1)}, u32[]{:S(2)}, u32[]{:S(2)}) collective-permute-start(bf16[512,256]{1,0:T(8,128)(2,1)S(1)} %fusion.2), channel_id=1, source_target_pairs={{0,16},{8,24},{16,0},{24,8},{1,17},{9,25},{17,1},{25,9},{2,18},{10... | collective-permute-start | bytes 786440 | tf_op jit(solution)/shard_map/ppermute | solution.py:10
  35.1 1.4 %collective-permute-start.12 = (bf16[512,256]{1,0:T(8,128)(2,1)S(1)}, bf16[512,256]{1,0:T(8,128)(2,1)S(1)}, u32[]{:S(2)}, u32[]{:S(2)}) collective-permute-start(bf16[512,256]{1,0:T(8,128)(2,1)S(1)} %fusion.2), channel_id=1, source_target_pairs={{0,24},{8,16},{16,8},{24,0},{1,25},{9,17},{17,9},{25,1},{2,26},{10... | collective-permute-start | bytes 786440 | tf_op jit(solution)/shard_map/ppermute | solution.py:10
  36.6 5.7 %collective-permute-done.10 = bf16[512,256]{1,0:T(8,128)(2,1)S(1)} collective-permute-done((bf16[512,256]{1,0:T(8,128)(2,1)S(1)}, bf16[512,256]{1,0:T(8,128)(2,1)S(1)}, u32[]{:S(2)}, u32[]{:S(2)}) %collective-permute-start.10) | collective-permute-done | bytes 262176 | tf_op jit(solution)/shard_map/ppermute | solution.py:10
  42.3 4.0 %collective-permute-done.11 = bf16[512,256]{1,0:T(8,128)(2,1)S(1)} collective-permute-done((bf16[512,256]{1,0:T(8,128)(2,1)S(1)}, bf16[512,256]{1,0:T(8,128)(2,1)S(1)}, u32[]{:S(2)}, u32[]{:S(2)}) %collective-permute-start.11) | collective-permute-done | bytes 262176 | tf_op jit(solution)/shard_map/ppermute | solution.py:10
  46.3 1.6 %collective-permute-done.12 = bf16[512,256]{1,0:T(8,128)(2,1)S(1)} collective-permute-done((bf16[512,256]{1,0:T(8,128)(2,1)S(1)}, bf16[512,256]{1,0:T(8,128)(2,1)S(1)}, u32[]{:S(2)}, u32[]{:S(2)}) %collective-permute-start.12) | collective-permute-done | bytes 262176 | tf_op jit(solution)/shard_map/ppermute | solution.py:10
  47.9 1.5 %fusion.1 = f32[512,256]{1,0:T(8,128)} fusion(bf16[512,2048]{1,0:T(8,128)(2,1)S(1)} %fusion.17, bf16[512,256]{1,0:T(8,128)(2,1)S(1)} %collective-permute-done.12, bf16[512,256]{1,0:T(8,128)(2,1)S(1)} %collective-permute-done.11, bf16[512,256]{1,0:T(8,128)(2,1)S(1)} %collective-permute-done.10, bf16[512,256]{1,0:T(8,128)(2,1)S(1)} %fusion.2, ...), kind=kOutput, calls=%fused_computation.3 | convolution fusion | flops 541720576 | bytes 4456448 | tf_op jit(solution)/shard_map/dot_general | solution.py:62
  (3 shorter events, 0.1 us)
Async XLA Ops:
  0.0 8.8 %copy-start = (bf16[512,256]{1,0:T(8,128)(2,1)S(1)}, bf16[512,256]{1,0:T(8,128)(2,1)}, u32[]{:S(2)}) copy-start(bf16[512,256]{1,0:T(8,128)(2,1)} %param.2) | copy-start | bytes 786436
  0.0 9.8 %collective-permute-start = (bf16[512,256]{1,0:T(8,128)(2,1)}, bf16[512,256]{1,0:T(8,128)(2,1)S(1)}, u32[]{:S(2)}, u32[]{:S(2)}) collective-permute-start(bf16[512,256]{1,0:T(8,128)(2,1)} %param.2), channel_id=1, source_target_pairs={{0,8},{8,0},{16,24},{24,16},{1,9},{9,1},{17,25},{25,17},{2,10},{10... | collective-permute-start | bytes 786440 | tf_op jit(solution)/shard_map/ppermute | solution.py:10
  1.5 11.4 %collective-permute-start.2 = (bf16[512,256]{1,0:T(8,128)(2,1)}, bf16[512,256]{1,0:T(8,128)(2,1)}, u32[]{:S(2)}, u32[]{:S(2)}) collective-permute-start(bf16[512,256]{1,0:T(8,128)(2,1)} %param.2), channel_id=1, source_target_pairs={{0,2},{1,3},{2,0},{3,1},{4,6},{5,7},{6,4},{7,5},{8,10},{9,11},{10,... | collective-permute-start | bytes 786440 | tf_op jit(solution)/shard_map/ppermute | solution.py:10
  3.1 18.7 %collective-permute-start.4 = (bf16[512,256]{1,0:T(8,128)(2,1)}, bf16[512,256]{1,0:T(8,128)(2,1)S(1)}, u32[]{:S(2)}, u32[]{:S(2)}) collective-permute-start(bf16[512,256]{1,0:T(8,128)(2,1)} %param.2), channel_id=1, source_target_pairs={{0,4},{1,5},{2,6},{3,7},{4,0},{5,1},{6,2},{7,3},{8,12},{9,13},{10,... | collective-permute-start | bytes 786440 | tf_op jit(solution)/shard_map/ppermute | solution.py:10
  3.4 24.1 %collective-permute-start.6 = (bf16[512,256]{1,0:T(8,128)(2,1)}, bf16[512,256]{1,0:T(8,128)(2,1)S(1)}, u32[]{:S(2)}, u32[]{:S(2)}) collective-permute-start(bf16[512,256]{1,0:T(8,128)(2,1)} %param.2), channel_id=1, source_target_pairs={{0,6},{1,7},{2,4},{3,5},{4,2},{5,3},{6,0},{7,1},{8,14},{9,15},{10,... | collective-permute-start | bytes 786440 | tf_op jit(solution)/shard_map/ppermute | solution.py:10
  5.0 22.6 %collective-permute-start.9 = (bf16[512,256]{1,0:T(8,128)(2,1)}, bf16[512,256]{1,0:T(8,128)(2,1)S(1)}, u32[]{:S(2)}, u32[]{:S(2)}) collective-permute-start(bf16[512,256]{1,0:T(8,128)(2,1)} %param.2), channel_id=1, source_target_pairs={{0,24},{8,16},{16,8},{24,0},{1,25},{9,17},{17,9},{25,1},{2,26},{10... | collective-permute-start | bytes 786440 | tf_op jit(solution)/shard_map/ppermute | solution.py:10
  9.8 18.6 %collective-permute-start.8 = (bf16[512,256]{1,0:T(8,128)(2,1)S(1)}, bf16[512,256]{1,0:T(8,128)(2,1)S(1)}, u32[]{:S(2)}, u32[]{:S(2)}) collective-permute-start(bf16[512,256]{1,0:T(8,128)(2,1)S(1)} %copy-done), channel_id=1, source_target_pairs={{0,16},{8,24},{16,0},{24,8},{1,17},{9,25},{17,1},{25,9},{2,18},{10... | collective-permute-start | bytes 786440 | tf_op jit(solution)/shard_map/ppermute | solution.py:10
  12.9 15.7 %collective-permute-start.1 = (bf16[512,256]{1,0:T(8,128)(2,1)S(1)}, bf16[512,256]{1,0:T(8,128)(2,1)S(1)}, u32[]{:S(2)}, u32[]{:S(2)}) collective-permute-start(bf16[512,256]{1,0:T(8,128)(2,1)S(1)} %copy-done), channel_id=1, source_target_pairs={{0,1},{1,0},{2,3},{3,2},{4,5},{5,4},{6,7},{7,6},{8,9},{9,8},{10,11... | collective-permute-start | bytes 786440 | tf_op jit(solution)/shard_map/ppermute | solution.py:10
  21.7 8.4 %collective-permute-start.3 = (bf16[512,256]{1,0:T(8,128)(2,1)}, bf16[512,256]{1,0:T(8,128)(2,1)S(1)}, u32[]{:S(2)}, u32[]{:S(2)}) collective-permute-start(bf16[512,256]{1,0:T(8,128)(2,1)} %collective-permute-done.2), channel_id=1, source_target_pairs={{0,1},{1,0},{2,3},{3,2},{4,5},{5,4},{6,7},{7,6},{8,9},{9,8},{10,11... | collective-permute-start | bytes 786440 | tf_op jit(solution)/shard_map/ppermute | solution.py:10
  27.6 3.2 %collective-permute-start.5 = (bf16[512,256]{1,0:T(8,128)(2,1)S(1)}, bf16[512,256]{1,0:T(8,128)(2,1)S(1)}, u32[]{:S(2)}, u32[]{:S(2)}) collective-permute-start(bf16[512,256]{1,0:T(8,128)(2,1)S(1)} %collective-permute-done.4), channel_id=1, source_target_pairs={{0,1},{1,0},{2,3},{3,2},{4,5},{5,4},{6,7},{7,6},{8,9},{9,8},{10,11... | collective-permute-start | bytes 786440 | tf_op jit(solution)/shard_map/ppermute | solution.py:10
  27.6 3.8 %collective-permute-start.7 = (bf16[512,256]{1,0:T(8,128)(2,1)S(1)}, bf16[512,256]{1,0:T(8,128)(2,1)S(1)}, u32[]{:S(2)}, u32[]{:S(2)}) collective-permute-start(bf16[512,256]{1,0:T(8,128)(2,1)S(1)} %collective-permute-done.6), channel_id=1, source_target_pairs={{0,1},{1,0},{2,3},{3,2},{4,5},{5,4},{6,7},{7,6},{8,9},{9,8},{10,11... | collective-permute-start | bytes 786440 | tf_op jit(solution)/shard_map/ppermute | solution.py:10
  30.8 1.5 %copy-start.1 = (bf16[512,256]{1,0:T(8,128)(2,1)S(1)}, bf16[512,256]{1,0:T(8,128)(2,1)}, u32[]{:S(2)}) copy-start(bf16[512,256]{1,0:T(8,128)(2,1)} %get-tuple-element.8) | copy-start | bytes 786436
  33.0 9.2 %collective-permute-start.10 = (bf16[512,256]{1,0:T(8,128)(2,1)S(1)}, bf16[512,256]{1,0:T(8,128)(2,1)S(1)}, u32[]{:S(2)}, u32[]{:S(2)}) collective-permute-start(bf16[512,256]{1,0:T(8,128)(2,1)S(1)} %fusion.2), channel_id=1, source_target_pairs={{0,8},{8,0},{16,24},{24,16},{1,9},{9,1},{17,25},{25,17},{2,10},{10... | collective-permute-start | bytes 786440 | tf_op jit(solution)/shard_map/ppermute | solution.py:10
  33.6 12.6 %collective-permute-start.11 = (bf16[512,256]{1,0:T(8,128)(2,1)S(1)}, bf16[512,256]{1,0:T(8,128)(2,1)S(1)}, u32[]{:S(2)}, u32[]{:S(2)}) collective-permute-start(bf16[512,256]{1,0:T(8,128)(2,1)S(1)} %fusion.2), channel_id=1, source_target_pairs={{0,16},{8,24},{16,0},{24,8},{1,17},{9,25},{17,1},{25,9},{2,18},{10... | collective-permute-start | bytes 786440 | tf_op jit(solution)/shard_map/ppermute | solution.py:10
  35.1 12.7 %collective-permute-start.12 = (bf16[512,256]{1,0:T(8,128)(2,1)S(1)}, bf16[512,256]{1,0:T(8,128)(2,1)S(1)}, u32[]{:S(2)}, u32[]{:S(2)}) collective-permute-start(bf16[512,256]{1,0:T(8,128)(2,1)S(1)} %fusion.2), channel_id=1, source_target_pairs={{0,24},{8,16},{16,8},{24,0},{1,25},{9,17},{17,9},{25,1},{2,26},{10... | collective-permute-start | bytes 786440 | tf_op jit(solution)/shard_map/ppermute | solution.py:10

commit v23 on v22

--- a/solution.py
+++ b/solution.py
@@ -56,11 +56,15 @@
         square = jnp.dot(
             row_f, jnp.concatenate(col_pieces, axis=0), preferred_element_type=jnp.float32
         )
-        mask_float = local_mask.astype(jnp.float32)
-        filtered = (mask_float * square).astype(jnp.bfloat16)
+        blocks_float = local_blocks.astype(jnp.float32)[:, None, :, None]
+
+        def mask_local(x):
+            return (x.reshape(block_rows, B, block_cols, B) * blocks_float).reshape(rows, cols)
+
+        filtered = mask_local(square).astype(jnp.bfloat16)
         f_pieces = [filtered] + [_swap(filtered, "row", n_row, k) for k in range(1, n_row)]
         cubic = jnp.dot(row_f, jnp.concatenate(f_pieces, axis=0), preferred_element_type=jnp.float32)
-        return mask_float * (1.5 * masked.astype(jnp.float32) - 0.5 * cubic)
+        return mask_local(1.5 * masked.astype(jnp.float32) - 0.5 * cubic)
 
     return body
 

time: 49.7 us -> 49.3 us (level)
    broadcast_in_dim x4 -> x2, local copies, waits for them, and re-layouts: 1.24 us -> 0.62 us  [body(): local_mask = jnp.repeat(jnp.repeat(local_blocks, B, axis=0), B, axis=1)]
  transfers between devices with their start and end apart: 13 -> 13, of which waited for: 6 -> 6; matrix products, arithmetic and copies ran while one was open for 13% -> 14% of each run, Pallas kernels for 0% -> 0%
where the time goes in v23:
time: 49.3 us; the launch traced here: 49 us
  waiting for transfers between devices  27.7 us (56%)
  starting transfers between devices  11.7 us (24%)
  other arithmetic  3.89 us (8%)
  local copies, waits for them, and re-layouts  3.22 us (7%)
  matrix products  2.24 us (5%)
    ppermute x13, waiting for transfers between devices, _swap(): return lax.ppermute(x, axis, [(i, i ^ d) for i in range(size)])  27.7 us
    ppermute x13, starting transfers between devices, _swap(): return lax.ppermute(x, axis, [(i, i ^ d) for i in range(size)])  11.7 us
    dynamic_update_slice x8, other arithmetic, body(): row_f = lax.dynamic_update_slice_in_dim(row_f, piece, (t ^ shift) * cols, 1)  2.29 us
    mul x10, local copies, waits for them, and re-layouts, mask_from(): return (x4 * blocks[:, None, :, None]).reshape(rows, cols)  2.05 us
    dot_general x1, matrix products, body(): jnp.dot(row_f, jnp.concatenate(f_pieces, axis=0), preferred_element_type=...  1.52 us
  transfers between devices with their start and end apart: 13, of which 6 were waited for; matrix products, arithmetic and copies ran while one was open for 14% of the time, Pallas kernels for 0%

profile of v23, /device:TPU:16, one launch (start us, length us, event | category | flops | bytes accessed | tf_op | source)
XLA Modules:
  0.0 49.0 jit_solution(5906506212455668376)
XLA Ops:
  0.0 0.0 copy-start
  0.0 1.5 %collective-permute-start = (bf16[512,256]{1,0:T(8,128)(2,1)}, bf16[512,256]{1,0:T(8,128)(2,1)S(1)}, u32[]{:S(2)}, u32[]{:S(2)}) collective-permute-start(bf16[512,256]{1,0:T(8,128)(2,1)} %param.2), channel_id=1, source_target_pairs={{0,8},{8,0},{16,24},{24,16},{1,9},{9,1},{17,25},{25,17},{2,10},{10... | collective-permute-start | bytes 786440 | tf_op jit(solution)/shard_map/ppermute | solution.py:10
  1.5 1.6 %collective-permute-start.2 = (bf16[512,256]{1,0:T(8,128)(2,1)}, bf16[512,256]{1,0:T(8,128)(2,1)}, u32[]{:S(2)}, u32[]{:S(2)}) collective-permute-start(bf16[512,256]{1,0:T(8,128)(2,1)} %param.2), channel_id=1, source_target_pairs={{0,2},{1,3},{2,0},{3,1},{4,6},{5,7},{6,4},{7,5},{8,10},{9,11},{10,... | collective-permute-start | bytes 786440 | tf_op jit(solution)/shard_map/ppermute | solution.py:10
  3.1 0.3 collective-permute-start.4
  3.4 1.6 %collective-permute-start.6 = (bf16[512,256]{1,0:T(8,128)(2,1)}, bf16[512,256]{1,0:T(8,128)(2,1)S(1)}, u32[]{:S(2)}, u32[]{:S(2)}) collective-permute-start(bf16[512,256]{1,0:T(8,128)(2,1)} %param.2), channel_id=1, source_target_pairs={{0,6},{1,7},{2,4},{3,5},{4,2},{5,3},{6,0},{7,1},{8,14},{9,15},{10,... | collective-permute-start | bytes 786440 | tf_op jit(solution)/shard_map/ppermute | solution.py:10
  5.0 1.5 %collective-permute-start.9 = (bf16[512,256]{1,0:T(8,128)(2,1)}, bf16[512,256]{1,0:T(8,128)(2,1)S(1)}, u32[]{:S(2)}, u32[]{:S(2)}) collective-permute-start(bf16[512,256]{1,0:T(8,128)(2,1)} %param.2), channel_id=1, source_target_pairs={{0,24},{8,16},{16,8},{24,0},{1,25},{9,17},{17,9},{25,1},{2,26},{10... | collective-permute-start | bytes 786440 | tf_op jit(solution)/shard_map/ppermute | solution.py:10
  6.5 0.7 %convert_element_type.27 = bf16[16,16]{1,0:T(8,128)(2,1)S(1)} convert(s32[16,16]{1,0:T(8,128)} %param.3) | non-fusion elementwise | flops 256 | bytes 1536 | tf_op jit(solution)/shard_map/convert_element_type | solution.py:28
  7.2 0.8 %dynamic-slice_convert_fusion = (f32[4,2]{1,0:T(4,128)S(1)}, bf16[4,2]{1,0:T(4,128)(2,1)S(1)}) fusion(s32[16,16]{1,0:T(8,128)} %param.3, s32[]{:T(128)S(6)} %select_n.70, s32[]{:T(128)S(6)} %select_n.71), kind=kLoop, calls=%fused_computation.38 | loop fusion | flops 16 | bytes 88 | tf_op jit(solution)/shard_map/convert_element_type | solution.py:59
  8.0 0.6 %broadcast_in_dim.7 = bf16[512,2,128]{2,1,0:T(2,128)(2,1)S(1)} broadcast(bf16[512,2]{1,0:T(8,128)(2,1)S(1)} %bitcast.77), dimensions={0,1} | broadcast | bytes 264192 | tf_op jit(solution)/shard_map/broadcast_in_dim | solution.py:26
  8.6 0.2 broadcast_in_dim.8
  8.8 0.0 copy-done
  8.8 0.8 %constant_dynamic-update-slice_fusion = (bf16[512,2048]{1,0:T(8,128)(2,1)S(1)}, bf16[512,256]{1,0:T(8,128)(2,1)}) fusion(bf16[512,2048]{1,0:T(8,128)(2,1)S(1)} %broadcast_in_dim.8, s32[]{:T(128)S(6)} %select_n.72, bf16[512,256]{1,0:T(8,128)(2,1)S(1)} %copy-done, bf16[64,8,2,128]{3,2,1,0:T(2,128)(2,1)S(1)} %bitcast.69), kind=kLoop, calls=%fused_computation.37 | loop fusion | flops 524288 | bytes 1048580 | tf_op jit(solution)/shard_map/dynamic_update_slice | solution.py:55
  9.6 0.1 fusion.26
  9.8 0.0 collective-permute-done
  9.8 1.1 %collective-permute-start.8 = (bf16[512,256]{1,0:T(8,128)(2,1)S(1)}, bf16[512,256]{1,0:T(8,128)(2,1)S(1)}, u32[]{:S(2)}, u32[]{:S(2)}) collective-permute-start(bf16[512,256]{1,0:T(8,128)(2,1)S(1)} %copy-done), channel_id=1, source_target_pairs={{0,16},{8,24},{16,0},{24,8},{1,17},{9,25},{17,1},{25,9},{2,18},{10... | collective-permute-start | bytes 786440 | tf_op jit(solution)/shard_map/ppermute | solution.py:10
  10.9 0.2 mul.259
  11.1 0.1 bitcast_multiply_fusion.2
  11.2 1.7 %collective-permute-done.2 = bf16[512,256]{1,0:T(8,128)(2,1)} collective-permute-done((bf16[512,256]{1,0:T(8,128)(2,1)}, bf16[512,256]{1,0:T(8,128)(2,1)}, u32[]{:S(2)}, u32[]{:S(2)}) %collective-permute-start.2) | collective-permute-done | bytes 262176 | tf_op jit(solution)/shard_map/ppermute | solution.py:10
  12.9 0.0 collective-permute-start.1
  12.9 8.8 %collective-permute-done.4 = bf16[512,256]{1,0:T(8,128)(2,1)S(1)} collective-permute-done((bf16[512,256]{1,0:T(8,128)(2,1)}, bf16[512,256]{1,0:T(8,128)(2,1)S(1)}, u32[]{:S(2)}, u32[]{:S(2)}) %collective-permute-start.4) | collective-permute-done | bytes 262176 | tf_op jit(solution)/shard_map/ppermute | solution.py:10
  21.7 0.0 collective-permute-start.3
  21.7 5.8 %collective-permute-done.6 = bf16[512,256]{1,0:T(8,128)(2,1)S(1)} collective-permute-done((bf16[512,256]{1,0:T(8,128)(2,1)}, bf16[512,256]{1,0:T(8,128)(2,1)S(1)}, u32[]{:S(2)}, u32[]{:S(2)}) %collective-permute-start.6) | collective-permute-done | bytes 262176 | tf_op jit(solution)/shard_map/ppermute | solution.py:10
  27.6 0.0 collective-permute-start.5
  27.6 0.0 collective-permute-done.9
  27.6 0.5 %collective-permute-start.7 = (bf16[512,256]{1,0:T(8,128)(2,1)S(1)}, bf16[512,256]{1,0:T(8,128)(2,1)S(1)}, u32[]{:S(2)}, u32[]{:S(2)}) collective-permute-start(bf16[512,256]{1,0:T(8,128)(2,1)S(1)} %collective-permute-done.6), channel_id=1, source_target_pairs={{0,1},{1,0},{2,3},{3,2},{4,5},{5,4},{6,7},{7,6},{8,9},{9,8},{10,11... | collective-permute-start | bytes 786440 | tf_op jit(solution)/shard_map/ppermute | solution.py:10
  28.1 0.2 mul.267
  28.3 0.1 bitcast_multiply_fusion
  28.3 0.0 collective-permute-done.8
  28.3 0.2 mul.263
  28.6 0.0 collective-permute-done.1
  28.6 0.2 mul.224
  28.8 0.1 fusion.23
  28.9 0.2 mul.229
  29.1 1.0 %fusion.22 = bf16[512,2048]{1,0:T(8,128)(2,1)S(1)} fusion(bf16[512,2048]{1,0:T(8,128)(2,1)S(1)} %fusion.23, s32[]{:T(128)S(6)} %select_n.76, bf16[512,256]{1,0:T(8,128)(2,1)} %collective-permute-done.2, bf16[64,8,2,128]{3,2,1,0:T(2,128)(2,1)S(1)} %bitcast.74), kind=kLoop, calls=%fused_computation.33 | loop fusion | flops 524288 | bytes 786436 | tf_op jit(solution)/shard_map/dynamic_update_slice | solution.py:55
  30.1 0.0 collective-permute-done.3
  30.2 0.2 mul.234
  30.4 0.1 fusion.21
  30.4 0.2 mul.239
  30.7 0.0 copy-start.1
  30.7 0.1 fusion.20
  30.8 0.0 collective-permute-done.5
  30.8 0.2 mul.244
  31.0 0.1 fusion.19
  31.1 0.2 mul.249
  31.3 0.1 fusion.18
  31.4 0.0 collective-permute-done.7
  31.4 0.2 mul.254
  31.6 0.1 fusion.17
  31.7 0.2 mul.270
  31.9 0.0 copy-done.1
  31.9 0.7 %fusion.2 = bf16[512,256]{1,0:T(8,128)(2,1)S(1)} fusion(bf16[512,2048]{1,0:T(8,128)(2,1)S(1)} %fusion.17, bf16[512,256]{1,0:T(8,128)(2,1)S(1)} %bitcast_multiply_fusion, bf16[512,256]{1,0:T(8,128)(2,1)S(1)} %bitcast_multiply_fusion.1, bf16[512,256]{1,0:T(8,128)(2,1)S(1)} %bitcast_multiply_fusion.2, bf16[512,256]{1,0:T(8,128)(2,1)S(1)} %copy-done.1, ...), kind=kOutput, calls=%fused_computation.4 | convolution fusion | flops 541327360 | bytes 3932160 | tf_op jit(solution)/shard_map/dot_general | solution.py:56
  32.6 0.6 %collective-permute-start.10 = (bf16[512,256]{1,0:T(8,128)(2,1)S(1)}, bf16[512,256]{1,0:T(8,128)(2,1)S(1)}, u32[]{:S(2)}, u32[]{:S(2)}) collective-permute-start(bf16[512,256]{1,0:T(8,128)(2,1)S(1)} %fusion.2), channel_id=1, source_target_pairs={{0,8},{8,0},{16,24},{24,16},{1,9},{9,1},{17,25},{25,17},{2,10},{10... | collective-permute-start | bytes 786440 | tf_op jit(solution)/shard_map/ppermute | solution.py:10
  33.2 1.5 %collective-permute-start.11 = (bf16[512,256]{1,0:T(8,128)(2,1)S(1)}, bf16[512,256]{1,0:T(8,128)(2,1)S(1)}, u32[]{:S(2)}, u32[]{:S(2)}) collective-permute-start(bf16[512,256]{1,0:T(8,128)(2,1)S(1)} %fusion.2), channel_id=1, source_target_pairs={{0,16},{8,24},{16,0},{24,8},{1,17},{9,25},{17,1},{25,9},{2,18},{10... | collective-permute-start | bytes 786440 | tf_op jit(solution)/shard_map/ppermute | solution.py:10
  34.7 1.4 %collective-permute-start.12 = (bf16[512,256]{1,0:T(8,128)(2,1)S(1)}, bf16[512,256]{1,0:T(8,128)(2,1)S(1)}, u32[]{:S(2)}, u32[]{:S(2)}) collective-permute-start(bf16[512,256]{1,0:T(8,128)(2,1)S(1)} %fusion.2), channel_id=1, source_target_pairs={{0,24},{8,16},{16,8},{24,0},{1,25},{9,17},{17,9},{25,1},{2,26},{10... | collective-permute-start | bytes 786440 | tf_op jit(solution)/shard_map/ppermute | solution.py:10
  36.2 5.7 %collective-permute-done.10 = bf16[512,256]{1,0:T(8,128)(2,1)S(1)} collective-permute-done((bf16[512,256]{1,0:T(8,128)(2,1)S(1)}, bf16[512,256]{1,0:T(8,128)(2,1)S(1)}, u32[]{:S(2)}, u32[]{:S(2)}) %collective-permute-start.10) | collective-permute-done | bytes 262176 | tf_op jit(solution)/shard_map/ppermute | solution.py:10
  41.8 4.0 %collective-permute-done.11 = bf16[512,256]{1,0:T(8,128)(2,1)S(1)} collective-permute-done((bf16[512,256]{1,0:T(8,128)(2,1)S(1)}, bf16[512,256]{1,0:T(8,128)(2,1)S(1)}, u32[]{:S(2)}, u32[]{:S(2)}) %collective-permute-start.11) | collective-permute-done | bytes 262176 | tf_op jit(solution)/shard_map/ppermute | solution.py:10
  45.8 1.6 %collective-permute-done.12 = bf16[512,256]{1,0:T(8,128)(2,1)S(1)} collective-permute-done((bf16[512,256]{1,0:T(8,128)(2,1)S(1)}, bf16[512,256]{1,0:T(8,128)(2,1)S(1)}, u32[]{:S(2)}, u32[]{:S(2)}) %collective-permute-start.12) | collective-permute-done | bytes 262176 | tf_op jit(solution)/shard_map/ppermute | solution.py:10
  47.5 1.5 %fusion.1 = f32[512,256]{1,0:T(8,128)} fusion(bf16[512,2048]{1,0:T(8,128)(2,1)S(1)} %fusion.17, bf16[512,256]{1,0:T(8,128)(2,1)S(1)} %collective-permute-done.12, bf16[512,256]{1,0:T(8,128)(2,1)S(1)} %collective-permute-done.11, bf16[512,256]{1,0:T(8,128)(2,1)S(1)} %collective-permute-done.10, bf16[512,256]{1,0:T(8,128)(2,1)S(1)} %fusion.2, ...), kind=kOutput, calls=%fused_computation.3 | convolution fusion | flops 541720576 | bytes 4456448 | tf_op jit(solution)/shard_map/dot_general | solution.py:66
  (2 shorter events, 0.1 us)
Async XLA Ops:
  0.0 8.8 %copy-start = (bf16[512,256]{1,0:T(8,128)(2,1)S(1)}, bf16[512,256]{1,0:T(8,128)(2,1)}, u32[]{:S(2)}) copy-start(bf16[512,256]{1,0:T(8,128)(2,1)} %param.2) | copy-start | bytes 786436
  0.0 9.8 %collective-permute-start = (bf16[512,256]{1,0:T(8,128)(2,1)}, bf16[512,256]{1,0:T(8,128)(2,1)S(1)}, u32[]{:S(2)}, u32[]{:S(2)}) collective-permute-start(bf16[512,256]{1,0:T(8,128)(2,1)} %param.2), channel_id=1, source_target_pairs={{0,8},{8,0},{16,24},{24,16},{1,9},{9,1},{17,25},{25,17},{2,10},{10... | collective-permute-start | bytes 786440 | tf_op jit(solution)/shard_map/ppermute | solution.py:10
  1.5 11.4 %collective-permute-start.2 = (bf16[512,256]{1,0:T(8,128)(2,1)}, bf16[512,256]{1,0:T(8,128)(2,1)}, u32[]{:S(2)}, u32[]{:S(2)}) collective-permute-start(bf16[512,256]{1,0:T(8,128)(2,1)} %param.2), channel_id=1, source_target_pairs={{0,2},{1,3},{2,0},{3,1},{4,6},{5,7},{6,4},{7,5},{8,10},{9,11},{10,... | collective-permute-start | bytes 786440 | tf_op jit(solution)/shard_map/ppermute | solution.py:10
  3.1 18.7 %collective-permute-start.4 = (bf16[512,256]{1,0:T(8,128)(2,1)}, bf16[512,256]{1,0:T(8,128)(2,1)S(1)}, u32[]{:S(2)}, u32[]{:S(2)}) collective-permute-start(bf16[512,256]{1,0:T(8,128)(2,1)} %param.2), channel_id=1, source_target_pairs={{0,4},{1,5},{2,6},{3,7},{4,0},{5,1},{6,2},{7,3},{8,12},{9,13},{10,... | collective-permute-start | bytes 786440 | tf_op jit(solution)/shard_map/ppermute | solution.py:10
  3.4 24.1 %collective-permute-start.6 = (bf16[512,256]{1,0:T(8,128)(2,1)}, bf16[512,256]{1,0:T(8,128)(2,1)S(1)}, u32[]{:S(2)}, u32[]{:S(2)}) collective-permute-start(bf16[512,256]{1,0:T(8,128)(2,1)} %param.2), channel_id=1, source_target_pairs={{0,6},{1,7},{2,4},{3,5},{4,2},{5,3},{6,0},{7,1},{8,14},{9,15},{10,... | collective-permute-start | bytes 786440 | tf_op jit(solution)/shard_map/ppermute | solution.py:10
  5.0 22.6 %collective-permute-start.9 = (bf16[512,256]{1,0:T(8,128)(2,1)}, bf16[512,256]{1,0:T(8,128)(2,1)S(1)}, u32[]{:S(2)}, u32[]{:S(2)}) collective-permute-start(bf16[512,256]{1,0:T(8,128)(2,1)} %param.2), channel_id=1, source_target_pairs={{0,24},{8,16},{16,8},{24,0},{1,25},{9,17},{17,9},{25,1},{2,26},{10... | collective-permute-start | bytes 786440 | tf_op jit(solution)/shard_map/ppermute | solution.py:10
  9.8 18.6 %collective-permute-start.8 = (bf16[512,256]{1,0:T(8,128)(2,1)S(1)}, bf16[512,256]{1,0:T(8,128)(2,1)S(1)}, u32[]{:S(2)}, u32[]{:S(2)}) collective-permute-start(bf16[512,256]{1,0:T(8,128)(2,1)S(1)} %copy-done), channel_id=1, source_target_pairs={{0,16},{8,24},{16,0},{24,8},{1,17},{9,25},{17,1},{25,9},{2,18},{10... | collective-permute-start | bytes 786440 | tf_op jit(solution)/shard_map/ppermute | solution.py:10
  12.9 15.7 %collective-permute-start.1 = (bf16[512,256]{1,0:T(8,128)(2,1)S(1)}, bf16[512,256]{1,0:T(8,128)(2,1)S(1)}, u32[]{:S(2)}, u32[]{:S(2)}) collective-permute-start(bf16[512,256]{1,0:T(8,128)(2,1)S(1)} %copy-done), channel_id=1, source_target_pairs={{0,1},{1,0},{2,3},{3,2},{4,5},{5,4},{6,7},{7,6},{8,9},{9,8},{10,11... | collective-permute-start | bytes 786440 | tf_op jit(solution)/shard_map/ppermute | solution.py:10
  21.7 8.4 %collective-permute-start.3 = (bf16[512,256]{1,0:T(8,128)(2,1)}, bf16[512,256]{1,0:T(8,128)(2,1)S(1)}, u32[]{:S(2)}, u32[]{:S(2)}) collective-permute-start(bf16[512,256]{1,0:T(8,128)(2,1)} %collective-permute-done.2), channel_id=1, source_target_pairs={{0,1},{1,0},{2,3},{3,2},{4,5},{5,4},{6,7},{7,6},{8,9},{9,8},{10,11... | collective-permute-start | bytes 786440 | tf_op jit(solution)/shard_map/ppermute | solution.py:10
  27.6 3.2 %collective-permute-start.5 = (bf16[512,256]{1,0:T(8,128)(2,1)S(1)}, bf16[512,256]{1,0:T(8,128)(2,1)S(1)}, u32[]{:S(2)}, u32[]{:S(2)}) collective-permute-start(bf16[512,256]{1,0:T(8,128)(2,1)S(1)} %collective-permute-done.4), channel_id=1, source_target_pairs={{0,1},{1,0},{2,3},{3,2},{4,5},{5,4},{6,7},{7,6},{8,9},{9,8},{10,11... | collective-permute-start | bytes 786440 | tf_op jit(solution)/shard_map/ppermute | solution.py:10
  27.6 3.8 %collective-permute-start.7 = (bf16[512,256]{1,0:T(8,128)(2,1)S(1)}, bf16[512,256]{1,0:T(8,128)(2,1)S(1)}, u32[]{:S(2)}, u32[]{:S(2)}) collective-permute-start(bf16[512,256]{1,0:T(8,128)(2,1)S(1)} %collective-permute-done.6), channel_id=1, source_target_pairs={{0,1},{1,0},{2,3},{3,2},{4,5},{5,4},{6,7},{7,6},{8,9},{9,8},{10,11... | collective-permute-start | bytes 786440 | tf_op jit(solution)/shard_map/ppermute | solution.py:10
  30.7 1.2 %copy-start.1 = (bf16[512,256]{1,0:T(8,128)(2,1)S(1)}, bf16[512,256]{1,0:T(8,128)(2,1)}, u32[]{:S(2)}) copy-start(bf16[512,256]{1,0:T(8,128)(2,1)} %get-tuple-element.8) | copy-start | bytes 786436
  32.6 9.2 %collective-permute-start.10 = (bf16[512,256]{1,0:T(8,128)(2,1)S(1)}, bf16[512,256]{1,0:T(8,128)(2,1)S(1)}, u32[]{:S(2)}, u32[]{:S(2)}) collective-permute-start(bf16[512,256]{1,0:T(8,128)(2,1)S(1)} %fusion.2), channel_id=1, source_target_pairs={{0,8},{8,0},{16,24},{24,16},{1,9},{9,1},{17,25},{25,17},{2,10},{10... | collective-permute-start | bytes 786440 | tf_op jit(solution)/shard_map/ppermute | solution.py:10
  33.2 12.6 %collective-permute-start.11 = (bf16[512,256]{1,0:T(8,128)(2,1)S(1)}, bf16[512,256]{1,0:T(8,128)(2,1)S(1)}, u32[]{:S(2)}, u32[]{:S(2)}) collective-permute-start(bf16[512,256]{1,0:T(8,128)(2,1)S(1)} %fusion.2), channel_id=1, source_target_pairs={{0,16},{8,24},{16,0},{24,8},{1,17},{9,25},{17,1},{25,9},{2,18},{10... | collective-permute-start | bytes 786440 | tf_op jit(solution)/shard_map/ppermute | solution.py:10
  34.7 12.7 %collective-permute-start.12 = (bf16[512,256]{1,0:T(8,128)(2,1)S(1)}, bf16[512,256]{1,0:T(8,128)(2,1)S(1)}, u32[]{:S(2)}, u32[]{:S(2)}) collective-permute-start(bf16[512,256]{1,0:T(8,128)(2,1)S(1)} %fusion.2), channel_id=1, source_target_pairs={{0,24},{8,16},{16,8},{24,0},{1,25},{9,17},{17,9},{25,1},{2,26},{10... | collective-permute-start | bytes 786440 | tf_op jit(solution)/shard_map/ppermute | solution.py:10

commit v24 on v23

--- a/solution.py
+++ b/solution.py
@@ -51,8 +51,9 @@
 
         shift = col_index ^ (row_index * ratio)
         row_f = jnp.zeros((rows, n_col * cols), matrix_in.dtype)
-        for t, piece in enumerate(row_pieces):
-            row_f = lax.dynamic_update_slice_in_dim(row_f, piece, (t ^ shift) * cols, 1)
+        order = [t for t in range(n_col) if t not in (4, 5)] + [t for t in (4, 5) if t < n_col]
+        for t in order:
+            row_f = lax.dynamic_update_slice_in_dim(row_f, row_pieces[t], (t ^ shift) * cols, 1)
         square = jnp.dot(
             row_f, jnp.concatenate(col_pieces, axis=0), preferred_element_type=jnp.float32
         )

time: 49.3 us -> 51.6 us (1.047)
  the two profiles are of different devices: /device:TPU:16 before, /device:TPU:0 now
where the time goes in v24:
time: 51.6 us; the launch traced here: 51.4 us
  waiting for transfers between devices  28.4 us (55%)
  starting transfers between devices  13.3 us (26%)
  other arithmetic  3.89 us (8%)
  local copies, waits for them, and re-layouts  3.22 us (6%)
  matrix products  2.24 us (4%)
    ppermute x13, waiting for transfers between devices, _swap(): return lax.ppermute(x, axis, [(i, i ^ d) for i in range(size)])  28.4 us
    ppermute x13, starting transfers between devices, _swap(): return lax.ppermute(x, axis, [(i, i ^ d) for i in range(size)])  13.3 us
    dynamic_update_slice x8, other arithmetic, body(): lax.dynamic_update_slice_in_dim(row_f, row_pieces[t], (t ^ shift) * cols, 1)  2.29 us
    mul x10, local copies, waits for them, and re-layouts, mask_from(): return (x4 * blocks[:, None, :, None]).reshape(rows, cols)  2.05 us
    dot_general x1, matrix products, body(): jnp.dot(row_f, jnp.concatenate(f_pieces, axis=0), preferred_element_type=...  1.52 us
  transfers between devices with their start and end apart: 13, of which 5 were waited for; matrix products, arithmetic and copies ran while one was open for 13% of the time, Pallas kernels for 0%

profile of v24, /device:TPU:0, one launch (start us, length us, event | category | flops | bytes accessed | tf_op | source)
XLA Modules:
  0.0 51.4 jit_solution(11664201508844944244)
XLA Ops:
  0.0 0.0 copy-start
  0.0 2.9 %collective-permute-start = (bf16[512,256]{1,0:T(8,128)(2,1)}, bf16[512,256]{1,0:T(8,128)(2,1)S(1)}, u32[]{:S(2)}, u32[]{:S(2)}) collective-permute-start(bf16[512,256]{1,0:T(8,128)(2,1)} %param.2), channel_id=1, source_target_pairs={{0,8},{8,0},{16,24},{24,16},{1,9},{9,1},{17,25},{25,17},{2,10},{10... | collective-permute-start | bytes 786440 | tf_op jit(solution)/shard_map/ppermute | solution.py:10
  2.9 1.6 %collective-permute-start.2 = (bf16[512,256]{1,0:T(8,128)(2,1)}, bf16[512,256]{1,0:T(8,128)(2,1)}, u32[]{:S(2)}, u32[]{:S(2)}) collective-permute-start(bf16[512,256]{1,0:T(8,128)(2,1)} %param.2), channel_id=1, source_target_pairs={{0,2},{1,3},{2,0},{3,1},{4,6},{5,7},{6,4},{7,5},{8,10},{9,11},{10,... | collective-permute-start | bytes 786440 | tf_op jit(solution)/shard_map/ppermute | solution.py:10
  4.5 2.5 %collective-permute-start.4 = (bf16[512,256]{1,0:T(8,128)(2,1)}, bf16[512,256]{1,0:T(8,128)(2,1)S(1)}, u32[]{:S(2)}, u32[]{:S(2)}) collective-permute-start(bf16[512,256]{1,0:T(8,128)(2,1)} %param.2), channel_id=1, source_target_pairs={{0,6},{1,7},{2,4},{3,5},{4,2},{5,3},{6,0},{7,1},{8,14},{9,15},{10,... | collective-permute-start | bytes 786440 | tf_op jit(solution)/shard_map/ppermute | solution.py:10
  7.0 0.1 collective-permute-start.6
  7.1 1.5 %collective-permute-start.9 = (bf16[512,256]{1,0:T(8,128)(2,1)}, bf16[512,256]{1,0:T(8,128)(2,1)S(1)}, u32[]{:S(2)}, u32[]{:S(2)}) collective-permute-start(bf16[512,256]{1,0:T(8,128)(2,1)} %param.2), channel_id=1, source_target_pairs={{0,24},{8,16},{16,8},{24,0},{1,25},{9,17},{17,9},{25,1},{2,26},{10... | collective-permute-start | bytes 786440 | tf_op jit(solution)/shard_map/ppermute | solution.py:10
  8.6 0.7 %convert_element_type.27 = bf16[16,16]{1,0:T(8,128)(2,1)S(1)} convert(s32[16,16]{1,0:T(8,128)} %param.3) | non-fusion elementwise | flops 256 | bytes 1536 | tf_op jit(solution)/shard_map/convert_element_type | solution.py:28
  9.3 0.8 %dynamic-slice_convert_fusion = (f32[4,2]{1,0:T(4,128)S(1)}, bf16[4,2]{1,0:T(4,128)(2,1)S(1)}) fusion(s32[16,16]{1,0:T(8,128)} %param.3, s32[]{:T(128)S(6)} %select_n.70, s32[]{:T(128)S(6)} %select_n.71), kind=kLoop, calls=%fused_computation.38 | loop fusion | flops 16 | bytes 88 | tf_op jit(solution)/shard_map/convert_element_type | solution.py:60
  10.1 0.6 %broadcast_in_dim.7 = bf16[512,2,128]{2,1,0:T(2,128)(2,1)S(1)} broadcast(bf16[512,2]{1,0:T(8,128)(2,1)S(1)} %bitcast.77), dimensions={0,1} | broadcast | bytes 264192 | tf_op jit(solution)/shard_map/broadcast_in_dim | solution.py:26
  10.7 0.2 broadcast_in_dim.8
  10.9 0.0 copy-done
  11.0 0.8 %constant_dynamic-update-slice_fusion = (bf16[512,2048]{1,0:T(8,128)(2,1)S(1)}, bf16[512,256]{1,0:T(8,128)(2,1)}) fusion(bf16[512,2048]{1,0:T(8,128)(2,1)S(1)} %broadcast_in_dim.8, s32[]{:T(128)S(6)} %select_n.72, bf16[512,256]{1,0:T(8,128)(2,1)S(1)} %copy-done, bf16[64,8,2,128]{3,2,1,0:T(2,128)(2,1)S(1)} %bitcast.69), kind=kLoop, calls=%fused_computation.37 | loop fusion | flops 524288 | bytes 1048580 | tf_op jit(solution)/shard_map/dynamic_update_slice | solution.py:56
  11.8 0.1 fusion.26
  11.9 0.0 collective-permute-done
  11.9 0.6 %collective-permute-start.8 = (bf16[512,256]{1,0:T(8,128)(2,1)S(1)}, bf16[512,256]{1,0:T(8,128)(2,1)S(1)}, u32[]{:S(2)}, u32[]{:S(2)}) collective-permute-start(bf16[512,256]{1,0:T(8,128)(2,1)S(1)} %copy-done), channel_id=1, source_target_pairs={{0,16},{8,24},{16,0},{24,8},{1,17},{9,25},{17,1},{25,9},{2,18},{10... | collective-permute-start | bytes 786440 | tf_op jit(solution)/shard_map/ppermute | solution.py:10
  12.5 0.2 mul.259
  12.7 0.1 bitcast_multiply_fusion.2
  12.7 0.0 collective-permute-done.2
  12.8 0.1 collective-permute-start.1
  12.8 7.3 %collective-permute-done.4 = bf16[512,256]{1,0:T(8,128)(2,1)S(1)} collective-permute-done((bf16[512,256]{1,0:T(8,128)(2,1)}, bf16[512,256]{1,0:T(8,128)(2,1)S(1)}, u32[]{:S(2)}, u32[]{:S(2)}) %collective-permute-start.4) | collective-permute-done | bytes 262176 | tf_op jit(solution)/shard_map/ppermute | solution.py:10
  20.1 0.0 collective-permute-start.3
  20.1 9.8 %collective-permute-done.6 = bf16[512,256]{1,0:T(8,128)(2,1)S(1)} collective-permute-done((bf16[512,256]{1,0:T(8,128)(2,1)}, bf16[512,256]{1,0:T(8,128)(2,1)S(1)}, u32[]{:S(2)}, u32[]{:S(2)}) %collective-permute-start.6) | collective-permute-done | bytes 262176 | tf_op jit(solution)/shard_map/ppermute | solution.py:10
  29.9 0.0 collective-permute-start.5
  29.9 0.0 collective-permute-done.9
  30.0 0.5 collective-permute-start.7
  30.5 0.2 mul.267
  30.7 0.1 bitcast_multiply_fusion
  30.7 0.0 collective-permute-done.8
  30.7 0.2 mul.263
  31.0 0.0 collective-permute-done.1
  31.0 0.2 mul.224
  31.2 0.1 fusion.23
  31.3 0.2 mul.229
  31.5 1.0 %fusion.22 = bf16[512,2048]{1,0:T(8,128)(2,1)S(1)} fusion(bf16[512,2048]{1,0:T(8,128)(2,1)S(1)} %fusion.23, s32[]{:T(128)S(6)} %select_n.76, bf16[512,256]{1,0:T(8,128)(2,1)} %collective-permute-done.2, bf16[64,8,2,128]{3,2,1,0:T(2,128)(2,1)S(1)} %bitcast.74), kind=kLoop, calls=%fused_computation.33 | loop fusion | flops 524288 | bytes 786436 | tf_op jit(solution)/shard_map/dynamic_update_slice | solution.py:56
  32.5 0.0 collective-permute-done.3
  32.6 0.2 mul.234
  32.8 0.1 fusion.21
  32.8 0.2 mul.239
  33.1 0.0 copy-start.1
  33.1 0.1 fusion.20
  33.2 0.0 collective-permute-done.5
  33.2 0.2 mul.244
  33.4 0.1 fusion.19
  33.5 0.2 mul.249
  33.7 0.1 fusion.18
  33.8 0.0 collective-permute-done.7
  33.8 0.2 mul.254
  34.0 0.1 fusion.17
  34.1 0.2 mul.270
  34.3 0.0 copy-done.1
  34.3 0.7 %fusion.2 = bf16[512,256]{1,0:T(8,128)(2,1)S(1)} fusion(bf16[512,2048]{1,0:T(8,128)(2,1)S(1)} %fusion.17, bf16[512,256]{1,0:T(8,128)(2,1)S(1)} %bitcast_multiply_fusion, bf16[512,256]{1,0:T(8,128)(2,1)S(1)} %bitcast_multiply_fusion.1, bf16[512,256]{1,0:T(8,128)(2,1)S(1)} %bitcast_multiply_fusion.2, bf16[512,256]{1,0:T(8,128)(2,1)S(1)} %copy-done.1, ...), kind=kOutput, calls=%fused_computation.4 | convolution fusion | flops 541327360 | bytes 3932160 | tf_op jit(solution)/shard_map/dot_general | solution.py:57
  35.0 0.6 %collective-permute-start.10 = (bf16[512,256]{1,0:T(8,128)(2,1)S(1)}, bf16[512,256]{1,0:T(8,128)(2,1)S(1)}, u32[]{:S(2)}, u32[]{:S(2)}) collective-permute-start(bf16[512,256]{1,0:T(8,128)(2,1)S(1)} %fusion.2), channel_id=1, source_target_pairs={{0,8},{8,0},{16,24},{24,16},{1,9},{9,1},{17,25},{25,17},{2,10},{10... | collective-permute-start | bytes 786440 | tf_op jit(solution)/shard_map/ppermute | solution.py:10
  35.6 1.5 %collective-permute-start.11 = (bf16[512,256]{1,0:T(8,128)(2,1)S(1)}, bf16[512,256]{1,0:T(8,128)(2,1)S(1)}, u32[]{:S(2)}, u32[]{:S(2)}) collective-permute-start(bf16[512,256]{1,0:T(8,128)(2,1)S(1)} %fusion.2), channel_id=1, source_target_pairs={{0,16},{8,24},{16,0},{24,8},{1,17},{9,25},{17,1},{25,9},{2,18},{10... | collective-permute-start | bytes 786440 | tf_op jit(solution)/shard_map/ppermute | solution.py:10
  37.1 1.4 %collective-permute-start.12 = (bf16[512,256]{1,0:T(8,128)(2,1)S(1)}, bf16[512,256]{1,0:T(8,128)(2,1)S(1)}, u32[]{:S(2)}, u32[]{:S(2)}) collective-permute-start(bf16[512,256]{1,0:T(8,128)(2,1)S(1)} %fusion.2), channel_id=1, source_target_pairs={{0,24},{8,16},{16,8},{24,0},{1,25},{9,17},{17,9},{25,1},{2,26},{10... | collective-permute-start | bytes 786440 | tf_op jit(solution)/shard_map/ppermute | solution.py:10
  38.6 5.7 %collective-permute-done.10 = bf16[512,256]{1,0:T(8,128)(2,1)S(1)} collective-permute-done((bf16[512,256]{1,0:T(8,128)(2,1)S(1)}, bf16[512,256]{1,0:T(8,128)(2,1)S(1)}, u32[]{:S(2)}, u32[]{:S(2)}) %collective-permute-start.10) | collective-permute-done | bytes 262176 | tf_op jit(solution)/shard_map/ppermute | solution.py:10
  44.2 4.0 %collective-permute-done.11 = bf16[512,256]{1,0:T(8,128)(2,1)S(1)} collective-permute-done((bf16[512,256]{1,0:T(8,128)(2,1)S(1)}, bf16[512,256]{1,0:T(8,128)(2,1)S(1)}, u32[]{:S(2)}, u32[]{:S(2)}) %collective-permute-start.11) | collective-permute-done | bytes 262176 | tf_op jit(solution)/shard_map/ppermute | solution.py:10
  48.2 1.6 %collective-permute-done.12 = bf16[512,256]{1,0:T(8,128)(2,1)S(1)} collective-permute-done((bf16[512,256]{1,0:T(8,128)(2,1)S(1)}, bf16[512,256]{1,0:T(8,128)(2,1)S(1)}, u32[]{:S(2)}, u32[]{:S(2)}) %collective-permute-start.12) | collective-permute-done | bytes 262176 | tf_op jit(solution)/shard_map/ppermute | solution.py:10
  49.9 1.5 %fusion.1 = f32[512,256]{1,0:T(8,128)} fusion(bf16[512,2048]{1,0:T(8,128)(2,1)S(1)} %fusion.17, bf16[512,256]{1,0:T(8,128)(2,1)S(1)} %collective-permute-done.12, bf16[512,256]{1,0:T(8,128)(2,1)S(1)} %collective-permute-done.11, bf16[512,256]{1,0:T(8,128)(2,1)S(1)} %collective-permute-done.10, bf16[512,256]{1,0:T(8,128)(2,1)S(1)} %fusion.2, ...), kind=kOutput, calls=%fused_computation.3 | convolution fusion | flops 541720576 | bytes 4456448 | tf_op jit(solution)/shard_map/dot_general | solution.py:67
  (2 shorter events, 0.1 us)
Async XLA Ops:
  0.0 11.0 %copy-start = (bf16[512,256]{1,0:T(8,128)(2,1)S(1)}, bf16[512,256]{1,0:T(8,128)(2,1)}, u32[]{:S(2)}) copy-start(bf16[512,256]{1,0:T(8,128)(2,1)} %param.2) | copy-start | bytes 786436
  0.0 11.9 %collective-permute-start = (bf16[512,256]{1,0:T(8,128)(2,1)}, bf16[512,256]{1,0:T(8,128)(2,1)S(1)}, u32[]{:S(2)}, u32[]{:S(2)}) collective-permute-start(bf16[512,256]{1,0:T(8,128)(2,1)} %param.2), channel_id=1, source_target_pairs={{0,8},{8,0},{16,24},{24,16},{1,9},{9,1},{17,25},{25,17},{2,10},{10... | collective-permute-start | bytes 786440 | tf_op jit(solution)/shard_map/ppermute | solution.py:10
  2.9 9.8 %collective-permute-start.2 = (bf16[512,256]{1,0:T(8,128)(2,1)}, bf16[512,256]{1,0:T(8,128)(2,1)}, u32[]{:S(2)}, u32[]{:S(2)}) collective-permute-start(bf16[512,256]{1,0:T(8,128)(2,1)} %param.2), channel_id=1, source_target_pairs={{0,2},{1,3},{2,0},{3,1},{4,6},{5,7},{6,4},{7,5},{8,10},{9,11},{10,... | collective-permute-start | bytes 786440 | tf_op jit(solution)/shard_map/ppermute | solution.py:10
  4.5 15.6 %collective-permute-start.4 = (bf16[512,256]{1,0:T(8,128)(2,1)}, bf16[512,256]{1,0:T(8,128)(2,1)S(1)}, u32[]{:S(2)}, u32[]{:S(2)}) collective-permute-start(bf16[512,256]{1,0:T(8,128)(2,1)} %param.2), channel_id=1, source_target_pairs={{0,6},{1,7},{2,4},{3,5},{4,2},{5,3},{6,0},{7,1},{8,14},{9,15},{10,... | collective-permute-start | bytes 786440 | tf_op jit(solution)/shard_map/ppermute | solution.py:10
  7.0 23.0 %collective-permute-start.6 = (bf16[512,256]{1,0:T(8,128)(2,1)}, bf16[512,256]{1,0:T(8,128)(2,1)S(1)}, u32[]{:S(2)}, u32[]{:S(2)}) collective-permute-start(bf16[512,256]{1,0:T(8,128)(2,1)} %param.2), channel_id=1, source_target_pairs={{0,4},{1,5},{2,6},{3,7},{4,0},{5,1},{6,2},{7,3},{8,12},{9,13},{10,... | collective-permute-start | bytes 786440 | tf_op jit(solution)/shard_map/ppermute | solution.py:10
  7.1 22.8 %collective-permute-start.9 = (bf16[512,256]{1,0:T(8,128)(2,1)}, bf16[512,256]{1,0:T(8,128)(2,1)S(1)}, u32[]{:S(2)}, u32[]{:S(2)}) collective-permute-start(bf16[512,256]{1,0:T(8,128)(2,1)} %param.2), channel_id=1, source_target_pairs={{0,24},{8,16},{16,8},{24,0},{1,25},{9,17},{17,9},{25,1},{2,26},{10... | collective-permute-start | bytes 786440 | tf_op jit(solution)/shard_map/ppermute | solution.py:10
  11.9 18.8 %collective-permute-start.8 = (bf16[512,256]{1,0:T(8,128)(2,1)S(1)}, bf16[512,256]{1,0:T(8,128)(2,1)S(1)}, u32[]{:S(2)}, u32[]{:S(2)}) collective-permute-start(bf16[512,256]{1,0:T(8,128)(2,1)S(1)} %copy-done), channel_id=1, source_target_pairs={{0,16},{8,24},{16,0},{24,8},{1,17},{9,25},{17,1},{25,9},{2,18},{10... | collective-permute-start | bytes 786440 | tf_op jit(solution)/shard_map/ppermute | solution.py:10
  12.8 18.2 %collective-permute-start.1 = (bf16[512,256]{1,0:T(8,128)(2,1)S(1)}, bf16[512,256]{1,0:T(8,128)(2,1)S(1)}, u32[]{:S(2)}, u32[]{:S(2)}) collective-permute-start(bf16[512,256]{1,0:T(8,128)(2,1)S(1)} %copy-done), channel_id=1, source_target_pairs={{0,1},{1,0},{2,3},{3,2},{4,5},{5,4},{6,7},{7,6},{8,9},{9,8},{10,11... | collective-permute-start | bytes 786440 | tf_op jit(solution)/shard_map/ppermute | solution.py:10
  20.1 12.4 %collective-permute-start.3 = (bf16[512,256]{1,0:T(8,128)(2,1)}, bf16[512,256]{1,0:T(8,128)(2,1)S(1)}, u32[]{:S(2)}, u32[]{:S(2)}) collective-permute-start(bf16[512,256]{1,0:T(8,128)(2,1)} %collective-permute-done.2), channel_id=1, source_target_pairs={{0,1},{1,0},{2,3},{3,2},{4,5},{5,4},{6,7},{7,6},{8,9},{9,8},{10,11... | collective-permute-start | bytes 786440 | tf_op jit(solution)/shard_map/ppermute | solution.py:10
  29.9 3.2 %collective-permute-start.5 = (bf16[512,256]{1,0:T(8,128)(2,1)S(1)}, bf16[512,256]{1,0:T(8,128)(2,1)S(1)}, u32[]{:S(2)}, u32[]{:S(2)}) collective-permute-start(bf16[512,256]{1,0:T(8,128)(2,1)S(1)} %collective-permute-done.4), channel_id=1, source_target_pairs={{0,1},{1,0},{2,3},{3,2},{4,5},{5,4},{6,7},{7,6},{8,9},{9,8},{10,11... | collective-permute-start | bytes 786440 | tf_op jit(solution)/shard_map/ppermute | solution.py:10
  30.0 3.8 %collective-permute-start.7 = (bf16[512,256]{1,0:T(8,128)(2,1)S(1)}, bf16[512,256]{1,0:T(8,128)(2,1)S(1)}, u32[]{:S(2)}, u32[]{:S(2)}) collective-permute-start(bf16[512,256]{1,0:T(8,128)(2,1)S(1)} %collective-permute-done.6), channel_id=1, source_target_pairs={{0,1},{1,0},{2,3},{3,2},{4,5},{5,4},{6,7},{7,6},{8,9},{9,8},{10,11... | collective-permute-start | bytes 786440 | tf_op jit(solution)/shard_map/ppermute | solution.py:10
  33.1 1.2 %copy-start.1 = (bf16[512,256]{1,0:T(8,128)(2,1)S(1)}, bf16[512,256]{1,0:T(8,128)(2,1)}, u32[]{:S(2)}) copy-start(bf16[512,256]{1,0:T(8,128)(2,1)} %get-tuple-element.8) | copy-start | bytes 786436
  35.0 9.2 %collective-permute-start.10 = (bf16[512,256]{1,0:T(8,128)(2,1)S(1)}, bf16[512,256]{1,0:T(8,128)(2,1)S(1)}, u32[]{:S(2)}, u32[]{:S(2)}) collective-permute-start(bf16[512,256]{1,0:T(8,128)(2,1)S(1)} %fusion.2), channel_id=1, source_target_pairs={{0,8},{8,0},{16,24},{24,16},{1,9},{9,1},{17,25},{25,17},{2,10},{10... | collective-permute-start | bytes 786440 | tf_op jit(solution)/shard_map/ppermute | solution.py:10
  35.6 12.6 %collective-permute-start.11 = (bf16[512,256]{1,0:T(8,128)(2,1)S(1)}, bf16[512,256]{1,0:T(8,128)(2,1)S(1)}, u32[]{:S(2)}, u32[]{:S(2)}) collective-permute-start(bf16[512,256]{1,0:T(8,128)(2,1)S(1)} %fusion.2), channel_id=1, source_target_pairs={{0,16},{8,24},{16,0},{24,8},{1,17},{9,25},{17,1},{25,9},{2,18},{10... | collective-permute-start | bytes 786440 | tf_op jit(solution)/shard_map/ppermute | solution.py:10
  37.1 12.7 %collective-permute-start.12 = (bf16[512,256]{1,0:T(8,128)(2,1)S(1)}, bf16[512,256]{1,0:T(8,128)(2,1)S(1)}, u32[]{:S(2)}, u32[]{:S(2)}) collective-permute-start(bf16[512,256]{1,0:T(8,128)(2,1)S(1)} %fusion.2), channel_id=1, source_target_pairs={{0,24},{8,16},{16,8},{24,0},{1,25},{9,17},{17,9},{25,1},{2,26},{10... | collective-permute-start | bytes 786440 | tf_op jit(solution)/shard_map/ppermute | solution.py:10

commit v25 on v23

--- a/solution.py
+++ b/solution.py
@@ -40,13 +40,15 @@
             mask_from(col_raw[j], row_index ^ j, col_index) for j in range(1, n_row)
         ]
 
-        late, _ = lax.optimization_barrier((matrix_in, col_raw[1]))
         raw = [None] * n_col
-        raw[1] = _swap(late, "col", n_col, 1)
         for k in range(1, n_z):
             piece = _swap(matrix_in, "col", n_col, 2 * k)
             raw[2 * k] = piece
             raw[2 * k + 1] = _swap(piece, "col", n_col, 1)
+        late = matrix_in
+        if n_z > 1:
+            late, _ = lax.optimization_barrier((matrix_in, raw[2 * (n_z - 1)]))
+        raw[1] = _swap(late, "col", n_col, 1)
         row_pieces = [masked] + [mask_from(raw[t], row_index, col_index ^ t) for t in range(1, n_col)]
 
         shift = col_index ^ (row_index * ratio)

time: 49.3 us -> 49.5 us (level)
  the two profiles are of different devices: /device:TPU:16 before, /device:TPU:0 now
where the time goes in v25:
time: 49.5 us; the launch traced here: 49.3 us
  waiting for transfers between devices  25.2 us (51%)
  starting transfers between devices  14.5 us (29%)
  other arithmetic  3.89 us (8%)
  local copies, waits for them, and re-layouts  3.22 us (7%)
  matrix products  2.24 us (5%)
    ppermute x13, waiting for transfers between devices, _swap(): return lax.ppermute(x, axis, [(i, i ^ d) for i in range(size)])  25.2 us
    ppermute x13, starting transfers between devices, _swap(): return lax.ppermute(x, axis, [(i, i ^ d) for i in range(size)])  14.5 us
    dynamic_update_slice x8, other arithmetic, body(): row_f = lax.dynamic_update_slice_in_dim(row_f, piece, (t ^ shift) * cols, 1)  2.29 us
    mul x10, local copies, waits for them, and re-layouts, mask_from(): return (x4 * blocks[:, None, :, None]).reshape(rows, cols)  2.05 us
    dot_general x1, matrix products, body(): jnp.dot(row_f, jnp.concatenate(f_pieces, axis=0), preferred_element_type=...  1.52 us
  transfers between devices with their start and end apart: 13, of which 6 were waited for; matrix products, arithmetic and copies ran while one was open for 13% of the time, Pallas kernels for 0%

profile of v25, /device:TPU:0, one launch (start us, length us, event | category | flops | bytes accessed | tf_op | source)
XLA Modules:
  0.0 49.3 jit_solution(126238844573411527)
XLA Ops:
  0.0 0.0 copy-start
  0.0 5.0 %collective-permute-start = (bf16[512,256]{1,0:T(8,128)(2,1)}, bf16[512,256]{1,0:T(8,128)(2,1)S(1)}, u32[]{:S(2)}, u32[]{:S(2)}) collective-permute-start(bf16[512,256]{1,0:T(8,128)(2,1)} %param.2), channel_id=1, source_target_pairs={{0,6},{1,7},{2,4},{3,5},{4,2},{5,3},{6,0},{7,1},{8,14},{9,15},{10,... | collective-permute-start | bytes 786440 | tf_op jit(solution)/shard_map/ppermute | solution.py:10
  5.1 0.0 collective-permute-start.2
  5.1 0.6 %collective-permute-start.4 = (bf16[512,256]{1,0:T(8,128)(2,1)}, bf16[512,256]{1,0:T(8,128)(2,1)S(1)}, u32[]{:S(2)}, u32[]{:S(2)}) collective-permute-start(bf16[512,256]{1,0:T(8,128)(2,1)} %param.2), channel_id=1, source_target_pairs={{0,4},{1,5},{2,6},{3,7},{4,0},{5,1},{6,2},{7,3},{8,12},{9,13},{10,... | collective-permute-start | bytes 786440 | tf_op jit(solution)/shard_map/ppermute | solution.py:10
  5.7 2.6 %collective-permute-start.9 = (bf16[512,256]{1,0:T(8,128)(2,1)}, bf16[512,256]{1,0:T(8,128)(2,1)S(1)}, u32[]{:S(2)}, u32[]{:S(2)}) collective-permute-start(bf16[512,256]{1,0:T(8,128)(2,1)} %param.2), channel_id=1, source_target_pairs={{0,24},{8,16},{16,8},{24,0},{1,25},{9,17},{17,9},{25,1},{2,26},{10... | collective-permute-start | bytes 786440 | tf_op jit(solution)/shard_map/ppermute | solution.py:10
  8.3 0.5 %collective-permute-start.8 = (bf16[512,256]{1,0:T(8,128)(2,1)}, bf16[512,256]{1,0:T(8,128)(2,1)S(1)}, u32[]{:S(2)}, u32[]{:S(2)}) collective-permute-start(bf16[512,256]{1,0:T(8,128)(2,1)} %param.2), channel_id=1, source_target_pairs={{0,16},{8,24},{16,0},{24,8},{1,17},{9,25},{17,1},{25,9},{2,18},{10... | collective-permute-start | bytes 786440 | tf_op jit(solution)/shard_map/ppermute | solution.py:10
  8.8 0.7 %convert_element_type.27 = bf16[16,16]{1,0:T(8,128)(2,1)S(1)} convert(s32[16,16]{1,0:T(8,128)} %param.3) | non-fusion elementwise | flops 256 | bytes 1536 | tf_op jit(solution)/shard_map/convert_element_type | solution.py:28
  9.5 0.8 %dynamic-slice_convert_fusion = (f32[4,2]{1,0:T(4,128)S(1)}, bf16[4,2]{1,0:T(4,128)(2,1)S(1)}) fusion(s32[16,16]{1,0:T(8,128)} %param.3, s32[]{:T(128)S(6)} %select_n.70, s32[]{:T(128)S(6)} %select_n.71), kind=kLoop, calls=%fused_computation.38 | loop fusion | flops 16 | bytes 88 | tf_op jit(solution)/shard_map/convert_element_type | solution.py:61
  10.3 0.6 %broadcast_in_dim.7 = bf16[512,2,128]{2,1,0:T(2,128)(2,1)S(1)} broadcast(bf16[512,2]{1,0:T(8,128)(2,1)S(1)} %bitcast.77), dimensions={0,1} | broadcast | bytes 264192 | tf_op jit(solution)/shard_map/broadcast_in_dim | solution.py:26
  10.9 0.2 broadcast_in_dim.8
  11.1 0.0 copy-done
  11.2 0.8 %constant_dynamic-update-slice_fusion = (bf16[512,2048]{1,0:T(8,128)(2,1)S(1)}, bf16[512,256]{1,0:T(8,128)(2,1)}) fusion(bf16[512,2048]{1,0:T(8,128)(2,1)S(1)} %broadcast_in_dim.8, s32[]{:T(128)S(6)} %select_n.72, bf16[512,256]{1,0:T(8,128)(2,1)S(1)} %copy-done, bf16[64,8,2,128]{3,2,1,0:T(2,128)(2,1)S(1)} %bitcast.69), kind=kLoop, calls=%fused_computation.37 | loop fusion | flops 524288 | bytes 1048580 | tf_op jit(solution)/shard_map/dynamic_update_slice | solution.py:57
  11.9 0.1 fusion.26
  12.1 0.5 collective-permute-done
  12.6 1.6 %collective-permute-start.7 = (bf16[512,256]{1,0:T(8,128)(2,1)S(1)}, bf16[512,256]{1,0:T(8,128)(2,1)S(1)}, u32[]{:S(2)}, u32[]{:S(2)}) collective-permute-start(bf16[512,256]{1,0:T(8,128)(2,1)S(1)} %copy-done), channel_id=1, source_target_pairs={{0,8},{8,0},{16,24},{24,16},{1,9},{9,1},{17,25},{25,17},{2,10},{10... | collective-permute-start | bytes 786440 | tf_op jit(solution)/shard_map/ppermute | solution.py:10
  14.2 0.2 collective-permute-done.9
  14.4 0.0 collective-permute-start.1
  14.4 0.2 mul.267
  14.6 0.1 bitcast_multiply_fusion
  14.6 3.9 %collective-permute-done.2 = bf16[512,256]{1,0:T(8,128)(2,1)} collective-permute-done((bf16[512,256]{1,0:T(8,128)(2,1)}, bf16[512,256]{1,0:T(8,128)(2,1)}, u32[]{:S(2)}, u32[]{:S(2)}) %collective-permute-start.2) | collective-permute-done | bytes 262176 | tf_op jit(solution)/shard_map/ppermute | solution.py:10
  18.6 0.0 collective-permute-start.6
  18.6 9.0 %collective-permute-done.4 = bf16[512,256]{1,0:T(8,128)(2,1)S(1)} collective-permute-done((bf16[512,256]{1,0:T(8,128)(2,1)}, bf16[512,256]{1,0:T(8,128)(2,1)S(1)}, u32[]{:S(2)}, u32[]{:S(2)}) %collective-permute-start.4) | collective-permute-done | bytes 262176 | tf_op jit(solution)/shard_map/ppermute | solution.py:10
  27.6 0.0 collective-permute-start.3
  27.6 0.0 collective-permute-done.8
  27.6 0.5 %collective-permute-start.5 = (bf16[512,256]{1,0:T(8,128)(2,1)S(1)}, bf16[512,256]{1,0:T(8,128)(2,1)S(1)}, u32[]{:S(2)}, u32[]{:S(2)}) collective-permute-start(bf16[512,256]{1,0:T(8,128)(2,1)S(1)} %collective-permute-done.4), channel_id=1, source_target_pairs={{0,1},{1,0},{2,3},{3,2},{4,5},{5,4},{6,7},{7,6},{8,9},{9,8},{10,11... | collective-permute-start | bytes 786440 | tf_op jit(solution)/shard_map/ppermute | solution.py:10
  28.1 0.2 mul.263
  28.3 0.1 bitcast_multiply_fusion.1
  28.4 0.0 collective-permute-done.7
  28.4 0.2 mul.259
  28.6 0.0 collective-permute-done.1
  28.6 0.2 mul.224
  28.8 0.1 fusion.23
  28.9 0.2 mul.229
  29.1 1.0 %fusion.22 = bf16[512,2048]{1,0:T(8,128)(2,1)S(1)} fusion(bf16[512,2048]{1,0:T(8,128)(2,1)S(1)} %fusion.23, s32[]{:T(128)S(6)} %select_n.76, bf16[512,256]{1,0:T(8,128)(2,1)} %collective-permute-done.2, bf16[64,8,2,128]{3,2,1,0:T(2,128)(2,1)S(1)} %bitcast.74), kind=kLoop, calls=%fused_computation.33 | loop fusion | flops 524288 | bytes 786436 | tf_op jit(solution)/shard_map/dynamic_update_slice | solution.py:57
  30.2 0.0 collective-permute-done.3
  30.2 0.2 mul.234
  30.4 0.1 fusion.21
  30.5 0.2 mul.239
  30.7 0.0 copy-start.1
  30.7 0.1 fusion.20
  30.8 0.0 collective-permute-done.5
  30.8 0.2 mul.244
  31.0 0.1 fusion.19
  31.1 0.2 mul.249
  31.3 0.1 fusion.18
  31.4 0.0 collective-permute-done.6
  31.4 0.2 mul.254
  31.6 0.1 fusion.17
  31.7 0.2 mul.270
  31.9 0.0 copy-done.1
  31.9 0.7 %fusion.2 = bf16[512,256]{1,0:T(8,128)(2,1)S(1)} fusion(bf16[512,2048]{1,0:T(8,128)(2,1)S(1)} %fusion.17, bf16[512,256]{1,0:T(8,128)(2,1)S(1)} %bitcast_multiply_fusion, bf16[512,256]{1,0:T(8,128)(2,1)S(1)} %bitcast_multiply_fusion.1, bf16[512,256]{1,0:T(8,128)(2,1)S(1)} %bitcast_multiply_fusion.2, bf16[512,256]{1,0:T(8,128)(2,1)S(1)} %copy-done.1, ...), kind=kOutput, calls=%fused_computation.4 | convolution fusion | flops 541327360 | bytes 3932160 | tf_op jit(solution)/shard_map/dot_general | solution.py:58
  32.6 1.6 %collective-permute-start.10 = (bf16[512,256]{1,0:T(8,128)(2,1)S(1)}, bf16[512,256]{1,0:T(8,128)(2,1)S(1)}, u32[]{:S(2)}, u32[]{:S(2)}) collective-permute-start(bf16[512,256]{1,0:T(8,128)(2,1)S(1)} %fusion.2), channel_id=1, source_target_pairs={{0,8},{8,0},{16,24},{24,16},{1,9},{9,1},{17,25},{25,17},{2,10},{10... | collective-permute-start | bytes 786440 | tf_op jit(solution)/shard_map/ppermute | solution.py:10
  34.2 1.5 %collective-permute-start.11 = (bf16[512,256]{1,0:T(8,128)(2,1)S(1)}, bf16[512,256]{1,0:T(8,128)(2,1)S(1)}, u32[]{:S(2)}, u32[]{:S(2)}) collective-permute-start(bf16[512,256]{1,0:T(8,128)(2,1)S(1)} %fusion.2), channel_id=1, source_target_pairs={{0,16},{8,24},{16,0},{24,8},{1,17},{9,25},{17,1},{25,9},{2,18},{10... | collective-permute-start | bytes 786440 | tf_op jit(solution)/shard_map/ppermute | solution.py:10
  35.7 0.5 collective-permute-start.12
  36.2 5.7 %collective-permute-done.10 = bf16[512,256]{1,0:T(8,128)(2,1)S(1)} collective-permute-done((bf16[512,256]{1,0:T(8,128)(2,1)S(1)}, bf16[512,256]{1,0:T(8,128)(2,1)S(1)}, u32[]{:S(2)}, u32[]{:S(2)}) %collective-permute-start.10) | collective-permute-done | bytes 262176 | tf_op jit(solution)/shard_map/ppermute | solution.py:10
  41.9 5.9 %collective-permute-done.11 = bf16[512,256]{1,0:T(8,128)(2,1)S(1)} collective-permute-done((bf16[512,256]{1,0:T(8,128)(2,1)S(1)}, bf16[512,256]{1,0:T(8,128)(2,1)S(1)}, u32[]{:S(2)}, u32[]{:S(2)}) %collective-permute-start.11) | collective-permute-done | bytes 262176 | tf_op jit(solution)/shard_map/ppermute | solution.py:10
  47.7 0.0 collective-permute-done.12
  47.7 1.5 %fusion.1 = f32[512,256]{1,0:T(8,128)} fusion(bf16[512,2048]{1,0:T(8,128)(2,1)S(1)} %fusion.17, bf16[512,256]{1,0:T(8,128)(2,1)S(1)} %collective-permute-done.12, bf16[512,256]{1,0:T(8,128)(2,1)S(1)} %collective-permute-done.11, bf16[512,256]{1,0:T(8,128)(2,1)S(1)} %collective-permute-done.10, bf16[512,256]{1,0:T(8,128)(2,1)S(1)} %fusion.2, ...), kind=kOutput, calls=%fused_computation.3 | convolution fusion | flops 541720576 | bytes 4456448 | tf_op jit(solution)/shard_map/dot_general | solution.py:68
  (2 shorter events, 0.1 us)
Async XLA Ops:
  0.0 11.1 %copy-start = (bf16[512,256]{1,0:T(8,128)(2,1)S(1)}, bf16[512,256]{1,0:T(8,128)(2,1)}, u32[]{:S(2)}) copy-start(bf16[512,256]{1,0:T(8,128)(2,1)} %param.2) | copy-start | bytes 786436
  0.0 12.6 %collective-permute-start = (bf16[512,256]{1,0:T(8,128)(2,1)}, bf16[512,256]{1,0:T(8,128)(2,1)S(1)}, u32[]{:S(2)}, u32[]{:S(2)}) collective-permute-start(bf16[512,256]{1,0:T(8,128)(2,1)} %param.2), channel_id=1, source_target_pairs={{0,6},{1,7},{2,4},{3,5},{4,2},{5,3},{6,0},{7,1},{8,14},{9,15},{10,... | collective-permute-start | bytes 786440 | tf_op jit(solution)/shard_map/ppermute | solution.py:10
  5.1 13.5 %collective-permute-start.2 = (bf16[512,256]{1,0:T(8,128)(2,1)}, bf16[512,256]{1,0:T(8,128)(2,1)}, u32[]{:S(2)}, u32[]{:S(2)}) collective-permute-start(bf16[512,256]{1,0:T(8,128)(2,1)} %param.2), channel_id=1, source_target_pairs={{0,2},{1,3},{2,0},{3,1},{4,6},{5,7},{6,4},{7,5},{8,10},{9,11},{10,... | collective-permute-start | bytes 786440 | tf_op jit(solution)/shard_map/ppermute | solution.py:10
  5.1 22.5 %collective-permute-start.4 = (bf16[512,256]{1,0:T(8,128)(2,1)}, bf16[512,256]{1,0:T(8,128)(2,1)S(1)}, u32[]{:S(2)}, u32[]{:S(2)}) collective-permute-start(bf16[512,256]{1,0:T(8,128)(2,1)} %param.2), channel_id=1, source_target_pairs={{0,4},{1,5},{2,6},{3,7},{4,0},{5,1},{6,2},{7,3},{8,12},{9,13},{10,... | collective-permute-start | bytes 786440 | tf_op jit(solution)/shard_map/ppermute | solution.py:10
  5.7 8.7 %collective-permute-start.9 = (bf16[512,256]{1,0:T(8,128)(2,1)}, bf16[512,256]{1,0:T(8,128)(2,1)S(1)}, u32[]{:S(2)}, u32[]{:S(2)}) collective-permute-start(bf16[512,256]{1,0:T(8,128)(2,1)} %param.2), channel_id=1, source_target_pairs={{0,24},{8,16},{16,8},{24,0},{1,25},{9,17},{17,9},{25,1},{2,26},{10... | collective-permute-start | bytes 786440 | tf_op jit(solution)/shard_map/ppermute | solution.py:10
  8.3 19.3 %collective-permute-start.8 = (bf16[512,256]{1,0:T(8,128)(2,1)}, bf16[512,256]{1,0:T(8,128)(2,1)S(1)}, u32[]{:S(2)}, u32[]{:S(2)}) collective-permute-start(bf16[512,256]{1,0:T(8,128)(2,1)} %param.2), channel_id=1, source_target_pairs={{0,16},{8,24},{16,0},{24,8},{1,17},{9,25},{17,1},{25,9},{2,18},{10... | collective-permute-start | bytes 786440 | tf_op jit(solution)/shard_map/ppermute | solution.py:10
  12.6 15.8 %collective-permute-start.7 = (bf16[512,256]{1,0:T(8,128)(2,1)S(1)}, bf16[512,256]{1,0:T(8,128)(2,1)S(1)}, u32[]{:S(2)}, u32[]{:S(2)}) collective-permute-start(bf16[512,256]{1,0:T(8,128)(2,1)S(1)} %copy-done), channel_id=1, source_target_pairs={{0,8},{8,0},{16,24},{24,16},{1,9},{9,1},{17,25},{25,17},{2,10},{10... | collective-permute-start | bytes 786440 | tf_op jit(solution)/shard_map/ppermute | solution.py:10
  14.4 14.2 %collective-permute-start.1 = (bf16[512,256]{1,0:T(8,128)(2,1)S(1)}, bf16[512,256]{1,0:T(8,128)(2,1)S(1)}, u32[]{:S(2)}, u32[]{:S(2)}) collective-permute-start(bf16[512,256]{1,0:T(8,128)(2,1)S(1)} %copy-done), channel_id=1, source_target_pairs={{0,1},{1,0},{2,3},{3,2},{4,5},{5,4},{6,7},{7,6},{8,9},{9,8},{10,11... | collective-permute-start | bytes 786440 | tf_op jit(solution)/shard_map/ppermute | solution.py:10
  18.6 12.8 %collective-permute-start.6 = (bf16[512,256]{1,0:T(8,128)(2,1)S(1)}, bf16[512,256]{1,0:T(8,128)(2,1)S(1)}, u32[]{:S(2)}, u32[]{:S(2)}) collective-permute-start(bf16[512,256]{1,0:T(8,128)(2,1)S(1)} %collective-permute-done), channel_id=1, source_target_pairs={{0,1},{1,0},{2,3},{3,2},{4,5},{5,4},{6,7},{7,6},{8,9},{9,8},{10,11... | collective-permute-start | bytes 786440 | tf_op jit(solution)/shard_map/ppermute | solution.py:10
  27.6 2.6 %collective-permute-start.3 = (bf16[512,256]{1,0:T(8,128)(2,1)}, bf16[512,256]{1,0:T(8,128)(2,1)S(1)}, u32[]{:S(2)}, u32[]{:S(2)}) collective-permute-start(bf16[512,256]{1,0:T(8,128)(2,1)} %collective-permute-done.2), channel_id=1, source_target_pairs={{0,1},{1,0},{2,3},{3,2},{4,5},{5,4},{6,7},{7,6},{8,9},{9,8},{10,11... | collective-permute-start | bytes 786440 | tf_op jit(solution)/shard_map/ppermute | solution.py:10
  27.6 3.2 %collective-permute-start.5 = (bf16[512,256]{1,0:T(8,128)(2,1)S(1)}, bf16[512,256]{1,0:T(8,128)(2,1)S(1)}, u32[]{:S(2)}, u32[]{:S(2)}) collective-permute-start(bf16[512,256]{1,0:T(8,128)(2,1)S(1)} %collective-permute-done.4), channel_id=1, source_target_pairs={{0,1},{1,0},{2,3},{3,2},{4,5},{5,4},{6,7},{7,6},{8,9},{9,8},{10,11... | collective-permute-start | bytes 786440 | tf_op jit(solution)/shard_map/ppermute | solution.py:10
  30.7 1.2 %copy-start.1 = (bf16[512,256]{1,0:T(8,128)(2,1)S(1)}, bf16[512,256]{1,0:T(8,128)(2,1)}, u32[]{:S(2)}) copy-start(bf16[512,256]{1,0:T(8,128)(2,1)} %get-tuple-element.8) | copy-start | bytes 786436
  32.6 9.2 %collective-permute-start.10 = (bf16[512,256]{1,0:T(8,128)(2,1)S(1)}, bf16[512,256]{1,0:T(8,128)(2,1)S(1)}, u32[]{:S(2)}, u32[]{:S(2)}) collective-permute-start(bf16[512,256]{1,0:T(8,128)(2,1)S(1)} %fusion.2), channel_id=1, source_target_pairs={{0,8},{8,0},{16,24},{24,16},{1,9},{9,1},{17,25},{25,17},{2,10},{10... | collective-permute-start | bytes 786440 | tf_op jit(solution)/shard_map/ppermute | solution.py:10
  34.2 13.6 %collective-permute-start.11 = (bf16[512,256]{1,0:T(8,128)(2,1)S(1)}, bf16[512,256]{1,0:T(8,128)(2,1)S(1)}, u32[]{:S(2)}, u32[]{:S(2)}) collective-permute-start(bf16[512,256]{1,0:T(8,128)(2,1)S(1)} %fusion.2), channel_id=1, source_target_pairs={{0,16},{8,24},{16,0},{24,8},{1,17},{9,25},{17,1},{25,9},{2,18},{10... | collective-permute-start | bytes 786440 | tf_op jit(solution)/shard_map/ppermute | solution.py:10
  35.7 12.0 %collective-permute-start.12 = (bf16[512,256]{1,0:T(8,128)(2,1)S(1)}, bf16[512,256]{1,0:T(8,128)(2,1)S(1)}, u32[]{:S(2)}, u32[]{:S(2)}) collective-permute-start(bf16[512,256]{1,0:T(8,128)(2,1)S(1)} %fusion.2), channel_id=1, source_target_pairs={{0,24},{8,16},{16,8},{24,0},{1,25},{9,17},{17,9},{25,1},{2,26},{10... | collective-permute-start | bytes 786440 | tf_op jit(solution)/shard_map/ppermute | solution.py:10

commit v26 on v23

--- a/solution.py
+++ b/solution.py
@@ -48,6 +48,15 @@
             raw[2 * k] = piece
             raw[2 * k + 1] = _swap(piece, "col", n_col, 1)
         row_pieces = [masked] + [mask_from(raw[t], row_index, col_index ^ t) for t in range(1, n_col)]
+        if n_col > 5:
+            early = [t for t in range(1, n_col) if t not in (4, 5)]
+            tied = lax.optimization_barrier(
+                (row_pieces[4], row_pieces[5], [row_pieces[t] for t in early], col_pieces)
+            )
+            row_pieces[4], row_pieces[5] = tied[0], tied[1]
+            for t, piece in zip(early, tied[2]):
+                row_pieces[t] = piece
+            col_pieces = list(tied[3])
 
         shift = col_index ^ (row_index * ratio)
         row_f = jnp.zeros((rows, n_col * cols), matrix_in.dtype)

time: 49.3 us -> 47.1 us (0.955)
  waiting for transfers between devices: 27.7 us -> 26 us
  other arithmetic: 3.89 us -> 2.7 us
  local copies, waits for them, and re-layouts: 3.22 us -> 3.95 us
    ppermute x13, waiting for transfers between devices: 27.7 us -> 26 us  [_swap(): return lax.ppermute(x, axis, [(i, i ^ d) for i in range(size)])]
    dynamic_update_slice x8 -> x1, other arithmetic: 2.29 us -> 0.78 us  [body(): row_f = lax.dynamic_update_slice_in_dim(row_f, piece, (t ^ shift) * cols, 1)]
    unnamed x4, local copies, waits for them, and re-layouts: 0.01 us -> 0.53 us
  transfers between devices with their start and end apart: 13 -> 13, of which waited for: 6 -> 6; matrix products, arithmetic and copies ran while one was open for 14% -> 12% of each run, Pallas kernels for 0% -> 0%
where the time goes in v26:
time: 47.1 us; the launch traced here: 46.8 us
  waiting for transfers between devices  26 us (55%)
  starting transfers between devices  11.5 us (24%)
  local copies, waits for them, and re-layouts  3.95 us (8%)
  other arithmetic  2.7 us (6%)
  matrix products  2.22 us (5%)
    ppermute x13, waiting for transfers between devices, _swap(): return lax.ppermute(x, axis, [(i, i ^ d) for i in range(size)])  26 us
    ppermute x13, starting transfers between devices, _swap(): return lax.ppermute(x, axis, [(i, i ^ d) for i in range(size)])  11.5 us
    mul x10, local copies, waits for them, and re-layouts, mask_from(): return (x4 * blocks[:, None, :, None]).reshape(rows, cols)  2.04 us
    dot_general x1, matrix products, body(): jnp.dot(row_f, jnp.concatenate(f_pieces, axis=0), preferred_element_type=...  1.51 us
  transfers between devices with their start and end apart: 13, of which 6 were waited for; matrix products, arithmetic and copies ran while one was open for 12% of the time, Pallas kernels for 0%

profile of v26, /device:TPU:16, one launch (start us, length us, event | category | flops | bytes accessed | tf_op | source)
XLA Modules:
  0.0 46.8 jit_solution(17165744130423185518)
XLA Ops:
  0.0 0.0 collective-permute-start
  0.0 1.8 %collective-permute-start.2 = (bf16[512,256]{1,0:T(8,128)(2,1)}, bf16[512,256]{1,0:T(8,128)(2,1)S(1)}, u32[]{:S(2)}, u32[]{:S(2)}) collective-permute-start(bf16[512,256]{1,0:T(8,128)(2,1)} %param.2), channel_id=1, source_target_pairs={{0,8},{8,0},{16,24},{24,16},{1,9},{9,1},{17,25},{25,17},{2,10},{10... | collective-permute-start | bytes 786440 | tf_op jit(solution)/shard_map/ppermute | solution.py:10
  1.8 1.6 %collective-permute-start.4 = (bf16[512,256]{1,0:T(8,128)(2,1)}, bf16[512,256]{1,0:T(8,128)(2,1)S(1)}, u32[]{:S(2)}, u32[]{:S(2)}) collective-permute-start(bf16[512,256]{1,0:T(8,128)(2,1)} %param.2), channel_id=1, source_target_pairs={{0,2},{1,3},{2,0},{3,1},{4,6},{5,7},{6,4},{7,5},{8,10},{9,11},{10,... | collective-permute-start | bytes 786440 | tf_op jit(solution)/shard_map/ppermute | solution.py:10
  3.4 1.6 %collective-permute-start.6 = (bf16[512,256]{1,0:T(8,128)(2,1)}, bf16[512,256]{1,0:T(8,128)(2,1)S(1)}, u32[]{:S(2)}, u32[]{:S(2)}) collective-permute-start(bf16[512,256]{1,0:T(8,128)(2,1)} %param.2), channel_id=1, source_target_pairs={{0,6},{1,7},{2,4},{3,5},{4,2},{5,3},{6,0},{7,1},{8,14},{9,15},{10,... | collective-permute-start | bytes 786440 | tf_op jit(solution)/shard_map/ppermute | solution.py:10
  5.0 1.5 %collective-permute-start.8 = (bf16[512,256]{1,0:T(8,128)(2,1)}, bf16[512,256]{1,0:T(8,128)(2,1)S(1)}, u32[]{:S(2)}, u32[]{:S(2)}) collective-permute-start(bf16[512,256]{1,0:T(8,128)(2,1)} %param.2), channel_id=1, source_target_pairs={{0,16},{8,24},{16,0},{24,8},{1,17},{9,25},{17,1},{25,9},{2,18},{10... | collective-permute-start | bytes 786440 | tf_op jit(solution)/shard_map/ppermute | solution.py:10
  6.5 0.7 %convert_element_type.27 = bf16[16,16]{1,0:T(8,128)(2,1)S(1)} convert(s32[16,16]{1,0:T(8,128)} %param.3) | non-fusion elementwise | flops 256 | bytes 1536 | tf_op jit(solution)/shard_map/convert_element_type | solution.py:28
  7.2 0.8 %dynamic-slice_convert_fusion = (f32[4,2]{1,0:T(4,128)S(1)}, bf16[4,2]{1,0:T(4,128)(2,1)S(1)}) fusion(s32[16,16]{1,0:T(8,128)} %param.3, s32[]{:T(128)S(6)} %select_n.70, s32[]{:T(128)S(6)} %select_n.71), kind=kLoop, calls=%fused_computation.38 | loop fusion | flops 16 | bytes 88 | tf_op jit(solution)/shard_map/convert_element_type | solution.py:68
  8.0 0.0 copy-start
  8.0 0.6 %broadcast_in_dim.7 = bf16[512,2,128]{2,1,0:T(2,128)(2,1)S(1)} broadcast(bf16[512,2]{1,0:T(8,128)(2,1)S(1)} %bitcast.63), dimensions={0,1} | broadcast | bytes 264192 | tf_op jit(solution)/shard_map/broadcast_in_dim | solution.py:26
  8.6 0.2 broadcast_in_dim.8
  8.8 0.1 copy-done
  8.9 0.8 %constant_dynamic-update-slice_fusion.7 = (bf16[512,2048]{1,0:T(8,128)(2,1)S(1)}, bf16[512,256]{1,0:T(8,128)(2,1)}) fusion(bf16[512,2048]{1,0:T(8,128)(2,1)S(1)} %broadcast_in_dim.8, s32[]{:T(128)S(6)} %select_n.72, bf16[512,256]{1,0:T(8,128)(2,1)S(1)} %copy-done, bf16[64,8,2,128]{3,2,1,0:T(2,128)(2,1)S(1)} %bitcast.62), kind=kLoop, calls=%fused_computation.37 | loop fusion | flops 524288 | bytes 1048580 | tf_op jit(solution)/shard_map/dynamic_update_slice | solution.py:64
  9.7 0.1 fusion.19
  9.8 0.0 collective-permute-done.2
  9.8 0.9 %collective-permute-start.9 = (bf16[512,256]{1,0:T(8,128)(2,1)}, bf16[512,256]{1,0:T(8,128)(2,1)S(1)}, u32[]{:S(2)}, u32[]{:S(2)}) collective-permute-start(bf16[512,256]{1,0:T(8,128)(2,1)} %param.2), channel_id=1, source_target_pairs={{0,24},{8,16},{16,8},{24,0},{1,25},{9,17},{17,9},{25,1},{2,26},{10... | collective-permute-start | bytes 786440 | tf_op jit(solution)/shard_map/ppermute | solution.py:10
  10.8 0.2 mul.252
  11.0 0.1 bitcast_multiply_fusion.2
  11.0 2.0 %collective-permute-done = bf16[512,256]{1,0:T(8,128)(2,1)S(1)} collective-permute-done((bf16[512,256]{1,0:T(8,128)(2,1)}, bf16[512,256]{1,0:T(8,128)(2,1)S(1)}, u32[]{:S(2)}, u32[]{:S(2)}) %collective-permute-start) | collective-permute-done | bytes 262176 | tf_op jit(solution)/shard_map/ppermute | solution.py:10
  13.0 0.0 collective-permute-start.3
  13.0 0.2 mul.224
  13.2 0.1 bitcast_multiply_fusion.9
  13.3 6.7 %collective-permute-done.4 = bf16[512,256]{1,0:T(8,128)(2,1)S(1)} collective-permute-done((bf16[512,256]{1,0:T(8,128)(2,1)}, bf16[512,256]{1,0:T(8,128)(2,1)S(1)}, u32[]{:S(2)}, u32[]{:S(2)}) %collective-permute-start.4) | collective-permute-done | bytes 262176 | tf_op jit(solution)/shard_map/ppermute | solution.py:10
  20.0 0.0 collective-permute-start.1
  20.0 0.2 mul.236
  20.2 0.1 bitcast_multiply_fusion.6
  20.2 5.8 %collective-permute-done.6 = bf16[512,256]{1,0:T(8,128)(2,1)S(1)} collective-permute-done((bf16[512,256]{1,0:T(8,128)(2,1)}, bf16[512,256]{1,0:T(8,128)(2,1)S(1)}, u32[]{:S(2)}, u32[]{:S(2)}) %collective-permute-start.6) | collective-permute-done | bytes 262176 | tf_op jit(solution)/shard_map/ppermute | solution.py:10
  26.1 0.0 collective-permute-start.5
  26.1 0.2 mul.244
  26.3 0.1 bitcast_multiply_fusion.4
  26.3 0.0 collective-permute-done.8
  26.3 0.6 %collective-permute-start.7 = (bf16[512,256]{1,0:T(8,128)(2,1)S(1)}, bf16[512,256]{1,0:T(8,128)(2,1)S(1)}, u32[]{:S(2)}, u32[]{:S(2)}) collective-permute-start(bf16[512,256]{1,0:T(8,128)(2,1)S(1)} %collective-permute-done.6), channel_id=1, source_target_pairs={{0,1},{1,0},{2,3},{3,2},{4,5},{5,4},{6,7},{7,6},{8,9},{9,8},{10,11... | collective-permute-start | bytes 786440 | tf_op jit(solution)/shard_map/ppermute | solution.py:10
  26.9 0.2 mul.256
  27.1 0.1 bitcast_multiply_fusion.1
  27.2 0.0 collective-permute-done.9
  27.2 0.2 mul.260
  27.4 0.0 collective-permute-done.1
  27.4 0.2 mul.228
  27.7 0.0 collective-permute-done.3
  27.7 0.2 mul.232
  28.0 0.0 collective-permute-done.5
  28.0 0.2 mul.240
  28.2 0.0 collective-permute-done.7
  28.3 0.2 mul.248
  28.5 0.0 copy-start.1
  28.8 0.2 mul.270
  29.0 0.5 copy-done.1
  29.5 0.7 %fusion.2 = bf16[512,256]{1,0:T(8,128)(2,1)S(1)} fusion(bf16[512,2048]{1,0:T(8,128)(2,1)S(1)} %constant_dynamic-update-slice_fusion, bf16[512,256]{1,0:T(8,128)(2,1)S(1)} %bitcast_multiply_fusion, bf16[512,256]{1,0:T(8,128)(2,1)S(1)} %bitcast_multiply_fusion.1, bf16[512,256]{1,0:T(8,128)(2,1)S(1)} %bitcast_multiply_fusion.2, ...), kind=kOutput, calls=%fused_computation.4 | convolution fusion | flops 541327360 | bytes 3932160 | tf_op jit(solution)/shard_map/dot_general | solution.py:65
  30.2 2.5 %collective-permute-start.12 = (bf16[512,256]{1,0:T(8,128)(2,1)S(1)}, bf16[512,256]{1,0:T(8,128)(2,1)S(1)}, u32[]{:S(2)}, u32[]{:S(2)}) collective-permute-start(bf16[512,256]{1,0:T(8,128)(2,1)S(1)} %fusion.2), channel_id=1, source_target_pairs={{0,24},{8,16},{16,8},{24,0},{1,25},{9,17},{17,9},{25,1},{2,26},{10... | collective-permute-start | bytes 786440 | tf_op jit(solution)/shard_map/ppermute | solution.py:10
  32.6 0.5 %collective-permute-start.11 = (bf16[512,256]{1,0:T(8,128)(2,1)S(1)}, bf16[512,256]{1,0:T(8,128)(2,1)S(1)}, u32[]{:S(2)}, u32[]{:S(2)}) collective-permute-start(bf16[512,256]{1,0:T(8,128)(2,1)S(1)} %fusion.2), channel_id=1, source_target_pairs={{0,16},{8,24},{16,0},{24,8},{1,17},{9,25},{17,1},{25,9},{2,18},{10... | collective-permute-start | bytes 786440 | tf_op jit(solution)/shard_map/ppermute | solution.py:10
  33.2 0.6 %collective-permute-start.10 = (bf16[512,256]{1,0:T(8,128)(2,1)S(1)}, bf16[512,256]{1,0:T(8,128)(2,1)S(1)}, u32[]{:S(2)}, u32[]{:S(2)}) collective-permute-start(bf16[512,256]{1,0:T(8,128)(2,1)S(1)} %fusion.2), channel_id=1, source_target_pairs={{0,8},{8,0},{16,24},{24,16},{1,9},{9,1},{17,25},{25,17},{2,10},{10... | collective-permute-start | bytes 786440 | tf_op jit(solution)/shard_map/ppermute | solution.py:10
  33.7 6.6 %collective-permute-done.12 = bf16[512,256]{1,0:T(8,128)(2,1)S(1)} collective-permute-done((bf16[512,256]{1,0:T(8,128)(2,1)S(1)}, bf16[512,256]{1,0:T(8,128)(2,1)S(1)}, u32[]{:S(2)}, u32[]{:S(2)}) %collective-permute-start.12) | collective-permute-done | bytes 262176 | tf_op jit(solution)/shard_map/ppermute | solution.py:10
  40.3 4.8 %collective-permute-done.11 = bf16[512,256]{1,0:T(8,128)(2,1)S(1)} collective-permute-done((bf16[512,256]{1,0:T(8,128)(2,1)S(1)}, bf16[512,256]{1,0:T(8,128)(2,1)S(1)}, u32[]{:S(2)}, u32[]{:S(2)}) %collective-permute-start.11) | collective-permute-done | bytes 262176 | tf_op jit(solution)/shard_map/ppermute | solution.py:10
  45.2 0.1 collective-permute-done.10
  45.3 1.5 %fusion.1 = f32[512,256]{1,0:T(8,128)} fusion(bf16[512,2048]{1,0:T(8,128)(2,1)S(1)} %constant_dynamic-update-slice_fusion, bf16[512,256]{1,0:T(8,128)(2,1)S(1)} %collective-permute-done.12, bf16[512,256]{1,0:T(8,128)(2,1)S(1)} %collective-permute-done.11, bf16[512,256]{1,0:T(8,128)(2,1)S(1)} %collective-permute-done.10, bf16[512,256]{1,0:T(8,128)(2,1)S(1)} %fusion.2, ...), kind=kOutput, calls=%fused_computation.3 | convolution fusion | flops 541720576 | bytes 4456448 | tf_op jit(solution)/shard_map/dot_general | solution.py:75
  (13 shorter events, 0.4 us)
Async XLA Ops:
  0.0 13.0 %collective-permute-start = (bf16[512,256]{1,0:T(8,128)(2,1)}, bf16[512,256]{1,0:T(8,128)(2,1)S(1)}, u32[]{:S(2)}, u32[]{:S(2)}) collective-permute-start(bf16[512,256]{1,0:T(8,128)(2,1)} %param.2), channel_id=1, source_target_pairs={{0,4},{1,5},{2,6},{3,7},{4,0},{5,1},{6,2},{7,3},{8,12},{9,13},{10,... | collective-permute-start | bytes 786440 | tf_op jit(solution)/shard_map/ppermute | solution.py:10
  0.0 9.8 %collective-permute-start.2 = (bf16[512,256]{1,0:T(8,128)(2,1)}, bf16[512,256]{1,0:T(8,128)(2,1)S(1)}, u32[]{:S(2)}, u32[]{:S(2)}) collective-permute-start(bf16[512,256]{1,0:T(8,128)(2,1)} %param.2), channel_id=1, source_target_pairs={{0,8},{8,0},{16,24},{24,16},{1,9},{9,1},{17,25},{25,17},{2,10},{10... | collective-permute-start | bytes 786440 | tf_op jit(solution)/shard_map/ppermute | solution.py:10
  1.8 18.1 %collective-permute-start.4 = (bf16[512,256]{1,0:T(8,128)(2,1)}, bf16[512,256]{1,0:T(8,128)(2,1)S(1)}, u32[]{:S(2)}, u32[]{:S(2)}) collective-permute-start(bf16[512,256]{1,0:T(8,128)(2,1)} %param.2), channel_id=1, source_target_pairs={{0,2},{1,3},{2,0},{3,1},{4,6},{5,7},{6,4},{7,5},{8,10},{9,11},{10,... | collective-permute-start | bytes 786440 | tf_op jit(solution)/shard_map/ppermute | solution.py:10
  3.4 22.7 %collective-permute-start.6 = (bf16[512,256]{1,0:T(8,128)(2,1)}, bf16[512,256]{1,0:T(8,128)(2,1)S(1)}, u32[]{:S(2)}, u32[]{:S(2)}) collective-permute-start(bf16[512,256]{1,0:T(8,128)(2,1)} %param.2), channel_id=1, source_target_pairs={{0,6},{1,7},{2,4},{3,5},{4,2},{5,3},{6,0},{7,1},{8,14},{9,15},{10,... | collective-permute-start | bytes 786440 | tf_op jit(solution)/shard_map/ppermute | solution.py:10
  5.0 21.4 %collective-permute-start.8 = (bf16[512,256]{1,0:T(8,128)(2,1)}, bf16[512,256]{1,0:T(8,128)(2,1)S(1)}, u32[]{:S(2)}, u32[]{:S(2)}) collective-permute-start(bf16[512,256]{1,0:T(8,128)(2,1)} %param.2), channel_id=1, source_target_pairs={{0,16},{8,24},{16,0},{24,8},{1,17},{9,25},{17,1},{25,9},{2,18},{10... | collective-permute-start | bytes 786440 | tf_op jit(solution)/shard_map/ppermute | solution.py:10
  8.0 0.9 %copy-start = (bf16[512,256]{1,0:T(8,128)(2,1)S(1)}, bf16[512,256]{1,0:T(8,128)(2,1)}, u32[]{:S(2)}) copy-start(bf16[512,256]{1,0:T(8,128)(2,1)} %param.2) | copy-start | bytes 786436
  9.8 17.3 %collective-permute-start.9 = (bf16[512,256]{1,0:T(8,128)(2,1)}, bf16[512,256]{1,0:T(8,128)(2,1)S(1)}, u32[]{:S(2)}, u32[]{:S(2)}) collective-permute-start(bf16[512,256]{1,0:T(8,128)(2,1)} %param.2), channel_id=1, source_target_pairs={{0,24},{8,16},{16,8},{24,0},{1,25},{9,17},{17,9},{25,1},{2,26},{10... | collective-permute-start | bytes 786440 | tf_op jit(solution)/shard_map/ppermute | solution.py:10
  13.0 14.7 %collective-permute-start.3 = (bf16[512,256]{1,0:T(8,128)(2,1)}, bf16[512,256]{1,0:T(8,128)(2,1)S(1)}, u32[]{:S(2)}, u32[]{:S(2)}) collective-permute-start(bf16[512,256]{1,0:T(8,128)(2,1)} %param.2), channel_id=1, source_target_pairs={{0,1},{1,0},{2,3},{3,2},{4,5},{5,4},{6,7},{7,6},{8,9},{9,8},{10,11... | collective-permute-start | bytes 786440 | tf_op jit(solution)/shard_map/ppermute | solution.py:10
  20.0 7.5 %collective-permute-start.1 = (bf16[512,256]{1,0:T(8,128)(2,1)S(1)}, bf16[512,256]{1,0:T(8,128)(2,1)S(1)}, u32[]{:S(2)}, u32[]{:S(2)}) collective-permute-start(bf16[512,256]{1,0:T(8,128)(2,1)S(1)} %collective-permute-done), channel_id=1, source_target_pairs={{0,1},{1,0},{2,3},{3,2},{4,5},{5,4},{6,7},{7,6},{8,9},{9,8},{10,11... | collective-permute-start | bytes 786440 | tf_op jit(solution)/shard_map/ppermute | solution.py:10
  26.1 1.9 %collective-permute-start.5 = (bf16[512,256]{1,0:T(8,128)(2,1)S(1)}, bf16[512,256]{1,0:T(8,128)(2,1)S(1)}, u32[]{:S(2)}, u32[]{:S(2)}) collective-permute-start(bf16[512,256]{1,0:T(8,128)(2,1)S(1)} %collective-permute-done.4), channel_id=1, source_target_pairs={{0,1},{1,0},{2,3},{3,2},{4,5},{5,4},{6,7},{7,6},{8,9},{9,8},{10,11... | collective-permute-start | bytes 786440 | tf_op jit(solution)/shard_map/ppermute | solution.py:10
  26.3 1.9 %collective-permute-start.7 = (bf16[512,256]{1,0:T(8,128)(2,1)S(1)}, bf16[512,256]{1,0:T(8,128)(2,1)S(1)}, u32[]{:S(2)}, u32[]{:S(2)}) collective-permute-start(bf16[512,256]{1,0:T(8,128)(2,1)S(1)} %collective-permute-done.6), channel_id=1, source_target_pairs={{0,1},{1,0},{2,3},{3,2},{4,5},{5,4},{6,7},{7,6},{8,9},{9,8},{10,11... | collective-permute-start | bytes 786440 | tf_op jit(solution)/shard_map/ppermute | solution.py:10
  28.5 1.0 %copy-start.1 = (bf16[512,256]{1,0:T(8,128)(2,1)S(1)}, bf16[512,256]{1,0:T(8,128)(2,1)}, u32[]{:S(2)}) copy-start(bf16[512,256]{1,0:T(8,128)(2,1)} %get-tuple-element.25) | copy-start | bytes 786436
  30.2 10.2 %collective-permute-start.12 = (bf16[512,256]{1,0:T(8,128)(2,1)S(1)}, bf16[512,256]{1,0:T(8,128)(2,1)S(1)}, u32[]{:S(2)}, u32[]{:S(2)}) collective-permute-start(bf16[512,256]{1,0:T(8,128)(2,1)S(1)} %fusion.2), channel_id=1, source_target_pairs={{0,24},{8,16},{16,8},{24,0},{1,25},{9,17},{17,9},{25,1},{2,26},{10... | collective-permute-start | bytes 786440 | tf_op jit(solution)/shard_map/ppermute | solution.py:10
  32.6 12.5 %collective-permute-start.11 = (bf16[512,256]{1,0:T(8,128)(2,1)S(1)}, bf16[512,256]{1,0:T(8,128)(2,1)S(1)}, u32[]{:S(2)}, u32[]{:S(2)}) collective-permute-start(bf16[512,256]{1,0:T(8,128)(2,1)S(1)} %fusion.2), channel_id=1, source_target_pairs={{0,16},{8,24},{16,0},{24,8},{1,17},{9,25},{17,1},{25,9},{2,18},{10... | collective-permute-start | bytes 786440 | tf_op jit(solution)/shard_map/ppermute | solution.py:10
  33.2 12.1 %collective-permute-start.10 = (bf16[512,256]{1,0:T(8,128)(2,1)S(1)}, bf16[512,256]{1,0:T(8,128)(2,1)S(1)}, u32[]{:S(2)}, u32[]{:S(2)}) collective-permute-start(bf16[512,256]{1,0:T(8,128)(2,1)S(1)} %fusion.2), channel_id=1, source_target_pairs={{0,8},{8,0},{16,24},{24,16},{1,9},{9,1},{17,25},{25,17},{2,10},{10... | collective-permute-start | bytes 786440 | tf_op jit(solution)/shard_map/ppermute | solution.py:10

commit v27 on v23

--- a/solution.py
+++ b/solution.py
@@ -48,14 +48,21 @@
             raw[2 * k] = piece
             raw[2 * k + 1] = _swap(piece, "col", n_col, 1)
         row_pieces = [masked] + [mask_from(raw[t], row_index, col_index ^ t) for t in range(1, n_col)]
-
         shift = col_index ^ (row_index * ratio)
+        col_cat = jnp.concatenate(col_pieces, axis=0)
         row_f = jnp.zeros((rows, n_col * cols), matrix_in.dtype)
-        for t, piece in enumerate(row_pieces):
-            row_f = lax.dynamic_update_slice_in_dim(row_f, piece, (t ^ shift) * cols, 1)
-        square = jnp.dot(
-            row_f, jnp.concatenate(col_pieces, axis=0), preferred_element_type=jnp.float32
-        )
+        last = [t for t in (4, 5) if n_col > 5]
+        for t in range(n_col):
+            if t not in last:
+                row_f = lax.dynamic_update_slice_in_dim(row_f, row_pieces[t], (t ^ shift) * cols, 1)
+        square = jnp.dot(row_f, col_cat, preferred_element_type=jnp.float32)
+        if last:
+            tied = lax.optimization_barrier(([row_pieces[t] for t in last], row_f, square))
+            row_f, square = tied[1], tied[2]
+            for t, piece in zip(last, tied[0]):
+                rows_t = lax.dynamic_slice_in_dim(col_cat, (t ^ shift) * cols, cols, 0)
+                square = square + jnp.dot(piece, rows_t, preferred_element_type=jnp.float32)
+                row_f = lax.dynamic_update_slice_in_dim(row_f, piece, (t ^ shift) * cols, 1)
         blocks_float = local_blocks.astype(jnp.float32)[:, None, :, None]
 
         def mask_local(x):

time: 49.3 us -> 49.3 us (level)
  waiting for transfers between devices: 27.7 us -> 25.7 us
  starting transfers between devices: 11.7 us -> 12.7 us
    ppermute x13, waiting for transfers between devices: 27.7 us -> 25.7 us  [_swap(): return lax.ppermute(x, axis, [(i, i ^ d) for i in range(size)])]
    ppermute x13, starting transfers between devices: 11.7 us -> 12.7 us  [_swap(): return lax.ppermute(x, axis, [(i, i ^ d) for i in range(size)])]
    dot_general x1 -> x3, matrix products: 0.72 us -> 1.17 us  [the longest x1 0.72 us: body(): square = jnp.dot(row_f, col_cat, preferred_element_type=jnp.float32)]
    dynamic_update_slice x8 -> x6, other arithmetic: 2.29 us -> 2.4 us  [body(): lax.dynamic_update_slice_in_dim(row_f, row_pieces[t], (t ^ shift) * cols, 1)]
  transfers between devices with their start and end apart: 13 -> 13, of which waited for: 6 -> 6; matrix products, arithmetic and copies ran while one was open for 14% -> 16% of each run, Pallas kernels for 0% -> 0%
where the time goes in v27:
time: 49.3 us; the launch traced here: 49 us
  waiting for transfers between devices  25.7 us (52%)
  starting transfers between devices  12.7 us (26%)
  other arithmetic  4.33 us (9%)
  local copies, waits for them, and re-layouts  3.28 us (7%)
  matrix products  2.69 us (5%)
    ppermute x13, waiting for transfers between devices, _swap(): return lax.ppermute(x, axis, [(i, i ^ d) for i in range(size)])  25.7 us
    ppermute x13, starting transfers between devices, _swap(): return lax.ppermute(x, axis, [(i, i ^ d) for i in range(size)])  12.7 us
    dynamic_update_slice x6, other arithmetic, body(): lax.dynamic_update_slice_in_dim(row_f, row_pieces[t], (t ^ shift) * cols, 1)  2.4 us
    mul x10, local copies, waits for them, and re-layouts, mask_from(): return (x4 * blocks[:, None, :, None]).reshape(rows, cols)  2.05 us
    dot_general x1, matrix products, body(): jnp.dot(row_f, jnp.concatenate(f_pieces, axis=0), preferred_element_type=...  1.52 us
  transfers between devices with their start and end apart: 13, of which 6 were waited for; matrix products, arithmetic and copies ran while one was open for 16% of the time, Pallas kernels for 0%

profile of v27, /device:TPU:16, one launch (start us, length us, event | category | flops | bytes accessed | tf_op | source)
XLA Modules:
  0.0 49.0 jit_solution(12119378818434741124)
XLA Ops:
  0.0 0.0 copy-start
  0.0 0.0 collective-permute-start
  0.0 1.8 %collective-permute-start.2 = (bf16[512,256]{1,0:T(8,128)(2,1)}, bf16[512,256]{1,0:T(8,128)(2,1)S(1)}, u32[]{:S(2)}, u32[]{:S(2)}) collective-permute-start(bf16[512,256]{1,0:T(8,128)(2,1)} %param.2), channel_id=1, source_target_pairs={{0,8},{8,0},{16,24},{24,16},{1,9},{9,1},{17,25},{25,17},{2,10},{10... | collective-permute-start | bytes 786440 | tf_op jit(solution)/shard_map/ppermute | solution.py:10
  1.8 1.6 %collective-permute-start.4 = (bf16[512,256]{1,0:T(8,128)(2,1)}, bf16[512,256]{1,0:T(8,128)(2,1)}, u32[]{:S(2)}, u32[]{:S(2)}) collective-permute-start(bf16[512,256]{1,0:T(8,128)(2,1)} %param.2), channel_id=1, source_target_pairs={{0,2},{1,3},{2,0},{3,1},{4,6},{5,7},{6,4},{7,5},{8,10},{9,11},{10,... | collective-permute-start | bytes 786440 | tf_op jit(solution)/shard_map/ppermute | solution.py:10
  3.4 1.6 %collective-permute-start.6 = (bf16[512,256]{1,0:T(8,128)(2,1)}, bf16[512,256]{1,0:T(8,128)(2,1)}, u32[]{:S(2)}, u32[]{:S(2)}) collective-permute-start(bf16[512,256]{1,0:T(8,128)(2,1)} %param.2), channel_id=1, source_target_pairs={{0,6},{1,7},{2,4},{3,5},{4,2},{5,3},{6,0},{7,1},{8,14},{9,15},{10,... | collective-permute-start | bytes 786440 | tf_op jit(solution)/shard_map/ppermute | solution.py:10
  5.0 1.5 %collective-permute-start.9 = (bf16[512,256]{1,0:T(8,128)(2,1)}, bf16[512,256]{1,0:T(8,128)(2,1)S(1)}, u32[]{:S(2)}, u32[]{:S(2)}) collective-permute-start(bf16[512,256]{1,0:T(8,128)(2,1)} %param.2), channel_id=1, source_target_pairs={{0,24},{8,16},{16,8},{24,0},{1,25},{9,17},{17,9},{25,1},{2,26},{10... | collective-permute-start | bytes 786440 | tf_op jit(solution)/shard_map/ppermute | solution.py:10
  6.5 0.7 %convert_element_type.27 = bf16[16,16]{1,0:T(8,128)(2,1)S(1)} convert(s32[16,16]{1,0:T(8,128)} %param.3) | non-fusion elementwise | flops 256 | bytes 1536 | tf_op jit(solution)/shard_map/convert_element_type | solution.py:28
  7.2 0.8 %dynamic-slice_convert_fusion = (f32[4,2]{1,0:T(4,128)S(1)}, bf16[4,2]{1,0:T(4,128)(2,1)S(1)}) fusion(s32[16,16]{1,0:T(8,128)} %param.3, s32[]{:T(128)S(6)} %select_n.72, s32[]{:T(128)S(6)} %select_n.73), kind=kLoop, calls=%fused_computation.38 | loop fusion | flops 16 | bytes 88 | tf_op jit(solution)/shard_map/convert_element_type | solution.py:66
  8.0 0.6 %broadcast_in_dim.7 = bf16[512,2,128]{2,1,0:T(2,128)(2,1)S(1)} broadcast(bf16[512,2]{1,0:T(8,128)(2,1)S(1)} %bitcast.79), dimensions={0,1} | broadcast | bytes 264192 | tf_op jit(solution)/shard_map/broadcast_in_dim | solution.py:26
  8.6 0.2 broadcast_in_dim.8
  8.8 0.0 copy-done
  8.8 0.1 constant_dynamic-update-slice_fusion.2
  8.9 0.1 fusion.23
  9.1 0.0 collective-permute-done.2
  9.1 2.2 %collective-permute-start.8 = (bf16[512,256]{1,0:T(8,128)(2,1)S(1)}, bf16[512,256]{1,0:T(8,128)(2,1)S(1)}, u32[]{:S(2)}, u32[]{:S(2)}) collective-permute-start(bf16[512,256]{1,0:T(8,128)(2,1)S(1)} %copy-done), channel_id=1, source_target_pairs={{0,16},{8,24},{16,0},{24,8},{1,17},{9,25},{17,1},{25,9},{2,18},{10... | collective-permute-start | bytes 786440 | tf_op jit(solution)/shard_map/ppermute | solution.py:10
  11.3 0.2 mul.259
  11.5 0.1 bitcast_multiply_fusion.3
  11.6 1.6 %collective-permute-done = bf16[512,256]{1,0:T(8,128)(2,1)S(1)} collective-permute-done((bf16[512,256]{1,0:T(8,128)(2,1)}, bf16[512,256]{1,0:T(8,128)(2,1)S(1)}, u32[]{:S(2)}, u32[]{:S(2)}) %collective-permute-start) | collective-permute-done | bytes 262176 | tf_op jit(solution)/shard_map/ppermute | solution.py:10
  13.1 0.0 collective-permute-start.3
  13.1 0.2 mul.224
  13.3 0.1 bitcast_multiply_fusion.10
  13.4 6.6 %collective-permute-done.4 = bf16[512,256]{1,0:T(8,128)(2,1)} collective-permute-done((bf16[512,256]{1,0:T(8,128)(2,1)}, bf16[512,256]{1,0:T(8,128)(2,1)}, u32[]{:S(2)}, u32[]{:S(2)}) %collective-permute-start.4) | collective-permute-done | bytes 262176 | tf_op jit(solution)/shard_map/ppermute | solution.py:10
  20.0 0.0 collective-permute-start.1
  20.0 6.2 %collective-permute-done.6 = bf16[512,256]{1,0:T(8,128)(2,1)} collective-permute-done((bf16[512,256]{1,0:T(8,128)(2,1)}, bf16[512,256]{1,0:T(8,128)(2,1)}, u32[]{:S(2)}, u32[]{:S(2)}) %collective-permute-start.6) | collective-permute-done | bytes 262176 | tf_op jit(solution)/shard_map/ppermute | solution.py:10
  26.2 0.0 collective-permute-start.5
  26.2 0.0 collective-permute-done.9
  26.2 0.5 %collective-permute-start.7 = (bf16[512,256]{1,0:T(8,128)(2,1)}, bf16[512,256]{1,0:T(8,128)(2,1)S(1)}, u32[]{:S(2)}, u32[]{:S(2)}) collective-permute-start(bf16[512,256]{1,0:T(8,128)(2,1)} %collective-permute-done.6), channel_id=1, source_target_pairs={{0,1},{1,0},{2,3},{3,2},{4,5},{5,4},{6,7},{7,6},{8,9},{9,8},{10,11... | collective-permute-start | bytes 786440 | tf_op jit(solution)/shard_map/ppermute | solution.py:10
  26.7 0.2 mul.267
  26.9 0.1 bitcast_multiply_fusion.1
  26.9 0.0 collective-permute-done.8
  27.0 0.2 mul.263
  27.2 0.1 bitcast_multiply_fusion.2
  27.2 0.1 pad_maximum_fusion
  27.3 0.0 collective-permute-done.3
  27.3 0.2 mul.234
  27.5 0.1 fusion.14
  27.6 0.2 mul.239
  27.8 1.0 %fusion.13 = bf16[512,2048]{1,0:T(8,128)(2,1)S(1)} fusion(bf16[512,2048]{1,0:T(8,128)(2,1)S(1)} %fusion.14, s32[]{:T(128)S(6)} %select_n.80, bf16[512,256]{1,0:T(8,128)(2,1)} %collective-permute-done.4, bf16[64,8,2,128]{3,2,1,0:T(2,128)(2,1)S(1)} %bitcast.77), kind=kLoop, calls=%fused_computation.23 | loop fusion | flops 524288 | bytes 786436 | tf_op jit(solution)/shard_map/dynamic_update_slice | solution.py:57
  28.8 0.0 collective-permute-done.5
  28.9 0.2 mul.244
  29.1 0.1 fusion.12
  29.2 0.2 mul.249
  29.4 1.0 %fusion.11 = bf16[512,2048]{1,0:T(8,128)(2,1)S(1)} fusion(bf16[512,2048]{1,0:T(8,128)(2,1)S(1)} %fusion.12, s32[]{:T(128)S(6)} %select_n.84, bf16[512,256]{1,0:T(8,128)(2,1)} %collective-permute-done.6, bf16[64,8,2,128]{3,2,1,0:T(2,128)(2,1)S(1)} %bitcast.78), kind=kLoop, calls=%fused_computation.19 | loop fusion | flops 524288 | bytes 786436 | tf_op jit(solution)/shard_map/dynamic_update_slice | solution.py:57
  30.4 0.0 collective-permute-done.7
  30.4 0.2 mul.254
  30.6 0.1 fusion.10
  30.7 0.7 %fusion.22 = f32[512,256]{1,0:T(8,128)S(1)} fusion(bf16[512,2048]{1,0:T(8,128)(2,1)S(1)} %fusion.10, bf16[512,256]{1,0:T(8,128)(2,1)S(1)} %bitcast_multiply_fusion.1, bf16[512,256]{1,0:T(8,128)(2,1)S(1)} %bitcast_multiply_fusion.2, bf16[512,256]{1,0:T(8,128)(2,1)S(1)} %bitcast_multiply_fusion.3, bf16[512,256]{1,0:T(8,128)(2,1)S(1)} %get-tuple-element.16), kind=kOutput, calls=%fused_computation.41 | convolution fusion | flops 541065216 | bytes 3670016 | tf_op jit(solution)/shard_map/dot_general | solution.py:58
  31.4 0.0 collective-permute-done.1
  31.5 0.2 mul.228
  31.7 0.1 bitcast_multiply_fusion.9
  31.7 0.2 fusion.15
  32.0 0.2 fusion.17
  32.2 0.2 mul.272
  32.4 0.1 fusion.9
  32.5 2.5 %collective-permute-start.12 = (bf16[512,256]{1,0:T(8,128)(2,1)S(1)}, bf16[512,256]{1,0:T(8,128)(2,1)S(1)}, u32[]{:S(2)}, u32[]{:S(2)}) collective-permute-start(bf16[512,256]{1,0:T(8,128)(2,1)S(1)} %fusion.9), channel_id=1, source_target_pairs={{0,24},{8,16},{16,8},{24,0},{1,25},{9,17},{17,9},{25,1},{2,26},{10... | collective-permute-start | bytes 786440 | tf_op jit(solution)/shard_map/ppermute | solution.py:10
  35.0 0.5 %collective-permute-start.11 = (bf16[512,256]{1,0:T(8,128)(2,1)S(1)}, bf16[512,256]{1,0:T(8,128)(2,1)S(1)}, u32[]{:S(2)}, u32[]{:S(2)}) collective-permute-start(bf16[512,256]{1,0:T(8,128)(2,1)S(1)} %fusion.9), channel_id=1, source_target_pairs={{0,16},{8,24},{16,0},{24,8},{1,17},{9,25},{17,1},{25,9},{2,18},{10... | collective-permute-start | bytes 786440 | tf_op jit(solution)/shard_map/ppermute | solution.py:10
  35.5 0.6 %collective-permute-start.10 = (bf16[512,256]{1,0:T(8,128)(2,1)S(1)}, bf16[512,256]{1,0:T(8,128)(2,1)S(1)}, u32[]{:S(2)}, u32[]{:S(2)}) collective-permute-start(bf16[512,256]{1,0:T(8,128)(2,1)S(1)} %fusion.9), channel_id=1, source_target_pairs={{0,8},{8,0},{16,24},{24,16},{1,9},{9,1},{17,25},{25,17},{2,10},{10... | collective-permute-start | bytes 786440 | tf_op jit(solution)/shard_map/ppermute | solution.py:10
  36.2 6.6 %collective-permute-done.12 = bf16[512,256]{1,0:T(8,128)(2,1)S(1)} collective-permute-done((bf16[512,256]{1,0:T(8,128)(2,1)S(1)}, bf16[512,256]{1,0:T(8,128)(2,1)S(1)}, u32[]{:S(2)}, u32[]{:S(2)}) %collective-permute-start.12) | collective-permute-done | bytes 262176 | tf_op jit(solution)/shard_map/ppermute | solution.py:10
  42.7 4.6 %collective-permute-done.11 = bf16[512,256]{1,0:T(8,128)(2,1)S(1)} collective-permute-done((bf16[512,256]{1,0:T(8,128)(2,1)S(1)}, bf16[512,256]{1,0:T(8,128)(2,1)S(1)}, u32[]{:S(2)}, u32[]{:S(2)}) %collective-permute-start.11) | collective-permute-done | bytes 262176 | tf_op jit(solution)/shard_map/ppermute | solution.py:10
  47.4 0.1 collective-permute-done.10
  47.5 1.5 %fusion.1 = f32[512,256]{1,0:T(8,128)} fusion(bf16[512,2048]{1,0:T(8,128)(2,1)S(1)} %constant_dynamic-update-slice_fusion, bf16[512,256]{1,0:T(8,128)(2,1)S(1)} %collective-permute-done.12, bf16[512,256]{1,0:T(8,128)(2,1)S(1)} %collective-permute-done.11, bf16[512,256]{1,0:T(8,128)(2,1)S(1)} %collective-permute-done.10, bf16[512,256]{1,0:T(8,128)(2,1)S(1)} %fusion.9, ...), kind=kOutput, calls=%fused_computation.2 | convolution fusion | flops 541720576 | bytes 4456448 | tf_op jit(solution)/shard_map/dot_general | solution.py:73
  (3 shorter events, 0.1 us)
Async XLA Ops:
  0.0 8.8 %copy-start = (bf16[512,256]{1,0:T(8,128)(2,1)S(1)}, bf16[512,256]{1,0:T(8,128)(2,1)}, u32[]{:S(2)}) copy-start(bf16[512,256]{1,0:T(8,128)(2,1)} %param.2) | copy-start | bytes 786436
  0.0 13.1 %collective-permute-start = (bf16[512,256]{1,0:T(8,128)(2,1)}, bf16[512,256]{1,0:T(8,128)(2,1)S(1)}, u32[]{:S(2)}, u32[]{:S(2)}) collective-permute-start(bf16[512,256]{1,0:T(8,128)(2,1)} %param.2), channel_id=1, source_target_pairs={{0,4},{1,5},{2,6},{3,7},{4,0},{5,1},{6,2},{7,3},{8,12},{9,13},{10,... | collective-permute-start | bytes 786440 | tf_op jit(solution)/shard_map/ppermute | solution.py:10
  0.0 9.1 %collective-permute-start.2 = (bf16[512,256]{1,0:T(8,128)(2,1)}, bf16[512,256]{1,0:T(8,128)(2,1)S(1)}, u32[]{:S(2)}, u32[]{:S(2)}) collective-permute-start(bf16[512,256]{1,0:T(8,128)(2,1)} %param.2), channel_id=1, source_target_pairs={{0,8},{8,0},{16,24},{24,16},{1,9},{9,1},{17,25},{25,17},{2,10},{10... | collective-permute-start | bytes 786440 | tf_op jit(solution)/shard_map/ppermute | solution.py:10
  1.8 18.1 %collective-permute-start.4 = (bf16[512,256]{1,0:T(8,128)(2,1)}, bf16[512,256]{1,0:T(8,128)(2,1)}, u32[]{:S(2)}, u32[]{:S(2)}) collective-permute-start(bf16[512,256]{1,0:T(8,128)(2,1)} %param.2), channel_id=1, source_target_pairs={{0,2},{1,3},{2,0},{3,1},{4,6},{5,7},{6,4},{7,5},{8,10},{9,11},{10,... | collective-permute-start | bytes 786440 | tf_op jit(solution)/shard_map/ppermute | solution.py:10
  3.4 22.8 %collective-permute-start.6 = (bf16[512,256]{1,0:T(8,128)(2,1)}, bf16[512,256]{1,0:T(8,128)(2,1)}, u32[]{:S(2)}, u32[]{:S(2)}) collective-permute-start(bf16[512,256]{1,0:T(8,128)(2,1)} %param.2), channel_id=1, source_target_pairs={{0,6},{1,7},{2,4},{3,5},{4,2},{5,3},{6,0},{7,1},{8,14},{9,15},{10,... | collective-permute-start | bytes 786440 | tf_op jit(solution)/shard_map/ppermute | solution.py:10
  5.0 21.2 %collective-permute-start.9 = (bf16[512,256]{1,0:T(8,128)(2,1)}, bf16[512,256]{1,0:T(8,128)(2,1)S(1)}, u32[]{:S(2)}, u32[]{:S(2)}) collective-permute-start(bf16[512,256]{1,0:T(8,128)(2,1)} %param.2), channel_id=1, source_target_pairs={{0,24},{8,16},{16,8},{24,0},{1,25},{9,17},{17,9},{25,1},{2,26},{10... | collective-permute-start | bytes 786440 | tf_op jit(solution)/shard_map/ppermute | solution.py:10
  9.1 17.8 %collective-permute-start.8 = (bf16[512,256]{1,0:T(8,128)(2,1)S(1)}, bf16[512,256]{1,0:T(8,128)(2,1)S(1)}, u32[]{:S(2)}, u32[]{:S(2)}) collective-permute-start(bf16[512,256]{1,0:T(8,128)(2,1)S(1)} %copy-done), channel_id=1, source_target_pairs={{0,16},{8,24},{16,0},{24,8},{1,17},{9,25},{17,1},{25,9},{2,18},{10... | collective-permute-start | bytes 786440 | tf_op jit(solution)/shard_map/ppermute | solution.py:10
  13.1 14.2 %collective-permute-start.3 = (bf16[512,256]{1,0:T(8,128)(2,1)S(1)}, bf16[512,256]{1,0:T(8,128)(2,1)S(1)}, u32[]{:S(2)}, u32[]{:S(2)}) collective-permute-start(bf16[512,256]{1,0:T(8,128)(2,1)S(1)} %copy-done), channel_id=1, source_target_pairs={{0,1},{1,0},{2,3},{3,2},{4,5},{5,4},{6,7},{7,6},{8,9},{9,8},{10,11... | collective-permute-start | bytes 786440 | tf_op jit(solution)/shard_map/ppermute | solution.py:10
  20.0 11.5 %collective-permute-start.1 = (bf16[512,256]{1,0:T(8,128)(2,1)S(1)}, bf16[512,256]{1,0:T(8,128)(2,1)S(1)}, u32[]{:S(2)}, u32[]{:S(2)}) collective-permute-start(bf16[512,256]{1,0:T(8,128)(2,1)S(1)} %collective-permute-done), channel_id=1, source_target_pairs={{0,1},{1,0},{2,3},{3,2},{4,5},{5,4},{6,7},{7,6},{8,9},{9,8},{10,11... | collective-permute-start | bytes 786440 | tf_op jit(solution)/shard_map/ppermute | solution.py:10
  26.2 2.7 %collective-permute-start.5 = (bf16[512,256]{1,0:T(8,128)(2,1)}, bf16[512,256]{1,0:T(8,128)(2,1)S(1)}, u32[]{:S(2)}, u32[]{:S(2)}) collective-permute-start(bf16[512,256]{1,0:T(8,128)(2,1)} %collective-permute-done.4), channel_id=1, source_target_pairs={{0,1},{1,0},{2,3},{3,2},{4,5},{5,4},{6,7},{7,6},{8,9},{9,8},{10,11... | collective-permute-start | bytes 786440 | tf_op jit(solution)/shard_map/ppermute | solution.py:10
  26.2 4.2 %collective-permute-start.7 = (bf16[512,256]{1,0:T(8,128)(2,1)}, bf16[512,256]{1,0:T(8,128)(2,1)S(1)}, u32[]{:S(2)}, u32[]{:S(2)}) collective-permute-start(bf16[512,256]{1,0:T(8,128)(2,1)} %collective-permute-done.6), channel_id=1, source_target_pairs={{0,1},{1,0},{2,3},{3,2},{4,5},{5,4},{6,7},{7,6},{8,9},{9,8},{10,11... | collective-permute-start | bytes 786440 | tf_op jit(solution)/shard_map/ppermute | solution.py:10
  32.5 10.2 %collective-permute-start.12 = (bf16[512,256]{1,0:T(8,128)(2,1)S(1)}, bf16[512,256]{1,0:T(8,128)(2,1)S(1)}, u32[]{:S(2)}, u32[]{:S(2)}) collective-permute-start(bf16[512,256]{1,0:T(8,128)(2,1)S(1)} %fusion.9), channel_id=1, source_target_pairs={{0,24},{8,16},{16,8},{24,0},{1,25},{9,17},{17,9},{25,1},{2,26},{10... | collective-permute-start | bytes 786440 | tf_op jit(solution)/shard_map/ppermute | solution.py:10
  35.0 12.3 %collective-permute-start.11 = (bf16[512,256]{1,0:T(8,128)(2,1)S(1)}, bf16[512,256]{1,0:T(8,128)(2,1)S(1)}, u32[]{:S(2)}, u32[]{:S(2)}) collective-permute-start(bf16[512,256]{1,0:T(8,128)(2,1)S(1)} %fusion.9), channel_id=1, source_target_pairs={{0,16},{8,24},{16,0},{24,8},{1,17},{9,25},{17,1},{25,9},{2,18},{10... | collective-permute-start | bytes 786440 | tf_op jit(solution)/shard_map/ppermute | solution.py:10
  35.5 11.9 %collective-permute-start.10 = (bf16[512,256]{1,0:T(8,128)(2,1)S(1)}, bf16[512,256]{1,0:T(8,128)(2,1)S(1)}, u32[]{:S(2)}, u32[]{:S(2)}) collective-permute-start(bf16[512,256]{1,0:T(8,128)(2,1)S(1)} %fusion.9), channel_id=1, source_target_pairs={{0,8},{8,0},{16,24},{24,16},{1,9},{9,1},{17,25},{25,17},{2,10},{10... | collective-permute-start | bytes 786440 | tf_op jit(solution)/shard_map/ppermute | solution.py:10

commit v28 on v26

--- a/solution.py
+++ b/solution.py
@@ -48,15 +48,20 @@
             raw[2 * k] = piece
             raw[2 * k + 1] = _swap(piece, "col", n_col, 1)
         row_pieces = [masked] + [mask_from(raw[t], row_index, col_index ^ t) for t in range(1, n_col)]
+        mask_float = jnp.broadcast_to(
+            local_blocks.astype(jnp.float32)[:, None, :, None], (block_rows, B, block_cols, B)
+        )
         if n_col > 5:
             early = [t for t in range(1, n_col) if t not in (4, 5)]
             tied = lax.optimization_barrier(
-                (row_pieces[4], row_pieces[5], [row_pieces[t] for t in early], col_pieces)
+                (row_pieces[4], row_pieces[5], [row_pieces[t] for t in early], col_pieces,
+                 mask_float)
             )
             row_pieces[4], row_pieces[5] = tied[0], tied[1]
             for t, piece in zip(early, tied[2]):
                 row_pieces[t] = piece
             col_pieces = list(tied[3])
+            mask_float = tied[4]
 
         shift = col_index ^ (row_index * ratio)
         row_f = jnp.zeros((rows, n_col * cols), matrix_in.dtype)
@@ -65,10 +70,8 @@
         square = jnp.dot(
             row_f, jnp.concatenate(col_pieces, axis=0), preferred_element_type=jnp.float32
         )
-        blocks_float = local_blocks.astype(jnp.float32)[:, None, :, None]
-
         def mask_local(x):
-            return (x.reshape(block_rows, B, block_cols, B) * blocks_float).reshape(rows, cols)
+            return (x.reshape(block_rows, B, block_cols, B) * mask_float).reshape(rows, cols)
 
         filtered = mask_local(square).astype(jnp.bfloat16)
         f_pieces = [filtered] + [_swap(filtered, "row", n_row, k) for k in range(1, n_row)]

time: 47.1 us -> 52.7 us (1.12)
  the two profiles are of different devices: /device:TPU:16 before, /device:TPU:0 now
where the time goes in v28:
time: 52.7 us; the launch traced here: 52.5 us
  waiting for transfers between devices  27 us (51%)
  starting transfers between devices  13.3 us (25%)
  local copies, waits for them, and re-layouts  6.33 us (12%)
  other arithmetic  3.3 us (6%)
  matrix products  2.23 us (4%)
    ppermute x13, waiting for transfers between devices, _swap(): return lax.ppermute(x, axis, [(i, i ^ d) for i in range(size)])  27 us
    ppermute x13, starting transfers between devices, _swap(): return lax.ppermute(x, axis, [(i, i ^ d) for i in range(size)])  13.3 us
    mul x10, local copies, waits for them, and re-layouts, mask_from(): return (x4 * blocks[:, None, :, None]).reshape(rows, cols)  2.04 us
    reshape x2, local copies, waits for them, and re-layouts, mask_local(): x.reshape(block_rows, B, block_cols, B) * mask_float  1.57 us
    dot_general x1, matrix products, body(): jnp.dot(row_f, jnp.concatenate(col_pieces, axis=0), preferred_element_typ...  1.51 us
    unnamed x6, local copies, waits for them, and re-layouts  1.34 us
  transfers between devices with their start and end apart: 13, of which 6 were waited for; matrix products, arithmetic and copies ran while one was open for 10% of the time, Pallas kernels for 0%

profile of v28, /device:TPU:0, one launch (start us, length us, event | category | flops | bytes accessed | tf_op | source)
XLA Modules:
  0.0 52.5 jit_solution(17911252518279015043)
XLA Ops:
  0.0 2.9 %collective-permute-start.2 = (bf16[512,256]{1,0:T(8,128)(2,1)}, bf16[512,256]{1,0:T(8,128)(2,1)S(1)}, u32[]{:S(2)}, u32[]{:S(2)}) collective-permute-start(bf16[512,256]{1,0:T(8,128)(2,1)} %param.2), channel_id=1, source_target_pairs={{0,8},{8,0},{16,24},{24,16},{1,9},{9,1},{17,25},{25,17},{2,10},{10... | collective-permute-start | bytes 786440 | tf_op jit(solution)/shard_map/ppermute | solution.py:10
  2.9 3.6 %collective-permute-start.6 = (bf16[512,256]{1,0:T(8,128)(2,1)}, bf16[512,256]{1,0:T(8,128)(2,1)S(1)}, u32[]{:S(2)}, u32[]{:S(2)}) collective-permute-start(bf16[512,256]{1,0:T(8,128)(2,1)} %param.2), channel_id=1, source_target_pairs={{0,6},{1,7},{2,4},{3,5},{4,2},{5,3},{6,0},{7,1},{8,14},{9,15},{10,... | collective-permute-start | bytes 786440 | tf_op jit(solution)/shard_map/ppermute | solution.py:10
  6.5 0.0 collective-permute-start.4
  6.5 0.8 %collective-permute-start = (bf16[512,256]{1,0:T(8,128)(2,1)}, bf16[512,256]{1,0:T(8,128)(2,1)S(1)}, u32[]{:S(2)}, u32[]{:S(2)}) collective-permute-start(bf16[512,256]{1,0:T(8,128)(2,1)} %param.2), channel_id=1, source_target_pairs={{0,4},{1,5},{2,6},{3,7},{4,0},{5,1},{6,2},{7,3},{8,12},{9,13},{10,... | collective-permute-start | bytes 786440 | tf_op jit(solution)/shard_map/ppermute | solution.py:10
  7.3 1.5 %collective-permute-start.9 = (bf16[512,256]{1,0:T(8,128)(2,1)}, bf16[512,256]{1,0:T(8,128)(2,1)S(1)}, u32[]{:S(2)}, u32[]{:S(2)}) collective-permute-start(bf16[512,256]{1,0:T(8,128)(2,1)} %param.2), channel_id=1, source_target_pairs={{0,24},{8,16},{16,8},{24,0},{1,25},{9,17},{17,9},{25,1},{2,26},{10... | collective-permute-start | bytes 786440 | tf_op jit(solution)/shard_map/ppermute | solution.py:10
  8.8 0.7 %convert_element_type.30 = bf16[16,16]{1,0:T(8,128)(2,1)S(1)} convert(s32[16,16]{1,0:T(8,128)} %param.3) | non-fusion elementwise | flops 256 | bytes 1536 | tf_op jit(solution)/shard_map/convert_element_type | solution.py:28
  9.5 0.0 copy-start
  9.5 0.8 %dynamic-slice_convert_fusion = (f32[4,2]{1,0:T(4,128)S(1)}, bf16[4,2]{1,0:T(4,128)(2,1)S(1)}) fusion(s32[16,16]{1,0:T(8,128)} %param.3, s32[]{:T(128)S(6)} %select_n.70, s32[]{:T(128)S(6)} %select_n.71), kind=kLoop, calls=%fused_computation.39 | loop fusion | flops 16 | bytes 88 | tf_op jit(solution)/shard_map/convert_element_type | solution.py:52
  10.4 0.6 %broadcast_in_dim.9 = bf16[512,2,128]{2,1,0:T(2,128)(2,1)S(1)} broadcast(bf16[512,2]{1,0:T(8,128)(2,1)S(1)} %bitcast.70), dimensions={0,1} | broadcast | bytes 264192 | tf_op jit(solution)/shard_map/broadcast_in_dim | solution.py:26
  11.0 0.2 broadcast_in_dim.10
  11.2 0.0 copy-done
  11.2 0.8 %constant_dynamic-update-slice_fusion.7 = (bf16[512,2048]{1,0:T(8,128)(2,1)S(1)}, bf16[512,256]{1,0:T(8,128)(2,1)}) fusion(bf16[512,2048]{1,0:T(8,128)(2,1)S(1)} %broadcast_in_dim.10, s32[]{:T(128)S(6)} %select_n.72, bf16[512,256]{1,0:T(8,128)(2,1)S(1)} %copy-done, bf16[64,8,2,128]{3,2,1,0:T(2,128)(2,1)S(1)} %bitcast.69), kind=kLoop, calls=%fused_computation.38 | loop fusion | flops 524288 | bytes 1048580 | tf_op jit(solution)/shard_map/dynamic_update_slice | solution.py:69
  12.0 0.1 fusion.18
  12.2 0.0 collective-permute-done.2
  12.2 0.4 collective-permute-start.8
  12.5 0.2 mul.240
  12.7 0.1 bitcast_multiply_fusion.2
  12.8 1.4 %collective-permute-done.6 = bf16[512,256]{1,0:T(8,128)(2,1)S(1)} collective-permute-done((bf16[512,256]{1,0:T(8,128)(2,1)}, bf16[512,256]{1,0:T(8,128)(2,1)S(1)}, u32[]{:S(2)}, u32[]{:S(2)}) %collective-permute-start.6) | collective-permute-done | bytes 262176 | tf_op jit(solution)/shard_map/ppermute | solution.py:10
  14.2 0.0 collective-permute-start.3
  14.2 0.2 mul.232
  14.4 0.1 bitcast_multiply_fusion.4
  14.5 4.9 %collective-permute-done.4 = bf16[512,256]{1,0:T(8,128)(2,1)S(1)} collective-permute-done((bf16[512,256]{1,0:T(8,128)(2,1)}, bf16[512,256]{1,0:T(8,128)(2,1)S(1)}, u32[]{:S(2)}, u32[]{:S(2)}) %collective-permute-start.4) | collective-permute-done | bytes 262176 | tf_op jit(solution)/shard_map/ppermute | solution.py:10
  19.4 0.0 collective-permute-start.7
  19.4 0.2 mul.224
  19.6 0.1 bitcast_multiply_fusion.6
  19.7 9.1 %collective-permute-done = bf16[512,256]{1,0:T(8,128)(2,1)S(1)} collective-permute-done((bf16[512,256]{1,0:T(8,128)(2,1)}, bf16[512,256]{1,0:T(8,128)(2,1)S(1)}, u32[]{:S(2)}, u32[]{:S(2)}) %collective-permute-start) | collective-permute-done | bytes 262176 | tf_op jit(solution)/shard_map/ppermute | solution.py:10
  28.8 0.0 collective-permute-start.5
  28.8 0.2 mul.212
  29.0 0.1 bitcast_multiply_fusion.9
  29.1 0.0 collective-permute-done.9
  29.1 0.6 %collective-permute-start.1 = (bf16[512,256]{1,0:T(8,128)(2,1)S(1)}, bf16[512,256]{1,0:T(8,128)(2,1)S(1)}, u32[]{:S(2)}, u32[]{:S(2)}) collective-permute-start(bf16[512,256]{1,0:T(8,128)(2,1)S(1)} %collective-permute-done), channel_id=1, source_target_pairs={{0,1},{1,0},{2,3},{3,2},{4,5},{5,4},{6,7},{7,6},{8,9},{9,8},{10,11... | collective-permute-start | bytes 786440 | tf_op jit(solution)/shard_map/ppermute | solution.py:10
  29.6 0.2 mul.248
  29.8 0.1 bitcast_multiply_fusion
  29.9 0.0 collective-permute-done.8
  29.9 0.2 mul.244
  30.2 0.0 collective-permute-done.3
  30.2 0.2 mul.220
  30.4 0.0 collective-permute-done.7
  30.4 0.2 mul.236
  30.7 0.0 collective-permute-done.5
  30.7 0.2 mul.228
  31.0 0.0 collective-permute-done.1
  31.0 0.2 mul.216
  31.2 0.0 copy-start.1
  31.2 0.2 broadcast_in_dim.11
  31.7 0.5 copy-done.1
  32.2 1.5 %fusion.1 = f32[512,256]{1,0:T(8,128)} fusion(bf16[512,2048]{1,0:T(8,128)(2,1)S(1)} %constant_dynamic-update-slice_fusion, bf16[512,256]{1,0:T(8,128)(2,1)S(1)} %bitcast_multiply_fusion, bf16[512,256]{1,0:T(8,128)(2,1)S(1)} %bitcast_multiply_fusion.1, bf16[512,256]{1,0:T(8,128)(2,1)S(1)} %bitcast_multiply_fusion.2, bf16[512,256]{1,0:T(8,128)(2,1)S(1)} %copy-done.1), kind=kOutput, calls=%fused_computation.2 | convolution fusion | flops 541065216 | bytes 3670016 | tf_op jit(solution)/shard_map/dot_general | solution.py:70
  33.7 1.3 %reshape.56 = f32[4,128,2,128]{3,2,1,0:T(2,128)S(1)} reshape(f32[512,256]{1,0:T(8,128)} %fusion.1) | data formatting | bytes 1048576 | tf_op jit(solution)/shard_map/reshape | solution.py:74
  35.0 0.3 multiply_convert_fusion
  35.3 0.6 %collective-permute-start.10 = (bf16[512,256]{1,0:T(8,128)(2,1)S(1)}, bf16[512,256]{1,0:T(8,128)(2,1)S(1)}, u32[]{:S(2)}, u32[]{:S(2)}) collective-permute-start(bf16[512,256]{1,0:T(8,128)(2,1)S(1)} %bitcast.71), channel_id=1, source_target_pairs={{0,8},{8,0},{16,24},{24,16},{1,9},{9,1},{17,25},{25,17},{2,10},{10... | collective-permute-start | bytes 786440 | tf_op jit(solution)/shard_map/ppermute | solution.py:10
  35.9 1.5 %collective-permute-start.11 = (bf16[512,256]{1,0:T(8,128)(2,1)S(1)}, bf16[512,256]{1,0:T(8,128)(2,1)S(1)}, u32[]{:S(2)}, u32[]{:S(2)}) collective-permute-start(bf16[512,256]{1,0:T(8,128)(2,1)S(1)} %bitcast.72), channel_id=1, source_target_pairs={{0,16},{8,24},{16,0},{24,8},{1,17},{9,25},{17,1},{25,9},{2,18},{10... | collective-permute-start | bytes 786440 | tf_op jit(solution)/shard_map/ppermute | solution.py:10
  37.4 1.4 %collective-permute-start.12 = (bf16[512,256]{1,0:T(8,128)(2,1)S(1)}, bf16[512,256]{1,0:T(8,128)(2,1)S(1)}, u32[]{:S(2)}, u32[]{:S(2)}) collective-permute-start(bf16[512,256]{1,0:T(8,128)(2,1)S(1)} %bitcast.73), channel_id=1, source_target_pairs={{0,24},{8,16},{16,8},{24,0},{1,25},{9,17},{17,9},{25,1},{2,26},{10... | collective-permute-start | bytes 786440 | tf_op jit(solution)/shard_map/ppermute | solution.py:10
  38.9 5.7 %collective-permute-done.10 = bf16[512,256]{1,0:T(8,128)(2,1)S(1)} collective-permute-done((bf16[512,256]{1,0:T(8,128)(2,1)S(1)}, bf16[512,256]{1,0:T(8,128)(2,1)S(1)}, u32[]{:S(2)}, u32[]{:S(2)}) %collective-permute-start.10) | collective-permute-done | bytes 262176 | tf_op jit(solution)/shard_map/ppermute | solution.py:10
  44.5 4.2 %collective-permute-done.11 = bf16[512,256]{1,0:T(8,128)(2,1)S(1)} collective-permute-done((bf16[512,256]{1,0:T(8,128)(2,1)S(1)}, bf16[512,256]{1,0:T(8,128)(2,1)S(1)}, u32[]{:S(2)}, u32[]{:S(2)}) %collective-permute-start.11) | collective-permute-done | bytes 262176 | tf_op jit(solution)/shard_map/ppermute | solution.py:10
  48.7 1.6 %collective-permute-done.12 = bf16[512,256]{1,0:T(8,128)(2,1)S(1)} collective-permute-done((bf16[512,256]{1,0:T(8,128)(2,1)S(1)}, bf16[512,256]{1,0:T(8,128)(2,1)S(1)}, u32[]{:S(2)}, u32[]{:S(2)}) %collective-permute-start.12) | collective-permute-done | bytes 262176 | tf_op jit(solution)/shard_map/ppermute | solution.py:10
  50.4 0.7 %fusion = f32[512,256]{1,0:T(8,128)S(1)} fusion(bf16[512,2048]{1,0:T(8,128)(2,1)S(1)} %constant_dynamic-update-slice_fusion, bf16[512,256]{1,0:T(8,128)(2,1)S(1)} %collective-permute-done.12, bf16[512,256]{1,0:T(8,128)(2,1)S(1)} %collective-permute-done.11, bf16[512,256]{1,0:T(8,128)(2,1)S(1)} %collective-permute-done.10, bf16[512,256]{1,0:T(8,128)(2,1)S(1)} %bitcast.74, ...), kind=kOutput, calls=%fused_computation.1 | convolution fusion | flops 541589504 | bytes 3932160 | tf_op jit(solution)/shard_map/dot_general | solution.py:78
  51.1 0.3 reshape.57
  51.4 0.3 mul.261
  51.7 0.8 %copy.30 = f32[64,8,2,128]{3,1,2,0:T(8,128)} copy(f32[64,8,2,128]{3,2,1,0:T(2,128)S(1)} %bitcast.57) | data formatting | bytes 1048576
  (14 shorter events, 0.5 us)
Async XLA Ops:
  0.0 12.2 %collective-permute-start.2 = (bf16[512,256]{1,0:T(8,128)(2,1)}, bf16[512,256]{1,0:T(8,128)(2,1)S(1)}, u32[]{:S(2)}, u32[]{:S(2)}) collective-permute-start(bf16[512,256]{1,0:T(8,128)(2,1)} %param.2), channel_id=1, source_target_pairs={{0,8},{8,0},{16,24},{24,16},{1,9},{9,1},{17,25},{25,17},{2,10},{10... | collective-permute-start | bytes 786440 | tf_op jit(solution)/shard_map/ppermute | solution.py:10
  2.9 11.3 %collective-permute-start.6 = (bf16[512,256]{1,0:T(8,128)(2,1)}, bf16[512,256]{1,0:T(8,128)(2,1)S(1)}, u32[]{:S(2)}, u32[]{:S(2)}) collective-permute-start(bf16[512,256]{1,0:T(8,128)(2,1)} %param.2), channel_id=1, source_target_pairs={{0,6},{1,7},{2,4},{3,5},{4,2},{5,3},{6,0},{7,1},{8,14},{9,15},{10,... | collective-permute-start | bytes 786440 | tf_op jit(solution)/shard_map/ppermute | solution.py:10
  6.5 12.9 %collective-permute-start.4 = (bf16[512,256]{1,0:T(8,128)(2,1)}, bf16[512,256]{1,0:T(8,128)(2,1)S(1)}, u32[]{:S(2)}, u32[]{:S(2)}) collective-permute-start(bf16[512,256]{1,0:T(8,128)(2,1)} %param.2), channel_id=1, source_target_pairs={{0,2},{1,3},{2,0},{3,1},{4,6},{5,7},{6,4},{7,5},{8,10},{9,11},{10,... | collective-permute-start | bytes 786440 | tf_op jit(solution)/shard_map/ppermute | solution.py:10
  6.5 22.2 %collective-permute-start = (bf16[512,256]{1,0:T(8,128)(2,1)}, bf16[512,256]{1,0:T(8,128)(2,1)S(1)}, u32[]{:S(2)}, u32[]{:S(2)}) collective-permute-start(bf16[512,256]{1,0:T(8,128)(2,1)} %param.2), channel_id=1, source_target_pairs={{0,4},{1,5},{2,6},{3,7},{4,0},{5,1},{6,2},{7,3},{8,12},{9,13},{10,... | collective-permute-start | bytes 786440 | tf_op jit(solution)/shard_map/ppermute | solution.py:10
  7.3 21.7 %collective-permute-start.9 = (bf16[512,256]{1,0:T(8,128)(2,1)}, bf16[512,256]{1,0:T(8,128)(2,1)S(1)}, u32[]{:S(2)}, u32[]{:S(2)}) collective-permute-start(bf16[512,256]{1,0:T(8,128)(2,1)} %param.2), channel_id=1, source_target_pairs={{0,24},{8,16},{16,8},{24,0},{1,25},{9,17},{17,9},{25,1},{2,26},{10... | collective-permute-start | bytes 786440 | tf_op jit(solution)/shard_map/ppermute | solution.py:10
  9.5 1.7 %copy-start = (bf16[512,256]{1,0:T(8,128)(2,1)S(1)}, bf16[512,256]{1,0:T(8,128)(2,1)}, u32[]{:S(2)}) copy-start(bf16[512,256]{1,0:T(8,128)(2,1)} %param.2) | copy-start | bytes 786436
  12.2 17.7 %collective-permute-start.8 = (bf16[512,256]{1,0:T(8,128)(2,1)}, bf16[512,256]{1,0:T(8,128)(2,1)S(1)}, u32[]{:S(2)}, u32[]{:S(2)}) collective-permute-start(bf16[512,256]{1,0:T(8,128)(2,1)} %param.2), channel_id=1, source_target_pairs={{0,16},{8,24},{16,0},{24,8},{1,17},{9,25},{17,1},{25,9},{2,18},{10... | collective-permute-start | bytes 786440 | tf_op jit(solution)/shard_map/ppermute | solution.py:10
  14.2 15.9 %collective-permute-start.3 = (bf16[512,256]{1,0:T(8,128)(2,1)}, bf16[512,256]{1,0:T(8,128)(2,1)S(1)}, u32[]{:S(2)}, u32[]{:S(2)}) collective-permute-start(bf16[512,256]{1,0:T(8,128)(2,1)} %param.2), channel_id=1, source_target_pairs={{0,1},{1,0},{2,3},{3,2},{4,5},{5,4},{6,7},{7,6},{8,9},{9,8},{10,11... | collective-permute-start | bytes 786440 | tf_op jit(solution)/shard_map/ppermute | solution.py:10
  19.4 11.0 %collective-permute-start.7 = (bf16[512,256]{1,0:T(8,128)(2,1)S(1)}, bf16[512,256]{1,0:T(8,128)(2,1)S(1)}, u32[]{:S(2)}, u32[]{:S(2)}) collective-permute-start(bf16[512,256]{1,0:T(8,128)(2,1)S(1)} %collective-permute-done.6), channel_id=1, source_target_pairs={{0,1},{1,0},{2,3},{3,2},{4,5},{5,4},{6,7},{7,6},{8,9},{9,8},{10,11... | collective-permute-start | bytes 786440 | tf_op jit(solution)/shard_map/ppermute | solution.py:10
  28.8 1.9 %collective-permute-start.5 = (bf16[512,256]{1,0:T(8,128)(2,1)S(1)}, bf16[512,256]{1,0:T(8,128)(2,1)S(1)}, u32[]{:S(2)}, u32[]{:S(2)}) collective-permute-start(bf16[512,256]{1,0:T(8,128)(2,1)S(1)} %collective-permute-done.4), channel_id=1, source_target_pairs={{0,1},{1,0},{2,3},{3,2},{4,5},{5,4},{6,7},{7,6},{8,9},{9,8},{10,11... | collective-permute-start | bytes 786440 | tf_op jit(solution)/shard_map/ppermute | solution.py:10
  29.1 1.9 %collective-permute-start.1 = (bf16[512,256]{1,0:T(8,128)(2,1)S(1)}, bf16[512,256]{1,0:T(8,128)(2,1)S(1)}, u32[]{:S(2)}, u32[]{:S(2)}) collective-permute-start(bf16[512,256]{1,0:T(8,128)(2,1)S(1)} %collective-permute-done), channel_id=1, source_target_pairs={{0,1},{1,0},{2,3},{3,2},{4,5},{5,4},{6,7},{7,6},{8,9},{9,8},{10,11... | collective-permute-start | bytes 786440 | tf_op jit(solution)/shard_map/ppermute | solution.py:10
  31.2 1.0 %copy-start.1 = (bf16[512,256]{1,0:T(8,128)(2,1)S(1)}, bf16[512,256]{1,0:T(8,128)(2,1)}, u32[]{:S(2)}) copy-start(bf16[512,256]{1,0:T(8,128)(2,1)} %get-tuple-element.26) | copy-start | bytes 786436
  35.3 9.2 %collective-permute-start.10 = (bf16[512,256]{1,0:T(8,128)(2,1)S(1)}, bf16[512,256]{1,0:T(8,128)(2,1)S(1)}, u32[]{:S(2)}, u32[]{:S(2)}) collective-permute-start(bf16[512,256]{1,0:T(8,128)(2,1)S(1)} %bitcast.71), channel_id=1, source_target_pairs={{0,8},{8,0},{16,24},{24,16},{1,9},{9,1},{17,25},{25,17},{2,10},{10... | collective-permute-start | bytes 786440 | tf_op jit(solution)/shard_map/ppermute | solution.py:10
  35.9 12.8 %collective-permute-start.11 = (bf16[512,256]{1,0:T(8,128)(2,1)S(1)}, bf16[512,256]{1,0:T(8,128)(2,1)S(1)}, u32[]{:S(2)}, u32[]{:S(2)}) collective-permute-start(bf16[512,256]{1,0:T(8,128)(2,1)S(1)} %bitcast.72), channel_id=1, source_target_pairs={{0,16},{8,24},{16,0},{24,8},{1,17},{9,25},{17,1},{25,9},{2,18},{10... | collective-permute-start | bytes 786440 | tf_op jit(solution)/shard_map/ppermute | solution.py:10
  37.4 12.9 %collective-permute-start.12 = (bf16[512,256]{1,0:T(8,128)(2,1)S(1)}, bf16[512,256]{1,0:T(8,128)(2,1)S(1)}, u32[]{:S(2)}, u32[]{:S(2)}) collective-permute-start(bf16[512,256]{1,0:T(8,128)(2,1)S(1)} %bitcast.73), channel_id=1, source_target_pairs={{0,24},{8,16},{16,8},{24,0},{1,25},{9,17},{17,9},{25,1},{2,26},{10... | collective-permute-start | bytes 786440 | tf_op jit(solution)/shard_map/ppermute | solution.py:10
